TPU v7x, 32 devices: a whole 2x2x4 slice. The times are simulated.
32 devices in a mesh: pairs: 2 (over x), row: 16 (over z, y, core).
Axes of the slice: x: 2, y: 2, z: 4, core: 2. Of those that a mesh axis runs over, the one named last changes fastest.
Arguments:
- frame_one: bfloat16 [128, 512, 128], P(('pairs', 'row')), parts along dimension 0, may hold values from -100 to 100
- frame_two: bfloat16 [128, 512, 128], P(('pairs', 'row')), parts along dimension 0, may hold values from -20 to 20
- tile_lists: int32 [128, 9], P(('pairs', 'row')), parts along dimension 0, may hold values from -1 to 63, as said below
- conv_one: bfloat16 [3, 3, 128, 128], replicated, may hold values from -0.1875 to 0.1875
- conv_two: bfloat16 [3, 3, 128, 128], replicated, may hold values from -0.1875 to 0.1875
Outputs:
- refined: bfloat16 [128, 512, 128], P(('pairs', 'row')), parts along dimension 0
There are 2 independent parts, one for each index of `pairs`. A program takes and returns all parts, laid end to end along the dimension named above; an argument that names none is the same for every part. Nothing has to cross between parts.
Inputs may be any that keep to these rules, and one draw needn't show every extreme that they name: `tile_lists`: each query tile names 1 to 9 frame-2 tiles in its first slots and -1 in the rest; some tile names 9. The lists of the 4 query tiles of one device never name two different tiles held by the same device; one tile may be named by several of them.
All inputs are finite; a program needn't handle non-finite values.
Results may differ from a plain program's by a relative error of at most 0.0021.
Values may be sent and summed in bfloat16 or wider, within the bound.
No kernel may reach another device: no remote copies, remote signals or barrier semaphores. Data moves between devices by JAX's collectives and lax.ppermute only.
A program may use at most 64 MiB of HBM per device.

v0:
```python
import functools

import jax
import jax.numpy as jnp
from jax import lax
from jax.experimental import pallas as pl
from jax.experimental.pallas import tpu as pltpu
from jax.sharding import PartitionSpec as P


def halo_rows(cells, axis, width):
    count = lax.axis_size(axis)
    ends = count - 1
    head = cells[:width]
    tail = cells[cells.shape[0] - width :]
    from_above = lax.ppermute(tail, axis, [(i, i + 1) for i in range(ends)])
    from_below = lax.ppermute(head, axis, [(i + 1, i) for i in range(ends)])
    return jnp.concatenate([from_above, cells, from_below], axis=0)


def convolve_rows(padded, weights, out_rows, out_cols):
    channels = padded.shape[2]
    summed = jnp.zeros((out_rows * out_cols, channels), jnp.float32)
    for row_shift in range(3):
        for col_shift in range(3):
            window = padded[row_shift : row_shift + out_rows, col_shift : col_shift + out_cols]
            window = window.reshape(out_rows * out_cols, channels)
            summed = summed + jnp.dot(
                window, weights[row_shift, col_shift], preferred_element_type=jnp.float32
            )
    return summed.reshape(out_rows, out_cols, channels)


def pad_columns(image):
    return jnp.pad(image, ((0, 0), (1, 1), (0, 0)))


def attend_kernel(owner_ref, count_ref, q_ref, k_ref, m_in, t_in, a_in, m_out, t_out, a_out, s_ref, *, scale):
    t = pl.program_id(0)
    n = count_ref[t]
    qt = q_ref[0]
    m_old = m_in[0]

    def score(j, m):
        kc = k_ref[owner_ref[t, j]]
        s = jnp.dot(kc, qt, preferred_element_type=jnp.float32) * scale
        s_ref[j] = s
        return jnp.maximum(m, jnp.max(s, axis=0, keepdims=True))

    m_new = lax.fori_loop(0, n, score, m_old)
    alpha = jnp.exp(m_old - m_new)
    m_out[0] = m_new
    a_out[0] = a_in[0] * alpha

    def mix(j, tot):
        p = jnp.exp(s_ref[j] - m_new)
        kc = k_ref[owner_ref[t, j]]
        a_out[0] += lax.dot_general(
            kc, p.astype(jnp.bfloat16), (((0,), (0,)), ((), ())),
            preferred_element_type=jnp.float32,
        )
        return tot + jnp.sum(p, axis=0, keepdims=True)

    t_out[0] = lax.fori_loop(0, n, mix, t_in[0] * alpha)


def attend_chunk(state, query_t, chunk, slot_owner, counts, scale):
    tiles, channels, tile_size = query_t.shape
    owners, chunk_len, _ = chunk.shape
    slots = slot_owner.shape[1]
    m, tot, acc = state
    row_spec = pl.BlockSpec((1, 1, tile_size), lambda t, o, c: (t, 0, 0))
    acc_spec = pl.BlockSpec((1, channels, tile_size), lambda t, o, c: (t, 0, 0))
    grid_spec = pltpu.PrefetchScalarGridSpec(
        num_scalar_prefetch=2,
        grid=(tiles,),
        in_specs=[
            pl.BlockSpec((1, channels, tile_size), lambda t, o, c: (t, 0, 0)),
            pl.BlockSpec((owners, chunk_len, channels), lambda t, o, c: (0, 0, 0)),
            row_spec,
            row_spec,
            acc_spec,
        ],
        out_specs=[row_spec, row_spec, acc_spec],
        scratch_shapes=[pltpu.VMEM((slots, chunk_len, tile_size), jnp.float32)],
    )
    return pl.pallas_call(
        functools.partial(attend_kernel, scale=scale),
        grid_spec=grid_spec,
        out_shape=[
            jax.ShapeDtypeStruct(m.shape, jnp.float32),
            jax.ShapeDtypeStruct(tot.shape, jnp.float32),
            jax.ShapeDtypeStruct(acc.shape, jnp.float32),
        ],
        input_output_aliases={4: 0, 5: 1, 6: 2},
        compiler_params=pltpu.CompilerParams(vmem_limit_bytes=48 * 1024 * 1024),
    )(slot_owner, counts, query_t, chunk, m, tot, acc)


def on_device(frame_one, frame_two, tile_lists, conv_one, conv_two):
    band_rows, band_width, channels = frame_one.shape
    per_device = tile_lists.shape[0]
    tile_cols = band_width // per_device
    tile_size = band_rows * tile_cols
    owners = lax.axis_size("row")
    scale = float(channels) ** (-0.5)

    def band_to_tiles(band):
        return (
            band.reshape(band_rows, per_device, tile_cols, channels)
            .transpose(1, 0, 2, 3)
            .reshape(per_device, tile_size, channels)
        )

    query_tiles = band_to_tiles(frame_one)
    own_keys = band_to_tiles(frame_two)
    valid = tile_lists >= 0
    slot_owner = jnp.where(valid, tile_lists // per_device, 0).astype(jnp.int32)
    counts = jnp.sum(valid.astype(jnp.int32), axis=1)
    owner_iota = jnp.arange(owners, dtype=jnp.int32)
    matches = (slot_owner[:, :, None] == owner_iota[None, None, :]) & valid[:, :, None]
    wanted = jnp.max(jnp.where(matches, (tile_lists % per_device)[:, :, None], -1), axis=(0, 1))
    asked = lax.all_to_all(
        wanted.reshape(owners, 1), "row", split_axis=0, concat_axis=0, tiled=True
    )[:, 0]
    picked = jnp.take(own_keys, jnp.maximum(asked, 0), axis=0)
    outgoing = jnp.where((asked >= 0)[:, None, None], picked, jnp.zeros_like(picked))
    query_t = query_tiles.transpose(0, 2, 1)
    pieces = 4
    chunk_len = tile_size // pieces
    state = (
        jnp.full((per_device, 1, tile_size), -jnp.inf, jnp.float32),
        jnp.zeros((per_device, 1, tile_size), jnp.float32),
        jnp.zeros((per_device, channels, tile_size), jnp.float32),
    )
    previous = None
    for piece in range(pieces):
        sending = outgoing[:, piece * chunk_len : (piece + 1) * chunk_len]
        if previous is not None:
            previous, sending, state = lax.optimization_barrier((previous, sending, state))
        current = lax.all_to_all(sending, "row", split_axis=0, concat_axis=0, tiled=True)
        if previous is not None:
            state = attend_chunk(state, query_t, previous, slot_owner, counts, scale)
        previous = current
    state = attend_chunk(state, query_t, previous, slot_owner, counts, scale)
    warped_tiles = (state[2] / state[1]).astype(jnp.bfloat16).transpose(0, 2, 1)
    warped = (
        warped_tiles.reshape(per_device, band_rows, tile_cols, channels)
        .transpose(1, 0, 2, 3)
        .reshape(band_rows, band_width, channels)
    )
    me = lax.axis_index("row")
    extended = halo_rows(warped, "row", 2)
    hidden = jax.nn.relu(
        convolve_rows(pad_columns(extended), conv_one, band_rows + 2, band_width)
    ).astype(jnp.bfloat16)
    row_ids = jnp.arange(band_rows + 2)
    inside = ((row_ids > 0) | (me > 0)) & ((row_ids < band_rows + 1) | (me < owners - 1))
    hidden = jnp.where(inside[:, None, None], hidden, jnp.zeros_like(hidden))
    branch = convolve_rows(pad_columns(hidden), conv_two, band_rows, band_width)
    return (frame_one.astype(jnp.float32) + branch).astype(jnp.bfloat16)


def solution(mesh):
    in_specs = (
        P(("pairs", "row"), None, None),
        P(("pairs", "row"), None, None),
        P(("pairs", "row"), None),
        P(),
        P(),
    )
    out_specs = P(("pairs", "row"), None, None)
    return jax.shard_map(
        on_device, mesh=mesh, in_specs=in_specs, out_specs=out_specs, check_vma=False
    )
```

profile of v0, /device:TPU:9, one launch (start us, length us, event | category | flops | bytes accessed | tf_op | source)
XLA Modules:
  0.0 128.7 jit_solution(15148960644992629037)
XLA Ops:
  0.0 0.8 convert_reduce_fusion
  0.8 0.7 fusion.44.owner_ref
  1.9 0.7 copy.36
  2.6 6.6 %all-to-all-start = ((s32[16,1,1]{2,1,0:T(1,128)}), s32[16,1,1]{2,1,0:T(1,128)S(1)}, u32[]{:S(2)}, u32[]{:S(2)}) async-start(s32[16,1,1]{2,1,0:T(1,128)} %copy.36), calls=%async_computation | async-start | bytes 16384 | tf_op jit(solution)/shard_map/all_to_all | solution.py:123
  9.2 1.1 copy.37
  10.3 3.5 %all-to-all-done = s32[16,1,1]{2,1,0:T(1,128)S(1)} async-done(((s32[16,1,1]{2,1,0:T(1,128)}), s32[16,1,1]{2,1,0:T(1,128)S(1)}, u32[]{:S(2)}, u32[]{:S(2)}) %all-to-all-start) | async-done | bytes 96 | tf_op jit(solution)/shard_map/all_to_all | solution.py:123
  13.8 0.4 maximum_reduce_fusion
  14.2 1.0 gather_fusion
  15.2 0.7 compare_reduce_fusion.1
  15.8 0.3 select_select_fusion
  16.2 1.2 fusion.46
  17.3 18.6 %all_to_all.29.k_ref = bf16[16,128,128]{2,1,0:T(8,128)(2,1)S(1)} all-to-all(bf16[16,128,128]{2,1,0:T(8,128)(2,1)S(1)} %get-tuple-element.64), channel_id=1, replica_groups=mesh['pairs'=2,'row'=16] {'row'}, dimensions={0} | all-to-all | bytes 1048576 | tf_op jit(solution)/shard_map/all_to_all | solution.py:141
  35.9 4.4 %all-to-all-start.2 = ((bf16[16,128,128]{2,1,0:T(8,128)(2,1)}), bf16[16,128,128]{2,1,0:T(8,128)(2,1)S(1)}, u32[]{:S(2)}, u32[]{:S(2)}) async-start(bf16[16,128,128]{2,1,0:T(8,128)(2,1)} %get-tuple-element.31), calls=%async_computation.2 | async-start | bytes 1048576 | tf_op jit(solution)/shard_map/all_to_all | solution.py:141
  40.3 0.3 copy.32
  40.6 0.2 reshape.120
  40.9 14.6 %shard_map.55 = (f32[4,1,512]{2,1,0:T(1,128)S(1)}, f32[4,1,512]{2,1,0:T(1,128)S(1)}, f32[4,128,512]{2,1,0:T(8,128)S(1)}) custom-call(s32[4,9]{1,0:T(4,128)S(1)} %fusion.44.owner_ref, s32[4]{0:T(128)S(1)} %get-tuple-element.59.count_ref, bf16[4,128,512]{2,1,0:T(8,128)(2,1)S(1)} %bitcast.114, ...), custom_call_target="tpu_custom_call", output_to_operand_aliasing={{0}: (4, {}), {1}: (5, {}), {2}: (6, {})} | custom-call | tf_op jit(solution)/shard_map/pallas_call | solution.py:87
  55.6 4.8 %all-to-all-start.3 = ((bf16[16,128,128]{2,1,0:T(8,128)(2,1)}), bf16[16,128,128]{2,1,0:T(8,128)(2,1)S(1)}, u32[]{:S(2)}, u32[]{:S(2)}) async-start(bf16[16,128,128]{2,1,0:T(8,128)(2,1)} %get-tuple-element.39), calls=%async_computation.3 | async-start | bytes 1048576 | tf_op jit(solution)/shard_map/all_to_all | solution.py:141
  60.4 14.6 %shard_map.56 = (f32[4,1,512]{2,1,0:T(1,128)S(1)}, f32[4,1,512]{2,1,0:T(1,128)S(1)}, f32[4,128,512]{2,1,0:T(8,128)S(1)}) custom-call(s32[4,9]{1,0:T(4,128)S(1)} %fusion.44.owner_ref, s32[4]{0:T(128)S(1)} %get-tuple-element.59.count_ref, bf16[4,128,512]{2,1,0:T(8,128)(2,1)S(1)} %bitcast.115, ...), custom_call_target="tpu_custom_call", output_to_operand_aliasing={{0}: (4, {}), {1}: (5, {}), {2}: (6, {})} | custom-call | tf_op jit(solution)/shard_map/pallas_call | solution.py:87
  75.0 4.8 %all-to-all-start.4 = ((bf16[16,128,128]{2,1,0:T(8,128)(2,1)}), bf16[16,128,128]{2,1,0:T(8,128)(2,1)S(1)}, u32[]{:S(2)}, u32[]{:S(2)}) async-start(bf16[16,128,128]{2,1,0:T(8,128)(2,1)} %get-tuple-element.47), calls=%async_computation.4 | async-start | bytes 1048576 | tf_op jit(solution)/shard_map/all_to_all | solution.py:141
  79.8 14.6 %shard_map.57 = (f32[4,1,512]{2,1,0:T(1,128)S(1)}, f32[4,1,512]{2,1,0:T(1,128)S(1)}, f32[4,128,512]{2,1,0:T(8,128)S(1)}) custom-call(s32[4,9]{1,0:T(4,128)S(1)} %fusion.44.owner_ref, s32[4]{0:T(128)S(1)} %get-tuple-element.59.count_ref, bf16[4,128,512]{2,1,0:T(8,128)(2,1)S(1)} %bitcast.116, ...), custom_call_target="tpu_custom_call", output_to_operand_aliasing={{0}: (4, {}), {1}: (5, {}), {2}: (6, {})} | custom-call | tf_op jit(solution)/shard_map/pallas_call | solution.py:87
  94.4 14.6 %shard_map.58 = (f32[4,1,512]{2,1,0:T(1,128)S(1)}, f32[4,1,512]{2,1,0:T(1,128)S(1)}, f32[4,128,512]{2,1,0:T(8,128)S(1)}) custom-call(s32[4,9]{1,0:T(4,128)S(1)} %fusion.44.owner_ref, s32[4]{0:T(128)S(1)} %get-tuple-element.59.count_ref, bf16[4,128,512]{2,1,0:T(8,128)(2,1)S(1)} %bitcast.117, ...), custom_call_target="tpu_custom_call", output_to_operand_aliasing={{0}: (4, {}), {1}: (5, {}), {2}: (6, {})} | custom-call | tf_op jit(solution)/shard_map/pallas_call | solution.py:87
  109.3 0.4 copy.38
  109.7 1.9 %collective-permute-start = (bf16[2,512,128]{2,1,0:T(8,128)(2,1)S(1)}, bf16[2,512,128]{2,1,0:T(8,128)(2,1)S(1)}, u32[]{:S(2)}, u32[]{:S(2)}) collective-permute-start(bf16[2,512,128]{2,1,0:T(8,128)(2,1)S(1)} %bitcast.146), channel_id=1, source_target_pairs={{0,1},{1,2},{2,3},{3,4},{4,5},{5,6},{6,7},{7,8},{8,9},{9,10},{10,1... | collective-permute-start | bytes 786440 | tf_op jit(solution)/shard_map/ppermute | solution.py:16
  111.7 2.4 %collective-permute-start.1 = (bf16[2,512,128]{2,1,0:T(8,128)(2,1)S(1)}, bf16[2,512,128]{2,1,0:T(8,128)(2,1)S(1)}, u32[]{:S(2)}, u32[]{:S(2)}) collective-permute-start(bf16[2,512,128]{2,1,0:T(8,128)(2,1)S(1)} %bitcast.145), channel_id=1, source_target_pairs={{1,0},{2,1},{3,2},{4,3},{5,4},{6,5},{7,6},{8,7},{9,8},{10,9},{11,1... | collective-permute-start | bytes 786440 | tf_op jit(solution)/shard_map/ppermute | solution.py:17
  114.1 0.9 collective-permute-done
  115.0 4.4 %collective-permute-done.1 = bf16[2,512,128]{2,1,0:T(8,128)(2,1)S(1)} collective-permute-done((bf16[2,512,128]{2,1,0:T(8,128)(2,1)S(1)}, bf16[2,512,128]{2,1,0:T(8,128)(2,1)S(1)}, u32[]{:S(2)}, u32[]{:S(2)}) %collective-permute-start.1) | collective-permute-done | bytes 262176 | tf_op jit(solution)/shard_map/ppermute | solution.py:17
  119.5 1.3 pad_slice_fusion.1
  120.8 0.3 fusion.23
  121.1 0.3 fusion.14
  121.5 0.1 pad_maximum_fusion.2
  121.6 0.3 convolution_add_fusion.6
  122.0 0.4 convolution_add_fusion.5
  122.3 0.4 convolution_add_fusion.4
  122.7 0.4 convolution_add_fusion.3
  123.1 0.4 convolution_add_fusion.2
  123.4 0.4 convolution_add_fusion.1
  123.8 0.4 fusion.2
  124.3 0.9 pad_slice_fusion.6
  125.3 0.3 fusion.12
  125.5 0.3 convolution_add_fusion.14
  125.8 0.3 convolution_add_fusion.13
  126.1 0.3 convolution_add_fusion.12
  126.4 0.3 convolution_add_fusion.11
  126.7 0.3 convolution_add_fusion.10
  127.0 0.3 convolution_add_fusion.9
  127.2 0.3 convolution_add_fusion.8
  127.5 0.3 convolution_add_fusion.7
  127.8 0.9 add_convert_fusion
  (24 shorter events, 1.2 us)
Async XLA Ops:
  2.6 11.2 %all-to-all-start = ((s32[16,1,1]{2,1,0:T(1,128)}), s32[16,1,1]{2,1,0:T(1,128)S(1)}, u32[]{:S(2)}, u32[]{:S(2)}) async-start(s32[16,1,1]{2,1,0:T(1,128)} %copy.36), calls=%async_computation | async-start | bytes 16384 | tf_op jit(solution)/shard_map/all_to_all | solution.py:123
  17.3 22.9 %copy-start = (bf16[4,512,128]{2,1,0:T(8,128)(2,1)S(1)}, bf16[4,512,128]{2,1,0:T(8,128)(2,1)}, u32[]{:S(2)}) copy-start(bf16[4,512,128]{2,1,0:T(8,128)(2,1)} %param.5) | copy-start | bytes 1572868
  35.9 19.7 %all-to-all-start.2 = ((bf16[16,128,128]{2,1,0:T(8,128)(2,1)}), bf16[16,128,128]{2,1,0:T(8,128)(2,1)S(1)}, u32[]{:S(2)}, u32[]{:S(2)}) async-start(bf16[16,128,128]{2,1,0:T(8,128)(2,1)} %get-tuple-element.31), calls=%async_computation.2 | async-start | bytes 1048576 | tf_op jit(solution)/shard_map/all_to_all | solution.py:141
  55.6 19.4 %all-to-all-start.3 = ((bf16[16,128,128]{2,1,0:T(8,128)(2,1)}), bf16[16,128,128]{2,1,0:T(8,128)(2,1)S(1)}, u32[]{:S(2)}, u32[]{:S(2)}) async-start(bf16[16,128,128]{2,1,0:T(8,128)(2,1)} %get-tuple-element.39), calls=%async_computation.3 | async-start | bytes 1048576 | tf_op jit(solution)/shard_map/all_to_all | solution.py:141
  75.0 19.4 %all-to-all-start.4 = ((bf16[16,128,128]{2,1,0:T(8,128)(2,1)}), bf16[16,128,128]{2,1,0:T(8,128)(2,1)S(1)}, u32[]{:S(2)}, u32[]{:S(2)}) async-start(bf16[16,128,128]{2,1,0:T(8,128)(2,1)} %get-tuple-element.47), calls=%async_computation.4 | async-start | bytes 1048576 | tf_op jit(solution)/shard_map/all_to_all | solution.py:141
  109.7 5.2 %collective-permute-start = (bf16[2,512,128]{2,1,0:T(8,128)(2,1)S(1)}, bf16[2,512,128]{2,1,0:T(8,128)(2,1)S(1)}, u32[]{:S(2)}, u32[]{:S(2)}) collective-permute-start(bf16[2,512,128]{2,1,0:T(8,128)(2,1)S(1)} %bitcast.146), channel_id=1, source_target_pairs={{0,1},{1,2},{2,3},{3,4},{4,5},{5,6},{6,7},{7,8},{8,9},{9,10},{10,1... | collective-permute-start | bytes 786440 | tf_op jit(solution)/shard_map/ppermute | solution.py:16
  111.7 7.7 %collective-permute-start.1 = (bf16[2,512,128]{2,1,0:T(8,128)(2,1)S(1)}, bf16[2,512,128]{2,1,0:T(8,128)(2,1)S(1)}, u32[]{:S(2)}, u32[]{:S(2)}) collective-permute-start(bf16[2,512,128]{2,1,0:T(8,128)(2,1)S(1)} %bitcast.145), channel_id=1, source_target_pairs={{1,0},{2,1},{3,2},{4,3},{5,4},{6,5},{7,6},{8,7},{9,8},{10,9},{11,1... | collective-permute-start | bytes 786440 | tf_op jit(solution)/shard_map/ppermute | solution.py:17
  119.5 1.3 %copy-start.1 = (bf16[3,3,128,128]{3,2,1,0:T(8,128)(2,1)S(1)}, bf16[3,3,128,128]{3,2,1,0:T(8,128)(2,1)}, u32[]{:S(2)}) copy-start(bf16[3,3,128,128]{3,2,1,0:T(8,128)(2,1)} %param.8) | copy-start | bytes 884740
  124.3 1.0 copy-start.2
where the time goes:
time: 131 us; the launch traced here: 129 us
  Pallas kernels  58.4 us (45%)
  starting transfers between devices  24.9 us (19%)
  blocking collectives  18.6 us (14%)
  waiting for transfers between devices  8.79 us (7%)
  local copies, waits for them, and re-layouts  7.6 us (6%)
  matrix products  5.69 us (4%)
  other arithmetic  4.39 us (3%)
    pallas_call x4, Pallas kernels, attend_chunk(): pl.pallas_call(functools.partial(attend_kernel, scale=scale), grid_spec=g...  58.4 us
    all_to_all x1, blocking collectives, on_device(): lax.all_to_all(sending, 'row', split_axis=0, concat_axis=0, tiled=True)  18.6 us
    all_to_all x3, starting transfers between devices, on_device(): lax.all_to_all(sending, 'row', split_axis=0, concat_axis=0, tiled=True)  14 us
    all_to_all x1, starting transfers between devices, on_device(): lax.all_to_all(wanted.reshape(owners, 1), 'row', split_axis=0, concat_axi...  6.61 us
    dot_general x18, matrix products, convolve_rows(): jnp.dot(window, weights[row_shift, col_shift], preferred_element_type=jnp...  5.69 us
    ppermute x1, waiting for transfers between devices, halo_rows(): from_below = lax.ppermute(head, axis, [(i + 1, i) for i in range(ends)])  4.4 us
    all_to_all x1, waiting for transfers between devices, on_device(): lax.all_to_all(wanted.reshape(owners, 1), 'row', split_axis=0, concat_axi...  3.53 us
  transfers between devices with their start and end apart: 6, of which 3 were waited for; matrix products, arithmetic and copies ran while one was open for 1% of the time, Pallas kernels for 34%

commit v1 on v0

v1 whole, which is shorter than its diff:
```python
import jax
import jax.numpy as jnp
from jax import lax
from jax.sharding import PartitionSpec as P


def halo_rows(cells, axis, width):
    count = lax.axis_size(axis)
    ends = count - 1
    head = cells[:width]
    tail = cells[cells.shape[0] - width :]
    from_above = lax.ppermute(tail, axis, [(i, i + 1) for i in range(ends)])
    from_below = lax.ppermute(head, axis, [(i + 1, i) for i in range(ends)])
    return jnp.concatenate([from_above, cells, from_below], axis=0)


def convolve_rows(padded, weights, out_rows, out_cols):
    channels = padded.shape[2]
    summed = jnp.zeros((out_rows * out_cols, channels), jnp.float32)
    for row_shift in range(3):
        for col_shift in range(3):
            window = padded[row_shift : row_shift + out_rows, col_shift : col_shift + out_cols]
            window = window.reshape(out_rows * out_cols, channels)
            summed = summed + jnp.dot(
                window, weights[row_shift, col_shift], preferred_element_type=jnp.float32
            )
    return summed.reshape(out_rows, out_cols, channels)


def pad_columns(image):
    return jnp.pad(image, ((0, 0), (1, 1), (0, 0)))


def attend_chunk(state, queries, chunk, slot_owner, valid, scale):
    peak_old, total_old, mixed_old = state
    chosen = jnp.take(chunk, slot_owner, axis=0)
    scores = jnp.einsum("tqc,tjkc->tqjk", queries, chosen, preferred_element_type=jnp.float32) * scale
    scores = jnp.where(valid[:, None, :, None], scores, -1e30)
    peak = jnp.maximum(peak_old, jnp.max(scores, axis=(2, 3)))
    alpha = jnp.exp(peak_old - peak)
    probs = jnp.exp(scores - peak[:, :, None, None])
    total = total_old * alpha + jnp.sum(probs, axis=(2, 3))
    mixed = mixed_old * alpha[:, :, None] + jnp.einsum(
        "tqjk,tjkc->tqc", probs.astype(jnp.bfloat16), chosen, preferred_element_type=jnp.float32
    )
    return peak, total, mixed


def on_device(frame_one, frame_two, tile_lists, conv_one, conv_two):
    band_rows, band_width, channels = frame_one.shape
    per_device = tile_lists.shape[0]
    tile_cols = band_width // per_device
    tile_size = band_rows * tile_cols
    owners = lax.axis_size("row")
    scale = float(channels) ** (-0.5)

    def band_to_tiles(band):
        return (
            band.reshape(band_rows, per_device, tile_cols, channels)
            .transpose(1, 0, 2, 3)
            .reshape(per_device, tile_size, channels)
        )

    query_tiles = band_to_tiles(frame_one)
    own_keys = band_to_tiles(frame_two)
    valid = tile_lists >= 0
    slot_owner = jnp.where(valid, tile_lists // per_device, 0).astype(jnp.int32)
    owner_iota = jnp.arange(owners, dtype=jnp.int32)
    matches = (slot_owner[:, :, None] == owner_iota[None, None, :]) & valid[:, :, None]
    wanted = jnp.max(jnp.where(matches, (tile_lists % per_device)[:, :, None], -1), axis=(0, 1))
    asked = lax.all_to_all(
        wanted.reshape(owners, 1), "row", split_axis=0, concat_axis=0, tiled=True
    )[:, 0]
    picked = jnp.take(own_keys, jnp.maximum(asked, 0), axis=0)
    outgoing = jnp.where((asked >= 0)[:, None, None], picked, jnp.zeros_like(picked))
    pieces = 4
    chunk_len = tile_size // pieces
    state = (
        jnp.full((per_device, tile_size), -jnp.inf, jnp.float32),
        jnp.zeros((per_device, tile_size), jnp.float32),
        jnp.zeros((per_device, tile_size, channels), jnp.float32),
    )
    previous = None
    for piece in range(pieces):
        sending = outgoing[:, piece * chunk_len : (piece + 1) * chunk_len]
        if previous is not None:
            previous, sending, state = lax.optimization_barrier((previous, sending, state))
        current = lax.all_to_all(sending, "row", split_axis=0, concat_axis=0, tiled=True)
        if previous is not None:
            state = attend_chunk(state, query_tiles, previous, slot_owner, valid, scale)
        previous = current
    state = attend_chunk(state, query_tiles, previous, slot_owner, valid, scale)
    warped_tiles = (state[2] / state[1][:, :, None]).astype(jnp.bfloat16)
    warped = (
        warped_tiles.reshape(per_device, band_rows, tile_cols, channels)
        .transpose(1, 0, 2, 3)
        .reshape(band_rows, band_width, channels)
    )
    me = lax.axis_index("row")
    extended = halo_rows(warped, "row", 2)
    hidden = jax.nn.relu(
        convolve_rows(pad_columns(extended), conv_one, band_rows + 2, band_width)
    ).astype(jnp.bfloat16)
    row_ids = jnp.arange(band_rows + 2)
    inside = ((row_ids > 0) | (me > 0)) & ((row_ids < band_rows + 1) | (me < owners - 1))
    hidden = jnp.where(inside[:, None, None], hidden, jnp.zeros_like(hidden))
    branch = convolve_rows(pad_columns(hidden), conv_two, band_rows, band_width)
    return (frame_one.astype(jnp.float32) + branch).astype(jnp.bfloat16)


def solution(mesh):
    in_specs = (
        P(("pairs", "row"), None, None),
        P(("pairs", "row"), None, None),
        P(("pairs", "row"), None),
        P(),
        P(),
    )
    out_specs = P(("pairs", "row"), None, None)
    return jax.shard_map(
        on_device, mesh=mesh, in_specs=in_specs, out_specs=out_specs, check_vma=False
    )
```

time: 131 us -> 142 us (1.084)
  Pallas kernels: 58.4 us -> 0 us
  matrix products: 5.69 us -> 44.4 us
  waiting for transfers between devices: 8.79 us -> 39.4 us
  blocking collectives: 18.6 us -> 0 us
  other arithmetic: 4.39 us -> 14.4 us
  starting transfers between devices: 24.9 us -> 30 us
  local copies, waits for them, and re-layouts: 7.6 us -> 11.4 us
    pallas_call x4 -> x0, Pallas kernels: 58.4 us -> none  [attend_chunk(): pl.pallas_call(functools.partial(attend_kernel, scale=scale), grid_spec=g...]
    dot_general x0 -> x8, matrix products: none -> 38.7 us  [the longest x4 19.7 us: attend_chunk(): jnp.einsum('tqjk,tjkc->tqc', probs.astype(jnp.bfloat16), chosen, preferre...]
    all_to_all x3 -> x4, waiting for transfers between devices: 0.01 us -> 30.2 us  [on_device(): lax.all_to_all(sending, 'row', split_axis=0, concat_axis=0, tiled=True)]
    all_to_all x1 -> x0, blocking collectives: 18.6 us -> none  [on_device(): lax.all_to_all(sending, 'row', split_axis=0, concat_axis=0, tiled=True)]
    reduce_sum x1 -> x3, other arithmetic: 0.8 us -> 10.2 us  [attend_chunk(): total = total_old * alpha + jnp.sum(probs, axis=(2, 3))]
    all_to_all x3 -> x4, starting transfers between devices: 14 us -> 18.6 us  [on_device(): lax.all_to_all(sending, 'row', split_axis=0, concat_axis=0, tiled=True)]
    gather x0 -> x4, local copies, waits for them, and re-layouts: none -> 4.1 us  [attend_chunk(): chosen = jnp.take(chunk, slot_owner, axis=0)]
  transfers between devices with their start and end apart: 6 -> 7, of which waited for: 3 -> 7; matrix products, arithmetic and copies ran while one was open for 1% -> 19% of each run, Pallas kernels for 34% -> 0%
where the time goes in v1:
time: 142 us; the launch traced here: 140 us
  matrix products  44.4 us (31%)
  waiting for transfers between devices  39.4 us (28%)
  starting transfers between devices  30 us (21%)
  other arithmetic  14.4 us (10%)
  local copies, waits for them, and re-layouts  11.4 us (8%)
    all_to_all x4, waiting for transfers between devices, on_device(): lax.all_to_all(sending, 'row', split_axis=0, concat_axis=0, tiled=True)  30.2 us
    dot_general x4, matrix products, attend_chunk(): jnp.einsum('tqjk,tjkc->tqc', probs.astype(jnp.bfloat16), chosen, preferre...  19.7 us
    dot_general x4, matrix products, attend_chunk(): jnp.einsum('tqc,tjkc->tqjk', queries, chosen, preferred_element_type=jnp....  19.1 us
    all_to_all x4, starting transfers between devices, on_device(): lax.all_to_all(sending, 'row', split_axis=0, concat_axis=0, tiled=True)  18.6 us
    reduce_sum x3, other arithmetic, attend_chunk(): total = total_old * alpha + jnp.sum(probs, axis=(2, 3))  10.2 us
    all_to_all x1, starting transfers between devices, on_device(): lax.all_to_all(wanted.reshape(owners, 1), 'row', split_axis=0, concat_axi...  6.61 us
    dot_general x18, matrix products, convolve_rows(): jnp.dot(window, weights[row_shift, col_shift], preferred_element_type=jnp...  5.69 us
    ppermute x1, waiting for transfers between devices, halo_rows(): from_below = lax.ppermute(head, axis, [(i + 1, i) for i in range(ends)])  4.62 us
  transfers between devices with their start and end apart: 7, of which 7 were waited for; matrix products, arithmetic and copies ran while one was open for 19% of the time, Pallas kernels for 0%

profile of v1, /device:TPU:9, one launch (start us, length us, event | category | flops | bytes accessed | tf_op | source)
XLA Modules:
  0.0 140.2 jit_solution(7131264903693641151)
XLA Ops:
  0.0 0.7 compare_and_fusion
  0.7 0.7 add_select_fusion
  1.8 0.7 copy.43
  2.5 6.6 %all-to-all-start = ((s32[16,1,1]{2,1,0:T(1,128)}), s32[16,1,1]{2,1,0:T(1,128)S(1)}, u32[]{:S(2)}, u32[]{:S(2)}) async-start(s32[16,1,1]{2,1,0:T(1,128)} %copy.43), calls=%async_computation | async-start | bytes 16384 | tf_op jit(solution)/shard_map/all_to_all | solution.py:71
  9.1 1.1 copy.44
  10.2 3.5 %all-to-all-done = s32[16,1,1]{2,1,0:T(1,128)S(1)} async-done(((s32[16,1,1]{2,1,0:T(1,128)}), s32[16,1,1]{2,1,0:T(1,128)S(1)}, u32[]{:S(2)}, u32[]{:S(2)}) %all-to-all-start) | async-done | bytes 96 | tf_op jit(solution)/shard_map/all_to_all | solution.py:71
  13.7 0.4 maximum_reduce_fusion
  14.1 1.0 gather_fusion
  15.1 0.7 compare_reduce_fusion.1
  16.1 1.4 fusion.127
  17.4 5.2 %all-to-all-start.1 = ((bf16[16,128,128]{2,1,0:T(8,128)(2,1)}), bf16[16,128,128]{2,1,0:T(8,128)(2,1)S(1)}, u32[]{:S(2)}, u32[]{:S(2)}) async-start(bf16[16,128,128]{2,1,0:T(8,128)(2,1)} %get-tuple-element.52), calls=%async_computation.1 | async-start | bytes 1048576 | tf_op jit(solution)/shard_map/all_to_all | solution.py:88
  22.8 14.0 %all-to-all-done.1 = bf16[16,128,128]{2,1,0:T(8,128)(2,1)S(1)} async-done(((bf16[16,128,128]{2,1,0:T(8,128)(2,1)}), bf16[16,128,128]{2,1,0:T(8,128)(2,1)S(1)}, u32[]{:S(2)}, u32[]{:S(2)}) %all-to-all-start.1) | async-done | bytes 524320 | tf_op jit(solution)/shard_map/all_to_all | solution.py:88
  36.8 4.4 %all-to-all-start.2 = ((bf16[16,128,128]{2,1,0:T(8,128)(2,1)}), bf16[16,128,128]{2,1,0:T(8,128)(2,1)S(1)}, u32[]{:S(2)}, u32[]{:S(2)}) async-start(bf16[16,128,128]{2,1,0:T(8,128)(2,1)} %get-tuple-element.21), calls=%async_computation.2 | async-start | bytes 1048576 | tf_op jit(solution)/shard_map/all_to_all | solution.py:88
  41.2 0.8 gather_fusion.1
  42.0 1.7 %bitcast_reduce_fusion.3 = (f32[4,512]{1,0:T(4,128)S(1)}, f32[4,9,128,512]{3,2,1,0:T(8,128)S(1)}) fusion(pred[4,9]{1,0:T(4,128)(4,1)S(1)} %get-tuple-element.75, bf16[4,512,128,1]{2,1,3,0:T(8,128)(2,1)S(1)} %bitcast.238, bf16[4,9,128,128]{3,2,1,0:T(8,128)(2,1)S(1)} %bitcast.233, pred[4,9]{1,0:T(4,128)(4,1)S(1)} %get-tuple-element.47), kind=kOutput, calls=%fused_computation.15 | convolution fusion | flops 611645440 | bytes 11149384 | tf_op jit(solution)/shard_map/tqc,tjkc->tqjk/dot_general | solution.py:37
  43.8 2.1 %fusion.5 = f32[4,512]{1,0:T(4,128)S(1)} fusion(f32[4,9,128,512]{3,2,1,0:T(8,128)S(1)} %get-tuple-element.77, f32[4,512]{1,0:T(4,128)S(1)} %max.39, pred[4,9]{1,0:T(4,128)(4,1)S(1)} %get-tuple-element.75), kind=kLoop, calls=%fused_computation.22 | loop fusion | flops 9435136 | bytes 9453604 | tf_op jit(solution)/shard_map/reduce_sum | solution.py:42
  46.0 4.6 %fusion.48 = f32[4,512,128]{2,1,0:T(8,128)} fusion(f32[4,9,128,512]{3,2,1,0:T(8,128)S(1)} %get-tuple-element.77, f32[4,512]{1,0:T(4,128)S(1)} %max.39, pred[4,9]{1,0:T(4,128)(4,1)S(1)} %get-tuple-element.75, f32[4,512,128]{2,1,0:T(8,128)S(1)} %broadcast_in_dim.119, bf16[4,9,128,128]{3,2,1,0:T(8,128)(2,1)S(1)} %bitcast.234, ...), kind=kOutput, calls=%fused_computation.63 | convolution fusion | flops 614531072 | bytes 12730440 | tf_op jit(solution)/shard_map/tqjk,tjkc->tqc/dot_general | solution.py:43
  50.6 4.7 %all-to-all-done.2 = bf16[16,128,128]{2,1,0:T(8,128)(2,1)S(1)} async-done(((bf16[16,128,128]{2,1,0:T(8,128)(2,1)}), bf16[16,128,128]{2,1,0:T(8,128)(2,1)S(1)}, u32[]{:S(2)}, u32[]{:S(2)}) %all-to-all-start.2) | async-done | bytes 524320 | tf_op jit(solution)/shard_map/all_to_all | solution.py:88
  55.3 0.8 gather_fusion.2
  56.1 5.1 %bitcast_reduce_fusion.2 = (f32[4,512]{1,0:T(4,128)S(1)}, f32[4,9,128,512]{3,2,1,0:T(8,128)}) fusion(pred[4,9]{1,0:T(4,128)(4,1)S(1)} %get-tuple-element.75, bf16[4,512,128,1]{2,1,3,0:T(8,128)(2,1)S(1)} %bitcast.239, bf16[4,9,128,128]{3,2,1,0:T(8,128)(2,1)S(1)} %bitcast.235, pred[4,9]{1,0:T(4,128)(4,1)S(1)} %get-tuple-element.47), kind=kOutput, calls=%fused_computation.12 | convolution fusion | flops 611645440 | bytes 11149384 | tf_op jit(solution)/shard_map/tqc,tjkc->tqjk/dot_general | solution.py:37
  61.2 4.6 %all-to-all-start.3 = ((bf16[16,128,128]{2,1,0:T(8,128)(2,1)}), bf16[16,128,128]{2,1,0:T(8,128)(2,1)S(1)}, u32[]{:S(2)}, u32[]{:S(2)}) async-start(bf16[16,128,128]{2,1,0:T(8,128)(2,1)} %get-tuple-element.26), calls=%async_computation.3 | async-start | bytes 1048576 | tf_op jit(solution)/shard_map/all_to_all | solution.py:88
  65.8 5.9 %fusion.7 = f32[4,512]{1,0:T(4,128)S(1)} fusion(f32[4,9,128,512]{3,2,1,0:T(8,128)} %get-tuple-element.79, f32[4,512]{1,0:T(4,128)S(1)} %max.40, pred[4,9]{1,0:T(4,128)(4,1)S(1)} %get-tuple-element.75), kind=kLoop, calls=%fused_computation.24 | loop fusion | flops 9435136 | bytes 9453604 | tf_op jit(solution)/shard_map/reduce_sum | solution.py:42
  71.8 0.4 copy-done
  72.2 4.6 %fusion.45 = f32[4,512,128]{2,1,0:T(8,128)} fusion(f32[4,9,128,512]{3,2,1,0:T(8,128)S(1)} %copy-done, f32[4,512]{1,0:T(4,128)S(1)} %max.40, pred[4,9]{1,0:T(4,128)(4,1)S(1)} %get-tuple-element.75, f32[4,512,128]{2,1,0:T(8,128)S(1)} %copy-done.9, bf16[4,9,128,128]{3,2,1,0:T(8,128)(2,1)S(1)} %bitcast.236, pred[4,9]{1,0:T(4,128)(4,1)S(1)} %get-tuple-element.47, ...), kind=kOutput, calls=%fused_computation.62 | convolution fusion | flops 614531072 | bytes 12730440 | tf_op jit(solution)/shard_map/tqjk,tjkc->tqc/dot_general | solution.py:43
  76.8 3.2 %all-to-all-done.3 = bf16[16,128,128]{2,1,0:T(8,128)(2,1)S(1)} async-done(((bf16[16,128,128]{2,1,0:T(8,128)(2,1)}), bf16[16,128,128]{2,1,0:T(8,128)(2,1)S(1)}, u32[]{:S(2)}, u32[]{:S(2)}) %all-to-all-start.3) | async-done | bytes 524320 | tf_op jit(solution)/shard_map/all_to_all | solution.py:88
  80.0 4.4 %all-to-all-start.4 = ((bf16[16,128,128]{2,1,0:T(8,128)(2,1)}), bf16[16,128,128]{2,1,0:T(8,128)(2,1)S(1)}, u32[]{:S(2)}, u32[]{:S(2)}) async-start(bf16[16,128,128]{2,1,0:T(8,128)(2,1)} %get-tuple-element.34), calls=%async_computation.4 | async-start | bytes 1048576 | tf_op jit(solution)/shard_map/all_to_all | solution.py:88
  84.4 0.8 gather_fusion.3
  85.2 5.1 %bitcast_reduce_fusion.1 = (f32[4,512]{1,0:T(4,128)S(1)}, f32[4,9,128,512]{3,2,1,0:T(8,128)}) fusion(pred[4,9]{1,0:T(4,128)(4,1)S(1)} %get-tuple-element.75, bf16[4,512,128,1]{2,1,3,0:T(8,128)(2,1)S(1)} %bitcast.240, bf16[4,9,128,128]{3,2,1,0:T(8,128)(2,1)S(1)} %bitcast.229, pred[4,9]{1,0:T(4,128)(4,1)S(1)} %get-tuple-element.47), kind=kOutput, calls=%fused_computation.9 | convolution fusion | flops 611645440 | bytes 11149384 | tf_op jit(solution)/shard_map/tqc,tjkc->tqjk/dot_general | solution.py:37
  90.3 8.2 %all-to-all-done.4 = bf16[16,128,128]{2,1,0:T(8,128)(2,1)S(1)} async-done(((bf16[16,128,128]{2,1,0:T(8,128)(2,1)}), bf16[16,128,128]{2,1,0:T(8,128)(2,1)S(1)}, u32[]{:S(2)}, u32[]{:S(2)}) %all-to-all-start.4) | async-done | bytes 524320 | tf_op jit(solution)/shard_map/all_to_all | solution.py:88
  98.5 1.8 %gather_fusion.4 = bf16[36,128,128]{2,1,0:T(8,128)(2,1)} fusion(bf16[16,128,128]{2,1,0:T(8,128)(2,1)S(1)} %all-to-all-done.4, s32[1024]{0:T(1024)S(1)} %pad_clamp_fusion), kind=kCustom, calls=%fused_computation.3.clone | custom fusion | bytes 2359440 | tf_op jit(solution)/shard_map/jit(_take)/gather | solution.py:36
  100.3 7.1 %fusion.8 = (f32[4,512]{1,0:T(4,128)S(1)}, f32[4,512]{1,0:T(4,128)S(1)}, f32[4,9,128,512]{3,2,1,0:T(8,128)S(1)}) fusion(f32[4,9,128,512]{3,2,1,0:T(8,128)} %get-tuple-element.81, f32[4,512]{1,0:T(4,128)S(1)} %max.41, pred[4,9]{1,0:T(4,128)(4,1)S(1)} %get-tuple-element.75, bf16[4,512,128,1]{2,1,3,0:T(8,128)(2,1)S(1)} %bitcast.241, ...), kind=kOutput, calls=%fused_computation.25 | convolution fusion | flops 621080576 | bytes 20602952 | tf_op jit(solution)/shard_map/tqc,tjkc->tqjk/dot_general | solution.py:37
  107.4 2.1 %fusion.10 = f32[4,512]{1,0:T(4,128)S(1)} fusion(f32[4,9,128,512]{3,2,1,0:T(8,128)S(1)} %get-tuple-element.82, f32[4,512]{1,0:T(4,128)S(1)} %max.42, pred[4,9]{1,0:T(4,128)(4,1)S(1)} %get-tuple-element.75), kind=kLoop, calls=%fused_computation.27 | loop fusion | flops 9435136 | bytes 9453604 | tf_op jit(solution)/shard_map/reduce_sum | solution.py:42
  109.6 6.7 %fusion.51 = f32[4,512,128]{2,1,0:T(8,128)S(1)} fusion(f32[4,9,128,512]{3,2,1,0:T(8,128)} %get-tuple-element.81, f32[4,512]{1,0:T(4,128)S(1)} %max.41, pred[4,9]{1,0:T(4,128)(4,1)S(1)} %get-tuple-element.75, f32[4,512,128]{2,1,0:T(8,128)S(1)} %copy-done.8, bf16[4,9,128,128]{3,2,1,0:T(8,128)(2,1)S(1)} %bitcast.230, pred[4,9]{1,0:T(4,128)(4,1)S(1)} %get-tuple-element.47, ...), kind=kOutput, calls=%fused_computation.64 | convolution fusion | flops 614793216 | bytes 12738632 | tf_op jit(solution)/shard_map/tqjk,tjkc->tqc/dot_general | solution.py:43
  116.3 3.9 %divide_convert_fusion = bf16[4,512,128]{2,1,0:T(8,128)(2,1)S(1)} fusion(f32[4,512,128]{2,1,0:T(8,128)S(1)} %fusion.51, bf16[4,9,128,128]{3,2,1,0:T(8,128)(2,1)S(1)} %bitcast.232, pred[4,9]{1,0:T(4,128)(4,1)S(1)} %get-tuple-element.47, f32[4,9,128,512]{3,2,1,0:T(8,128)S(1)} %get-tuple-element.82, f32[4,512]{1,0:T(4,128)S(1)} %max.42, ...), kind=kOutput, calls=%fused_computation.71 | convolution fusion | flops 614793216 | bytes 12206152 | tf_op jit(solution)/shard_map/tqjk,tjkc->tqc/dot_general | solution.py:43
  120.2 2.6 %collective-permute-start = (bf16[2,512,128]{2,1,0:T(8,128)(2,1)S(1)}, bf16[2,512,128]{2,1,0:T(8,128)(2,1)S(1)}, u32[]{:S(2)}, u32[]{:S(2)}) collective-permute-start(bf16[2,512,128]{2,1,0:T(8,128)(2,1)S(1)} %bitcast.244), channel_id=1, source_target_pairs={{0,1},{1,2},{2,3},{3,4},{4,5},{5,6},{6,7},{7,8},{8,9},{9,10},{10,1... | collective-permute-start | bytes 786440 | tf_op jit(solution)/shard_map/ppermute | solution.py:12
  122.9 2.1 %collective-permute-start.1 = (bf16[2,512,128]{2,1,0:T(8,128)(2,1)S(1)}, bf16[2,512,128]{2,1,0:T(8,128)(2,1)S(1)}, u32[]{:S(2)}, u32[]{:S(2)}) collective-permute-start(bf16[2,512,128]{2,1,0:T(8,128)(2,1)S(1)} %bitcast.243), channel_id=1, source_target_pairs={{1,0},{2,1},{3,2},{4,3},{5,4},{6,5},{7,6},{8,7},{9,8},{10,9},{11,1... | collective-permute-start | bytes 786440 | tf_op jit(solution)/shard_map/ppermute | solution.py:13
  125.0 1.1 collective-permute-done
  126.2 4.6 %collective-permute-done.1 = bf16[2,512,128]{2,1,0:T(8,128)(2,1)S(1)} collective-permute-done((bf16[2,512,128]{2,1,0:T(8,128)(2,1)S(1)}, bf16[2,512,128]{2,1,0:T(8,128)(2,1)S(1)}, u32[]{:S(2)}, u32[]{:S(2)}) %collective-permute-start.1) | collective-permute-done | bytes 262176 | tf_op jit(solution)/shard_map/ppermute | solution.py:13
  130.9 1.3 pad_slice_fusion.1
  132.2 0.3 fusion.87
  133.4 0.4 convolution_add_fusion.5
  133.8 0.4 convolution_add_fusion.4
  134.1 0.4 convolution_add_fusion.3
  134.5 0.4 convolution_add_fusion.2
  134.9 0.4 convolution_add_fusion.1
  135.2 0.4 fusion.26
  135.7 0.9 pad_slice_fusion.6
  139.3 0.9 add_convert_fusion
  (56 shorter events, 4.8 us)
Async XLA Ops:
  2.5 11.2 %all-to-all-start = ((s32[16,1,1]{2,1,0:T(1,128)}), s32[16,1,1]{2,1,0:T(1,128)S(1)}, u32[]{:S(2)}, u32[]{:S(2)}) async-start(s32[16,1,1]{2,1,0:T(1,128)} %copy.43), calls=%async_computation | async-start | bytes 16384 | tf_op jit(solution)/shard_map/all_to_all | solution.py:71
  16.1 6.7 %copy-start.1 = (bf16[4,512,128]{2,1,0:T(8,128)(2,1)S(1)}, bf16[4,512,128]{2,1,0:T(8,128)(2,1)}, u32[]{:S(2)}) copy-start(bf16[4,512,128]{2,1,0:T(8,128)(2,1)} %param.7) | copy-start | bytes 1572868
  17.4 19.4 %all-to-all-start.1 = ((bf16[16,128,128]{2,1,0:T(8,128)(2,1)}), bf16[16,128,128]{2,1,0:T(8,128)(2,1)S(1)}, u32[]{:S(2)}, u32[]{:S(2)}) async-start(bf16[16,128,128]{2,1,0:T(8,128)(2,1)} %get-tuple-element.52), calls=%async_computation.1 | async-start | bytes 1048576 | tf_op jit(solution)/shard_map/all_to_all | solution.py:88
  22.8 21.0 %copy-start.3 = (bf16[4,4,128,128]{3,2,1,0:T(8,128)(2,1)}, bf16[4,4,128,128]{3,2,1,0:T(8,128)(2,1)S(1)}, u32[]{:S(2)}) copy-start(bf16[4,4,128,128]{3,2,1,0:T(8,128)(2,1)S(1)} %copy.45) | copy-start | bytes 1572868
  36.8 18.5 %all-to-all-start.2 = ((bf16[16,128,128]{2,1,0:T(8,128)(2,1)}), bf16[16,128,128]{2,1,0:T(8,128)(2,1)S(1)}, u32[]{:S(2)}, u32[]{:S(2)}) async-start(bf16[16,128,128]{2,1,0:T(8,128)(2,1)} %get-tuple-element.21), calls=%async_computation.2 | async-start | bytes 1048576 | tf_op jit(solution)/shard_map/all_to_all | solution.py:88
  50.6 5.5 %copy-start.4 = (bf16[4,4,128,128]{3,2,1,0:T(8,128)(2,1)S(1)}, bf16[4,4,128,128]{3,2,1,0:T(8,128)(2,1)}, u32[]{:S(2)}) copy-start(bf16[4,4,128,128]{3,2,1,0:T(8,128)(2,1)} %copy-done.3) | copy-start | bytes 1572868
  61.2 10.6 %copy-start.9 = (f32[4,512,128]{2,1,0:T(8,128)S(1)}, f32[4,512,128]{2,1,0:T(8,128)}, u32[]{:S(2)}) copy-start(f32[4,512,128]{2,1,0:T(8,128)} %fusion.48) | copy-start | bytes 3145732
  61.2 18.7 %all-to-all-start.3 = ((bf16[16,128,128]{2,1,0:T(8,128)(2,1)}), bf16[16,128,128]{2,1,0:T(8,128)(2,1)S(1)}, u32[]{:S(2)}, u32[]{:S(2)}) async-start(bf16[16,128,128]{2,1,0:T(8,128)(2,1)} %get-tuple-element.26), calls=%async_computation.3 | async-start | bytes 1048576 | tf_op jit(solution)/shard_map/all_to_all | solution.py:88
  65.8 6.4 %copy-start = (f32[4,9,128,512]{3,2,1,0:T(8,128)S(1)}, f32[4,9,128,512]{3,2,1,0:T(8,128)}, u32[]{:S(2)}) copy-start(f32[4,9,128,512]{3,2,1,0:T(8,128)} %get-tuple-element.79) | copy-start | bytes 28311556
  76.7 8.4 %copy-start.5 = (bf16[4,4,128,128]{3,2,1,0:T(8,128)(2,1)S(1)}, bf16[4,4,128,128]{3,2,1,0:T(8,128)(2,1)}, u32[]{:S(2)}) copy-start(bf16[4,4,128,128]{3,2,1,0:T(8,128)(2,1)} %copy-done.3) | copy-start | bytes 1572868
  80.0 18.6 %all-to-all-start.4 = ((bf16[16,128,128]{2,1,0:T(8,128)(2,1)}), bf16[16,128,128]{2,1,0:T(8,128)(2,1)S(1)}, u32[]{:S(2)}, u32[]{:S(2)}) async-start(bf16[16,128,128]{2,1,0:T(8,128)(2,1)} %get-tuple-element.34), calls=%async_computation.4 | async-start | bytes 1048576 | tf_op jit(solution)/shard_map/all_to_all | solution.py:88
  107.4 2.2 %copy-start.8 = (f32[4,512,128]{2,1,0:T(8,128)S(1)}, f32[4,512,128]{2,1,0:T(8,128)}, u32[]{:S(2)}) copy-start(f32[4,512,128]{2,1,0:T(8,128)} %fusion.45) | copy-start | bytes 3145732
  109.6 6.7 %copy-start.2 = (bf16[36,128,128]{2,1,0:T(8,128)(2,1)S(1)}, bf16[36,128,128]{2,1,0:T(8,128)(2,1)}, u32[]{:S(2)}) copy-start(bf16[36,128,128]{2,1,0:T(8,128)(2,1)} %gather_fusion.4) | copy-start | bytes 3538948
  120.2 5.9 %collective-permute-start = (bf16[2,512,128]{2,1,0:T(8,128)(2,1)S(1)}, bf16[2,512,128]{2,1,0:T(8,128)(2,1)S(1)}, u32[]{:S(2)}, u32[]{:S(2)}) collective-permute-start(bf16[2,512,128]{2,1,0:T(8,128)(2,1)S(1)} %bitcast.244), channel_id=1, source_target_pairs={{0,1},{1,2},{2,3},{3,4},{4,5},{5,6},{6,7},{7,8},{8,9},{9,10},{10,1... | collective-permute-start | bytes 786440 | tf_op jit(solution)/shard_map/ppermute | solution.py:12
  122.9 7.9 %collective-permute-start.1 = (bf16[2,512,128]{2,1,0:T(8,128)(2,1)S(1)}, bf16[2,512,128]{2,1,0:T(8,128)(2,1)S(1)}, u32[]{:S(2)}, u32[]{:S(2)}) collective-permute-start(bf16[2,512,128]{2,1,0:T(8,128)(2,1)S(1)} %bitcast.243), channel_id=1, source_target_pairs={{1,0},{2,1},{3,2},{4,3},{5,4},{6,5},{7,6},{8,7},{9,8},{10,9},{11,1... | collective-permute-start | bytes 786440 | tf_op jit(solution)/shard_map/ppermute | solution.py:13
  130.9 1.3 copy-start.6
  135.7 1.0 copy-start.7

commit v2 on v0

--- a/solution.py
+++ b/solution.py
@@ -35,54 +35,59 @@
     return jnp.pad(image, ((0, 0), (1, 1), (0, 0)))
 
 
-def attend_kernel(owner_ref, count_ref, q_ref, k_ref, m_in, t_in, a_in, m_out, t_out, a_out, s_ref, *, scale):
+def attend_kernel(owner_ref, count_ref, q_ref, k_ref, m_in, t_in, a_in, m_out, t_out, a_out, kall_ref, *, scale):
     t = pl.program_id(0)
     n = count_ref[t]
-    qt = q_ref[0]
+    slots = owner_ref.shape[1]
+    span = k_ref.shape[1]
+    lanes = 128
+    for j in range(slots):
+        kall_ref[j * span : (j + 1) * span, :] = k_ref[owner_ref[t, j]]
+    q = q_ref[0]
+    kall = kall_ref[...]
+    s = lax.dot_general(q, kall, (((1,), (1,)), ((), ())), preferred_element_type=jnp.float32)
+    penalty = [jnp.where(j < n, 0.0, jnp.inf).astype(jnp.float32) for j in range(slots)]
+    blocks = [(j, j * span + c * lanes) for j in range(slots) for c in range(span // lanes)]
+    mx = None
+    for j, at in blocks:
+        blk = s[:, at : at + lanes] - penalty[j]
+        mx = blk if mx is None else jnp.maximum(mx, blk)
     m_old = m_in[0]
-
-    def score(j, m):
-        kc = k_ref[owner_ref[t, j]]
-        s = jnp.dot(kc, qt, preferred_element_type=jnp.float32) * scale
-        s_ref[j] = s
-        return jnp.maximum(m, jnp.max(s, axis=0, keepdims=True))
-
-    m_new = lax.fori_loop(0, n, score, m_old)
+    m_new = jnp.maximum(m_old, jnp.max(mx, axis=1, keepdims=True) * scale)
     alpha = jnp.exp(m_old - m_new)
+    mb = jnp.broadcast_to(m_new, (m_new.shape[0], lanes))
+    shifted = [mb + penalty[j] for j in range(slots)]
+    acc = None
+    ps = []
+    for j, at in blocks:
+        p = jnp.exp(s[:, at : at + lanes] * scale - shifted[j])
+        acc = p if acc is None else acc + p
+        ps.append(p.astype(jnp.bfloat16))
+    pb = jnp.concatenate(ps, axis=1)
     m_out[0] = m_new
-    a_out[0] = a_in[0] * alpha
-
-    def mix(j, tot):
-        p = jnp.exp(s_ref[j] - m_new)
-        kc = k_ref[owner_ref[t, j]]
-        a_out[0] += lax.dot_general(
-            kc, p.astype(jnp.bfloat16), (((0,), (0,)), ((), ())),
-            preferred_element_type=jnp.float32,
-        )
-        return tot + jnp.sum(p, axis=0, keepdims=True)
-
-    t_out[0] = lax.fori_loop(0, n, mix, t_in[0] * alpha)
+    a_out[0] = a_in[0] * alpha + jnp.dot(pb, kall, preferred_element_type=jnp.float32)
+    t_out[0] = t_in[0] * alpha + jnp.sum(acc, axis=1, keepdims=True)
 
 
-def attend_chunk(state, query_t, chunk, slot_owner, counts, scale):
-    tiles, channels, tile_size = query_t.shape
+def attend_chunk(state, queries, chunk, slot_owner, counts, scale):
+    tiles, tile_size, channels = queries.shape
     owners, chunk_len, _ = chunk.shape
     slots = slot_owner.shape[1]
     m, tot, acc = state
-    row_spec = pl.BlockSpec((1, 1, tile_size), lambda t, o, c: (t, 0, 0))
-    acc_spec = pl.BlockSpec((1, channels, tile_size), lambda t, o, c: (t, 0, 0))
+    col_spec = pl.BlockSpec((1, tile_size, 1), lambda t, o, c: (t, 0, 0))
+    acc_spec = pl.BlockSpec((1, tile_size, channels), lambda t, o, c: (t, 0, 0))
     grid_spec = pltpu.PrefetchScalarGridSpec(
         num_scalar_prefetch=2,
         grid=(tiles,),
         in_specs=[
-            pl.BlockSpec((1, channels, tile_size), lambda t, o, c: (t, 0, 0)),
+            acc_spec,
             pl.BlockSpec((owners, chunk_len, channels), lambda t, o, c: (0, 0, 0)),
-            row_spec,
-            row_spec,
+            col_spec,
+            col_spec,
             acc_spec,
         ],
-        out_specs=[row_spec, row_spec, acc_spec],
-        scratch_shapes=[pltpu.VMEM((slots, chunk_len, tile_size), jnp.float32)],
+        out_specs=[col_spec, col_spec, acc_spec],
+        scratch_shapes=[pltpu.VMEM((slots * chunk_len, channels), jnp.bfloat16)],
     )
     return pl.pallas_call(
         functools.partial(attend_kernel, scale=scale),
@@ -94,7 +99,7 @@
         ],
         input_output_aliases={4: 0, 5: 1, 6: 2},
         compiler_params=pltpu.CompilerParams(vmem_limit_bytes=48 * 1024 * 1024),
-    )(slot_owner, counts, query_t, chunk, m, tot, acc)
+    )(slot_owner, counts, queries, chunk, m, tot, acc)
 
 
 def on_device(frame_one, frame_two, tile_lists, conv_one, conv_two):
@@ -125,13 +130,12 @@
     )[:, 0]
     picked = jnp.take(own_keys, jnp.maximum(asked, 0), axis=0)
     outgoing = jnp.where((asked >= 0)[:, None, None], picked, jnp.zeros_like(picked))
-    query_t = query_tiles.transpose(0, 2, 1)
-    pieces = 4
+    pieces = 2
     chunk_len = tile_size // pieces
     state = (
-        jnp.full((per_device, 1, tile_size), -jnp.inf, jnp.float32),
-        jnp.zeros((per_device, 1, tile_size), jnp.float32),
-        jnp.zeros((per_device, channels, tile_size), jnp.float32),
+        jnp.full((per_device, tile_size, 1), -jnp.inf, jnp.float32),
+        jnp.zeros((per_device, tile_size, 1), jnp.float32),
+        jnp.zeros((per_device, tile_size, channels), jnp.float32),
     )
     previous = None
     for piece in range(pieces):
@@ -140,10 +144,10 @@
             previous, sending, state = lax.optimization_barrier((previous, sending, state))
         current = lax.all_to_all(sending, "row", split_axis=0, concat_axis=0, tiled=True)
         if previous is not None:
-            state = attend_chunk(state, query_t, previous, slot_owner, counts, scale)
+            state = attend_chunk(state, query_tiles, previous, slot_owner, counts, scale)
         previous = current
-    state = attend_chunk(state, query_t, previous, slot_owner, counts, scale)
-    warped_tiles = (state[2] / state[1]).astype(jnp.bfloat16).transpose(0, 2, 1)
+    state = attend_chunk(state, query_tiles, previous, slot_owner, counts, scale)
+    warped_tiles = (state[2] / state[1]).astype(jnp.bfloat16)
     warped = (
         warped_tiles.reshape(per_device, band_rows, tile_cols, channels)
         .transpose(1, 0, 2, 3)

time: 131 us -> 114 us (0.87)
  Pallas kernels: 58.4 us -> 23 us
  waiting for transfers between devices: 8.79 us -> 21.7 us
  blocking collectives: 18.6 us -> 30.4 us
  starting transfers between devices: 24.9 us -> 16.4 us
  local copies, waits for them, and re-layouts: 7.6 us -> 9.69 us
    pallas_call x4 -> x2, Pallas kernels: 58.4 us -> 23 us  [attend_chunk(): pl.pallas_call(functools.partial(attend_kernel, scale=scale), grid_spec=g...]
    all_to_all x3 -> x1, waiting for transfers between devices: 0.01 us -> 12.6 us  [on_device(): lax.all_to_all(sending, 'row', split_axis=0, concat_axis=0, tiled=True)]
    all_to_all x1, blocking collectives: 18.6 us -> 30.4 us  [on_device(): lax.all_to_all(sending, 'row', split_axis=0, concat_axis=0, tiled=True)]
    all_to_all x3 -> x1, starting transfers between devices: 14 us -> 4.51 us  [on_device(): lax.all_to_all(sending, 'row', split_axis=0, concat_axis=0, tiled=True)]
    unnamed x7 -> x14, local copies, waits for them, and re-layouts: 0.09 us -> 3.05 us
  transfers between devices with their start and end apart: 6 -> 4, of which waited for: 3 -> 4; matrix products, arithmetic and copies ran while one was open for 1% -> 1% of each run, Pallas kernels for 34% -> 10%
where the time goes in v2:
time: 114 us; the launch traced here: 112 us
  blocking collectives  30.4 us (27%)
  Pallas kernels  23 us (20%)
  waiting for transfers between devices  21.7 us (19%)
  starting transfers between devices  16.4 us (14%)
  local copies, waits for them, and re-layouts  9.69 us (8%)
  matrix products  5.68 us (5%)
  other arithmetic  4.95 us (4%)
    all_to_all x1, blocking collectives, on_device(): lax.all_to_all(sending, 'row', split_axis=0, concat_axis=0, tiled=True)  30.4 us
    pallas_call x2, Pallas kernels, attend_chunk(): pl.pallas_call(functools.partial(attend_kernel, scale=scale), grid_spec=g...  23 us
    all_to_all x1, waiting for transfers between devices, on_device(): lax.all_to_all(sending, 'row', split_axis=0, concat_axis=0, tiled=True)  12.6 us
    all_to_all x1, starting transfers between devices, on_device(): lax.all_to_all(wanted.reshape(owners, 1), 'row', split_axis=0, concat_axi...  6.61 us
    dot_general x18, matrix products, convolve_rows(): jnp.dot(window, weights[row_shift, col_shift], preferred_element_type=jnp...  5.68 us
    all_to_all x1, starting transfers between devices, on_device(): lax.all_to_all(sending, 'row', split_axis=0, concat_axis=0, tiled=True)  4.51 us
    ppermute x1, waiting for transfers between devices, halo_rows(): from_below = lax.ppermute(head, axis, [(i + 1, i) for i in range(ends)])  4.4 us
    all_to_all x1, waiting for transfers between devices, on_device(): lax.all_to_all(wanted.reshape(owners, 1), 'row', split_axis=0, concat_axi...  3.54 us
  transfers between devices with their start and end apart: 4, of which 4 were waited for; matrix products, arithmetic and copies ran while one was open for 1% of the time, Pallas kernels for 10%

profile of v2, /device:TPU:9, one launch (start us, length us, event | category | flops | bytes accessed | tf_op | source)
XLA Modules:
  0.0 112.1 jit_solution(5753159122200634429)
XLA Ops:
  0.0 0.8 convert_reduce_fusion
  0.8 0.7 fusion.43.owner_ref
  1.9 0.7 copy.30
  2.6 6.6 %all-to-all-start = ((s32[16,1,1]{2,1,0:T(1,128)}), s32[16,1,1]{2,1,0:T(1,128)S(1)}, u32[]{:S(2)}, u32[]{:S(2)}) async-start(s32[16,1,1]{2,1,0:T(1,128)} %copy.30), calls=%async_computation | async-start | bytes 16384 | tf_op jit(solution)/shard_map/all_to_all | solution.py:128
  9.2 1.1 copy.31
  10.3 3.5 %all-to-all-done = s32[16,1,1]{2,1,0:T(1,128)S(1)} async-done(((s32[16,1,1]{2,1,0:T(1,128)}), s32[16,1,1]{2,1,0:T(1,128)S(1)}, u32[]{:S(2)}, u32[]{:S(2)}) %all-to-all-start) | async-done | bytes 96 | tf_op jit(solution)/shard_map/all_to_all | solution.py:128
  13.8 0.4 maximum_reduce_fusion
  14.2 1.0 gather_fusion
  15.2 0.7 compare_reduce_fusion.1
  15.8 0.3 select_select_fusion
  16.2 1.1 %fusion.45 = (bf16[16,256,128]{2,1,0:T(8,128)(2,1)}, bf16[16,256,128]{2,1,0:T(8,128)(2,1)S(1)}) fusion(bf16[16,512,128]{2,1,0:T(8,128)(2,1)S(1)} %select_select_fusion), kind=kLoop, calls=%fused_computation.97 | loop fusion | bytes 4194304 | tf_op jit(solution)/shard_map/slice | solution.py:142
  17.3 30.4 %all_to_all.19.k_ref = bf16[16,256,128]{2,1,0:T(8,128)(2,1)} all-to-all(bf16[16,256,128]{2,1,0:T(8,128)(2,1)S(1)} %get-tuple-element.30), channel_id=1, replica_groups=mesh['pairs'=2,'row'=16] {'row'}, dimensions={0} | all-to-all | bytes 2097152 | tf_op jit(solution)/shard_map/all_to_all | solution.py:145
  47.6 4.5 %all-to-all-start.2 = ((bf16[16,256,128]{2,1,0:T(8,128)(2,1)}), bf16[16,256,128]{2,1,0:T(8,128)(2,1)}, u32[]{:S(2)}, u32[]{:S(2)}) async-start(bf16[16,256,128]{2,1,0:T(8,128)(2,1)} %get-tuple-element.15), calls=%async_computation.2 | async-start | bytes 2097152 | tf_op jit(solution)/shard_map/all_to_all | solution.py:145
  52.5 0.5 copy-done
  53.0 0.6 copy-done.2
  53.6 10.9 %shard_map.55 = (f32[4,512,1]{2,1,0:T(8,128)S(1)}, f32[4,512,1]{2,1,0:T(8,128)S(1)}, f32[4,512,128]{2,1,0:T(8,128)S(1)}) custom-call(s32[4,9]{1,0:T(4,128)S(1)} %fusion.43.owner_ref, s32[4]{0:T(128)S(1)} %get-tuple-element.27.count_ref, bf16[4,512,128]{2,1,0:T(8,128)(2,1)S(1)} %bitcast.108, ...), custom_call_target="tpu_custom_call", output_to_operand_aliasing={{0}: (4, {}), {1}: (5, {}), {2}: (6, {})} | custom-call | tf_op jit(solution)/shard_map/pallas_call | solution.py:92
  64.5 12.6 %all-to-all-done.2.k_ref = bf16[16,256,128]{2,1,0:T(8,128)(2,1)} async-done(((bf16[16,256,128]{2,1,0:T(8,128)(2,1)}), bf16[16,256,128]{2,1,0:T(8,128)(2,1)}, u32[]{:S(2)}, u32[]{:S(2)}) %all-to-all-start.2) | async-done | bytes 1048608 | tf_op jit(solution)/shard_map/all_to_all | solution.py:145
  77.1 1.0 copy-done.1
  78.2 12.1 %shard_map.56 = (f32[4,512,1]{2,1,0:T(8,128)S(1)}, f32[4,512,1]{2,1,0:T(8,128)S(1)}, f32[4,512,128]{2,1,0:T(8,128)S(1)}) custom-call(s32[4,9]{1,0:T(4,128)S(1)} %fusion.43.owner_ref, s32[4]{0:T(128)S(1)} %get-tuple-element.27.count_ref, bf16[4,512,128]{2,1,0:T(8,128)(2,1)S(1)} %bitcast.109, ...), custom_call_target="tpu_custom_call", output_to_operand_aliasing={{0}: (4, {}), {1}: (5, {}), {2}: (6, {})} | custom-call | tf_op jit(solution)/shard_map/pallas_call | solution.py:92
  90.3 0.3 reduce.3
  90.6 0.3 divide_convert_fusion
  91.1 3.2 %collective-permute-start = (bf16[2,512,128]{2,1,0:T(8,128)(2,1)S(1)}, bf16[2,512,128]{2,1,0:T(8,128)(2,1)S(1)}, u32[]{:S(2)}, u32[]{:S(2)}) collective-permute-start(bf16[2,512,128]{2,1,0:T(8,128)(2,1)S(1)} %bitcast.138), channel_id=1, source_target_pairs={{0,1},{1,2},{2,3},{3,4},{4,5},{5,6},{6,7},{7,8},{8,9},{9,10},{10,1... | collective-permute-start | bytes 786440 | tf_op jit(solution)/shard_map/ppermute | solution.py:16
  94.3 2.1 %collective-permute-start.1 = (bf16[2,512,128]{2,1,0:T(8,128)(2,1)S(1)}, bf16[2,512,128]{2,1,0:T(8,128)(2,1)S(1)}, u32[]{:S(2)}, u32[]{:S(2)}) collective-permute-start(bf16[2,512,128]{2,1,0:T(8,128)(2,1)S(1)} %bitcast.137), channel_id=1, source_target_pairs={{1,0},{2,1},{3,2},{4,3},{5,4},{6,5},{7,6},{8,7},{9,8},{10,9},{11,1... | collective-permute-start | bytes 786440 | tf_op jit(solution)/shard_map/ppermute | solution.py:17
  96.4 1.2 %collective-permute-done = bf16[2,512,128]{2,1,0:T(8,128)(2,1)S(1)} collective-permute-done((bf16[2,512,128]{2,1,0:T(8,128)(2,1)S(1)}, bf16[2,512,128]{2,1,0:T(8,128)(2,1)S(1)}, u32[]{:S(2)}, u32[]{:S(2)}) %collective-permute-start) | collective-permute-done | bytes 262176 | tf_op jit(solution)/shard_map/ppermute | solution.py:16
  97.6 4.4 %collective-permute-done.1 = bf16[2,512,128]{2,1,0:T(8,128)(2,1)S(1)} collective-permute-done((bf16[2,512,128]{2,1,0:T(8,128)(2,1)S(1)}, bf16[2,512,128]{2,1,0:T(8,128)(2,1)S(1)}, u32[]{:S(2)}, u32[]{:S(2)}) %collective-permute-start.1) | collective-permute-done | bytes 262176 | tf_op jit(solution)/shard_map/ppermute | solution.py:17
  102.1 1.3 %pad_slice_fusion.1 = (bf16[6,512,128]{2,1,0:T(8,128)(2,1)S(1)}, bf16[6,512,128]{2,1,0:T(8,128)(2,1)S(1)}, bf16[6,512,128]{2,1,0:T(8,128)(2,1)S(1)}, bf16[6,512,...) fusion(bf16[8,512,128]{2,1,0:T(8,128)(2,1)S(1)} %pad_maximum_fusion), kind=kLoop, calls=%fused_computation.27 | loop fusion | bytes 7340032 | tf_op jit(solution)/shard_map/slice | solution.py:26
  103.4 0.3 fusion.22
  103.8 0.3 fusion.13
  104.1 0.1 pad_maximum_fusion.2
  104.3 0.3 convolution_add_fusion.6
  104.6 0.4 convolution_add_fusion.5
  105.0 0.4 convolution_add_fusion.4
  105.3 0.4 convolution_add_fusion.3
  105.7 0.4 convolution_add_fusion.2
  106.1 0.4 convolution_add_fusion.1
  106.4 0.4 fusion.2
  106.9 0.9 pad_slice_fusion.6
  107.9 0.3 fusion.11
  108.2 0.3 convolution_add_fusion.14
  108.5 0.3 convolution_add_fusion.13
  108.7 0.3 convolution_add_fusion.12
  109.0 0.3 convolution_add_fusion.11
  109.3 0.3 convolution_add_fusion.10
  109.6 0.3 convolution_add_fusion.9
  109.9 0.3 convolution_add_fusion.8
  110.2 0.3 convolution_add_fusion.7
  110.5 0.7 copy-done.4
  111.2 0.9 add_convert_fusion
  (24 shorter events, 1.1 us)
Async XLA Ops:
  2.6 11.2 %all-to-all-start = ((s32[16,1,1]{2,1,0:T(1,128)}), s32[16,1,1]{2,1,0:T(1,128)S(1)}, u32[]{:S(2)}, u32[]{:S(2)}) async-start(s32[16,1,1]{2,1,0:T(1,128)} %copy.30), calls=%async_computation | async-start | bytes 16384 | tf_op jit(solution)/shard_map/all_to_all | solution.py:128
  47.6 4.5 %copy-start.3 = (bf16[4,512,128]{2,1,0:T(8,128)(2,1)S(1)}, bf16[4,512,128]{2,1,0:T(8,128)(2,1)}, u32[]{:S(2)}) copy-start(bf16[4,512,128]{2,1,0:T(8,128)(2,1)} %param.5) | copy-start | bytes 1572868
  47.6 29.5 %all-to-all-start.2 = ((bf16[16,256,128]{2,1,0:T(8,128)(2,1)}), bf16[16,256,128]{2,1,0:T(8,128)(2,1)}, u32[]{:S(2)}, u32[]{:S(2)}) async-start(bf16[16,256,128]{2,1,0:T(8,128)(2,1)} %get-tuple-element.15), calls=%async_computation.2 | async-start | bytes 2097152 | tf_op jit(solution)/shard_map/all_to_all | solution.py:145
  52.2 0.8 copy-start
  52.2 1.4 %copy-start.2 = (bf16[16,256,128]{2,1,0:T(8,128)(2,1)S(1)}, bf16[16,256,128]{2,1,0:T(8,128)(2,1)}, u32[]{:S(2)}) copy-start(bf16[16,256,128]{2,1,0:T(8,128)(2,1)} %all_to_all.19.k_ref) | copy-start | bytes 3145732
  77.1 1.0 copy-start.1
  91.1 6.5 %collective-permute-start = (bf16[2,512,128]{2,1,0:T(8,128)(2,1)S(1)}, bf16[2,512,128]{2,1,0:T(8,128)(2,1)S(1)}, u32[]{:S(2)}, u32[]{:S(2)}) collective-permute-start(bf16[2,512,128]{2,1,0:T(8,128)(2,1)S(1)} %bitcast.138), channel_id=1, source_target_pairs={{0,1},{1,2},{2,3},{3,4},{4,5},{5,6},{6,7},{7,8},{8,9},{9,10},{10,1... | collective-permute-start | bytes 786440 | tf_op jit(solution)/shard_map/ppermute | solution.py:16
  94.3 7.7 %collective-permute-start.1 = (bf16[2,512,128]{2,1,0:T(8,128)(2,1)S(1)}, bf16[2,512,128]{2,1,0:T(8,128)(2,1)S(1)}, u32[]{:S(2)}, u32[]{:S(2)}) collective-permute-start(bf16[2,512,128]{2,1,0:T(8,128)(2,1)S(1)} %bitcast.137), channel_id=1, source_target_pairs={{1,0},{2,1},{3,2},{4,3},{5,4},{6,5},{7,6},{8,7},{9,8},{10,9},{11,1... | collective-permute-start | bytes 786440 | tf_op jit(solution)/shard_map/ppermute | solution.py:17
  102.1 1.3 %copy-start.5 = (bf16[3,3,128,128]{3,2,1,0:T(8,128)(2,1)S(1)}, bf16[3,3,128,128]{3,2,1,0:T(8,128)(2,1)}, u32[]{:S(2)}) copy-start(bf16[3,3,128,128]{3,2,1,0:T(8,128)(2,1)} %param.8) | copy-start | bytes 884740
  106.9 1.0 copy-start.6
  110.2 1.0 copy-start.4

commit v3 on v2

--- a/solution.py
+++ b/solution.py
@@ -50,17 +50,18 @@
     blocks = [(j, j * span + c * lanes) for j in range(slots) for c in range(span // lanes)]
     mx = None
     for j, at in blocks:
-        blk = s[:, at : at + lanes] - penalty[j]
+        blk = s[:, at : at + lanes]
         mx = blk if mx is None else jnp.maximum(mx, blk)
     m_old = m_in[0]
     m_new = jnp.maximum(m_old, jnp.max(mx, axis=1, keepdims=True) * scale)
     alpha = jnp.exp(m_old - m_new)
-    mb = jnp.broadcast_to(m_new, (m_new.shape[0], lanes))
+    log2e = 1.4426950408889634
+    mb = jnp.broadcast_to(m_new * log2e, (m_new.shape[0], lanes))
     shifted = [mb + penalty[j] for j in range(slots)]
     acc = None
     ps = []
     for j, at in blocks:
-        p = jnp.exp(s[:, at : at + lanes] * scale - shifted[j])
+        p = jnp.exp2(s[:, at : at + lanes] * (scale * log2e) - shifted[j])
         acc = p if acc is None else acc + p
         ps.append(p.astype(jnp.bfloat16))
     pb = jnp.concatenate(ps, axis=1)
@@ -120,7 +121,7 @@
     query_tiles = band_to_tiles(frame_one)
     own_keys = band_to_tiles(frame_two)
     valid = tile_lists >= 0
-    slot_owner = jnp.where(valid, tile_lists // per_device, 0).astype(jnp.int32)
+    slot_owner = jnp.maximum(jnp.where(valid, tile_lists, tile_lists[:, :1]), 0) // per_device
     counts = jnp.sum(valid.astype(jnp.int32), axis=1)
     owner_iota = jnp.arange(owners, dtype=jnp.int32)
     matches = (slot_owner[:, :, None] == owner_iota[None, None, :]) & valid[:, :, None]

time: 114 us -> 114 us (level)
  Pallas kernels: 23 us -> 21.7 us
    pallas_call x2, Pallas kernels: 23 us -> 21.7 us  [attend_chunk(): pl.pallas_call(functools.partial(attend_kernel, scale=scale), grid_spec=g...]
  transfers between devices with their start and end apart: 4 -> 4, of which waited for: 4 -> 4; matrix products, arithmetic and copies ran while one was open for 1% -> 1% of each run, Pallas kernels for 10% -> 9%
where the time goes in v3:
time: 114 us; the launch traced here: 112 us
  blocking collectives  30.3 us (27%)
  waiting for transfers between devices  22.3 us (20%)
  Pallas kernels  21.7 us (19%)
  starting transfers between devices  16.4 us (14%)
  local copies, waits for them, and re-layouts  10.5 us (9%)
  matrix products  5.66 us (5%)
  other arithmetic  5.01 us (4%)
    all_to_all x1, blocking collectives, on_device(): lax.all_to_all(sending, 'row', split_axis=0, concat_axis=0, tiled=True)  30.3 us
    pallas_call x2, Pallas kernels, attend_chunk(): pl.pallas_call(functools.partial(attend_kernel, scale=scale), grid_spec=g...  21.7 us
    all_to_all x1, waiting for transfers between devices, on_device(): lax.all_to_all(sending, 'row', split_axis=0, concat_axis=0, tiled=True)  13.2 us
    all_to_all x1, starting transfers between devices, on_device(): lax.all_to_all(wanted.reshape(owners, 1), 'row', split_axis=0, concat_axi...  6.61 us
    dot_general x18, matrix products, convolve_rows(): jnp.dot(window, weights[row_shift, col_shift], preferred_element_type=jnp...  5.66 us
    all_to_all x1, starting transfers between devices, on_device(): lax.all_to_all(sending, 'row', split_axis=0, concat_axis=0, tiled=True)  4.51 us
    ppermute x1, waiting for transfers between devices, halo_rows(): from_below = lax.ppermute(head, axis, [(i + 1, i) for i in range(ends)])  4.4 us
    all_to_all x1, waiting for transfers between devices, on_device(): lax.all_to_all(wanted.reshape(owners, 1), 'row', split_axis=0, concat_axi...  3.54 us
  transfers between devices with their start and end apart: 4, of which 4 were waited for; matrix products, arithmetic and copies ran while one was open for 1% of the time, Pallas kernels for 9%

profile of v3, /device:TPU:9, one launch (start us, length us, event | category | flops | bytes accessed | tf_op | source)
XLA Modules:
  0.0 112.3 jit_solution(17576128717716683456)
XLA Ops:
  0.0 0.8 convert_reduce_fusion
  0.8 0.8 slice_reduce_fusion
  1.7 0.8 add_select_fusion.1.owner_ref
  2.8 0.7 copy.30
  3.5 6.6 %all-to-all-start = ((s32[16,1,1]{2,1,0:T(1,128)}), s32[16,1,1]{2,1,0:T(1,128)S(1)}, u32[]{:S(2)}, u32[]{:S(2)}) async-start(s32[16,1,1]{2,1,0:T(1,128)} %copy.30), calls=%async_computation | async-start | bytes 16384 | tf_op jit(solution)/shard_map/all_to_all | solution.py:129
  10.1 1.1 copy.31
  11.1 3.5 %all-to-all-done = s32[16,1,1]{2,1,0:T(1,128)S(1)} async-done(((s32[16,1,1]{2,1,0:T(1,128)}), s32[16,1,1]{2,1,0:T(1,128)S(1)}, u32[]{:S(2)}, u32[]{:S(2)}) %all-to-all-start) | async-done | bytes 96 | tf_op jit(solution)/shard_map/all_to_all | solution.py:129
  14.7 0.4 maximum_reduce_fusion
  15.1 1.0 gather_fusion
  16.0 0.7 compare_reduce_fusion.1
  16.7 0.3 select_select_fusion
  17.0 1.1 %fusion.45 = (bf16[16,256,128]{2,1,0:T(8,128)(2,1)}, bf16[16,256,128]{2,1,0:T(8,128)(2,1)S(1)}) fusion(bf16[16,512,128]{2,1,0:T(8,128)(2,1)S(1)} %select_select_fusion), kind=kLoop, calls=%fused_computation.98 | loop fusion | bytes 4194304 | tf_op jit(solution)/shard_map/slice | solution.py:143
  18.2 30.3 %all_to_all.19.k_ref = bf16[16,256,128]{2,1,0:T(8,128)(2,1)} all-to-all(bf16[16,256,128]{2,1,0:T(8,128)(2,1)S(1)} %get-tuple-element.30), channel_id=1, replica_groups=mesh['pairs'=2,'row'=16] {'row'}, dimensions={0} | all-to-all | bytes 2097152 | tf_op jit(solution)/shard_map/all_to_all | solution.py:146
  48.5 4.5 %all-to-all-start.2 = ((bf16[16,256,128]{2,1,0:T(8,128)(2,1)}), bf16[16,256,128]{2,1,0:T(8,128)(2,1)}, u32[]{:S(2)}, u32[]{:S(2)}) async-start(bf16[16,256,128]{2,1,0:T(8,128)(2,1)} %get-tuple-element.15), calls=%async_computation.2 | async-start | bytes 2097152 | tf_op jit(solution)/shard_map/all_to_all | solution.py:146
  53.3 0.5 copy-done
  53.9 0.6 copy-done.2
  54.5 10.2 %shard_map.55 = (f32[4,512,1]{2,1,0:T(8,128)S(1)}, f32[4,512,1]{2,1,0:T(8,128)S(1)}, f32[4,512,128]{2,1,0:T(8,128)S(1)}) custom-call(s32[4,9]{1,0:T(4,128)S(1)} %add_select_fusion.1.owner_ref, s32[4]{0:T(128)S(1)} %get-tuple-element.27.count_ref, bf16[4,512,128]{2,1,0:T(8,128)(2,1)S(1)} %bitcast.108, ...), custom_call_target="tpu_custom_call", output_to_operand_aliasing={{0}: (4, {}), {1}: (5, {}), {2}: (6, {})} | custom-call | tf_op jit(solution)/shard_map/pallas_call | solution.py:93
  64.8 13.2 %all-to-all-done.2.k_ref = bf16[16,256,128]{2,1,0:T(8,128)(2,1)} async-done(((bf16[16,256,128]{2,1,0:T(8,128)(2,1)}), bf16[16,256,128]{2,1,0:T(8,128)(2,1)}, u32[]{:S(2)}, u32[]{:S(2)}) %all-to-all-start.2) | async-done | bytes 1048608 | tf_op jit(solution)/shard_map/all_to_all | solution.py:146
  78.0 1.0 copy-done.1
  79.0 11.4 %shard_map.56 = (f32[4,512,1]{2,1,0:T(8,128)S(1)}, f32[4,512,1]{2,1,0:T(8,128)S(1)}, f32[4,512,128]{2,1,0:T(8,128)S(1)}) custom-call(s32[4,9]{1,0:T(4,128)S(1)} %add_select_fusion.1.owner_ref, s32[4]{0:T(128)S(1)} %get-tuple-element.27.count_ref, bf16[4,512,128]{2,1,0:T(8,128)(2,1)S(1)} %bitcast.109, ...), custom_call_target="tpu_custom_call", output_to_operand_aliasing={{0}: (4, {}), {1}: (5, {}), {2}: (6, {})} | custom-call | tf_op jit(solution)/shard_map/pallas_call | solution.py:93
  90.5 0.3 reduce.4
  90.8 0.3 divide_convert_fusion
  91.3 3.2 %collective-permute-start = (bf16[2,512,128]{2,1,0:T(8,128)(2,1)S(1)}, bf16[2,512,128]{2,1,0:T(8,128)(2,1)S(1)}, u32[]{:S(2)}, u32[]{:S(2)}) collective-permute-start(bf16[2,512,128]{2,1,0:T(8,128)(2,1)S(1)} %bitcast.138), channel_id=1, source_target_pairs={{0,1},{1,2},{2,3},{3,4},{4,5},{5,6},{6,7},{7,8},{8,9},{9,10},{10,1... | collective-permute-start | bytes 786440 | tf_op jit(solution)/shard_map/ppermute | solution.py:16
  94.5 2.1 %collective-permute-start.1 = (bf16[2,512,128]{2,1,0:T(8,128)(2,1)S(1)}, bf16[2,512,128]{2,1,0:T(8,128)(2,1)S(1)}, u32[]{:S(2)}, u32[]{:S(2)}) collective-permute-start(bf16[2,512,128]{2,1,0:T(8,128)(2,1)S(1)} %bitcast.137), channel_id=1, source_target_pairs={{1,0},{2,1},{3,2},{4,3},{5,4},{6,5},{7,6},{8,7},{9,8},{10,9},{11,1... | collective-permute-start | bytes 786440 | tf_op jit(solution)/shard_map/ppermute | solution.py:17
  96.6 1.2 %collective-permute-done = bf16[2,512,128]{2,1,0:T(8,128)(2,1)S(1)} collective-permute-done((bf16[2,512,128]{2,1,0:T(8,128)(2,1)S(1)}, bf16[2,512,128]{2,1,0:T(8,128)(2,1)S(1)}, u32[]{:S(2)}, u32[]{:S(2)}) %collective-permute-start) | collective-permute-done | bytes 262176 | tf_op jit(solution)/shard_map/ppermute | solution.py:16
  97.8 4.4 %collective-permute-done.1 = bf16[2,512,128]{2,1,0:T(8,128)(2,1)S(1)} collective-permute-done((bf16[2,512,128]{2,1,0:T(8,128)(2,1)S(1)}, bf16[2,512,128]{2,1,0:T(8,128)(2,1)S(1)}, u32[]{:S(2)}, u32[]{:S(2)}) %collective-permute-start.1) | collective-permute-done | bytes 262176 | tf_op jit(solution)/shard_map/ppermute | solution.py:17
  102.3 1.3 %pad_slice_fusion.1 = (bf16[6,512,128]{2,1,0:T(8,128)(2,1)S(1)}, bf16[6,512,128]{2,1,0:T(8,128)(2,1)S(1)}, bf16[6,512,128]{2,1,0:T(8,128)(2,1)S(1)}, bf16[6,512,...) fusion(bf16[8,512,128]{2,1,0:T(8,128)(2,1)S(1)} %pad_maximum_fusion), kind=kLoop, calls=%fused_computation.27 | loop fusion | bytes 7340032 | tf_op jit(solution)/shard_map/slice | solution.py:26
  103.6 0.3 fusion.22
  104.0 0.4 fusion.13
  104.5 0.3 convolution_add_fusion.6
  104.8 0.3 convolution_add_fusion.5
  105.2 0.4 convolution_add_fusion.4
  105.5 0.4 convolution_add_fusion.3
  105.9 0.4 convolution_add_fusion.2
  106.2 0.4 convolution_add_fusion.1
  106.6 0.4 fusion.2
  107.1 0.9 pad_slice_fusion.6
  108.1 0.3 fusion.11
  108.3 0.3 convolution_add_fusion.14
  108.6 0.3 convolution_add_fusion.13
  108.9 0.3 convolution_add_fusion.12
  109.2 0.3 convolution_add_fusion.11
  109.5 0.3 convolution_add_fusion.10
  109.8 0.3 convolution_add_fusion.9
  110.0 0.3 convolution_add_fusion.8
  110.3 0.3 convolution_add_fusion.7
  110.6 0.7 copy-done.4
  111.4 0.9 add_convert_fusion
  (25 shorter events, 1.2 us)
Async XLA Ops:
  3.5 11.2 %all-to-all-start = ((s32[16,1,1]{2,1,0:T(1,128)}), s32[16,1,1]{2,1,0:T(1,128)S(1)}, u32[]{:S(2)}, u32[]{:S(2)}) async-start(s32[16,1,1]{2,1,0:T(1,128)} %copy.30), calls=%async_computation | async-start | bytes 16384 | tf_op jit(solution)/shard_map/all_to_all | solution.py:129
  48.5 4.5 %copy-start.3 = (bf16[4,512,128]{2,1,0:T(8,128)(2,1)S(1)}, bf16[4,512,128]{2,1,0:T(8,128)(2,1)}, u32[]{:S(2)}) copy-start(bf16[4,512,128]{2,1,0:T(8,128)(2,1)} %param.5) | copy-start | bytes 1572868
  48.5 29.5 %all-to-all-start.2 = ((bf16[16,256,128]{2,1,0:T(8,128)(2,1)}), bf16[16,256,128]{2,1,0:T(8,128)(2,1)}, u32[]{:S(2)}, u32[]{:S(2)}) async-start(bf16[16,256,128]{2,1,0:T(8,128)(2,1)} %get-tuple-element.15), calls=%async_computation.2 | async-start | bytes 2097152 | tf_op jit(solution)/shard_map/all_to_all | solution.py:146
  53.1 0.8 copy-start
  53.1 1.4 %copy-start.2 = (bf16[16,256,128]{2,1,0:T(8,128)(2,1)S(1)}, bf16[16,256,128]{2,1,0:T(8,128)(2,1)}, u32[]{:S(2)}) copy-start(bf16[16,256,128]{2,1,0:T(8,128)(2,1)} %all_to_all.19.k_ref) | copy-start | bytes 3145732
  78.0 1.0 copy-start.1
  91.3 6.5 %collective-permute-start = (bf16[2,512,128]{2,1,0:T(8,128)(2,1)S(1)}, bf16[2,512,128]{2,1,0:T(8,128)(2,1)S(1)}, u32[]{:S(2)}, u32[]{:S(2)}) collective-permute-start(bf16[2,512,128]{2,1,0:T(8,128)(2,1)S(1)} %bitcast.138), channel_id=1, source_target_pairs={{0,1},{1,2},{2,3},{3,4},{4,5},{5,6},{6,7},{7,8},{8,9},{9,10},{10,1... | collective-permute-start | bytes 786440 | tf_op jit(solution)/shard_map/ppermute | solution.py:16
  94.5 7.7 %collective-permute-start.1 = (bf16[2,512,128]{2,1,0:T(8,128)(2,1)S(1)}, bf16[2,512,128]{2,1,0:T(8,128)(2,1)S(1)}, u32[]{:S(2)}, u32[]{:S(2)}) collective-permute-start(bf16[2,512,128]{2,1,0:T(8,128)(2,1)S(1)} %bitcast.137), channel_id=1, source_target_pairs={{1,0},{2,1},{3,2},{4,3},{5,4},{6,5},{7,6},{8,7},{9,8},{10,9},{11,1... | collective-permute-start | bytes 786440 | tf_op jit(solution)/shard_map/ppermute | solution.py:17
  102.3 1.3 %copy-start.5 = (bf16[3,3,128,128]{3,2,1,0:T(8,128)(2,1)S(1)}, bf16[3,3,128,128]{3,2,1,0:T(8,128)(2,1)}, u32[]{:S(2)}) copy-start(bf16[3,3,128,128]{3,2,1,0:T(8,128)(2,1)} %param.8) | copy-start | bytes 884740
  107.1 1.0 copy-start.6
  110.3 1.0 copy-start.4

commit v4 on v3

--- a/solution.py
+++ b/solution.py
@@ -129,18 +129,16 @@
     asked = lax.all_to_all(
         wanted.reshape(owners, 1), "row", split_axis=0, concat_axis=0, tiled=True
     )[:, 0]
-    picked = jnp.take(own_keys, jnp.maximum(asked, 0), axis=0)
-    outgoing = jnp.where((asked >= 0)[:, None, None], picked, jnp.zeros_like(picked))
-    pieces = 2
-    chunk_len = tile_size // pieces
+    outgoing = jnp.take(own_keys, jnp.maximum(asked, 0), axis=0)
+    edges = [0, tile_size - tile_size // 4, tile_size]
     state = (
         jnp.full((per_device, tile_size, 1), -jnp.inf, jnp.float32),
         jnp.zeros((per_device, tile_size, 1), jnp.float32),
         jnp.zeros((per_device, tile_size, channels), jnp.float32),
     )
     previous = None
-    for piece in range(pieces):
-        sending = outgoing[:, piece * chunk_len : (piece + 1) * chunk_len]
+    for start, stop in zip(edges[:-1], edges[1:]):
+        sending = outgoing[:, start:stop]
         if previous is not None:
             previous, sending, state = lax.optimization_barrier((previous, sending, state))
         current = lax.all_to_all(sending, "row", split_axis=0, concat_axis=0, tiled=True)

time: 114 us -> 121 us (1.061)
  blocking collectives: 30.3 us -> 0 us
  waiting for transfers between devices: 22.3 us -> 42.7 us
  Pallas kernels: 21.7 us -> 28.8 us
  starting transfers between devices: 16.4 us -> 23 us
  local copies, waits for them, and re-layouts: 10.5 us -> 14.1 us
    all_to_all x1 -> x0, blocking collectives: 30.3 us -> none  [on_device(): lax.all_to_all(sending, 'row', split_axis=0, concat_axis=0, tiled=True)]
    all_to_all x1 -> x2, waiting for transfers between devices: 13.2 us -> 33.5 us  [on_device(): lax.all_to_all(sending, 'row', split_axis=0, concat_axis=0, tiled=True)]
    pallas_call x2, Pallas kernels: 21.7 us -> 28.8 us  [attend_chunk(): pl.pallas_call(functools.partial(attend_kernel, scale=scale), grid_spec=g...]
    all_to_all x1 -> x2, starting transfers between devices: 4.51 us -> 10.9 us  [on_device(): lax.all_to_all(sending, 'row', split_axis=0, concat_axis=0, tiled=True)]
    slice x1 -> x2, local copies, waits for them, and re-layouts: 1.15 us -> 3.21 us  [on_device(): sending = outgoing[:, start:stop]]
    unnamed x14 -> x18, local copies, waits for them, and re-layouts: 3.05 us -> 4.58 us
  transfers between devices with their start and end apart: 4 -> 5, of which waited for: 4 -> 4; matrix products, arithmetic and copies ran while one was open for 1% -> 3% of each run, Pallas kernels for 9% -> 17%
where the time goes in v4:
time: 121 us; the launch traced here: 119 us
  waiting for transfers between devices  42.7 us (35%)
  Pallas kernels  28.8 us (24%)
  starting transfers between devices  23 us (19%)
  local copies, waits for them, and re-layouts  14.1 us (12%)
  matrix products  5.68 us (5%)
  other arithmetic  4.69 us (4%)
    all_to_all x2, waiting for transfers between devices, on_device(): lax.all_to_all(sending, 'row', split_axis=0, concat_axis=0, tiled=True)  33.5 us
    pallas_call x2, Pallas kernels, attend_chunk(): pl.pallas_call(functools.partial(attend_kernel, scale=scale), grid_spec=g...  28.8 us
    all_to_all x2, starting transfers between devices, on_device(): lax.all_to_all(sending, 'row', split_axis=0, concat_axis=0, tiled=True)  10.9 us
    all_to_all x1, starting transfers between devices, on_device(): lax.all_to_all(wanted.reshape(owners, 1), 'row', split_axis=0, concat_axi...  6.61 us
    dot_general x18, matrix products, convolve_rows(): jnp.dot(window, weights[row_shift, col_shift], preferred_element_type=jnp...  5.68 us
    unnamed x18, local copies, waits for them, and re-layouts  4.58 us
    ppermute x1, waiting for transfers between devices, halo_rows(): from_below = lax.ppermute(head, axis, [(i + 1, i) for i in range(ends)])  4.43 us
    all_to_all x1, waiting for transfers between devices, on_device(): lax.all_to_all(wanted.reshape(owners, 1), 'row', split_axis=0, concat_axi...  3.54 us
  transfers between devices with their start and end apart: 5, of which 4 were waited for; matrix products, arithmetic and copies ran while one was open for 3% of the time, Pallas kernels for 17%

profile of v4, /device:TPU:9, one launch (start us, length us, event | category | flops | bytes accessed | tf_op | source)
XLA Modules:
  0.0 119.3 jit_solution(10892065515831867866)
XLA Ops:
  0.0 0.8 convert_reduce_fusion
  0.8 0.8 slice_reduce_fusion
  1.7 0.8 add_select_fusion.1.owner_ref
  2.8 0.7 copy.30
  3.5 6.6 %all-to-all-start = ((s32[16,1,1]{2,1,0:T(1,128)}), s32[16,1,1]{2,1,0:T(1,128)S(1)}, u32[]{:S(2)}, u32[]{:S(2)}) async-start(s32[16,1,1]{2,1,0:T(1,128)} %copy.30), calls=%async_computation | async-start | bytes 16384 | tf_op jit(solution)/shard_map/all_to_all | solution.py:129
  10.1 1.1 copy.31
  11.1 3.5 %all-to-all-done = s32[16,1,1]{2,1,0:T(1,128)S(1)} async-done(((s32[16,1,1]{2,1,0:T(1,128)}), s32[16,1,1]{2,1,0:T(1,128)S(1)}, u32[]{:S(2)}, u32[]{:S(2)}) %all-to-all-start) | async-done | bytes 96 | tf_op jit(solution)/shard_map/all_to_all | solution.py:129
  14.7 0.4 maximum_reduce_fusion
  15.1 1.0 gather_fusion
  16.0 0.4 compare_reduce_fusion
  16.4 0.3 broadcast_select_fusion
  16.7 1.3 %copy-done.4 = bf16[16,512,128]{2,1,0:T(8,128)(2,1)} copy-done((bf16[16,512,128]{2,1,0:T(8,128)(2,1)}, bf16[16,512,128]{2,1,0:T(8,128)(2,1)S(1)}, u32[]{:S(2)}) %copy-start.4) | copy-done | bytes 2097176
  18.1 1.3 %slice.176 = bf16[16,384,128]{2,1,0:T(8,128)(2,1)} slice(bf16[16,512,128]{2,1,0:T(8,128)(2,1)S(1)} %broadcast_select_fusion), slice={[0:16], [0:384], [0:128]} | slice | bytes 3145728 | tf_op jit(solution)/shard_map/slice | solution.py:141
  19.3 5.3 %all-to-all-start.1 = ((bf16[16,384,128]{2,1,0:T(8,128)(2,1)}), bf16[16,384,128]{2,1,0:T(8,128)(2,1)S(1)}, u32[]{:S(2)}, u32[]{:S(2)}) async-start(bf16[16,384,128]{2,1,0:T(8,128)(2,1)} %slice.176), calls=%async_computation.1 | async-start | bytes 3145728 | tf_op jit(solution)/shard_map/all_to_all | solution.py:144
  24.6 1.9 %slice.177 = bf16[16,128,128]{2,1,0:T(8,128)(2,1)} slice(bf16[16,512,128]{2,1,0:T(8,128)(2,1)} %copy-done.4), slice={[0:16], [384:512], [0:128]} | slice | bytes 1048576 | tf_op jit(solution)/shard_map/slice | solution.py:141
  26.6 33.5 %all-to-all-done.1.k_ref = bf16[16,384,128]{2,1,0:T(8,128)(2,1)S(1)} async-done(((bf16[16,384,128]{2,1,0:T(8,128)(2,1)}), bf16[16,384,128]{2,1,0:T(8,128)(2,1)S(1)}, u32[]{:S(2)}, u32[]{:S(2)}) %all-to-all-start.1) | async-done | bytes 1572896 | tf_op jit(solution)/shard_map/all_to_all | solution.py:144
  60.1 5.6 %all-to-all-start.2 = ((bf16[16,128,128]{2,1,0:T(8,128)(2,1)}), bf16[16,128,128]{2,1,0:T(8,128)(2,1)}, u32[]{:S(2)}, u32[]{:S(2)}) async-start(bf16[16,128,128]{2,1,0:T(8,128)(2,1)} %slice.177), calls=%async_computation.2 | async-start | bytes 1048576 | tf_op jit(solution)/shard_map/all_to_all | solution.py:144
  66.1 0.5 copy-done.2
  66.6 0.8 copy-done.1
  67.4 20.0 %shard_map.55 = (f32[4,512,1]{2,1,0:T(8,128)S(1)}, f32[4,512,1]{2,1,0:T(8,128)S(1)}, f32[4,512,128]{2,1,0:T(8,128)S(1)}) custom-call(s32[4,9]{1,0:T(4,128)S(1)} %add_select_fusion.1.owner_ref, s32[4]{0:T(128)S(1)} %get-tuple-element.25.count_ref, bf16[4,512,128]{2,1,0:T(8,128)(2,1)S(1)} %bitcast.108, ...), custom_call_target="tpu_custom_call", output_to_operand_aliasing={{0}: (4, {}), {1}: (5, {}), {2}: (6, {})} | custom-call | tf_op jit(solution)/shard_map/pallas_call | solution.py:93
  87.4 1.0 copy-done.3
  88.5 8.8 %shard_map.56 = (f32[4,512,1]{2,1,0:T(8,128)S(1)}, f32[4,512,1]{2,1,0:T(8,128)S(1)}, f32[4,512,128]{2,1,0:T(8,128)S(1)}) custom-call(s32[4,9]{1,0:T(4,128)S(1)} %add_select_fusion.1.owner_ref, s32[4]{0:T(128)S(1)} %get-tuple-element.25.count_ref, bf16[4,512,128]{2,1,0:T(8,128)(2,1)S(1)} %bitcast.109, ...), custom_call_target="tpu_custom_call", output_to_operand_aliasing={{0}: (4, {}), {1}: (5, {}), {2}: (6, {})} | custom-call | tf_op jit(solution)/shard_map/pallas_call | solution.py:93
  97.3 0.3 reduce.3
  97.6 0.4 divide_convert_fusion
  98.1 3.3 %collective-permute-start = (bf16[2,512,128]{2,1,0:T(8,128)(2,1)S(1)}, bf16[2,512,128]{2,1,0:T(8,128)(2,1)S(1)}, u32[]{:S(2)}, u32[]{:S(2)}) collective-permute-start(bf16[2,512,128]{2,1,0:T(8,128)(2,1)S(1)} %bitcast.138), channel_id=1, source_target_pairs={{0,1},{1,2},{2,3},{3,4},{4,5},{5,6},{6,7},{7,8},{8,9},{9,10},{10,1... | collective-permute-start | bytes 786440 | tf_op jit(solution)/shard_map/ppermute | solution.py:16
  101.4 2.1 %collective-permute-start.1 = (bf16[2,512,128]{2,1,0:T(8,128)(2,1)S(1)}, bf16[2,512,128]{2,1,0:T(8,128)(2,1)S(1)}, u32[]{:S(2)}, u32[]{:S(2)}) collective-permute-start(bf16[2,512,128]{2,1,0:T(8,128)(2,1)S(1)} %bitcast.137), channel_id=1, source_target_pairs={{1,0},{2,1},{3,2},{4,3},{5,4},{6,5},{7,6},{8,7},{9,8},{10,9},{11,1... | collective-permute-start | bytes 786440 | tf_op jit(solution)/shard_map/ppermute | solution.py:17
  103.6 1.2 collective-permute-done
  104.7 4.4 %collective-permute-done.1 = bf16[2,512,128]{2,1,0:T(8,128)(2,1)S(1)} collective-permute-done((bf16[2,512,128]{2,1,0:T(8,128)(2,1)S(1)}, bf16[2,512,128]{2,1,0:T(8,128)(2,1)S(1)}, u32[]{:S(2)}, u32[]{:S(2)}) %collective-permute-start.1) | collective-permute-done | bytes 262176 | tf_op jit(solution)/shard_map/ppermute | solution.py:17
  109.3 1.3 %pad_slice_fusion.1 = (bf16[6,512,128]{2,1,0:T(8,128)(2,1)S(1)}, bf16[6,512,128]{2,1,0:T(8,128)(2,1)S(1)}, bf16[6,512,128]{2,1,0:T(8,128)(2,1)S(1)}, bf16[6,512,...) fusion(bf16[8,512,128]{2,1,0:T(8,128)(2,1)S(1)} %pad_maximum_fusion), kind=kLoop, calls=%fused_computation.27 | loop fusion | bytes 7340032 | tf_op jit(solution)/shard_map/slice | solution.py:26
  110.6 0.3 fusion.22
  110.9 0.3 fusion.13
  111.4 0.3 convolution_add_fusion.6
  111.8 0.4 convolution_add_fusion.5
  112.1 0.4 convolution_add_fusion.4
  112.5 0.4 convolution_add_fusion.3
  112.9 0.4 convolution_add_fusion.2
  113.2 0.4 convolution_add_fusion.1
  113.6 0.4 fusion.2
  114.1 0.9 pad_slice_fusion.6
  115.3 0.3 convolution_add_fusion.14
  115.6 0.3 convolution_add_fusion.13
  115.9 0.3 convolution_add_fusion.12
  116.5 0.3 convolution_add_fusion.10
  116.8 0.3 convolution_add_fusion.9
  117.1 0.3 convolution_add_fusion.8
  117.4 0.3 convolution_add_fusion.7
  117.6 0.7 copy-done.6
  118.4 0.9 add_convert_fusion
  (31 shorter events, 1.8 us)
Async XLA Ops:
  3.5 11.2 %all-to-all-start = ((s32[16,1,1]{2,1,0:T(1,128)}), s32[16,1,1]{2,1,0:T(1,128)S(1)}, u32[]{:S(2)}, u32[]{:S(2)}) async-start(s32[16,1,1]{2,1,0:T(1,128)} %copy.30), calls=%async_computation | async-start | bytes 16384 | tf_op jit(solution)/shard_map/all_to_all | solution.py:129
  16.7 1.4 %copy-start.4 = (bf16[16,512,128]{2,1,0:T(8,128)(2,1)}, bf16[16,512,128]{2,1,0:T(8,128)(2,1)S(1)}, u32[]{:S(2)}) copy-start(bf16[16,512,128]{2,1,0:T(8,128)(2,1)S(1)} %broadcast_select_fusion) | copy-start | bytes 6291460
  19.3 40.8 %all-to-all-start.1 = ((bf16[16,384,128]{2,1,0:T(8,128)(2,1)}), bf16[16,384,128]{2,1,0:T(8,128)(2,1)S(1)}, u32[]{:S(2)}, u32[]{:S(2)}) async-start(bf16[16,384,128]{2,1,0:T(8,128)(2,1)} %slice.176), calls=%async_computation.1 | async-start | bytes 3145728 | tf_op jit(solution)/shard_map/all_to_all | solution.py:144
  24.6 41.1 %copy-start.5 = (bf16[4,512,128]{2,1,0:T(8,128)(2,1)S(1)}, bf16[4,512,128]{2,1,0:T(8,128)(2,1)}, u32[]{:S(2)}) copy-start(bf16[4,512,128]{2,1,0:T(8,128)(2,1)} %param.5) | copy-start | bytes 1572868
  60.1 5.7 %copy-start = (bf16[16,384,128]{2,1,0:T(8,128)(2,1)}, bf16[16,384,128]{2,1,0:T(8,128)(2,1)S(1)}, u32[]{:S(2)}) copy-start(bf16[16,384,128]{2,1,0:T(8,128)(2,1)S(1)} %all-to-all-done.1.k_ref) | copy-start | bytes 4718596
  60.1 27.3 %all-to-all-start.2 = ((bf16[16,128,128]{2,1,0:T(8,128)(2,1)}), bf16[16,128,128]{2,1,0:T(8,128)(2,1)}, u32[]{:S(2)}, u32[]{:S(2)}) async-start(bf16[16,128,128]{2,1,0:T(8,128)(2,1)} %slice.177), calls=%async_computation.2 | async-start | bytes 1048576 | tf_op jit(solution)/shard_map/all_to_all | solution.py:144
  65.8 0.8 copy-start.2
  65.9 1.5 %copy-start.1 = (bf16[16,384,128]{2,1,0:T(8,128)(2,1)S(1)}, bf16[16,384,128]{2,1,0:T(8,128)(2,1)}, u32[]{:S(2)}) copy-start(bf16[16,384,128]{2,1,0:T(8,128)(2,1)} %copy-done) | copy-start | bytes 4718596
  87.4 1.0 copy-start.3
  98.1 6.6 %collective-permute-start = (bf16[2,512,128]{2,1,0:T(8,128)(2,1)S(1)}, bf16[2,512,128]{2,1,0:T(8,128)(2,1)S(1)}, u32[]{:S(2)}, u32[]{:S(2)}) collective-permute-start(bf16[2,512,128]{2,1,0:T(8,128)(2,1)S(1)} %bitcast.138), channel_id=1, source_target_pairs={{0,1},{1,2},{2,3},{3,4},{4,5},{5,6},{6,7},{7,8},{8,9},{9,10},{10,1... | collective-permute-start | bytes 786440 | tf_op jit(solution)/shard_map/ppermute | solution.py:16
  101.4 7.7 %collective-permute-start.1 = (bf16[2,512,128]{2,1,0:T(8,128)(2,1)S(1)}, bf16[2,512,128]{2,1,0:T(8,128)(2,1)S(1)}, u32[]{:S(2)}, u32[]{:S(2)}) collective-permute-start(bf16[2,512,128]{2,1,0:T(8,128)(2,1)S(1)} %bitcast.137), channel_id=1, source_target_pairs={{1,0},{2,1},{3,2},{4,3},{5,4},{6,5},{7,6},{8,7},{9,8},{10,9},{11,1... | collective-permute-start | bytes 786440 | tf_op jit(solution)/shard_map/ppermute | solution.py:17
  109.3 1.3 %copy-start.7 = (bf16[3,3,128,128]{3,2,1,0:T(8,128)(2,1)S(1)}, bf16[3,3,128,128]{3,2,1,0:T(8,128)(2,1)}, u32[]{:S(2)}) copy-start(bf16[3,3,128,128]{3,2,1,0:T(8,128)(2,1)} %param.8) | copy-start | bytes 884740
  114.1 1.0 copy-start.8
  117.3 1.0 copy-start.6

commit v5 on v3

--- a/solution.py
+++ b/solution.py
@@ -29,6 +29,18 @@
                 window, weights[row_shift, col_shift], preferred_element_type=jnp.float32
             )
     return summed.reshape(out_rows, out_cols, channels)
+
+
+def native_conv(rows, weights):
+    out = lax.conv_general_dilated(
+        rows[None],
+        weights,
+        window_strides=(1, 1),
+        padding=((0, 0), (1, 1)),
+        dimension_numbers=("NHWC", "HWIO", "NHWC"),
+        preferred_element_type=jnp.float32,
+    )
+    return out[0]
 
 
 def pad_columns(image):
@@ -156,13 +168,11 @@
     )
     me = lax.axis_index("row")
     extended = halo_rows(warped, "row", 2)
-    hidden = jax.nn.relu(
-        convolve_rows(pad_columns(extended), conv_one, band_rows + 2, band_width)
-    ).astype(jnp.bfloat16)
+    hidden = jax.nn.relu(native_conv(extended, conv_one)).astype(jnp.bfloat16)
     row_ids = jnp.arange(band_rows + 2)
     inside = ((row_ids > 0) | (me > 0)) & ((row_ids < band_rows + 1) | (me < owners - 1))
     hidden = jnp.where(inside[:, None, None], hidden, jnp.zeros_like(hidden))
-    branch = convolve_rows(pad_columns(hidden), conv_two, band_rows, band_width)
+    branch = native_conv(hidden, conv_two)
     return (frame_one.astype(jnp.float32) + branch).astype(jnp.bfloat16)
 
 

time: 114 us -> 110 us (0.965)
  matrix products: 5.66 us -> 3.51 us
    dot_general x18 -> x0, matrix products: 5.66 us -> none  [convolve_rows(): jnp.dot(window, weights[row_shift, col_shift], preferred_element_type=jnp...]
    conv_general_dilated x0 -> x2, matrix products: none -> 3.51 us  [native_conv(): lax.conv_general_dilated(rows[None], weights, window_strides=(1, 1), padd...]
    slice x2 -> x0, local copies, waits for them, and re-layouts: 2.15 us -> none  [convolve_rows(): padded[row_shift:row_shift + out_rows, col_shift:col_shift + out_cols]]
    unnamed x14 -> x17, local copies, waits for them, and re-layouts: 3.05 us -> 4.02 us
where the time goes in v5:
time: 110 us; the launch traced here: 109 us
  blocking collectives  30.5 us (28%)
  waiting for transfers between devices  21.7 us (20%)
  Pallas kernels  21.7 us (20%)
  starting transfers between devices  16.7 us (15%)
  local copies, waits for them, and re-layouts  9.92 us (9%)
  other arithmetic  4.79 us (4%)
  matrix products  3.51 us (3%)
    all_to_all x1, blocking collectives, on_device(): lax.all_to_all(sending, 'row', split_axis=0, concat_axis=0, tiled=True)  30.5 us
    pallas_call x2, Pallas kernels, attend_chunk(): pl.pallas_call(functools.partial(attend_kernel, scale=scale), grid_spec=g...  21.7 us
    all_to_all x1, waiting for transfers between devices, on_device(): lax.all_to_all(sending, 'row', split_axis=0, concat_axis=0, tiled=True)  13.2 us
    all_to_all x1, starting transfers between devices, on_device(): lax.all_to_all(wanted.reshape(owners, 1), 'row', split_axis=0, concat_axi...  6.61 us
    ppermute x1, waiting for transfers between devices, halo_rows(): from_below = lax.ppermute(head, axis, [(i + 1, i) for i in range(ends)])  4.72 us
    all_to_all x1, starting transfers between devices, on_device(): lax.all_to_all(sending, 'row', split_axis=0, concat_axis=0, tiled=True)  4.38 us
    unnamed x17, local copies, waits for them, and re-layouts  4.02 us
    ppermute x1, starting transfers between devices, halo_rows(): from_above = lax.ppermute(tail, axis, [(i, i + 1) for i in range(ends)])  3.82 us
  transfers between devices with their start and end apart: 4, of which 4 were waited for; matrix products, arithmetic and copies ran while one was open for 1% of the time, Pallas kernels for 9%

profile of v5, /device:TPU:9, one launch (start us, length us, event | category | flops | bytes accessed | tf_op | source)
XLA Modules:
  0.0 109.1 jit_solution(16748077674458776253)
XLA Ops:
  0.0 0.0 copy-start
  0.0 0.8 convert_reduce_fusion
  0.8 0.8 slice_reduce_fusion
  1.6 0.1 copy.65
  1.8 0.8 add_select_fusion.1.owner_ref
  2.5 0.1 copy.66
  2.6 0.1 copy.64
  2.7 0.1 select_reduce_fusion
  2.8 0.7 copy.67
  3.5 6.6 %all-to-all-start = ((s32[16,1,1]{2,1,0:T(1,128)}), s32[16,1,1]{2,1,0:T(1,128)S(1)}, u32[]{:S(2)}, u32[]{:S(2)}) async-start(s32[16,1,1]{2,1,0:T(1,128)} %copy.67), calls=%async_computation | async-start | bytes 16384 | tf_op jit(solution)/shard_map/all_to_all | solution.py:141
  10.1 1.1 copy.68
  11.2 3.5 %all-to-all-done = s32[16,1,1]{2,1,0:T(1,128)S(1)} async-done(((s32[16,1,1]{2,1,0:T(1,128)}), s32[16,1,1]{2,1,0:T(1,128)S(1)}, u32[]{:S(2)}, u32[]{:S(2)}) %all-to-all-start) | async-done | bytes 96 | tf_op jit(solution)/shard_map/all_to_all | solution.py:141
  14.7 0.4 maximum_reduce_fusion
  15.1 1.0 gather_fusion
  16.1 0.7 compare_reduce_fusion.1
  16.7 0.3 select_select_fusion
  17.1 1.2 %fusion.37 = (bf16[16,256,128]{2,1,0:T(8,128)(2,1)}, bf16[16,256,128]{2,1,0:T(8,128)(2,1)S(1)}) fusion(bf16[16,512,128]{2,1,0:T(8,128)(2,1)S(1)} %select_select_fusion), kind=kLoop, calls=%fused_computation.61 | loop fusion | bytes 4194304 | tf_op jit(solution)/shard_map/slice | solution.py:155
  18.2 30.5 %all_to_all.19.k_ref = bf16[16,256,128]{2,1,0:T(8,128)(2,1)} all-to-all(bf16[16,256,128]{2,1,0:T(8,128)(2,1)S(1)} %get-tuple-element.30), channel_id=1, replica_groups=mesh['pairs'=2,'row'=16] {'row'}, dimensions={0} | all-to-all | bytes 2097152 | tf_op jit(solution)/shard_map/all_to_all | solution.py:158
  48.7 4.4 %all-to-all-start.2 = ((bf16[16,256,128]{2,1,0:T(8,128)(2,1)}), bf16[16,256,128]{2,1,0:T(8,128)(2,1)}, u32[]{:S(2)}, u32[]{:S(2)}) async-start(bf16[16,256,128]{2,1,0:T(8,128)(2,1)} %get-tuple-element.15), calls=%async_computation.2 | async-start | bytes 2097152 | tf_op jit(solution)/shard_map/all_to_all | solution.py:158
  53.2 0.0 copy-start.1
  53.2 0.1 broadcast_in_dim.85.m_in
  53.3 0.1 broadcast_in_dim.86.t_in
  53.3 0.1 broadcast_in_dim.87.a_in
  53.4 0.5 copy-done.1
  54.0 0.6 copy-done.3
  54.6 10.3 %shard_map.55 = (f32[4,512,1]{2,1,0:T(8,128)S(1)}, f32[4,512,1]{2,1,0:T(8,128)S(1)}, f32[4,512,128]{2,1,0:T(8,128)S(1)}) custom-call(s32[4,9]{1,0:T(4,128)S(1)} %add_select_fusion.1.owner_ref, s32[4]{0:T(128)S(1)} %get-tuple-element.27.count_ref, bf16[4,512,128]{2,1,0:T(8,128)(2,1)S(1)} %bitcast.36, ...), custom_call_target="tpu_custom_call", output_to_operand_aliasing={{0}: (4, {}), {1}: (5, {}), {2}: (6, {})} | custom-call | tf_op jit(solution)/shard_map/pallas_call | solution.py:105
  64.8 13.2 %all-to-all-done.2.k_ref = bf16[16,256,128]{2,1,0:T(8,128)(2,1)} async-done(((bf16[16,256,128]{2,1,0:T(8,128)(2,1)}), bf16[16,256,128]{2,1,0:T(8,128)(2,1)}, u32[]{:S(2)}, u32[]{:S(2)}) %all-to-all-start.2) | async-done | bytes 1048608 | tf_op jit(solution)/shard_map/all_to_all | solution.py:158
  78.1 1.0 copy-done.2
  79.1 11.4 %shard_map.56 = (f32[4,512,1]{2,1,0:T(8,128)S(1)}, f32[4,512,1]{2,1,0:T(8,128)S(1)}, f32[4,512,128]{2,1,0:T(8,128)S(1)}) custom-call(s32[4,9]{1,0:T(4,128)S(1)} %add_select_fusion.1.owner_ref, s32[4]{0:T(128)S(1)} %get-tuple-element.27.count_ref, bf16[4,512,128]{2,1,0:T(8,128)(2,1)S(1)} %bitcast.37, ...), custom_call_target="tpu_custom_call", output_to_operand_aliasing={{0}: (4, {}), {1}: (5, {}), {2}: (6, {})} | custom-call | tf_op jit(solution)/shard_map/pallas_call | solution.py:105
  90.5 0.3 reduce.4
  90.9 0.3 divide_convert_fusion
  91.3 1.9 %collective-permute-start.1 = (bf16[2,512,128]{2,1,0:T(8,128)(2,1)S(1)}, bf16[2,512,128]{2,1,0:T(8,128)(2,1)S(1)}, u32[]{:S(2)}, u32[]{:S(2)}) collective-permute-start(bf16[2,512,128]{2,1,0:T(8,128)(2,1)S(1)} %bitcast.47), channel_id=1, source_target_pairs={{1,0},{2,1},{3,2},{4,3},{5,4},{6,5},{7,6},{8,7},{9,8},{10,9},{11,1... | collective-permute-start | bytes 786440 | tf_op jit(solution)/shard_map/ppermute | solution.py:17
  93.3 3.8 %collective-permute-start = (bf16[2,512,128]{2,1,0:T(8,128)(2,1)S(1)}, bf16[2,512,128]{2,1,0:T(8,128)(2,1)S(1)}, u32[]{:S(2)}, u32[]{:S(2)}) collective-permute-start(bf16[2,512,128]{2,1,0:T(8,128)(2,1)S(1)} %bitcast.46), channel_id=1, source_target_pairs={{0,1},{1,2},{2,3},{3,4},{4,5},{5,6},{6,7},{7,8},{8,9},{9,10},{10,1... | collective-permute-start | bytes 786440 | tf_op jit(solution)/shard_map/ppermute | solution.py:16
  97.1 4.7 %collective-permute-done.1 = bf16[2,512,128]{2,1,0:T(8,128)(2,1)S(1)} collective-permute-done((bf16[2,512,128]{2,1,0:T(8,128)(2,1)S(1)}, bf16[2,512,128]{2,1,0:T(8,128)(2,1)S(1)}, u32[]{:S(2)}, u32[]{:S(2)}) %collective-permute-start.1) | collective-permute-done | bytes 262176 | tf_op jit(solution)/shard_map/ppermute | solution.py:17
  101.8 0.2 collective-permute-done
  102.0 0.1 maximum_bitcast_fusion
  102.2 0.7 copy.76
  102.9 0.0 copy-start.7
  102.9 0.1 pad.clone
  102.9 0.1 copy.72
  103.1 0.4 copy-done.7
  103.6 2.1 %fusion.5 = bf16[6,1,8,65,128]{4,2,3,0,1:T(8,128)(2,1)S(1)} fusion(bf16[3,3,128,128]{3,2,1,0:T(8,128)(2,1)S(1)} %copy-done, bf16[8,1,7,2,128]{4,2,3,0,1:T(8,128)(2,1)S(1)} %slice.38, bf16[8,1,8,65,128]{4,2,3,0,1:T(8,128)(2,1)S(1)} %copy.72, pred[6]{0:T(512)(128)(4,1)S(1)} %or_and_fusion, pred[8,65]{0,1:T(8,128)(4,1)S(1)} %copy-done.7), kind=kOutput, calls=%fused_computation.11 | convolution fusion | flops 925415424 | bytes 2187790 | tf_op jit(solution)/shard_map/conv_general_dilated | solution.py:35
  105.7 1.4 %fusion.16 = f32[4,8,65,128]{3,1,2,0:T(8,128)S(1)} fusion(bf16[3,3,128,128]{3,2,1,0:T(8,128)(2,1)S(1)} %copy-done.6, bf16[6,1,7,1,128]{4,2,3,0,1:T(8,128)(2,1)S(1)} %get-tuple-element.32, bf16[6,1,7,1,128]{4,2,3,0,1:T(8,128)(2,1)S(1)} %get-tuple-element.31, bf16[6,1,8,65,128]{4,2,3,0,1:T(8,128)(2,1)S(1)} %fusion.5), kind=kOutput, calls=%fused_computation.24 | convolution fusion | flops 617533440 | bytes 2180096 | tf_op jit(solution)/shard_map/conv_general_dilated | solution.py:35
  107.1 0.0 copy-start.5
  107.1 0.3 copy.73
  107.4 0.1 slice.41
  107.5 0.7 copy-done.5
  108.2 0.9 fusion.13
  (14 shorter events, 0.2 us)
Async XLA Ops:
  0.0 103.1 %copy-start = (bf16[3,3,128,128]{3,2,1,0:T(8,128)(2,1)S(1)}, bf16[3,3,128,128]{3,2,1,0:T(8,128)(2,1)}, u32[]{:S(2)}) copy-start(bf16[3,3,128,128]{3,2,1,0:T(8,128)(2,1)} %param.8) | copy-start | bytes 884740
  3.5 11.2 %all-to-all-start = ((s32[16,1,1]{2,1,0:T(1,128)}), s32[16,1,1]{2,1,0:T(1,128)S(1)}, u32[]{:S(2)}, u32[]{:S(2)}) async-start(s32[16,1,1]{2,1,0:T(1,128)} %copy.67), calls=%async_computation | async-start | bytes 16384 | tf_op jit(solution)/shard_map/all_to_all | solution.py:141
  18.2 34.9 %copy-start.4 = (bf16[4,512,128]{2,1,0:T(8,128)(2,1)S(1)}, bf16[4,512,128]{2,1,0:T(8,128)(2,1)}, u32[]{:S(2)}) copy-start(bf16[4,512,128]{2,1,0:T(8,128)(2,1)} %param.5) | copy-start | bytes 1572868
  48.7 29.3 %all-to-all-start.2 = ((bf16[16,256,128]{2,1,0:T(8,128)(2,1)}), bf16[16,256,128]{2,1,0:T(8,128)(2,1)}, u32[]{:S(2)}, u32[]{:S(2)}) async-start(bf16[16,256,128]{2,1,0:T(8,128)(2,1)} %get-tuple-element.15), calls=%async_computation.2 | async-start | bytes 2097152 | tf_op jit(solution)/shard_map/all_to_all | solution.py:158
  53.2 0.8 copy-start.1
  53.2 1.4 %copy-start.3 = (bf16[16,256,128]{2,1,0:T(8,128)(2,1)S(1)}, bf16[16,256,128]{2,1,0:T(8,128)(2,1)}, u32[]{:S(2)}) copy-start(bf16[16,256,128]{2,1,0:T(8,128)(2,1)} %all_to_all.19.k_ref) | copy-start | bytes 3145732
  78.1 1.0 copy-start.2
  91.3 10.5 %collective-permute-start.1 = (bf16[2,512,128]{2,1,0:T(8,128)(2,1)S(1)}, bf16[2,512,128]{2,1,0:T(8,128)(2,1)S(1)}, u32[]{:S(2)}, u32[]{:S(2)}) collective-permute-start(bf16[2,512,128]{2,1,0:T(8,128)(2,1)S(1)} %bitcast.47), channel_id=1, source_target_pairs={{1,0},{2,1},{3,2},{4,3},{5,4},{6,5},{7,6},{8,7},{9,8},{10,9},{11,1... | collective-permute-start | bytes 786440 | tf_op jit(solution)/shard_map/ppermute | solution.py:17
  93.3 8.8 %collective-permute-start = (bf16[2,512,128]{2,1,0:T(8,128)(2,1)S(1)}, bf16[2,512,128]{2,1,0:T(8,128)(2,1)S(1)}, u32[]{:S(2)}, u32[]{:S(2)}) collective-permute-start(bf16[2,512,128]{2,1,0:T(8,128)(2,1)S(1)} %bitcast.46), channel_id=1, source_target_pairs={{0,1},{1,2},{2,3},{3,4},{4,5},{5,6},{6,7},{7,8},{8,9},{9,10},{10,1... | collective-permute-start | bytes 786440 | tf_op jit(solution)/shard_map/ppermute | solution.py:16
  102.9 0.7 copy-start.7
  103.6 2.1 %copy-start.6 = (bf16[3,3,128,128]{3,2,1,0:T(8,128)(2,1)S(1)}, bf16[3,3,128,128]{3,2,1,0:T(8,128)(2,1)}, u32[]{:S(2)}) copy-start(bf16[3,3,128,128]{3,2,1,0:T(8,128)(2,1)} %param.9) | copy-start | bytes 884740
  107.1 1.0 copy-start.5

commit v6 on v5

--- a/solution.py
+++ b/solution.py
@@ -47,7 +47,13 @@
     return jnp.pad(image, ((0, 0), (1, 1), (0, 0)))
 
 
-def attend_kernel(owner_ref, count_ref, q_ref, k_ref, m_in, t_in, a_in, m_out, t_out, a_out, kall_ref, *, scale):
+def attend_kernel(owner_ref, count_ref, q_ref, k_ref, *refs, scale, first, last):
+    if first:
+        m_out, t_out, a_out, kall_ref = refs
+    elif last:
+        m_in, t_in, a_in, o_ref, kall_ref = refs
+    else:
+        m_in, t_in, a_in, m_out, t_out, a_out, kall_ref = refs
     t = pl.program_id(0)
     n = count_ref[t]
     slots = owner_ref.shape[1]
@@ -64,9 +70,11 @@
     for j, at in blocks:
         blk = s[:, at : at + lanes]
         mx = blk if mx is None else jnp.maximum(mx, blk)
-    m_old = m_in[0]
-    m_new = jnp.maximum(m_old, jnp.max(mx, axis=1, keepdims=True) * scale)
-    alpha = jnp.exp(m_old - m_new)
+    m_new = jnp.max(mx, axis=1, keepdims=True) * scale
+    if not first:
+        m_old = m_in[0]
+        m_new = jnp.maximum(m_old, m_new)
+        alpha = jnp.exp(m_old - m_new)
     log2e = 1.4426950408889634
     mb = jnp.broadcast_to(m_new * log2e, (m_new.shape[0], lanes))
     shifted = [mb + penalty[j] for j in range(slots)]
@@ -77,42 +85,53 @@
         acc = p if acc is None else acc + p
         ps.append(p.astype(jnp.bfloat16))
     pb = jnp.concatenate(ps, axis=1)
-    m_out[0] = m_new
-    a_out[0] = a_in[0] * alpha + jnp.dot(pb, kall, preferred_element_type=jnp.float32)
-    t_out[0] = t_in[0] * alpha + jnp.sum(acc, axis=1, keepdims=True)
-
-
-def attend_chunk(state, queries, chunk, slot_owner, counts, scale):
+    mixed = jnp.dot(pb, kall, preferred_element_type=jnp.float32)
+    total = jnp.sum(acc, axis=1, keepdims=True)
+    if not first:
+        mixed = a_in[0] * alpha + mixed
+        total = t_in[0] * alpha + total
+    if last:
+        o_ref[0] = (mixed / total).astype(o_ref.dtype)
+    else:
+        m_out[0] = m_new
+        t_out[0] = total
+        a_out[0] = mixed
+
+
+def attend_chunk(state, queries, chunk, slot_owner, counts, scale, first, last):
     tiles, tile_size, channels = queries.shape
     owners, chunk_len, _ = chunk.shape
     slots = slot_owner.shape[1]
-    m, tot, acc = state
     col_spec = pl.BlockSpec((1, tile_size, 1), lambda t, o, c: (t, 0, 0))
     acc_spec = pl.BlockSpec((1, tile_size, channels), lambda t, o, c: (t, 0, 0))
+    state_specs = [] if first else [col_spec, col_spec, acc_spec]
+    if last:
+        out_specs = acc_spec
+        out_shape = jax.ShapeDtypeStruct(queries.shape, jnp.bfloat16)
+    else:
+        out_specs = [col_spec, col_spec, acc_spec]
+        out_shape = [
+            jax.ShapeDtypeStruct((tiles, tile_size, 1), jnp.float32),
+            jax.ShapeDtypeStruct((tiles, tile_size, 1), jnp.float32),
+            jax.ShapeDtypeStruct((tiles, tile_size, channels), jnp.float32),
+        ]
     grid_spec = pltpu.PrefetchScalarGridSpec(
         num_scalar_prefetch=2,
         grid=(tiles,),
         in_specs=[
             acc_spec,
             pl.BlockSpec((owners, chunk_len, channels), lambda t, o, c: (0, 0, 0)),
-            col_spec,
-            col_spec,
-            acc_spec,
-        ],
-        out_specs=[col_spec, col_spec, acc_spec],
+        ]
+        + state_specs,
+        out_specs=out_specs,
         scratch_shapes=[pltpu.VMEM((slots * chunk_len, channels), jnp.bfloat16)],
     )
     return pl.pallas_call(
-        functools.partial(attend_kernel, scale=scale),
+        functools.partial(attend_kernel, scale=scale, first=first, last=last),
         grid_spec=grid_spec,
-        out_shape=[
-            jax.ShapeDtypeStruct(m.shape, jnp.float32),
-            jax.ShapeDtypeStruct(tot.shape, jnp.float32),
-            jax.ShapeDtypeStruct(acc.shape, jnp.float32),
-        ],
-        input_output_aliases={4: 0, 5: 1, 6: 2},
+        out_shape=out_shape,
         compiler_params=pltpu.CompilerParams(vmem_limit_bytes=48 * 1024 * 1024),
-    )(slot_owner, counts, queries, chunk, m, tot, acc)
+    )(slot_owner, counts, queries, chunk, *([] if first else state))
 
 
 def on_device(frame_one, frame_two, tile_lists, conv_one, conv_two):
@@ -141,26 +160,21 @@
     asked = lax.all_to_all(
         wanted.reshape(owners, 1), "row", split_axis=0, concat_axis=0, tiled=True
     )[:, 0]
-    picked = jnp.take(own_keys, jnp.maximum(asked, 0), axis=0)
-    outgoing = jnp.where((asked >= 0)[:, None, None], picked, jnp.zeros_like(picked))
-    pieces = 2
-    chunk_len = tile_size // pieces
-    state = (
-        jnp.full((per_device, tile_size, 1), -jnp.inf, jnp.float32),
-        jnp.zeros((per_device, tile_size, 1), jnp.float32),
-        jnp.zeros((per_device, tile_size, channels), jnp.float32),
-    )
+    outgoing = jnp.take(own_keys, jnp.maximum(asked, 0), axis=0)
+    edges = [0, tile_size // 2, tile_size]
+    state = ()
     previous = None
-    for piece in range(pieces):
-        sending = outgoing[:, piece * chunk_len : (piece + 1) * chunk_len]
+    for index, (start, stop) in enumerate(zip(edges[:-1], edges[1:])):
+        sending = outgoing[:, start:stop]
         if previous is not None:
             previous, sending, state = lax.optimization_barrier((previous, sending, state))
         current = lax.all_to_all(sending, "row", split_axis=0, concat_axis=0, tiled=True)
         if previous is not None:
-            state = attend_chunk(state, query_tiles, previous, slot_owner, counts, scale)
+            state = attend_chunk(state, query_tiles, previous, slot_owner, counts, scale, index == 1, False)
         previous = current
-    state = attend_chunk(state, query_tiles, previous, slot_owner, counts, scale)
-    warped_tiles = (state[2] / state[1]).astype(jnp.bfloat16)
+    warped_tiles = attend_chunk(
+        state, query_tiles, previous, slot_owner, counts, scale, len(edges) == 2, True
+    )
     warped = (
         warped_tiles.reshape(per_device, band_rows, tile_cols, channels)
         .transpose(1, 0, 2, 3)

time: 110 us -> 109 us (level)
  waiting for transfers between devices: 21.7 us -> 16.7 us
  local copies, waits for them, and re-layouts: 9.92 us -> 13.4 us
  Pallas kernels: 21.7 us -> 23.1 us
    all_to_all x1, waiting for transfers between devices: 13.2 us -> 8.22 us  [on_device(): lax.all_to_all(sending, 'row', split_axis=0, concat_axis=0, tiled=True)]
    unnamed x17 -> x21, local copies, waits for them, and re-layouts: 4.02 us -> 7.82 us
    pallas_call x2, Pallas kernels: 21.7 us -> 23.1 us  [attend_chunk(): pl.pallas_call(functools.partial(attend_kernel, scale=scale, first=first,...]
  transfers between devices with their start and end apart: 4 -> 4, of which waited for: 4 -> 4; matrix products, arithmetic and copies ran while one was open for 1% -> 1% of each run, Pallas kernels for 9% -> 13%
where the time goes in v6:
time: 109 us; the launch traced here: 107 us
  blocking collectives  29.8 us (27%)
  Pallas kernels  23.1 us (21%)
  starting transfers between devices  16.7 us (15%)
  waiting for transfers between devices  16.7 us (15%)
  local copies, waits for them, and re-layouts  13.4 us (12%)
  other arithmetic  3.78 us (3%)
  matrix products  3.51 us (3%)
    all_to_all x1, blocking collectives, on_device(): lax.all_to_all(sending, 'row', split_axis=0, concat_axis=0, tiled=True)  29.8 us
    pallas_call x2, Pallas kernels, attend_chunk(): pl.pallas_call(functools.partial(attend_kernel, scale=scale, first=first,...  23.1 us
    all_to_all x1, waiting for transfers between devices, on_device(): lax.all_to_all(sending, 'row', split_axis=0, concat_axis=0, tiled=True)  8.22 us
    unnamed x21, local copies, waits for them, and re-layouts  7.82 us
    all_to_all x1, starting transfers between devices, on_device(): lax.all_to_all(wanted.reshape(owners, 1), 'row', split_axis=0, concat_axi...  6.61 us
    ppermute x1, waiting for transfers between devices, halo_rows(): from_below = lax.ppermute(head, axis, [(i + 1, i) for i in range(ends)])  4.72 us
    all_to_all x1, starting transfers between devices, on_device(): lax.all_to_all(sending, 'row', split_axis=0, concat_axis=0, tiled=True)  4.38 us
    ppermute x1, starting transfers between devices, halo_rows(): from_above = lax.ppermute(tail, axis, [(i, i + 1) for i in range(ends)])  3.82 us
  transfers between devices with their start and end apart: 4, of which 4 were waited for; matrix products, arithmetic and copies ran while one was open for 1% of the time, Pallas kernels for 13%

profile of v6, /device:TPU:9, one launch (start us, length us, event | category | flops | bytes accessed | tf_op | source)
XLA Modules:
  0.0 107.3 jit_solution(2045824127367515829)
XLA Ops:
  0.0 0.0 copy-start
  0.0 0.8 convert_reduce_fusion
  0.8 0.8 slice_reduce_fusion
  1.6 0.1 copy.59
  1.8 0.8 add_select_fusion.1.owner_ref
  2.5 0.1 copy.60
  2.6 0.1 copy.58
  2.7 0.1 select_reduce_fusion
  2.8 0.7 copy.61
  3.5 6.6 %all-to-all-start = ((s32[16,1,1]{2,1,0:T(1,128)}), s32[16,1,1]{2,1,0:T(1,128)S(1)}, u32[]{:S(2)}, u32[]{:S(2)}) async-start(s32[16,1,1]{2,1,0:T(1,128)} %copy.61), calls=%async_computation | async-start | bytes 16384 | tf_op jit(solution)/shard_map/all_to_all | solution.py:160
  10.1 1.1 %copy.62 = bf16[4,4,128,128]{3,2,1,0:T(8,128)(2,1)S(1)} copy(bf16[4,4,128,128]{3,2,0,1:T(8,128)(2,1)} %bitcast.45) | data formatting | bytes 1048576 | tf_op jit(solution)/shard_map/transpose | solution.py:148
  11.2 3.5 %all-to-all-done = s32[16,1,1]{2,1,0:T(1,128)S(1)} async-done(((s32[16,1,1]{2,1,0:T(1,128)}), s32[16,1,1]{2,1,0:T(1,128)S(1)}, u32[]{:S(2)}, u32[]{:S(2)}) %all-to-all-start) | async-done | bytes 96 | tf_op jit(solution)/shard_map/all_to_all | solution.py:160
  14.7 0.4 maximum_reduce_fusion
  15.1 1.0 gather_fusion
  16.1 0.4 compare_reduce_fusion
  16.5 0.3 broadcast_select_fusion
  16.7 1.1 %fusion.37 = (bf16[16,256,128]{2,1,0:T(8,128)(2,1)}, bf16[16,256,128]{2,1,0:T(8,128)(2,1)S(1)}) fusion(bf16[16,512,128]{2,1,0:T(8,128)(2,1)S(1)} %broadcast_select_fusion), kind=kLoop, calls=%fused_computation.59 | loop fusion | bytes 4194304 | tf_op jit(solution)/shard_map/slice | solution.py:168
  17.9 0.0 copy-start.7
  17.9 29.8 %all_to_all.19.k_ref = bf16[16,256,128]{2,1,0:T(8,128)(2,1)S(1)} all-to-all(bf16[16,256,128]{2,1,0:T(8,128)(2,1)S(1)} %get-tuple-element.18), channel_id=1, replica_groups=mesh['pairs'=2,'row'=16] {'row'}, dimensions={0} | all-to-all | bytes 2097152 | tf_op jit(solution)/shard_map/all_to_all | solution.py:171
  47.7 4.4 %all-to-all-start.2 = ((bf16[16,256,128]{2,1,0:T(8,128)(2,1)}), bf16[16,256,128]{2,1,0:T(8,128)(2,1)S(1)}, u32[]{:S(2)}, u32[]{:S(2)}) async-start(bf16[16,256,128]{2,1,0:T(8,128)(2,1)} %get-tuple-element.10), calls=%async_computation.2 | async-start | bytes 2097152 | tf_op jit(solution)/shard_map/all_to_all | solution.py:171
  52.0 0.0 copy-done.7
  52.1 13.5 %shard_map.55 = (f32[4,512,1]{2,1,0:T(8,128)S(1)}, f32[4,512,1]{2,1,0:T(8,128)S(1)}, f32[4,512,128]{2,1,0:T(8,128)S(1)}) custom-call(s32[4,9]{1,0:T(4,128)S(1)} %add_select_fusion.1.owner_ref, s32[4]{0:T(128)S(1)} %get-tuple-element.15.count_ref, bf16[4,512,128]{2,1,0:T(8,128)(2,1)S(1)} %bitcast.36, bf16[16,256,128]{2,1,0:T(8,128)(2,1)S(1)} %all_to_all.19.k_ref), custom_call_target="tpu_custom_call" | custom-call | tf_op jit(solution)/shard_map/pallas_call | solution.py:129
  65.6 0.0 copy-start.1
  65.6 1.0 copy-done.1
  66.7 1.0 copy-done.3
  67.7 1.0 copy-done.5
  68.7 8.2 %all-to-all-done.2.k_ref = bf16[16,256,128]{2,1,0:T(8,128)(2,1)S(1)} async-done(((bf16[16,256,128]{2,1,0:T(8,128)(2,1)}), bf16[16,256,128]{2,1,0:T(8,128)(2,1)S(1)}, u32[]{:S(2)}, u32[]{:S(2)}) %all-to-all-start.2) | async-done | bytes 1048608 | tf_op jit(solution)/shard_map/all_to_all | solution.py:171
  76.9 1.2 %copy-done.2 = f32[4,512,1]{2,1,0:T(8,128)S(1)} copy-done((f32[4,512,1]{2,1,0:T(8,128)S(1)}, f32[4,512,1]{2,1,0:T(8,128)}, u32[]{:S(2)}) %copy-start.2) | copy-done | bytes 8216
  78.1 1.2 %copy-done.4 = f32[4,512,1]{2,1,0:T(8,128)S(1)} copy-done((f32[4,512,1]{2,1,0:T(8,128)S(1)}, f32[4,512,1]{2,1,0:T(8,128)}, u32[]{:S(2)}) %copy-start.4) | copy-done | bytes 8216
  79.3 1.2 %copy-done.6 = f32[4,512,128]{2,1,0:T(8,128)S(1)} copy-done((f32[4,512,128]{2,1,0:T(8,128)S(1)}, f32[4,512,128]{2,1,0:T(8,128)}, u32[]{:S(2)}) %copy-start.6) | copy-done | bytes 1048600
  80.6 9.6 %shard_map.56 = bf16[4,512,128]{2,1,0:T(8,128)(2,1)S(1)} custom-call(s32[4,9]{1,0:T(4,128)S(1)} %add_select_fusion.1.owner_ref, s32[4]{0:T(128)S(1)} %get-tuple-element.15.count_ref, bf16[4,512,128]{2,1,0:T(8,128)(2,1)S(1)} %bitcast.37, bf16[16,256,128]{2,1,0:T(8,128)(2,1)S(1)} %all-to-all-done.2.k_ref, f32[4,512,1]{2,1,0:T(8,128)S(1)} %copy-done.2, ...), custom_call_target="tpu_custom_call" | custom-call | tf_op jit(solution)/shard_map/pallas_call | solution.py:129
  90.3 1.9 %collective-permute-start.1 = (bf16[2,512,128]{2,1,0:T(8,128)(2,1)S(1)}, bf16[2,512,128]{2,1,0:T(8,128)(2,1)S(1)}, u32[]{:S(2)}, u32[]{:S(2)}) collective-permute-start(bf16[2,512,128]{2,1,0:T(8,128)(2,1)S(1)} %bitcast.47), channel_id=1, source_target_pairs={{1,0},{2,1},{3,2},{4,3},{5,4},{6,5},{7,6},{8,7},{9,8},{10,9},{11,1... | collective-permute-start | bytes 786440 | tf_op jit(solution)/shard_map/ppermute | solution.py:17
  92.2 3.8 %collective-permute-start = (bf16[2,512,128]{2,1,0:T(8,128)(2,1)S(1)}, bf16[2,512,128]{2,1,0:T(8,128)(2,1)S(1)}, u32[]{:S(2)}, u32[]{:S(2)}) collective-permute-start(bf16[2,512,128]{2,1,0:T(8,128)(2,1)S(1)} %bitcast.46), channel_id=1, source_target_pairs={{0,1},{1,2},{2,3},{3,4},{4,5},{5,6},{6,7},{7,8},{8,9},{9,10},{10,1... | collective-permute-start | bytes 786440 | tf_op jit(solution)/shard_map/ppermute | solution.py:16
  96.0 4.7 %collective-permute-done.1 = bf16[2,512,128]{2,1,0:T(8,128)(2,1)S(1)} collective-permute-done((bf16[2,512,128]{2,1,0:T(8,128)(2,1)S(1)}, bf16[2,512,128]{2,1,0:T(8,128)(2,1)S(1)}, u32[]{:S(2)}, u32[]{:S(2)}) %collective-permute-start.1) | collective-permute-done | bytes 262176 | tf_op jit(solution)/shard_map/ppermute | solution.py:17
  100.8 0.2 collective-permute-done
  101.0 0.1 maximum_bitcast_fusion
  101.1 0.7 copy.70
  101.8 0.0 copy-start.9
  101.8 0.1 pad.clone
  101.9 0.1 copy.66
  102.0 0.0 copy-done
  102.1 0.4 copy-done.9
  102.5 2.1 %fusion.5 = bf16[6,1,8,65,128]{4,2,3,0,1:T(8,128)(2,1)S(1)} fusion(bf16[3,3,128,128]{3,2,1,0:T(8,128)(2,1)S(1)} %copy-done, bf16[8,1,7,2,128]{4,2,3,0,1:T(8,128)(2,1)S(1)} %slice.38, bf16[8,1,8,65,128]{4,2,3,0,1:T(8,128)(2,1)S(1)} %copy.66, pred[6]{0:T(512)(128)(4,1)S(1)} %or_and_fusion, pred[8,65]{0,1:T(8,128)(4,1)S(1)} %copy-done.9), kind=kOutput, calls=%fused_computation.11 | convolution fusion | flops 925415424 | bytes 2187790 | tf_op jit(solution)/shard_map/conv_general_dilated | solution.py:35
  104.6 0.0 copy-done.8
  104.6 1.5 %fusion.16 = f32[4,8,65,128]{3,1,2,0:T(8,128)S(1)} fusion(bf16[3,3,128,128]{3,2,1,0:T(8,128)(2,1)S(1)} %copy-done.8, bf16[6,1,7,1,128]{4,2,3,0,1:T(8,128)(2,1)S(1)} %get-tuple-element.20, bf16[6,1,7,1,128]{4,2,3,0,1:T(8,128)(2,1)S(1)} %get-tuple-element.19, bf16[6,1,8,65,128]{4,2,3,0,1:T(8,128)(2,1)S(1)} %fusion.5), kind=kOutput, calls=%fused_computation.23 | convolution fusion | flops 617533440 | bytes 2180096 | tf_op jit(solution)/shard_map/conv_general_dilated | solution.py:35
  106.0 0.3 copy.67
  106.3 0.1 slice.41
  106.4 0.9 fusion.13
  (13 shorter events, 0.2 us)
Async XLA Ops:
  0.0 102.0 %copy-start = (bf16[3,3,128,128]{3,2,1,0:T(8,128)(2,1)S(1)}, bf16[3,3,128,128]{3,2,1,0:T(8,128)(2,1)}, u32[]{:S(2)}) copy-start(bf16[3,3,128,128]{3,2,1,0:T(8,128)(2,1)} %param.8) | copy-start | bytes 884740
  3.5 11.2 %all-to-all-start = ((s32[16,1,1]{2,1,0:T(1,128)}), s32[16,1,1]{2,1,0:T(1,128)S(1)}, u32[]{:S(2)}, u32[]{:S(2)}) async-start(s32[16,1,1]{2,1,0:T(1,128)} %copy.61), calls=%async_computation | async-start | bytes 16384 | tf_op jit(solution)/shard_map/all_to_all | solution.py:160
  17.9 34.2 %copy-start.7 = (bf16[4,512,128]{2,1,0:T(8,128)(2,1)S(1)}, bf16[4,512,128]{2,1,0:T(8,128)(2,1)}, u32[]{:S(2)}) copy-start(bf16[4,512,128]{2,1,0:T(8,128)(2,1)} %param.5) | copy-start | bytes 1572868
  47.7 29.2 %all-to-all-start.2 = ((bf16[16,256,128]{2,1,0:T(8,128)(2,1)}), bf16[16,256,128]{2,1,0:T(8,128)(2,1)S(1)}, u32[]{:S(2)}, u32[]{:S(2)}) async-start(bf16[16,256,128]{2,1,0:T(8,128)(2,1)} %get-tuple-element.10), calls=%async_computation.2 | async-start | bytes 2097152 | tf_op jit(solution)/shard_map/all_to_all | solution.py:171
  65.6 1.0 copy-start.1
  66.7 1.0 copy-start.3
  67.7 1.0 copy-start.5
  76.9 1.2 %copy-start.2 = (f32[4,512,1]{2,1,0:T(8,128)S(1)}, f32[4,512,1]{2,1,0:T(8,128)}, u32[]{:S(2)}) copy-start(f32[4,512,1]{2,1,0:T(8,128)} %copy-done.1) | copy-start | bytes 24580
  78.1 1.2 %copy-start.4 = (f32[4,512,1]{2,1,0:T(8,128)S(1)}, f32[4,512,1]{2,1,0:T(8,128)}, u32[]{:S(2)}) copy-start(f32[4,512,1]{2,1,0:T(8,128)} %copy-done.3) | copy-start | bytes 24580
  79.3 1.2 %copy-start.6 = (f32[4,512,128]{2,1,0:T(8,128)S(1)}, f32[4,512,128]{2,1,0:T(8,128)}, u32[]{:S(2)}) copy-start(f32[4,512,128]{2,1,0:T(8,128)} %copy-done.5) | copy-start | bytes 3145732
  90.3 10.5 %collective-permute-start.1 = (bf16[2,512,128]{2,1,0:T(8,128)(2,1)S(1)}, bf16[2,512,128]{2,1,0:T(8,128)(2,1)S(1)}, u32[]{:S(2)}, u32[]{:S(2)}) collective-permute-start(bf16[2,512,128]{2,1,0:T(8,128)(2,1)S(1)} %bitcast.47), channel_id=1, source_target_pairs={{1,0},{2,1},{3,2},{4,3},{5,4},{6,5},{7,6},{8,7},{9,8},{10,9},{11,1... | collective-permute-start | bytes 786440 | tf_op jit(solution)/shard_map/ppermute | solution.py:17
  92.2 8.8 %collective-permute-start = (bf16[2,512,128]{2,1,0:T(8,128)(2,1)S(1)}, bf16[2,512,128]{2,1,0:T(8,128)(2,1)S(1)}, u32[]{:S(2)}, u32[]{:S(2)}) collective-permute-start(bf16[2,512,128]{2,1,0:T(8,128)(2,1)S(1)} %bitcast.46), channel_id=1, source_target_pairs={{0,1},{1,2},{2,3},{3,4},{4,5},{5,6},{6,7},{7,8},{8,9},{9,10},{10,1... | collective-permute-start | bytes 786440 | tf_op jit(solution)/shard_map/ppermute | solution.py:16
  101.8 0.7 copy-start.9
  102.5 2.1 %copy-start.8 = (bf16[3,3,128,128]{3,2,1,0:T(8,128)(2,1)S(1)}, bf16[3,3,128,128]{3,2,1,0:T(8,128)(2,1)}, u32[]{:S(2)}) copy-start(bf16[3,3,128,128]{3,2,1,0:T(8,128)(2,1)} %param.9) | copy-start | bytes 884740

commit v7 on v6

--- a/solution.py
+++ b/solution.py
@@ -70,13 +70,18 @@
     for j, at in blocks:
         blk = s[:, at : at + lanes]
         mx = blk if mx is None else jnp.maximum(mx, blk)
-    m_new = jnp.max(mx, axis=1, keepdims=True) * scale
+    rows = q.shape[0]
+
+    def column(row, width):
+        return jnp.broadcast_to(row, (width, rows)).T
+
+    m_new = jnp.max(mx.T, axis=0, keepdims=True) * scale
     if not first:
         m_old = m_in[0]
         m_new = jnp.maximum(m_old, m_new)
         alpha = jnp.exp(m_old - m_new)
     log2e = 1.4426950408889634
-    mb = jnp.broadcast_to(m_new * log2e, (m_new.shape[0], lanes))
+    mb = column(m_new * log2e, lanes)
     shifted = [mb + penalty[j] for j in range(slots)]
     acc = None
     ps = []
@@ -86,12 +91,13 @@
         ps.append(p.astype(jnp.bfloat16))
     pb = jnp.concatenate(ps, axis=1)
     mixed = jnp.dot(pb, kall, preferred_element_type=jnp.float32)
-    total = jnp.sum(acc, axis=1, keepdims=True)
+    total = jnp.sum(acc.T, axis=0, keepdims=True)
+    width = mixed.shape[1]
     if not first:
-        mixed = a_in[0] * alpha + mixed
+        mixed = a_in[0] * column(alpha, width) + mixed
         total = t_in[0] * alpha + total
     if last:
-        o_ref[0] = (mixed / total).astype(o_ref.dtype)
+        o_ref[0] = (mixed / column(total, width)).astype(o_ref.dtype)
     else:
         m_out[0] = m_new
         t_out[0] = total
@@ -102,7 +108,7 @@
     tiles, tile_size, channels = queries.shape
     owners, chunk_len, _ = chunk.shape
     slots = slot_owner.shape[1]
-    col_spec = pl.BlockSpec((1, tile_size, 1), lambda t, o, c: (t, 0, 0))
+    col_spec = pl.BlockSpec((1, 1, tile_size), lambda t, o, c: (t, 0, 0))
     acc_spec = pl.BlockSpec((1, tile_size, channels), lambda t, o, c: (t, 0, 0))
     state_specs = [] if first else [col_spec, col_spec, acc_spec]
     if last:
@@ -111,8 +117,8 @@
     else:
         out_specs = [col_spec, col_spec, acc_spec]
         out_shape = [
-            jax.ShapeDtypeStruct((tiles, tile_size, 1), jnp.float32),
-            jax.ShapeDtypeStruct((tiles, tile_size, 1), jnp.float32),
+            jax.ShapeDtypeStruct((tiles, 1, tile_size), jnp.float32),
+            jax.ShapeDtypeStruct((tiles, 1, tile_size), jnp.float32),
             jax.ShapeDtypeStruct((tiles, tile_size, channels), jnp.float32),
         ]
     grid_spec = pltpu.PrefetchScalarGridSpec(

time: 109 us -> 108 us (level)
  local copies, waits for them, and re-layouts: 13.4 us -> 8.99 us
  waiting for transfers between devices: 16.7 us -> 18.9 us
  Pallas kernels: 23.1 us -> 24.8 us
    unnamed x21 -> x13, local copies, waits for them, and re-layouts: 7.82 us -> 3.37 us
    pallas_call x2, Pallas kernels: 23.1 us -> 24.8 us  [attend_chunk(): pl.pallas_call(functools.partial(attend_kernel, scale=scale, first=first,...]
    all_to_all x1, waiting for transfers between devices: 8.22 us -> 9.81 us  [on_device(): lax.all_to_all(sending, 'row', split_axis=0, concat_axis=0, tiled=True)]
where the time goes in v7:
time: 108 us; the launch traced here: 106 us
  blocking collectives  29.8 us (28%)
  Pallas kernels  24.8 us (23%)
  waiting for transfers between devices  18.9 us (17%)
  starting transfers between devices  16.3 us (15%)
  local copies, waits for them, and re-layouts  8.99 us (8%)
  other arithmetic  3.78 us (4%)
  matrix products  3.51 us (3%)
    all_to_all x1, blocking collectives, on_device(): lax.all_to_all(sending, 'row', split_axis=0, concat_axis=0, tiled=True)  29.8 us
    pallas_call x2, Pallas kernels, attend_chunk(): pl.pallas_call(functools.partial(attend_kernel, scale=scale, first=first,...  24.8 us
    all_to_all x1, waiting for transfers between devices, on_device(): lax.all_to_all(sending, 'row', split_axis=0, concat_axis=0, tiled=True)  9.81 us
    all_to_all x1, starting transfers between devices, on_device(): lax.all_to_all(wanted.reshape(owners, 1), 'row', split_axis=0, concat_axi...  6.61 us
    ppermute x1, waiting for transfers between devices, halo_rows(): from_below = lax.ppermute(head, axis, [(i + 1, i) for i in range(ends)])  4.4 us
    all_to_all x1, starting transfers between devices, on_device(): lax.all_to_all(sending, 'row', split_axis=0, concat_axis=0, tiled=True)  4.38 us
    all_to_all x1, waiting for transfers between devices, on_device(): lax.all_to_all(wanted.reshape(owners, 1), 'row', split_axis=0, concat_axi...  3.54 us
    conv_general_dilated x2, matrix products, native_conv(): lax.conv_general_dilated(rows[None], weights, window_strides=(1, 1), padd...  3.51 us
  transfers between devices with their start and end apart: 4, of which 4 were waited for; matrix products, arithmetic and copies ran while one was open for 1% of the time, Pallas kernels for 13%

profile of v7, /device:TPU:9, one launch (start us, length us, event | category | flops | bytes accessed | tf_op | source)
XLA Modules:
  0.0 106.3 jit_solution(5241602365972503166)
XLA Ops:
  0.0 0.0 copy-start
  0.0 0.8 convert_reduce_fusion
  0.8 0.8 slice_reduce_fusion
  1.6 0.1 copy.59
  1.8 0.8 add_select_fusion.1.owner_ref
  2.5 0.1 copy.58
  2.6 0.1 copy.60
  2.7 0.1 select_reduce_fusion
  2.8 0.7 copy.61
  3.5 6.6 %all-to-all-start = ((s32[16,1,1]{2,1,0:T(1,128)}), s32[16,1,1]{2,1,0:T(1,128)S(1)}, u32[]{:S(2)}, u32[]{:S(2)}) async-start(s32[16,1,1]{2,1,0:T(1,128)} %copy.61), calls=%async_computation | async-start | bytes 16384 | tf_op jit(solution)/shard_map/all_to_all | solution.py:166
  10.1 1.1 %copy.62 = bf16[4,4,128,128]{3,2,1,0:T(8,128)(2,1)S(1)} copy(bf16[4,4,128,128]{3,2,0,1:T(8,128)(2,1)} %bitcast.45) | data formatting | bytes 1048576 | tf_op jit(solution)/shard_map/transpose | solution.py:154
  11.2 3.5 %all-to-all-done = s32[16,1,1]{2,1,0:T(1,128)S(1)} async-done(((s32[16,1,1]{2,1,0:T(1,128)}), s32[16,1,1]{2,1,0:T(1,128)S(1)}, u32[]{:S(2)}, u32[]{:S(2)}) %all-to-all-start) | async-done | bytes 96 | tf_op jit(solution)/shard_map/all_to_all | solution.py:166
  14.7 0.4 maximum_reduce_fusion
  15.1 1.0 gather_fusion
  16.1 0.4 compare_reduce_fusion
  16.5 0.3 broadcast_select_fusion
  16.7 1.1 %fusion.37 = (bf16[16,256,128]{2,1,0:T(8,128)(2,1)}, bf16[16,256,128]{2,1,0:T(8,128)(2,1)S(1)}) fusion(bf16[16,512,128]{2,1,0:T(8,128)(2,1)S(1)} %broadcast_select_fusion), kind=kLoop, calls=%fused_computation.59 | loop fusion | bytes 4194304 | tf_op jit(solution)/shard_map/slice | solution.py:174
  17.9 0.0 copy-start.3
  17.9 29.8 %all_to_all.19.k_ref = bf16[16,256,128]{2,1,0:T(8,128)(2,1)S(1)} all-to-all(bf16[16,256,128]{2,1,0:T(8,128)(2,1)S(1)} %get-tuple-element.18), channel_id=1, replica_groups=mesh['pairs'=2,'row'=16] {'row'}, dimensions={0} | all-to-all | bytes 2097152 | tf_op jit(solution)/shard_map/all_to_all | solution.py:177
  47.7 4.4 %all-to-all-start.2 = ((bf16[16,256,128]{2,1,0:T(8,128)(2,1)}), bf16[16,256,128]{2,1,0:T(8,128)(2,1)S(1)}, u32[]{:S(2)}, u32[]{:S(2)}) async-start(bf16[16,256,128]{2,1,0:T(8,128)(2,1)} %get-tuple-element.10), calls=%async_computation.2 | async-start | bytes 2097152 | tf_op jit(solution)/shard_map/all_to_all | solution.py:177
  52.0 0.0 copy-done.3
  52.1 14.0 %shard_map.55 = (f32[4,1,512]{2,1,0:T(1,128)S(1)}, f32[4,1,512]{2,1,0:T(1,128)S(1)}, f32[4,512,128]{2,1,0:T(8,128)S(1)}) custom-call(s32[4,9]{1,0:T(4,128)S(1)} %add_select_fusion.1.owner_ref, s32[4]{0:T(128)S(1)} %get-tuple-element.15.count_ref, bf16[4,512,128]{2,1,0:T(8,128)(2,1)S(1)} %bitcast.36, bf16[16,256,128]{2,1,0:T(8,128)(2,1)S(1)} %all_to_all.19.k_ref), custom_call_target="tpu_custom_call" | custom-call | tf_op jit(solution)/shard_map/pallas_call | solution.py:135
  66.1 0.0 copy-start.1
  66.1 1.0 copy-done.1
  67.1 9.8 %all-to-all-done.2.k_ref = bf16[16,256,128]{2,1,0:T(8,128)(2,1)S(1)} async-done(((bf16[16,256,128]{2,1,0:T(8,128)(2,1)}), bf16[16,256,128]{2,1,0:T(8,128)(2,1)S(1)}, u32[]{:S(2)}, u32[]{:S(2)}) %all-to-all-start.2) | async-done | bytes 1048608 | tf_op jit(solution)/shard_map/all_to_all | solution.py:177
  76.9 0.0 copy-start.2
  76.9 1.2 %copy-done.2 = f32[4,512,128]{2,1,0:T(8,128)S(1)} copy-done((f32[4,512,128]{2,1,0:T(8,128)S(1)}, f32[4,512,128]{2,1,0:T(8,128)}, u32[]{:S(2)}) %copy-start.2) | copy-done | bytes 1048600
  78.1 10.8 %shard_map.56 = bf16[4,512,128]{2,1,0:T(8,128)(2,1)S(1)} custom-call(s32[4,9]{1,0:T(4,128)S(1)} %add_select_fusion.1.owner_ref, s32[4]{0:T(128)S(1)} %get-tuple-element.15.count_ref, bf16[4,512,128]{2,1,0:T(8,128)(2,1)S(1)} %bitcast.37, bf16[16,256,128]{2,1,0:T(8,128)(2,1)S(1)} %all-to-all-done.2.k_ref, f32[4,1,512]{2,1,0:T(1,128)S(1)} %get-tuple-element.12.refs_0_, ...), custom_call_target="tpu_custom_call" | custom-call | tf_op jit(solution)/shard_map/pallas_call | solution.py:135
  89.0 3.2 %collective-permute-start = (bf16[2,512,128]{2,1,0:T(8,128)(2,1)S(1)}, bf16[2,512,128]{2,1,0:T(8,128)(2,1)S(1)}, u32[]{:S(2)}, u32[]{:S(2)}) collective-permute-start(bf16[2,512,128]{2,1,0:T(8,128)(2,1)S(1)} %bitcast.47), channel_id=1, source_target_pairs={{0,1},{1,2},{2,3},{3,4},{4,5},{5,6},{6,7},{7,8},{8,9},{9,10},{10,1... | collective-permute-start | bytes 786440 | tf_op jit(solution)/shard_map/ppermute | solution.py:16
  92.3 2.1 %collective-permute-start.1 = (bf16[2,512,128]{2,1,0:T(8,128)(2,1)S(1)}, bf16[2,512,128]{2,1,0:T(8,128)(2,1)S(1)}, u32[]{:S(2)}, u32[]{:S(2)}) collective-permute-start(bf16[2,512,128]{2,1,0:T(8,128)(2,1)S(1)} %bitcast.46), channel_id=1, source_target_pairs={{1,0},{2,1},{3,2},{4,3},{5,4},{6,5},{7,6},{8,7},{9,8},{10,9},{11,1... | collective-permute-start | bytes 786440 | tf_op jit(solution)/shard_map/ppermute | solution.py:17
  94.4 1.2 %collective-permute-done = bf16[2,512,128]{2,1,0:T(8,128)(2,1)S(1)} collective-permute-done((bf16[2,512,128]{2,1,0:T(8,128)(2,1)S(1)}, bf16[2,512,128]{2,1,0:T(8,128)(2,1)S(1)}, u32[]{:S(2)}, u32[]{:S(2)}) %collective-permute-start) | collective-permute-done | bytes 262176 | tf_op jit(solution)/shard_map/ppermute | solution.py:16
  95.5 4.4 %collective-permute-done.1 = bf16[2,512,128]{2,1,0:T(8,128)(2,1)S(1)} collective-permute-done((bf16[2,512,128]{2,1,0:T(8,128)(2,1)S(1)}, bf16[2,512,128]{2,1,0:T(8,128)(2,1)S(1)}, u32[]{:S(2)}, u32[]{:S(2)}) %collective-permute-start.1) | collective-permute-done | bytes 262176 | tf_op jit(solution)/shard_map/ppermute | solution.py:17
  99.9 0.1 maximum_bitcast_fusion
  100.1 0.7 copy.70
  100.8 0.0 copy-start.5
  100.8 0.1 pad.clone
  100.8 0.1 copy.66
  101.0 0.0 copy-done
  101.0 0.4 copy-done.5
  101.5 0.0 copy-start.4
  101.5 2.1 %fusion.5 = bf16[6,1,8,65,128]{4,2,3,0,1:T(8,128)(2,1)S(1)} fusion(bf16[3,3,128,128]{3,2,1,0:T(8,128)(2,1)S(1)} %copy-done, bf16[8,1,7,2,128]{4,2,3,0,1:T(8,128)(2,1)S(1)} %slice.38, bf16[8,1,8,65,128]{4,2,3,0,1:T(8,128)(2,1)S(1)} %copy.66, pred[6]{0:T(512)(128)(4,1)S(1)} %or_and_fusion, pred[8,65]{0,1:T(8,128)(4,1)S(1)} %copy-done.5), kind=kOutput, calls=%fused_computation.11 | convolution fusion | flops 925415424 | bytes 2187790 | tf_op jit(solution)/shard_map/conv_general_dilated | solution.py:35
  103.5 0.0 copy-done.4
  103.5 1.5 %fusion.16 = f32[4,8,65,128]{3,1,2,0:T(8,128)S(1)} fusion(bf16[3,3,128,128]{3,2,1,0:T(8,128)(2,1)S(1)} %copy-done.4, bf16[6,1,7,1,128]{4,2,3,0,1:T(8,128)(2,1)S(1)} %get-tuple-element.20, bf16[6,1,7,1,128]{4,2,3,0,1:T(8,128)(2,1)S(1)} %get-tuple-element.19, bf16[6,1,8,65,128]{4,2,3,0,1:T(8,128)(2,1)S(1)} %fusion.5), kind=kOutput, calls=%fused_computation.23 | convolution fusion | flops 617533440 | bytes 2180096 | tf_op jit(solution)/shard_map/conv_general_dilated | solution.py:35
  105.0 0.3 copy.67
  105.3 0.1 slice.41
  105.4 0.9 fusion.13
  (7 shorter events, 0.2 us)
Async XLA Ops:
  0.0 101.0 %copy-start = (bf16[3,3,128,128]{3,2,1,0:T(8,128)(2,1)S(1)}, bf16[3,3,128,128]{3,2,1,0:T(8,128)(2,1)}, u32[]{:S(2)}) copy-start(bf16[3,3,128,128]{3,2,1,0:T(8,128)(2,1)} %param.8) | copy-start | bytes 884740
  3.5 11.2 %all-to-all-start = ((s32[16,1,1]{2,1,0:T(1,128)}), s32[16,1,1]{2,1,0:T(1,128)S(1)}, u32[]{:S(2)}, u32[]{:S(2)}) async-start(s32[16,1,1]{2,1,0:T(1,128)} %copy.61), calls=%async_computation | async-start | bytes 16384 | tf_op jit(solution)/shard_map/all_to_all | solution.py:166
  17.9 34.2 %copy-start.3 = (bf16[4,512,128]{2,1,0:T(8,128)(2,1)S(1)}, bf16[4,512,128]{2,1,0:T(8,128)(2,1)}, u32[]{:S(2)}) copy-start(bf16[4,512,128]{2,1,0:T(8,128)(2,1)} %param.5) | copy-start | bytes 1572868
  47.7 29.2 %all-to-all-start.2 = ((bf16[16,256,128]{2,1,0:T(8,128)(2,1)}), bf16[16,256,128]{2,1,0:T(8,128)(2,1)S(1)}, u32[]{:S(2)}, u32[]{:S(2)}) async-start(bf16[16,256,128]{2,1,0:T(8,128)(2,1)} %get-tuple-element.10), calls=%async_computation.2 | async-start | bytes 2097152 | tf_op jit(solution)/shard_map/all_to_all | solution.py:177
  66.1 1.0 copy-start.1
  76.9 1.2 %copy-start.2 = (f32[4,512,128]{2,1,0:T(8,128)S(1)}, f32[4,512,128]{2,1,0:T(8,128)}, u32[]{:S(2)}) copy-start(f32[4,512,128]{2,1,0:T(8,128)} %copy-done.1) | copy-start | bytes 3145732
  89.0 6.5 %collective-permute-start = (bf16[2,512,128]{2,1,0:T(8,128)(2,1)S(1)}, bf16[2,512,128]{2,1,0:T(8,128)(2,1)S(1)}, u32[]{:S(2)}, u32[]{:S(2)}) collective-permute-start(bf16[2,512,128]{2,1,0:T(8,128)(2,1)S(1)} %bitcast.47), channel_id=1, source_target_pairs={{0,1},{1,2},{2,3},{3,4},{4,5},{5,6},{6,7},{7,8},{8,9},{9,10},{10,1... | collective-permute-start | bytes 786440 | tf_op jit(solution)/shard_map/ppermute | solution.py:16
  92.3 7.7 %collective-permute-start.1 = (bf16[2,512,128]{2,1,0:T(8,128)(2,1)S(1)}, bf16[2,512,128]{2,1,0:T(8,128)(2,1)S(1)}, u32[]{:S(2)}, u32[]{:S(2)}) collective-permute-start(bf16[2,512,128]{2,1,0:T(8,128)(2,1)S(1)} %bitcast.46), channel_id=1, source_target_pairs={{1,0},{2,1},{3,2},{4,3},{5,4},{6,5},{7,6},{8,7},{9,8},{10,9},{11,1... | collective-permute-start | bytes 786440 | tf_op jit(solution)/shard_map/ppermute | solution.py:17
  100.8 0.7 copy-start.5
  101.5 2.1 %copy-start.4 = (bf16[3,3,128,128]{3,2,1,0:T(8,128)(2,1)S(1)}, bf16[3,3,128,128]{3,2,1,0:T(8,128)(2,1)}, u32[]{:S(2)}) copy-start(bf16[3,3,128,128]{3,2,1,0:T(8,128)(2,1)} %param.9) | copy-start | bytes 884740

commit v8 on v7

--- a/solution.py
+++ b/solution.py
@@ -160,13 +160,12 @@
     valid = tile_lists >= 0
     slot_owner = jnp.maximum(jnp.where(valid, tile_lists, tile_lists[:, :1]), 0) // per_device
     counts = jnp.sum(valid.astype(jnp.int32), axis=1)
-    owner_iota = jnp.arange(owners, dtype=jnp.int32)
-    matches = (slot_owner[:, :, None] == owner_iota[None, None, :]) & valid[:, :, None]
-    wanted = jnp.max(jnp.where(matches, (tile_lists % per_device)[:, :, None], -1), axis=(0, 1))
-    asked = lax.all_to_all(
-        wanted.reshape(owners, 1), "row", split_axis=0, concat_axis=0, tiled=True
-    )[:, 0]
-    outgoing = jnp.take(own_keys, jnp.maximum(asked, 0), axis=0)
+    me = lax.axis_index("row")
+    lists_everywhere = jnp.broadcast_to(tile_lists[None], (owners,) + tile_lists.shape)
+    lists_of = lax.all_to_all(lists_everywhere, "row", split_axis=0, concat_axis=0, tiled=True)
+    mine = (lists_of >= 0) & (lists_of // per_device == me)
+    asked = jnp.max(jnp.where(mine, lists_of % per_device, 0), axis=(1, 2))
+    outgoing = jnp.take(own_keys, asked, axis=0)
     edges = [0, tile_size // 2, tile_size]
     state = ()
     previous = None
@@ -186,7 +185,6 @@
         .transpose(1, 0, 2, 3)
         .reshape(band_rows, band_width, channels)
     )
-    me = lax.axis_index("row")
     extended = halo_rows(warped, "row", 2)
     hidden = jax.nn.relu(native_conv(extended, conv_one)).astype(jnp.bfloat16)
     row_ids = jnp.arange(band_rows + 2)

time: 108 us -> 106 us (0.981)
  other arithmetic: 3.78 us -> 1.82 us
    broadcast_in_dim x0 -> x1, local copies, waits for them, and re-layouts: none -> 1.34 us  [on_device(): jnp.broadcast_to(tile_lists[None], (owners,) + tile_lists.shape)]
    unnamed x13 -> x15, local copies, waits for them, and re-layouts: 3.37 us -> 3.37 us
where the time goes in v8:
time: 106 us; the launch traced here: 104 us
  blocking collectives  29.7 us (28%)
  Pallas kernels  24.7 us (23%)
  waiting for transfers between devices  19.1 us (18%)
  starting transfers between devices  16.4 us (15%)
  local copies, waits for them, and re-layouts  8.66 us (8%)
  matrix products  3.51 us (3%)
  other arithmetic  1.82 us (2%)
    all_to_all x1, blocking collectives, on_device(): lax.all_to_all(sending, 'row', split_axis=0, concat_axis=0, tiled=True)  29.7 us
    pallas_call x2, Pallas kernels, attend_chunk(): pl.pallas_call(functools.partial(attend_kernel, scale=scale, first=first,...  24.7 us
    all_to_all x1, waiting for transfers between devices, on_device(): lax.all_to_all(sending, 'row', split_axis=0, concat_axis=0, tiled=True)  9.56 us
    all_to_all x1, starting transfers between devices, on_device(): lax.all_to_all(lists_everywhere, 'row', split_axis=0, concat_axis=0, tile...  6.61 us
    all_to_all x1, starting transfers between devices, on_device(): lax.all_to_all(sending, 'row', split_axis=0, concat_axis=0, tiled=True)  4.52 us
    ppermute x1, waiting for transfers between devices, halo_rows(): from_below = lax.ppermute(head, axis, [(i + 1, i) for i in range(ends)])  4.4 us
    all_to_all x1, waiting for transfers between devices, on_device(): lax.all_to_all(lists_everywhere, 'row', split_axis=0, concat_axis=0, tile...  3.94 us
    conv_general_dilated x2, matrix products, native_conv(): lax.conv_general_dilated(rows[None], weights, window_strides=(1, 1), padd...  3.51 us
  transfers between devices with their start and end apart: 4, of which 4 were waited for; matrix products, arithmetic and copies ran while one was open for 1% of the time, Pallas kernels for 13%

profile of v8, /device:TPU:9, one launch (start us, length us, event | category | flops | bytes accessed | tf_op | source)
XLA Modules:
  0.0 104.2 jit_solution(1108081651473968833)
XLA Ops:
  0.0 0.0 copy-start
  0.0 1.3 %broadcast_in_dim.47 = s32[16,4,9]{2,1,0:T(4,128)} broadcast(s32[4,9]{1,0:T(4,128)} %param.7), dimensions={1,2} | broadcast | bytes 2448 | tf_op jit(solution)/shard_map/broadcast_in_dim | solution.py:164
  1.3 6.6 %all-to-all-start = ((s32[16,4,9]{2,1,0:T(4,128)}), s32[16,4,9]{2,1,0:T(4,128)S(1)}, u32[]{:S(2)}, u32[]{:S(2)}) async-start(s32[16,4,9]{2,1,0:T(4,128)} %broadcast_in_dim.47), calls=%async_computation | async-start | bytes 65536 | tf_op jit(solution)/shard_map/all_to_all | solution.py:165
  8.0 1.1 %copy.57 = bf16[4,4,128,128]{3,2,1,0:T(8,128)(2,1)S(1)} copy(bf16[4,4,128,128]{3,2,0,1:T(8,128)(2,1)} %bitcast.48) | data formatting | bytes 1048576 | tf_op jit(solution)/shard_map/transpose | solution.py:154
  9.0 3.9 %all-to-all-done = s32[16,4,9]{2,1,0:T(4,128)S(1)} async-done(((s32[16,4,9]{2,1,0:T(4,128)}), s32[16,4,9]{2,1,0:T(4,128)S(1)}, u32[]{:S(2)}, u32[]{:S(2)}) %all-to-all-start) | async-done | bytes 2336 | tf_op jit(solution)/shard_map/all_to_all | solution.py:165
  13.0 0.4 fusion.29
  13.4 1.0 gather_fusion
  14.4 0.3 broadcast_select_fusion
  14.6 1.1 %fusion.42 = (bf16[16,256,128]{2,1,0:T(8,128)(2,1)}, bf16[16,256,128]{2,1,0:T(8,128)(2,1)S(1)}) fusion(bf16[16,512,128]{2,1,0:T(8,128)(2,1)S(1)} %broadcast_select_fusion), kind=kLoop, calls=%fused_computation.65 | loop fusion | bytes 4194304 | tf_op jit(solution)/shard_map/slice | solution.py:173
  15.7 0.0 copy-start.3
  15.7 29.7 %all_to_all.15.k_ref = bf16[16,256,128]{2,1,0:T(8,128)(2,1)S(1)} all-to-all(bf16[16,256,128]{2,1,0:T(8,128)(2,1)S(1)} %get-tuple-element.16), channel_id=1, replica_groups=mesh['pairs'=2,'row'=16] {'row'}, dimensions={0} | all-to-all | bytes 2097152 | tf_op jit(solution)/shard_map/all_to_all | solution.py:176
  45.4 0.0 copy-start.4
  45.4 4.5 %all-to-all-start.2 = ((bf16[16,256,128]{2,1,0:T(8,128)(2,1)}), bf16[16,256,128]{2,1,0:T(8,128)(2,1)S(1)}, u32[]{:S(2)}, u32[]{:S(2)}) async-start(bf16[16,256,128]{2,1,0:T(8,128)(2,1)} %get-tuple-element.10), calls=%async_computation.2 | async-start | bytes 2097152 | tf_op jit(solution)/shard_map/all_to_all | solution.py:176
  50.0 0.0 copy-done.3
  50.0 0.0 copy-done.4
  50.0 0.1 slice_reduce_fusion
  50.1 0.1 fusion.32
  50.3 14.0 %shard_map.55 = (f32[4,1,512]{2,1,0:T(1,128)S(1)}, f32[4,1,512]{2,1,0:T(1,128)S(1)}, f32[4,512,128]{2,1,0:T(8,128)S(1)}) custom-call(s32[4,9]{1,0:T(4,128)S(1)} %get-tuple-element.24.owner_ref, s32[4]{0:T(128)S(1)} %get-tuple-element.23.count_ref, bf16[4,512,128]{2,1,0:T(8,128)(2,1)S(1)} %bitcast.39, bf16[16,256,128]{2,1,0:T(8,128)(2,1)S(1)} %all_to_all.15.k_ref), custom_call_target="tpu_custom_call" | custom-call | tf_op jit(solution)/shard_map/pallas_call | solution.py:135
  64.2 0.0 copy-start.1
  64.2 1.0 copy-done.1
  65.2 9.6 %all-to-all-done.2.k_ref = bf16[16,256,128]{2,1,0:T(8,128)(2,1)S(1)} async-done(((bf16[16,256,128]{2,1,0:T(8,128)(2,1)}), bf16[16,256,128]{2,1,0:T(8,128)(2,1)S(1)}, u32[]{:S(2)}, u32[]{:S(2)}) %all-to-all-start.2) | async-done | bytes 1048608 | tf_op jit(solution)/shard_map/all_to_all | solution.py:176
  74.8 0.0 copy-start.2
  74.8 1.2 %copy-done.2 = f32[4,512,128]{2,1,0:T(8,128)S(1)} copy-done((f32[4,512,128]{2,1,0:T(8,128)S(1)}, f32[4,512,128]{2,1,0:T(8,128)}, u32[]{:S(2)}) %copy-start.2) | copy-done | bytes 1048600
  76.0 10.8 %shard_map.56 = bf16[4,512,128]{2,1,0:T(8,128)(2,1)S(1)} custom-call(s32[4,9]{1,0:T(4,128)S(1)} %get-tuple-element.24.owner_ref, s32[4]{0:T(128)S(1)} %get-tuple-element.23.count_ref, bf16[4,512,128]{2,1,0:T(8,128)(2,1)S(1)} %bitcast.40, bf16[16,256,128]{2,1,0:T(8,128)(2,1)S(1)} %all-to-all-done.2.k_ref, f32[4,1,512]{2,1,0:T(1,128)S(1)} %get-tuple-element.12.refs_0_, ...), custom_call_target="tpu_custom_call" | custom-call | tf_op jit(solution)/shard_map/pallas_call | solution.py:135
  86.9 3.2 %collective-permute-start = (bf16[2,512,128]{2,1,0:T(8,128)(2,1)S(1)}, bf16[2,512,128]{2,1,0:T(8,128)(2,1)S(1)}, u32[]{:S(2)}, u32[]{:S(2)}) collective-permute-start(bf16[2,512,128]{2,1,0:T(8,128)(2,1)S(1)} %bitcast.50), channel_id=1, source_target_pairs={{0,1},{1,2},{2,3},{3,4},{4,5},{5,6},{6,7},{7,8},{8,9},{9,10},{10,1... | collective-permute-start | bytes 786440 | tf_op jit(solution)/shard_map/ppermute | solution.py:16
  90.1 2.1 %collective-permute-start.1 = (bf16[2,512,128]{2,1,0:T(8,128)(2,1)S(1)}, bf16[2,512,128]{2,1,0:T(8,128)(2,1)S(1)}, u32[]{:S(2)}, u32[]{:S(2)}) collective-permute-start(bf16[2,512,128]{2,1,0:T(8,128)(2,1)S(1)} %bitcast.49), channel_id=1, source_target_pairs={{1,0},{2,1},{3,2},{4,3},{5,4},{6,5},{7,6},{8,7},{9,8},{10,9},{11,1... | collective-permute-start | bytes 786440 | tf_op jit(solution)/shard_map/ppermute | solution.py:17
  92.3 1.2 %collective-permute-done = bf16[2,512,128]{2,1,0:T(8,128)(2,1)S(1)} collective-permute-done((bf16[2,512,128]{2,1,0:T(8,128)(2,1)S(1)}, bf16[2,512,128]{2,1,0:T(8,128)(2,1)S(1)}, u32[]{:S(2)}, u32[]{:S(2)}) %collective-permute-start) | collective-permute-done | bytes 262176 | tf_op jit(solution)/shard_map/ppermute | solution.py:16
  93.4 4.4 %collective-permute-done.1 = bf16[2,512,128]{2,1,0:T(8,128)(2,1)S(1)} collective-permute-done((bf16[2,512,128]{2,1,0:T(8,128)(2,1)S(1)}, bf16[2,512,128]{2,1,0:T(8,128)(2,1)S(1)}, u32[]{:S(2)}, u32[]{:S(2)}) %collective-permute-start.1) | collective-permute-done | bytes 262176 | tf_op jit(solution)/shard_map/ppermute | solution.py:17
  97.8 0.1 maximum_bitcast_fusion
  97.9 0.7 copy.66
  98.6 0.0 copy-start.6
  98.6 0.1 pad.clone
  98.7 0.1 copy.61
  98.9 0.0 copy-done
  98.9 0.4 copy-done.6
  99.3 0.0 copy-start.5
  99.3 2.1 %fusion.5 = bf16[6,1,8,65,128]{4,2,3,0,1:T(8,128)(2,1)S(1)} fusion(bf16[3,3,128,128]{3,2,1,0:T(8,128)(2,1)S(1)} %copy-done, bf16[8,1,7,2,128]{4,2,3,0,1:T(8,128)(2,1)S(1)} %slice.38, bf16[8,1,8,65,128]{4,2,3,0,1:T(8,128)(2,1)S(1)} %copy.61, pred[6]{0:T(512)(128)(4,1)S(1)} %or_and_fusion, pred[8,65]{0,1:T(8,128)(4,1)S(1)} %copy-done.6), kind=kOutput, calls=%fused_computation.11 | convolution fusion | flops 925415424 | bytes 2187790 | tf_op jit(solution)/shard_map/conv_general_dilated | solution.py:35
  101.4 0.0 copy-done.5
  101.4 1.4 %fusion.16 = f32[4,8,65,128]{3,1,2,0:T(8,128)S(1)} fusion(bf16[3,3,128,128]{3,2,1,0:T(8,128)(2,1)S(1)} %copy-done.5, bf16[6,1,7,1,128]{4,2,3,0,1:T(8,128)(2,1)S(1)} %get-tuple-element.18, bf16[6,1,7,1,128]{4,2,3,0,1:T(8,128)(2,1)S(1)} %get-tuple-element.17, bf16[6,1,8,65,128]{4,2,3,0,1:T(8,128)(2,1)S(1)} %fusion.5), kind=kOutput, calls=%fused_computation.23 | convolution fusion | flops 617533440 | bytes 2180096 | tf_op jit(solution)/shard_map/conv_general_dilated | solution.py:35
  102.9 0.3 copy.62
  103.2 0.1 slice.41
  103.3 0.9 fusion.13
  (9 shorter events, 0.2 us)
Async XLA Ops:
  0.0 98.9 %copy-start = (bf16[3,3,128,128]{3,2,1,0:T(8,128)(2,1)S(1)}, bf16[3,3,128,128]{3,2,1,0:T(8,128)(2,1)}, u32[]{:S(2)}) copy-start(bf16[3,3,128,128]{3,2,1,0:T(8,128)(2,1)} %param.8) | copy-start | bytes 884740
  1.3 11.6 %all-to-all-start = ((s32[16,4,9]{2,1,0:T(4,128)}), s32[16,4,9]{2,1,0:T(4,128)S(1)}, u32[]{:S(2)}, u32[]{:S(2)}) async-start(s32[16,4,9]{2,1,0:T(4,128)} %broadcast_in_dim.47), calls=%async_computation | async-start | bytes 65536 | tf_op jit(solution)/shard_map/all_to_all | solution.py:165
  15.7 34.2 %copy-start.3 = (bf16[4,512,128]{2,1,0:T(8,128)(2,1)S(1)}, bf16[4,512,128]{2,1,0:T(8,128)(2,1)}, u32[]{:S(2)}) copy-start(bf16[4,512,128]{2,1,0:T(8,128)(2,1)} %param.5) | copy-start | bytes 1572868
  45.4 4.6 %copy-start.4 = (s32[4,9]{1,0:T(4,128)S(1)}, s32[4,9]{1,0:T(4,128)}, u32[]{:S(2)}) copy-start(s32[4,9]{1,0:T(4,128)} %param.7) | copy-start | bytes 436
  45.4 29.4 %all-to-all-start.2 = ((bf16[16,256,128]{2,1,0:T(8,128)(2,1)}), bf16[16,256,128]{2,1,0:T(8,128)(2,1)S(1)}, u32[]{:S(2)}, u32[]{:S(2)}) async-start(bf16[16,256,128]{2,1,0:T(8,128)(2,1)} %get-tuple-element.10), calls=%async_computation.2 | async-start | bytes 2097152 | tf_op jit(solution)/shard_map/all_to_all | solution.py:176
  64.2 1.0 copy-start.1
  74.8 1.2 %copy-start.2 = (f32[4,512,128]{2,1,0:T(8,128)S(1)}, f32[4,512,128]{2,1,0:T(8,128)}, u32[]{:S(2)}) copy-start(f32[4,512,128]{2,1,0:T(8,128)} %copy-done.1) | copy-start | bytes 3145732
  86.9 6.5 %collective-permute-start = (bf16[2,512,128]{2,1,0:T(8,128)(2,1)S(1)}, bf16[2,512,128]{2,1,0:T(8,128)(2,1)S(1)}, u32[]{:S(2)}, u32[]{:S(2)}) collective-permute-start(bf16[2,512,128]{2,1,0:T(8,128)(2,1)S(1)} %bitcast.50), channel_id=1, source_target_pairs={{0,1},{1,2},{2,3},{3,4},{4,5},{5,6},{6,7},{7,8},{8,9},{9,10},{10,1... | collective-permute-start | bytes 786440 | tf_op jit(solution)/shard_map/ppermute | solution.py:16
  90.1 7.7 %collective-permute-start.1 = (bf16[2,512,128]{2,1,0:T(8,128)(2,1)S(1)}, bf16[2,512,128]{2,1,0:T(8,128)(2,1)S(1)}, u32[]{:S(2)}, u32[]{:S(2)}) collective-permute-start(bf16[2,512,128]{2,1,0:T(8,128)(2,1)S(1)} %bitcast.49), channel_id=1, source_target_pairs={{1,0},{2,1},{3,2},{4,3},{5,4},{6,5},{7,6},{8,7},{9,8},{10,9},{11,1... | collective-permute-start | bytes 786440 | tf_op jit(solution)/shard_map/ppermute | solution.py:17
  98.6 0.7 copy-start.6
  99.3 2.1 %copy-start.5 = (bf16[3,3,128,128]{3,2,1,0:T(8,128)(2,1)S(1)}, bf16[3,3,128,128]{3,2,1,0:T(8,128)(2,1)}, u32[]{:S(2)}) copy-start(bf16[3,3,128,128]{3,2,1,0:T(8,128)(2,1)} %param.9) | copy-start | bytes 884740

commit v9 on v8

--- a/solution.py
+++ b/solution.py
@@ -161,10 +161,11 @@
     slot_owner = jnp.maximum(jnp.where(valid, tile_lists, tile_lists[:, :1]), 0) // per_device
     counts = jnp.sum(valid.astype(jnp.int32), axis=1)
     me = lax.axis_index("row")
-    lists_everywhere = jnp.broadcast_to(tile_lists[None], (owners,) + tile_lists.shape)
+    flat_lists = tile_lists.reshape(1, -1)
+    lists_everywhere = jnp.broadcast_to(flat_lists, (owners, flat_lists.shape[1]))
     lists_of = lax.all_to_all(lists_everywhere, "row", split_axis=0, concat_axis=0, tiled=True)
     mine = (lists_of >= 0) & (lists_of // per_device == me)
-    asked = jnp.max(jnp.where(mine, lists_of % per_device, 0), axis=(1, 2))
+    asked = jnp.max(jnp.where(mine, lists_of % per_device, 0), axis=1)
     outgoing = jnp.take(own_keys, asked, axis=0)
     edges = [0, tile_size // 2, tile_size]
     state = ()

time: 106 us -> 105 us (level)
  no operation moved by 1% of the time
where the time goes in v9:
time: 105 us; the launch traced here: 104 us
  blocking collectives  29.8 us (28%)
  Pallas kernels  24.7 us (24%)
  waiting for transfers between devices  18.7 us (18%)
  starting transfers between devices  16.4 us (16%)
  local copies, waits for them, and re-layouts  8.72 us (8%)
  matrix products  3.51 us (3%)
  other arithmetic  1.56 us (1%)
    all_to_all x1, blocking collectives, on_device(): lax.all_to_all(sending, 'row', split_axis=0, concat_axis=0, tiled=True)  29.8 us
    pallas_call x2, Pallas kernels, attend_chunk(): pl.pallas_call(functools.partial(attend_kernel, scale=scale, first=first,...  24.7 us
    all_to_all x1, waiting for transfers between devices, on_device(): lax.all_to_all(sending, 'row', split_axis=0, concat_axis=0, tiled=True)  9.56 us
    all_to_all x1, starting transfers between devices, on_device(): lax.all_to_all(lists_everywhere, 'row', split_axis=0, concat_axis=0, tile...  6.61 us
    all_to_all x1, starting transfers between devices, on_device(): lax.all_to_all(sending, 'row', split_axis=0, concat_axis=0, tiled=True)  4.52 us
    ppermute x1, waiting for transfers between devices, halo_rows(): from_below = lax.ppermute(head, axis, [(i + 1, i) for i in range(ends)])  4.4 us
    all_to_all x1, waiting for transfers between devices, on_device(): lax.all_to_all(lists_everywhere, 'row', split_axis=0, concat_axis=0, tile...  3.54 us
    conv_general_dilated x2, matrix products, native_conv(): lax.conv_general_dilated(rows[None], weights, window_strides=(1, 1), padd...  3.51 us
  transfers between devices with their start and end apart: 4, of which 4 were waited for; matrix products, arithmetic and copies ran while one was open for 1% of the time, Pallas kernels for 13%

profile of v9, /device:TPU:9, one launch (start us, length us, event | category | flops | bytes accessed | tf_op | source)
XLA Modules:
  0.0 103.7 jit_solution(6649700595290623203)
XLA Ops:
  0.0 0.0 copy-start
  0.0 0.8 broadcast_in_dim.48
  0.8 0.6 broadcast_in_dim.49
  1.4 6.6 %all-to-all-start = ((s32[16,1,36]{2,1,0:T(1,128)}), s32[16,1,36]{2,1,0:T(1,128)S(1)}, u32[]{:S(2)}, u32[]{:S(2)}) async-start(s32[16,1,36]{2,1,0:T(1,128)} %broadcast_in_dim.49), calls=%async_computation | async-start | bytes 16384 | tf_op jit(solution)/shard_map/all_to_all | solution.py:166
  8.0 1.1 %copy.43 = bf16[4,4,128,128]{3,2,1,0:T(8,128)(2,1)S(1)} copy(bf16[4,4,128,128]{3,2,0,1:T(8,128)(2,1)} %bitcast.49) | data formatting | bytes 1048576 | tf_op jit(solution)/shard_map/transpose | solution.py:154
  9.1 3.5 %all-to-all-done = s32[16,1,36]{2,1,0:T(1,128)S(1)} async-done(((s32[16,1,36]{2,1,0:T(1,128)}), s32[16,1,36]{2,1,0:T(1,128)S(1)}, u32[]{:S(2)}, u32[]{:S(2)}) %all-to-all-start) | async-done | bytes 2336 | tf_op jit(solution)/shard_map/all_to_all | solution.py:166
  12.6 0.1 fusion.29
  12.8 1.0 gather_fusion
  13.8 0.3 broadcast_select_fusion
  14.0 1.1 %fusion.42 = (bf16[16,256,128]{2,1,0:T(8,128)(2,1)}, bf16[16,256,128]{2,1,0:T(8,128)(2,1)S(1)}) fusion(bf16[16,512,128]{2,1,0:T(8,128)(2,1)S(1)} %broadcast_select_fusion), kind=kLoop, calls=%fused_computation.65 | loop fusion | bytes 4194304 | tf_op jit(solution)/shard_map/slice | solution.py:174
  15.1 0.0 copy-start.3
  15.1 29.8 %all_to_all.19.k_ref = bf16[16,256,128]{2,1,0:T(8,128)(2,1)S(1)} all-to-all(bf16[16,256,128]{2,1,0:T(8,128)(2,1)S(1)} %get-tuple-element.16), channel_id=1, replica_groups=mesh['pairs'=2,'row'=16] {'row'}, dimensions={0} | all-to-all | bytes 2097152 | tf_op jit(solution)/shard_map/all_to_all | solution.py:177
  44.9 0.0 copy-start.4
  44.9 4.5 %all-to-all-start.2 = ((bf16[16,256,128]{2,1,0:T(8,128)(2,1)}), bf16[16,256,128]{2,1,0:T(8,128)(2,1)S(1)}, u32[]{:S(2)}, u32[]{:S(2)}) async-start(bf16[16,256,128]{2,1,0:T(8,128)(2,1)} %get-tuple-element.10), calls=%async_computation.2 | async-start | bytes 2097152 | tf_op jit(solution)/shard_map/all_to_all | solution.py:177
  49.5 0.0 copy-done.3
  49.5 0.0 copy-done.4
  49.5 0.1 slice_reduce_fusion
  49.6 0.1 fusion.32
  49.8 14.0 %shard_map.55 = (f32[4,1,512]{2,1,0:T(1,128)S(1)}, f32[4,1,512]{2,1,0:T(1,128)S(1)}, f32[4,512,128]{2,1,0:T(8,128)S(1)}) custom-call(s32[4,9]{1,0:T(4,128)S(1)} %get-tuple-element.24.owner_ref, s32[4]{0:T(128)S(1)} %get-tuple-element.23.count_ref, bf16[4,512,128]{2,1,0:T(8,128)(2,1)S(1)} %bitcast.40, bf16[16,256,128]{2,1,0:T(8,128)(2,1)S(1)} %all_to_all.19.k_ref), custom_call_target="tpu_custom_call" | custom-call | tf_op jit(solution)/shard_map/pallas_call | solution.py:135
  63.7 0.0 copy-start.1
  63.7 1.0 copy-done.1
  64.7 9.6 %all-to-all-done.2.k_ref = bf16[16,256,128]{2,1,0:T(8,128)(2,1)S(1)} async-done(((bf16[16,256,128]{2,1,0:T(8,128)(2,1)}), bf16[16,256,128]{2,1,0:T(8,128)(2,1)S(1)}, u32[]{:S(2)}, u32[]{:S(2)}) %all-to-all-start.2) | async-done | bytes 1048608 | tf_op jit(solution)/shard_map/all_to_all | solution.py:177
  74.3 0.0 copy-start.2
  74.3 1.2 %copy-done.2 = f32[4,512,128]{2,1,0:T(8,128)S(1)} copy-done((f32[4,512,128]{2,1,0:T(8,128)S(1)}, f32[4,512,128]{2,1,0:T(8,128)}, u32[]{:S(2)}) %copy-start.2) | copy-done | bytes 1048600
  75.5 10.8 %shard_map.56 = bf16[4,512,128]{2,1,0:T(8,128)(2,1)S(1)} custom-call(s32[4,9]{1,0:T(4,128)S(1)} %get-tuple-element.24.owner_ref, s32[4]{0:T(128)S(1)} %get-tuple-element.23.count_ref, bf16[4,512,128]{2,1,0:T(8,128)(2,1)S(1)} %bitcast.41, bf16[16,256,128]{2,1,0:T(8,128)(2,1)S(1)} %all-to-all-done.2.k_ref, f32[4,1,512]{2,1,0:T(1,128)S(1)} %get-tuple-element.12.refs_0_, ...), custom_call_target="tpu_custom_call" | custom-call | tf_op jit(solution)/shard_map/pallas_call | solution.py:135
  86.4 3.2 %collective-permute-start = (bf16[2,512,128]{2,1,0:T(8,128)(2,1)S(1)}, bf16[2,512,128]{2,1,0:T(8,128)(2,1)S(1)}, u32[]{:S(2)}, u32[]{:S(2)}) collective-permute-start(bf16[2,512,128]{2,1,0:T(8,128)(2,1)S(1)} %bitcast.51), channel_id=1, source_target_pairs={{0,1},{1,2},{2,3},{3,4},{4,5},{5,6},{6,7},{7,8},{8,9},{9,10},{10,1... | collective-permute-start | bytes 786440 | tf_op jit(solution)/shard_map/ppermute | solution.py:16
  89.6 2.1 %collective-permute-start.1 = (bf16[2,512,128]{2,1,0:T(8,128)(2,1)S(1)}, bf16[2,512,128]{2,1,0:T(8,128)(2,1)S(1)}, u32[]{:S(2)}, u32[]{:S(2)}) collective-permute-start(bf16[2,512,128]{2,1,0:T(8,128)(2,1)S(1)} %bitcast.50), channel_id=1, source_target_pairs={{1,0},{2,1},{3,2},{4,3},{5,4},{6,5},{7,6},{8,7},{9,8},{10,9},{11,1... | collective-permute-start | bytes 786440 | tf_op jit(solution)/shard_map/ppermute | solution.py:17
  91.8 1.2 %collective-permute-done = bf16[2,512,128]{2,1,0:T(8,128)(2,1)S(1)} collective-permute-done((bf16[2,512,128]{2,1,0:T(8,128)(2,1)S(1)}, bf16[2,512,128]{2,1,0:T(8,128)(2,1)S(1)}, u32[]{:S(2)}, u32[]{:S(2)}) %collective-permute-start) | collective-permute-done | bytes 262176 | tf_op jit(solution)/shard_map/ppermute | solution.py:16
  92.9 4.4 %collective-permute-done.1 = bf16[2,512,128]{2,1,0:T(8,128)(2,1)S(1)} collective-permute-done((bf16[2,512,128]{2,1,0:T(8,128)(2,1)S(1)}, bf16[2,512,128]{2,1,0:T(8,128)(2,1)S(1)}, u32[]{:S(2)}, u32[]{:S(2)}) %collective-permute-start.1) | collective-permute-done | bytes 262176 | tf_op jit(solution)/shard_map/ppermute | solution.py:17
  97.3 0.1 maximum_bitcast_fusion
  97.4 0.7 copy.51
  98.1 0.0 copy-start.6
  98.1 0.1 pad.clone
  98.2 0.1 copy.47
  98.4 0.0 copy-done
  98.4 0.4 copy-done.6
  98.8 0.0 copy-start.5
  98.8 2.1 %fusion.5 = bf16[6,1,8,65,128]{4,2,3,0,1:T(8,128)(2,1)S(1)} fusion(bf16[3,3,128,128]{3,2,1,0:T(8,128)(2,1)S(1)} %copy-done, bf16[8,1,7,2,128]{4,2,3,0,1:T(8,128)(2,1)S(1)} %slice.38, bf16[8,1,8,65,128]{4,2,3,0,1:T(8,128)(2,1)S(1)} %copy.47, pred[6]{0:T(512)(128)(4,1)S(1)} %or_and_fusion, pred[8,65]{0,1:T(8,128)(4,1)S(1)} %copy-done.6), kind=kOutput, calls=%fused_computation.11 | convolution fusion | flops 925415424 | bytes 2187790 | tf_op jit(solution)/shard_map/conv_general_dilated | solution.py:35
  100.9 0.0 copy-done.5
  100.9 1.4 %fusion.16 = f32[4,8,65,128]{3,1,2,0:T(8,128)S(1)} fusion(bf16[3,3,128,128]{3,2,1,0:T(8,128)(2,1)S(1)} %copy-done.5, bf16[6,1,7,1,128]{4,2,3,0,1:T(8,128)(2,1)S(1)} %get-tuple-element.18, bf16[6,1,7,1,128]{4,2,3,0,1:T(8,128)(2,1)S(1)} %get-tuple-element.17, bf16[6,1,8,65,128]{4,2,3,0,1:T(8,128)(2,1)S(1)} %fusion.5), kind=kOutput, calls=%fused_computation.23 | convolution fusion | flops 617533440 | bytes 2180096 | tf_op jit(solution)/shard_map/conv_general_dilated | solution.py:35
  102.4 0.3 copy.48
  102.7 0.1 slice.41
  102.8 0.9 fusion.13
  (9 shorter events, 0.2 us)
Async XLA Ops:
  0.0 98.4 %copy-start = (bf16[3,3,128,128]{3,2,1,0:T(8,128)(2,1)S(1)}, bf16[3,3,128,128]{3,2,1,0:T(8,128)(2,1)}, u32[]{:S(2)}) copy-start(bf16[3,3,128,128]{3,2,1,0:T(8,128)(2,1)} %param.8) | copy-start | bytes 884740
  1.4 11.2 %all-to-all-start = ((s32[16,1,36]{2,1,0:T(1,128)}), s32[16,1,36]{2,1,0:T(1,128)S(1)}, u32[]{:S(2)}, u32[]{:S(2)}) async-start(s32[16,1,36]{2,1,0:T(1,128)} %broadcast_in_dim.49), calls=%async_computation | async-start | bytes 16384 | tf_op jit(solution)/shard_map/all_to_all | solution.py:166
  15.1 34.3 %copy-start.3 = (bf16[4,512,128]{2,1,0:T(8,128)(2,1)S(1)}, bf16[4,512,128]{2,1,0:T(8,128)(2,1)}, u32[]{:S(2)}) copy-start(bf16[4,512,128]{2,1,0:T(8,128)(2,1)} %param.5) | copy-start | bytes 1572868
  44.9 4.6 %copy-start.4 = (s32[4,9]{1,0:T(4,128)S(1)}, s32[4,9]{1,0:T(4,128)}, u32[]{:S(2)}) copy-start(s32[4,9]{1,0:T(4,128)} %param.7) | copy-start | bytes 436
  44.9 29.4 %all-to-all-start.2 = ((bf16[16,256,128]{2,1,0:T(8,128)(2,1)}), bf16[16,256,128]{2,1,0:T(8,128)(2,1)S(1)}, u32[]{:S(2)}, u32[]{:S(2)}) async-start(bf16[16,256,128]{2,1,0:T(8,128)(2,1)} %get-tuple-element.10), calls=%async_computation.2 | async-start | bytes 2097152 | tf_op jit(solution)/shard_map/all_to_all | solution.py:177
  63.7 1.0 copy-start.1
  74.3 1.2 %copy-start.2 = (f32[4,512,128]{2,1,0:T(8,128)S(1)}, f32[4,512,128]{2,1,0:T(8,128)}, u32[]{:S(2)}) copy-start(f32[4,512,128]{2,1,0:T(8,128)} %copy-done.1) | copy-start | bytes 3145732
  86.4 6.5 %collective-permute-start = (bf16[2,512,128]{2,1,0:T(8,128)(2,1)S(1)}, bf16[2,512,128]{2,1,0:T(8,128)(2,1)S(1)}, u32[]{:S(2)}, u32[]{:S(2)}) collective-permute-start(bf16[2,512,128]{2,1,0:T(8,128)(2,1)S(1)} %bitcast.51), channel_id=1, source_target_pairs={{0,1},{1,2},{2,3},{3,4},{4,5},{5,6},{6,7},{7,8},{8,9},{9,10},{10,1... | collective-permute-start | bytes 786440 | tf_op jit(solution)/shard_map/ppermute | solution.py:16
  89.6 7.7 %collective-permute-start.1 = (bf16[2,512,128]{2,1,0:T(8,128)(2,1)S(1)}, bf16[2,512,128]{2,1,0:T(8,128)(2,1)S(1)}, u32[]{:S(2)}, u32[]{:S(2)}) collective-permute-start(bf16[2,512,128]{2,1,0:T(8,128)(2,1)S(1)} %bitcast.50), channel_id=1, source_target_pairs={{1,0},{2,1},{3,2},{4,3},{5,4},{6,5},{7,6},{8,7},{9,8},{10,9},{11,1... | collective-permute-start | bytes 786440 | tf_op jit(solution)/shard_map/ppermute | solution.py:17
  98.1 0.7 copy-start.6
  98.8 2.1 %copy-start.5 = (bf16[3,3,128,128]{3,2,1,0:T(8,128)(2,1)S(1)}, bf16[3,3,128,128]{3,2,1,0:T(8,128)(2,1)}, u32[]{:S(2)}) copy-start(bf16[3,3,128,128]{3,2,1,0:T(8,128)(2,1)} %param.9) | copy-start | bytes 884740

commit v10 on v9

--- a/solution.py
+++ b/solution.py
@@ -166,12 +166,11 @@
     lists_of = lax.all_to_all(lists_everywhere, "row", split_axis=0, concat_axis=0, tiled=True)
     mine = (lists_of >= 0) & (lists_of // per_device == me)
     asked = jnp.max(jnp.where(mine, lists_of % per_device, 0), axis=1)
-    outgoing = jnp.take(own_keys, asked, axis=0)
     edges = [0, tile_size // 2, tile_size]
     state = ()
     previous = None
     for index, (start, stop) in enumerate(zip(edges[:-1], edges[1:])):
-        sending = outgoing[:, start:stop]
+        sending = jnp.take(own_keys[:, start:stop], asked, axis=0)
         if previous is not None:
             previous, sending, state = lax.optimization_barrier((previous, sending, state))
         current = lax.all_to_all(sending, "row", split_axis=0, concat_axis=0, tiled=True)

time: 105 us -> 105 us (level)
    slice x1, local copies, waits for them, and re-layouts: 1.1 us -> 0.04 us  [on_device(): sending = jnp.take(own_keys[:, start:stop], asked, axis=0)]
where the time goes in v10:
time: 105 us; the launch traced here: 104 us
  blocking collectives  29.7 us (28%)
  Pallas kernels  24.7 us (24%)
  waiting for transfers between devices  18 us (17%)
  starting transfers between devices  16.9 us (16%)
  local copies, waits for them, and re-layouts  8.29 us (8%)
  matrix products  3.51 us (3%)
  other arithmetic  2.52 us (2%)
    all_to_all x1, blocking collectives, on_device(): lax.all_to_all(sending, 'row', split_axis=0, concat_axis=0, tiled=True)  29.7 us
    pallas_call x2, Pallas kernels, attend_chunk(): pl.pallas_call(functools.partial(attend_kernel, scale=scale, first=first,...  24.7 us
    all_to_all x1, waiting for transfers between devices, on_device(): lax.all_to_all(sending, 'row', split_axis=0, concat_axis=0, tiled=True)  9.56 us
    all_to_all x1, starting transfers between devices, on_device(): lax.all_to_all(lists_everywhere, 'row', split_axis=0, concat_axis=0, tile...  6.61 us
    ppermute x1, waiting for transfers between devices, halo_rows(): from_below = lax.ppermute(head, axis, [(i + 1, i) for i in range(ends)])  4.72 us
    all_to_all x1, starting transfers between devices, on_device(): lax.all_to_all(sending, 'row', split_axis=0, concat_axis=0, tiled=True)  4.52 us
    ppermute x1, starting transfers between devices, halo_rows(): from_above = lax.ppermute(tail, axis, [(i, i + 1) for i in range(ends)])  3.82 us
    conv_general_dilated x2, matrix products, native_conv(): lax.conv_general_dilated(rows[None], weights, window_strides=(1, 1), padd...  3.51 us
  transfers between devices with their start and end apart: 4, of which 4 were waited for; matrix products, arithmetic and copies ran while one was open for 1% of the time, Pallas kernels for 13%

profile of v10, /device:TPU:9, one launch (start us, length us, event | category | flops | bytes accessed | tf_op | source)
XLA Modules:
  0.0 103.8 jit_solution(545283736726909001)
XLA Ops:
  0.0 0.0 copy-start
  0.0 0.8 broadcast_in_dim.47
  0.8 0.6 broadcast_in_dim.48
  1.4 6.6 %all-to-all-start = ((s32[16,1,36]{2,1,0:T(1,128)}), s32[16,1,36]{2,1,0:T(1,128)S(1)}, u32[]{:S(2)}, u32[]{:S(2)}) async-start(s32[16,1,36]{2,1,0:T(1,128)} %broadcast_in_dim.48), calls=%async_computation | async-start | bytes 16384 | tf_op jit(solution)/shard_map/all_to_all | solution.py:166
  8.0 1.1 %copy.43 = bf16[4,4,128,128]{3,2,1,0:T(8,128)(2,1)S(1)} copy(bf16[4,4,128,128]{3,2,0,1:T(8,128)(2,1)} %bitcast.45) | data formatting | bytes 1048576 | tf_op jit(solution)/shard_map/transpose | solution.py:154
  9.2 3.5 %all-to-all-done = s32[16,1,36]{2,1,0:T(1,128)S(1)} async-done(((s32[16,1,36]{2,1,0:T(1,128)}), s32[16,1,36]{2,1,0:T(1,128)S(1)}, u32[]{:S(2)}, u32[]{:S(2)}) %all-to-all-start) | async-done | bytes 2336 | tf_op jit(solution)/shard_map/all_to_all | solution.py:166
  12.6 0.1 fusion.29
  12.8 0.7 gather_fusion.1
  13.6 0.7 gather_fusion
  14.3 1.2 %broadcast_select_fusion = (bf16[16,256,128]{2,1,0:T(8,128)(2,1)}, bf16[16,256,128]{2,1,0:T(8,128)(2,1)S(1)}) fusion(bf16[16,256,128]{2,1,0:T(8,128)(2,1)S(1)} %gather_fusion.1, pred[16]{0:T(512)(128)(4,1)S(1)} %compare_and_fusion, bf16[16,256,128]{2,1,0:T(8,128)(2,1)S(1)} %gather_fusion), kind=kLoop, calls=%fused_computation.21 | loop fusion | flops 1048576 | bytes 4194320 | tf_op jit(solution)/shard_map/jit(_take)/select_n | solution.py:173
  15.6 29.7 %all_to_all.19.k_ref = bf16[16,256,128]{2,1,0:T(8,128)(2,1)S(1)} all-to-all(bf16[16,256,128]{2,1,0:T(8,128)(2,1)S(1)} %get-tuple-element.27), channel_id=1, replica_groups=mesh['pairs'=2,'row'=16] {'row'}, dimensions={0} | all-to-all | bytes 2097152 | tf_op jit(solution)/shard_map/all_to_all | solution.py:176
  45.2 0.0 copy-start.3
  45.2 0.0 copy-start.4
  45.2 4.5 %all-to-all-start.2 = ((bf16[16,256,128]{2,1,0:T(8,128)(2,1)}), bf16[16,256,128]{2,1,0:T(8,128)(2,1)S(1)}, u32[]{:S(2)}, u32[]{:S(2)}) async-start(bf16[16,256,128]{2,1,0:T(8,128)(2,1)} %get-tuple-element.11), calls=%async_computation.2 | async-start | bytes 2097152 | tf_op jit(solution)/shard_map/all_to_all | solution.py:176
  49.7 0.0 copy-done.3
  49.8 0.0 copy-done.4
  49.8 0.1 slice_reduce_fusion
  49.9 0.1 fusion.32
  50.0 14.0 %shard_map.55 = (f32[4,1,512]{2,1,0:T(1,128)S(1)}, f32[4,1,512]{2,1,0:T(1,128)S(1)}, f32[4,512,128]{2,1,0:T(8,128)S(1)}) custom-call(s32[4,9]{1,0:T(4,128)S(1)} %get-tuple-element.25.owner_ref, s32[4]{0:T(128)S(1)} %get-tuple-element.24.count_ref, bf16[4,512,128]{2,1,0:T(8,128)(2,1)S(1)} %bitcast.36, bf16[16,256,128]{2,1,0:T(8,128)(2,1)S(1)} %all_to_all.19.k_ref), custom_call_target="tpu_custom_call" | custom-call | tf_op jit(solution)/shard_map/pallas_call | solution.py:135
  64.0 0.0 copy-start.1
  64.0 1.0 copy-done.1
  65.0 9.6 %all-to-all-done.2.k_ref = bf16[16,256,128]{2,1,0:T(8,128)(2,1)S(1)} async-done(((bf16[16,256,128]{2,1,0:T(8,128)(2,1)}), bf16[16,256,128]{2,1,0:T(8,128)(2,1)S(1)}, u32[]{:S(2)}, u32[]{:S(2)}) %all-to-all-start.2) | async-done | bytes 1048608 | tf_op jit(solution)/shard_map/all_to_all | solution.py:176
  74.6 0.0 copy-start.2
  74.6 1.2 %copy-done.2 = f32[4,512,128]{2,1,0:T(8,128)S(1)} copy-done((f32[4,512,128]{2,1,0:T(8,128)S(1)}, f32[4,512,128]{2,1,0:T(8,128)}, u32[]{:S(2)}) %copy-start.2) | copy-done | bytes 1048600
  75.8 10.8 %shard_map.56 = bf16[4,512,128]{2,1,0:T(8,128)(2,1)S(1)} custom-call(s32[4,9]{1,0:T(4,128)S(1)} %get-tuple-element.25.owner_ref, s32[4]{0:T(128)S(1)} %get-tuple-element.24.count_ref, bf16[4,512,128]{2,1,0:T(8,128)(2,1)S(1)} %bitcast.37, bf16[16,256,128]{2,1,0:T(8,128)(2,1)S(1)} %all-to-all-done.2.k_ref, f32[4,1,512]{2,1,0:T(1,128)S(1)} %get-tuple-element.13.refs_0_, ...), custom_call_target="tpu_custom_call" | custom-call | tf_op jit(solution)/shard_map/pallas_call | solution.py:135
  86.7 1.9 %collective-permute-start.1 = (bf16[2,512,128]{2,1,0:T(8,128)(2,1)S(1)}, bf16[2,512,128]{2,1,0:T(8,128)(2,1)S(1)}, u32[]{:S(2)}, u32[]{:S(2)}) collective-permute-start(bf16[2,512,128]{2,1,0:T(8,128)(2,1)S(1)} %bitcast.47), channel_id=1, source_target_pairs={{1,0},{2,1},{3,2},{4,3},{5,4},{6,5},{7,6},{8,7},{9,8},{10,9},{11,1... | collective-permute-start | bytes 786440 | tf_op jit(solution)/shard_map/ppermute | solution.py:17
  88.6 3.8 %collective-permute-start = (bf16[2,512,128]{2,1,0:T(8,128)(2,1)S(1)}, bf16[2,512,128]{2,1,0:T(8,128)(2,1)S(1)}, u32[]{:S(2)}, u32[]{:S(2)}) collective-permute-start(bf16[2,512,128]{2,1,0:T(8,128)(2,1)S(1)} %bitcast.46), channel_id=1, source_target_pairs={{0,1},{1,2},{2,3},{3,4},{4,5},{5,6},{6,7},{7,8},{8,9},{9,10},{10,1... | collective-permute-start | bytes 786440 | tf_op jit(solution)/shard_map/ppermute | solution.py:16
  92.5 4.7 %collective-permute-done.1 = bf16[2,512,128]{2,1,0:T(8,128)(2,1)S(1)} collective-permute-done((bf16[2,512,128]{2,1,0:T(8,128)(2,1)S(1)}, bf16[2,512,128]{2,1,0:T(8,128)(2,1)S(1)}, u32[]{:S(2)}, u32[]{:S(2)}) %collective-permute-start.1) | collective-permute-done | bytes 262176 | tf_op jit(solution)/shard_map/ppermute | solution.py:17
  97.2 0.2 collective-permute-done
  97.4 0.1 maximum_bitcast_fusion
  97.5 0.7 copy.51
  98.2 0.1 pad.clone
  98.3 0.0 copy-start.6
  98.3 0.1 copy.47
  98.5 0.0 copy-done
  98.5 0.5 copy-done.6
  99.0 0.0 copy-start.5
  99.0 2.1 %fusion.5 = bf16[6,1,8,65,128]{4,2,3,0,1:T(8,128)(2,1)S(1)} fusion(bf16[3,3,128,128]{3,2,1,0:T(8,128)(2,1)S(1)} %copy-done, bf16[8,1,7,2,128]{4,2,3,0,1:T(8,128)(2,1)S(1)} %slice.40, bf16[8,1,8,65,128]{4,2,3,0,1:T(8,128)(2,1)S(1)} %copy.47, pred[6]{0:T(512)(128)(4,1)S(1)} %or_and_fusion, pred[8,65]{0,1:T(8,128)(4,1)S(1)} %copy-done.6), kind=kOutput, calls=%fused_computation.11 | convolution fusion | flops 925415424 | bytes 2187790 | tf_op jit(solution)/shard_map/conv_general_dilated | solution.py:35
  101.1 0.0 copy-done.5
  101.1 1.5 %fusion.16 = f32[4,8,65,128]{3,1,2,0:T(8,128)S(1)} fusion(bf16[3,3,128,128]{3,2,1,0:T(8,128)(2,1)S(1)} %copy-done.5, bf16[6,1,7,1,128]{4,2,3,0,1:T(8,128)(2,1)S(1)} %get-tuple-element.17, bf16[6,1,7,1,128]{4,2,3,0,1:T(8,128)(2,1)S(1)} %get-tuple-element.16, bf16[6,1,8,65,128]{4,2,3,0,1:T(8,128)(2,1)S(1)} %fusion.5), kind=kOutput, calls=%fused_computation.25 | convolution fusion | flops 617533440 | bytes 2180096 | tf_op jit(solution)/shard_map/conv_general_dilated | solution.py:35
  102.5 0.3 copy.48
  102.8 0.1 slice.43
  102.9 0.9 fusion.13
  (10 shorter events, 0.2 us)
Async XLA Ops:
  0.0 98.5 %copy-start = (bf16[3,3,128,128]{3,2,1,0:T(8,128)(2,1)S(1)}, bf16[3,3,128,128]{3,2,1,0:T(8,128)(2,1)}, u32[]{:S(2)}) copy-start(bf16[3,3,128,128]{3,2,1,0:T(8,128)(2,1)} %param.10) | copy-start | bytes 884740
  1.4 11.2 %all-to-all-start = ((s32[16,1,36]{2,1,0:T(1,128)}), s32[16,1,36]{2,1,0:T(1,128)S(1)}, u32[]{:S(2)}, u32[]{:S(2)}) async-start(s32[16,1,36]{2,1,0:T(1,128)} %broadcast_in_dim.48), calls=%async_computation | async-start | bytes 16384 | tf_op jit(solution)/shard_map/all_to_all | solution.py:166
  45.2 4.5 %copy-start.3 = (bf16[4,512,128]{2,1,0:T(8,128)(2,1)S(1)}, bf16[4,512,128]{2,1,0:T(8,128)(2,1)}, u32[]{:S(2)}) copy-start(bf16[4,512,128]{2,1,0:T(8,128)(2,1)} %param.7) | copy-start | bytes 1572868
  45.2 4.6 %copy-start.4 = (s32[4,9]{1,0:T(4,128)S(1)}, s32[4,9]{1,0:T(4,128)}, u32[]{:S(2)}) copy-start(s32[4,9]{1,0:T(4,128)} %param.9) | copy-start | bytes 436
  45.2 29.4 %all-to-all-start.2 = ((bf16[16,256,128]{2,1,0:T(8,128)(2,1)}), bf16[16,256,128]{2,1,0:T(8,128)(2,1)S(1)}, u32[]{:S(2)}, u32[]{:S(2)}) async-start(bf16[16,256,128]{2,1,0:T(8,128)(2,1)} %get-tuple-element.11), calls=%async_computation.2 | async-start | bytes 2097152 | tf_op jit(solution)/shard_map/all_to_all | solution.py:176
  64.0 1.0 copy-start.1
  74.6 1.2 %copy-start.2 = (f32[4,512,128]{2,1,0:T(8,128)S(1)}, f32[4,512,128]{2,1,0:T(8,128)}, u32[]{:S(2)}) copy-start(f32[4,512,128]{2,1,0:T(8,128)} %copy-done.1) | copy-start | bytes 3145732
  86.7 10.5 %collective-permute-start.1 = (bf16[2,512,128]{2,1,0:T(8,128)(2,1)S(1)}, bf16[2,512,128]{2,1,0:T(8,128)(2,1)S(1)}, u32[]{:S(2)}, u32[]{:S(2)}) collective-permute-start(bf16[2,512,128]{2,1,0:T(8,128)(2,1)S(1)} %bitcast.47), channel_id=1, source_target_pairs={{1,0},{2,1},{3,2},{4,3},{5,4},{6,5},{7,6},{8,7},{9,8},{10,9},{11,1... | collective-permute-start | bytes 786440 | tf_op jit(solution)/shard_map/ppermute | solution.py:17
  88.6 8.8 %collective-permute-start = (bf16[2,512,128]{2,1,0:T(8,128)(2,1)S(1)}, bf16[2,512,128]{2,1,0:T(8,128)(2,1)S(1)}, u32[]{:S(2)}, u32[]{:S(2)}) collective-permute-start(bf16[2,512,128]{2,1,0:T(8,128)(2,1)S(1)} %bitcast.46), channel_id=1, source_target_pairs={{0,1},{1,2},{2,3},{3,4},{4,5},{5,6},{6,7},{7,8},{8,9},{9,10},{10,1... | collective-permute-start | bytes 786440 | tf_op jit(solution)/shard_map/ppermute | solution.py:16
  98.3 0.7 copy-start.6
  99.0 2.1 %copy-start.5 = (bf16[3,3,128,128]{3,2,1,0:T(8,128)(2,1)S(1)}, bf16[3,3,128,128]{3,2,1,0:T(8,128)(2,1)}, u32[]{:S(2)}) copy-start(bf16[3,3,128,128]{3,2,1,0:T(8,128)(2,1)} %param.11) | copy-start | bytes 884740

commit v11 on v10

--- a/solution.py
+++ b/solution.py
@@ -10,11 +10,16 @@
 
 def halo_rows(cells, axis, width):
     count = lax.axis_size(axis)
-    ends = count - 1
+    even = lax.axis_index(axis) % 2 == 0
     head = cells[:width]
     tail = cells[cells.shape[0] - width :]
-    from_above = lax.ppermute(tail, axis, [(i, i + 1) for i in range(ends)])
-    from_below = lax.ppermute(head, axis, [(i + 1, i) for i in range(ends)])
+    same_chip = lax.ppermute(
+        jnp.where(even, tail, head), axis, [(i, i ^ 1) for i in range(count)]
+    )
+    links = [(i, i + 1) for i in range(1, count - 1, 2)] + [(i + 1, i) for i in range(1, count - 1, 2)]
+    across = lax.ppermute(jnp.where(even, head, tail), axis, links)
+    from_above = jnp.where(even, across, same_chip)
+    from_below = jnp.where(even, same_chip, across)
     return jnp.concatenate([from_above, cells, from_below], axis=0)
 
 

time: 105 us -> 105 us (level)
  starting transfers between devices: 16.9 us -> 14.9 us
  waiting for transfers between devices: 18 us -> 19.9 us
    ppermute x2, starting transfers between devices: 5.74 us -> 3.75 us  [the longest x1 3.68 us: halo_rows(): across = lax.ppermute(jnp.where(even, head, tail), axis, links)]
    ppermute x2, waiting for transfers between devices: 4.93 us -> 6.78 us  [the longest x1 6.78 us: halo_rows(): across = lax.ppermute(jnp.where(even, head, tail), axis, links)]
  transfers between devices with their start and end apart: 4 -> 4, of which waited for: 4 -> 3; matrix products, arithmetic and copies ran while one was open for 1% -> 1% of each run, Pallas kernels for 13% -> 13%
where the time goes in v11:
time: 105 us; the launch traced here: 104 us
  blocking collectives  29.7 us (28%)
  Pallas kernels  24.7 us (24%)
  waiting for transfers between devices  19.9 us (19%)
  starting transfers between devices  14.9 us (14%)
  local copies, waits for them, and re-layouts  8.22 us (8%)
  matrix products  3.52 us (3%)
  other arithmetic  2.6 us (2%)
    all_to_all x1, blocking collectives, on_device(): lax.all_to_all(sending, 'row', split_axis=0, concat_axis=0, tiled=True)  29.7 us
    pallas_call x2, Pallas kernels, attend_chunk(): pl.pallas_call(functools.partial(attend_kernel, scale=scale, first=first,...  24.7 us
    all_to_all x1, waiting for transfers between devices, on_device(): lax.all_to_all(sending, 'row', split_axis=0, concat_axis=0, tiled=True)  9.58 us
    ppermute x1, waiting for transfers between devices, halo_rows(): across = lax.ppermute(jnp.where(even, head, tail), axis, links)  6.78 us
    all_to_all x1, starting transfers between devices, on_device(): lax.all_to_all(lists_everywhere, 'row', split_axis=0, concat_axis=0, tile...  6.61 us
    all_to_all x1, starting transfers between devices, on_device(): lax.all_to_all(sending, 'row', split_axis=0, concat_axis=0, tiled=True)  4.52 us
    ppermute x1, starting transfers between devices, halo_rows(): across = lax.ppermute(jnp.where(even, head, tail), axis, links)  3.68 us
    conv_general_dilated x2, matrix products, native_conv(): lax.conv_general_dilated(rows[None], weights, window_strides=(1, 1), padd...  3.52 us
  transfers between devices with their start and end apart: 4, of which 3 were waited for; matrix products, arithmetic and copies ran while one was open for 1% of the time, Pallas kernels for 13%

profile of v11, /device:TPU:9, one launch (start us, length us, event | category | flops | bytes accessed | tf_op | source)
XLA Modules:
  0.0 103.7 jit_solution(15644983583221599698)
XLA Ops:
  0.0 0.0 copy-start
  0.0 0.8 broadcast_in_dim.47
  0.8 0.6 broadcast_in_dim.48
  1.4 6.6 %all-to-all-start = ((s32[16,1,36]{2,1,0:T(1,128)}), s32[16,1,36]{2,1,0:T(1,128)S(1)}, u32[]{:S(2)}, u32[]{:S(2)}) async-start(s32[16,1,36]{2,1,0:T(1,128)} %broadcast_in_dim.48), calls=%async_computation | async-start | bytes 16384 | tf_op jit(solution)/shard_map/all_to_all | solution.py:171
  8.0 1.1 %copy.43 = bf16[4,4,128,128]{3,2,1,0:T(8,128)(2,1)S(1)} copy(bf16[4,4,128,128]{3,2,0,1:T(8,128)(2,1)} %bitcast.45) | data formatting | bytes 1048576 | tf_op jit(solution)/shard_map/transpose | solution.py:159
  9.2 3.5 %all-to-all-done = s32[16,1,36]{2,1,0:T(1,128)S(1)} async-done(((s32[16,1,36]{2,1,0:T(1,128)}), s32[16,1,36]{2,1,0:T(1,128)S(1)}, u32[]{:S(2)}, u32[]{:S(2)}) %all-to-all-start) | async-done | bytes 2336 | tf_op jit(solution)/shard_map/all_to_all | solution.py:171
  12.6 0.1 fusion.29
  12.8 0.7 gather_fusion.1
  13.6 0.7 gather_fusion
  14.3 1.2 %broadcast_select_fusion = (bf16[16,256,128]{2,1,0:T(8,128)(2,1)}, bf16[16,256,128]{2,1,0:T(8,128)(2,1)S(1)}) fusion(bf16[16,256,128]{2,1,0:T(8,128)(2,1)S(1)} %gather_fusion.1, pred[16]{0:T(512)(128)(4,1)S(1)} %compare_and_fusion, bf16[16,256,128]{2,1,0:T(8,128)(2,1)S(1)} %gather_fusion), kind=kLoop, calls=%fused_computation.21 | loop fusion | flops 1048576 | bytes 4194320 | tf_op jit(solution)/shard_map/jit(_take)/select_n | solution.py:178
  15.5 29.7 %all_to_all.19.k_ref = bf16[16,256,128]{2,1,0:T(8,128)(2,1)S(1)} all-to-all(bf16[16,256,128]{2,1,0:T(8,128)(2,1)S(1)} %get-tuple-element.29), channel_id=1, replica_groups=mesh['pairs'=2,'row'=16] {'row'}, dimensions={0} | all-to-all | bytes 2097152 | tf_op jit(solution)/shard_map/all_to_all | solution.py:181
  45.2 0.0 copy-start.3
  45.2 0.0 copy-start.4
  45.2 4.5 %all-to-all-start.2 = ((bf16[16,256,128]{2,1,0:T(8,128)(2,1)}), bf16[16,256,128]{2,1,0:T(8,128)(2,1)S(1)}, u32[]{:S(2)}, u32[]{:S(2)}) async-start(bf16[16,256,128]{2,1,0:T(8,128)(2,1)} %get-tuple-element.11), calls=%async_computation.2 | async-start | bytes 2097152 | tf_op jit(solution)/shard_map/all_to_all | solution.py:181
  49.7 0.0 copy-done.3
  49.8 0.0 copy-done.4
  49.8 0.1 slice_reduce_fusion
  49.9 0.1 fusion.32
  50.0 14.0 %shard_map.55 = (f32[4,1,512]{2,1,0:T(1,128)S(1)}, f32[4,1,512]{2,1,0:T(1,128)S(1)}, f32[4,512,128]{2,1,0:T(8,128)S(1)}) custom-call(s32[4,9]{1,0:T(4,128)S(1)} %get-tuple-element.27.owner_ref, s32[4]{0:T(128)S(1)} %get-tuple-element.26.count_ref, bf16[4,512,128]{2,1,0:T(8,128)(2,1)S(1)} %bitcast.36, bf16[16,256,128]{2,1,0:T(8,128)(2,1)S(1)} %all_to_all.19.k_ref), custom_call_target="tpu_custom_call" | custom-call | tf_op jit(solution)/shard_map/pallas_call | solution.py:140
  64.0 0.0 copy-start.1
  64.0 1.0 copy-done.1
  65.0 9.6 %all-to-all-done.2.k_ref = bf16[16,256,128]{2,1,0:T(8,128)(2,1)S(1)} async-done(((bf16[16,256,128]{2,1,0:T(8,128)(2,1)}), bf16[16,256,128]{2,1,0:T(8,128)(2,1)S(1)}, u32[]{:S(2)}, u32[]{:S(2)}) %all-to-all-start.2) | async-done | bytes 1048608 | tf_op jit(solution)/shard_map/all_to_all | solution.py:181
  74.6 0.0 copy-start.2
  74.6 1.2 %copy-done.2 = f32[4,512,128]{2,1,0:T(8,128)S(1)} copy-done((f32[4,512,128]{2,1,0:T(8,128)S(1)}, f32[4,512,128]{2,1,0:T(8,128)}, u32[]{:S(2)}) %copy-start.2) | copy-done | bytes 1048600
  75.8 10.8 %shard_map.56 = bf16[4,512,128]{2,1,0:T(8,128)(2,1)S(1)} custom-call(s32[4,9]{1,0:T(4,128)S(1)} %get-tuple-element.27.owner_ref, s32[4]{0:T(128)S(1)} %get-tuple-element.26.count_ref, bf16[4,512,128]{2,1,0:T(8,128)(2,1)S(1)} %bitcast.37, bf16[16,256,128]{2,1,0:T(8,128)(2,1)S(1)} %all-to-all-done.2.k_ref, f32[4,1,512]{2,1,0:T(1,128)S(1)} %get-tuple-element.13.refs_0_, ...), custom_call_target="tpu_custom_call" | custom-call | tf_op jit(solution)/shard_map/pallas_call | solution.py:140
  86.7 0.1 collective-permute-start.1
  86.8 3.7 %collective-permute-start = (bf16[2,512,128]{2,1,0:T(8,128)(2,1)S(1)}, bf16[2,512,128]{2,1,0:T(8,128)(2,1)S(1)}, u32[]{:S(2)}, u32[]{:S(2)}) collective-permute-start(bf16[2,512,128]{2,1,0:T(8,128)(2,1)S(1)} %bitcast.46), channel_id=1, source_target_pairs={{1,2},{3,4},{5,6},{7,8},{9,10},{11,12},{13,14},{2,1},{4,3},{6,5},{... | collective-permute-start | bytes 786440 | tf_op jit(solution)/shard_map/ppermute | solution.py:20
  90.5 0.0 collective-permute-done.1
  90.5 6.8 %collective-permute-done = bf16[2,512,128]{2,1,0:T(8,128)(2,1)S(1)} collective-permute-done((bf16[2,512,128]{2,1,0:T(8,128)(2,1)S(1)}, bf16[2,512,128]{2,1,0:T(8,128)(2,1)S(1)}, u32[]{:S(2)}, u32[]{:S(2)}) %collective-permute-start) | collective-permute-done | bytes 262176 | tf_op jit(solution)/shard_map/ppermute | solution.py:20
  97.3 0.1 maximum_bitcast_fusion
  97.4 0.7 copy.51
  98.1 0.1 pad.clone
  98.2 0.0 copy-start.6
  98.2 0.1 copy.47
  98.4 0.0 copy-done
  98.4 0.5 copy-done.6
  98.9 0.0 copy-start.5
  98.9 2.1 %fusion.5 = bf16[6,1,8,65,128]{4,2,3,0,1:T(8,128)(2,1)S(1)} fusion(bf16[3,3,128,128]{3,2,1,0:T(8,128)(2,1)S(1)} %copy-done, bf16[8,1,7,2,128]{4,2,3,0,1:T(8,128)(2,1)S(1)} %slice.34, bf16[8,1,8,65,128]{4,2,3,0,1:T(8,128)(2,1)S(1)} %copy.47, pred[6]{0:T(512)(128)(4,1)S(1)} %or_and_fusion, pred[8,65]{0,1:T(8,128)(4,1)S(1)} %copy-done.6), kind=kOutput, calls=%fused_computation.11 | convolution fusion | flops 925415424 | bytes 2187790 | tf_op jit(solution)/shard_map/conv_general_dilated | solution.py:40
  101.0 0.0 copy-done.5
  101.0 1.5 %fusion.16 = f32[4,8,65,128]{3,1,2,0:T(8,128)S(1)} fusion(bf16[3,3,128,128]{3,2,1,0:T(8,128)(2,1)S(1)} %copy-done.5, bf16[6,1,7,1,128]{4,2,3,0,1:T(8,128)(2,1)S(1)} %get-tuple-element.17, bf16[6,1,7,1,128]{4,2,3,0,1:T(8,128)(2,1)S(1)} %get-tuple-element.16, bf16[6,1,8,65,128]{4,2,3,0,1:T(8,128)(2,1)S(1)} %fusion.5), kind=kOutput, calls=%fused_computation.25 | convolution fusion | flops 617533440 | bytes 2180096 | tf_op jit(solution)/shard_map/conv_general_dilated | solution.py:40
  102.5 0.3 copy.48
  102.7 0.1 slice.37
  102.8 0.9 fusion.13
  (11 shorter events, 0.2 us)
Async XLA Ops:
  0.0 98.4 %copy-start = (bf16[3,3,128,128]{3,2,1,0:T(8,128)(2,1)S(1)}, bf16[3,3,128,128]{3,2,1,0:T(8,128)(2,1)}, u32[]{:S(2)}) copy-start(bf16[3,3,128,128]{3,2,1,0:T(8,128)(2,1)} %param.10) | copy-start | bytes 884740
  1.4 11.2 %all-to-all-start = ((s32[16,1,36]{2,1,0:T(1,128)}), s32[16,1,36]{2,1,0:T(1,128)S(1)}, u32[]{:S(2)}, u32[]{:S(2)}) async-start(s32[16,1,36]{2,1,0:T(1,128)} %broadcast_in_dim.48), calls=%async_computation | async-start | bytes 16384 | tf_op jit(solution)/shard_map/all_to_all | solution.py:171
  45.2 4.5 %copy-start.3 = (bf16[4,512,128]{2,1,0:T(8,128)(2,1)S(1)}, bf16[4,512,128]{2,1,0:T(8,128)(2,1)}, u32[]{:S(2)}) copy-start(bf16[4,512,128]{2,1,0:T(8,128)(2,1)} %param.7) | copy-start | bytes 1572868
  45.2 4.6 %copy-start.4 = (s32[4,9]{1,0:T(4,128)S(1)}, s32[4,9]{1,0:T(4,128)}, u32[]{:S(2)}) copy-start(s32[4,9]{1,0:T(4,128)} %param.9) | copy-start | bytes 436
  45.2 29.4 %all-to-all-start.2 = ((bf16[16,256,128]{2,1,0:T(8,128)(2,1)}), bf16[16,256,128]{2,1,0:T(8,128)(2,1)S(1)}, u32[]{:S(2)}, u32[]{:S(2)}) async-start(bf16[16,256,128]{2,1,0:T(8,128)(2,1)} %get-tuple-element.11), calls=%async_computation.2 | async-start | bytes 2097152 | tf_op jit(solution)/shard_map/all_to_all | solution.py:181
  64.0 1.0 copy-start.1
  74.6 1.2 %copy-start.2 = (f32[4,512,128]{2,1,0:T(8,128)S(1)}, f32[4,512,128]{2,1,0:T(8,128)}, u32[]{:S(2)}) copy-start(f32[4,512,128]{2,1,0:T(8,128)} %copy-done.1) | copy-start | bytes 3145732
  86.7 3.8 %collective-permute-start.1 = (bf16[2,512,128]{2,1,0:T(8,128)(2,1)S(1)}, bf16[2,512,128]{2,1,0:T(8,128)(2,1)S(1)}, u32[]{:S(2)}, u32[]{:S(2)}) collective-permute-start(bf16[2,512,128]{2,1,0:T(8,128)(2,1)S(1)} %bitcast.47), channel_id=1, source_target_pairs={{0,1},{1,0},{2,3},{3,2},{4,5},{5,4},{6,7},{7,6},{8,9},{9,8},{10,11... | collective-permute-start | bytes 786440 | tf_op jit(solution)/shard_map/ppermute | solution.py:16
  86.8 10.5 %collective-permute-start = (bf16[2,512,128]{2,1,0:T(8,128)(2,1)S(1)}, bf16[2,512,128]{2,1,0:T(8,128)(2,1)S(1)}, u32[]{:S(2)}, u32[]{:S(2)}) collective-permute-start(bf16[2,512,128]{2,1,0:T(8,128)(2,1)S(1)} %bitcast.46), channel_id=1, source_target_pairs={{1,2},{3,4},{5,6},{7,8},{9,10},{11,12},{13,14},{2,1},{4,3},{6,5},{... | collective-permute-start | bytes 786440 | tf_op jit(solution)/shard_map/ppermute | solution.py:20
  98.2 0.7 copy-start.6
  98.9 2.1 %copy-start.5 = (bf16[3,3,128,128]{3,2,1,0:T(8,128)(2,1)S(1)}, bf16[3,3,128,128]{3,2,1,0:T(8,128)(2,1)}, u32[]{:S(2)}) copy-start(bf16[3,3,128,128]{3,2,1,0:T(8,128)(2,1)} %param.11) | copy-start | bytes 884740

commit v12 on v11

--- a/solution.py
+++ b/solution.py
@@ -145,6 +145,38 @@
     )(slot_owner, counts, queries, chunk, *([] if first else state))
 
 
+def attend_last_half(state, queries, chunk, slot_owner, counts, half, scale):
+    tiles, tile_size, channels = queries.shape
+    owners, chunk_len, _ = chunk.shape
+    slots = slot_owner.shape[1]
+    part = tile_size // 2
+    row_spec = pl.BlockSpec((1, 1, part), lambda t, o, c, h: (t, 0, h[0]))
+    acc_spec = pl.BlockSpec((1, part, channels), lambda t, o, c, h: (t, h[0], 0))
+    grid_spec = pltpu.PrefetchScalarGridSpec(
+        num_scalar_prefetch=3,
+        grid=(tiles,),
+        in_specs=[
+            acc_spec,
+            pl.BlockSpec((owners, chunk_len, channels), lambda t, o, c, h: (0, 0, 0)),
+            row_spec,
+            row_spec,
+            acc_spec,
+        ],
+        out_specs=pl.BlockSpec((1, part, channels), lambda t, o, c, h: (t, 0, 0)),
+        scratch_shapes=[pltpu.VMEM((slots * chunk_len, channels), jnp.bfloat16)],
+    )
+
+    def kernel(owner_ref, count_ref, half_ref, *refs):
+        attend_kernel(owner_ref, count_ref, *refs, scale=scale, first=False, last=True)
+
+    return pl.pallas_call(
+        kernel,
+        grid_spec=grid_spec,
+        out_shape=jax.ShapeDtypeStruct((tiles, part, channels), jnp.bfloat16),
+        compiler_params=pltpu.CompilerParams(vmem_limit_bytes=48 * 1024 * 1024),
+    )(slot_owner, counts, half, queries, chunk, *state)
+
+
 def on_device(frame_one, frame_two, tile_lists, conv_one, conv_two):
     band_rows, band_width, channels = frame_one.shape
     per_device = tile_lists.shape[0]
@@ -182,15 +214,31 @@
         if previous is not None:
             state = attend_chunk(state, query_tiles, previous, slot_owner, counts, scale, index == 1, False)
         previous = current
-    warped_tiles = attend_chunk(
-        state, query_tiles, previous, slot_owner, counts, scale, len(edges) == 2, True
-    )
-    warped = (
-        warped_tiles.reshape(per_device, band_rows, tile_cols, channels)
-        .transpose(1, 0, 2, 3)
-        .reshape(band_rows, band_width, channels)
-    )
-    extended = halo_rows(warped, "row", 2)
+    even = me % 2 == 0
+    crossing = jnp.where(even, 0, 1).astype(jnp.int32).reshape(1)
+    staying = (1 - crossing).astype(jnp.int32)
+    crossing_tiles = attend_last_half(state, query_tiles, previous, slot_owner, counts, crossing, scale)
+    staying_tiles = attend_last_half(state, query_tiles, previous, slot_owner, counts, staying, scale)
+
+    def to_rows(tiles):
+        return tiles.reshape(per_device, -1, tile_cols, channels).transpose(1, 0, 2, 3).reshape(
+            -1, band_width, channels
+        )
+
+    crossing_rows = to_rows(crossing_tiles)
+    staying_rows = to_rows(staying_tiles)
+    count = lax.axis_size("row")
+    links = [(i, i + 1) for i in range(1, count - 1, 2)] + [(i + 1, i) for i in range(1, count - 1, 2)]
+    across = lax.ppermute(crossing_rows, "row", links)
+    same_chip = lax.ppermute(staying_rows, "row", [(i, i ^ 1) for i in range(count)])
+    warped = jnp.where(
+        even,
+        jnp.concatenate([crossing_rows, staying_rows], axis=0),
+        jnp.concatenate([staying_rows, crossing_rows], axis=0),
+    )
+    from_above = jnp.where(even, across, same_chip)
+    from_below = jnp.where(even, same_chip, across)
+    extended = jnp.concatenate([from_above, warped, from_below], axis=0)
     hidden = jax.nn.relu(native_conv(extended, conv_one)).astype(jnp.bfloat16)
     row_ids = jnp.arange(band_rows + 2)
     inside = ((row_ids > 0) | (me > 0)) & ((row_ids < band_rows + 1) | (me < owners - 1))

time: 105 us -> 102 us (0.971)
  waiting for transfers between devices: 19.9 us -> 13.2 us
  other arithmetic: 2.6 us -> 4.62 us
  Pallas kernels: 24.7 us -> 26.7 us
    pallas_call x0 -> x2, Pallas kernels: none -> 12.8 us  [attend_last_half(): pl.pallas_call(kernel, grid_spec=grid_spec, out_shape=jax.ShapeDtypeStruc...]
    pallas_call x2 -> x1, Pallas kernels: 24.7 us -> 13.9 us  [attend_chunk(): pl.pallas_call(functools.partial(attend_kernel, scale=scale, first=first,...]
    ppermute x2, waiting for transfers between devices: 6.78 us -> 0.38 us  [the longest x1 0.37 us: on_device(): lax.ppermute(staying_rows, 'row', [(i, i ^ 1) for i in range(count)])]
    select_n x2, other arithmetic: 0.08 us -> 2.1 us  [the longest x1 1.12 us: on_device(): jnp.where(even, jnp.concatenate([crossing_rows, staying_rows], axis=0), j...]
    unnamed x15 -> x13, local copies, waits for them, and re-layouts: 3.43 us -> 2.44 us
  transfers between devices with their start and end apart: 4 -> 4, of which waited for: 3 -> 3; matrix products, arithmetic and copies ran while one was open for 1% -> 2% of each run, Pallas kernels for 13% -> 20%
where the time goes in v12:
time: 102 us; the launch traced here: 101 us
  blocking collectives  30.3 us (30%)
  Pallas kernels  26.7 us (26%)
  starting transfers between devices  14.6 us (14%)
  waiting for transfers between devices  13.2 us (13%)
  local copies, waits for them, and re-layouts  7.93 us (8%)
  other arithmetic  4.62 us (5%)
  matrix products  3.47 us (3%)
    all_to_all x1, blocking collectives, on_device(): lax.all_to_all(sending, 'row', split_axis=0, concat_axis=0, tiled=True)  30.3 us
    pallas_call x1, Pallas kernels, attend_chunk(): pl.pallas_call(functools.partial(attend_kernel, scale=scale, first=first,...  13.9 us
    pallas_call x2, Pallas kernels, attend_last_half(): pl.pallas_call(kernel, grid_spec=grid_spec, out_shape=jax.ShapeDtypeStruc...  12.8 us
    all_to_all x1, waiting for transfers between devices, on_device(): lax.all_to_all(sending, 'row', split_axis=0, concat_axis=0, tiled=True)  9.35 us
    all_to_all x1, starting transfers between devices, on_device(): lax.all_to_all(lists_everywhere, 'row', split_axis=0, concat_axis=0, tile...  6.61 us
    all_to_all x1, starting transfers between devices, on_device(): lax.all_to_all(sending, 'row', split_axis=0, concat_axis=0, tiled=True)  4.51 us
    all_to_all x1, waiting for transfers between devices, on_device(): lax.all_to_all(lists_everywhere, 'row', split_axis=0, concat_axis=0, tile...  3.49 us
    conv_general_dilated x2, matrix products, native_conv(): lax.conv_general_dilated(rows[None], weights, window_strides=(1, 1), padd...  3.47 us
  transfers between devices with their start and end apart: 4, of which 3 were waited for; matrix products, arithmetic and copies ran while one was open for 2% of the time, Pallas kernels for 20%

profile of v12, /device:TPU:9, one launch (start us, length us, event | category | flops | bytes accessed | tf_op | source)
XLA Modules:
  0.0 101.1 jit_solution(2148444722267207472)
XLA Ops:
  0.0 0.0 copy-start
  0.0 0.8 broadcast_in_dim.47
  0.8 0.6 broadcast_in_dim.48
  1.4 6.6 %all-to-all-start = ((s32[16,1,36]{2,1,0:T(1,128)}), s32[16,1,36]{2,1,0:T(1,128)S(1)}, u32[]{:S(2)}, u32[]{:S(2)}) async-start(s32[16,1,36]{2,1,0:T(1,128)} %broadcast_in_dim.48), calls=%async_computation | async-start | bytes 16384 | tf_op jit(solution)/shard_map/all_to_all | solution.py:203
  8.0 1.1 %copy.47 = bf16[4,4,128,128]{3,2,1,0:T(8,128)(2,1)S(1)} copy(bf16[4,4,128,128]{3,2,0,1:T(8,128)(2,1)} %bitcast.49) | data formatting | bytes 1048576 | tf_op jit(solution)/shard_map/transpose | solution.py:191
  9.2 3.5 %all-to-all-done = s32[16,1,36]{2,1,0:T(1,128)S(1)} async-done(((s32[16,1,36]{2,1,0:T(1,128)}), s32[16,1,36]{2,1,0:T(1,128)S(1)}, u32[]{:S(2)}, u32[]{:S(2)}) %all-to-all-start) | async-done | bytes 2336 | tf_op jit(solution)/shard_map/all_to_all | solution.py:203
  12.6 0.1 fusion.29
  12.8 0.7 gather_fusion.1
  13.6 0.7 gather_fusion
  14.3 1.2 %broadcast_select_fusion = (bf16[16,256,128]{2,1,0:T(8,128)(2,1)}, bf16[16,256,128]{2,1,0:T(8,128)(2,1)S(1)}) fusion(bf16[16,256,128]{2,1,0:T(8,128)(2,1)S(1)} %gather_fusion.1, pred[16]{0:T(512)(128)(4,1)S(1)} %compare_and_fusion, bf16[16,256,128]{2,1,0:T(8,128)(2,1)S(1)} %gather_fusion), kind=kLoop, calls=%fused_computation.21 | loop fusion | flops 1048576 | bytes 4194320 | tf_op jit(solution)/shard_map/jit(_take)/select_n | solution.py:210
  15.5 30.3 %all_to_all.19.k_ref = bf16[16,256,128]{2,1,0:T(8,128)(2,1)} all-to-all(bf16[16,256,128]{2,1,0:T(8,128)(2,1)S(1)} %get-tuple-element.25), channel_id=1, replica_groups=mesh['pairs'=2,'row'=16] {'row'}, dimensions={0} | all-to-all | bytes 2097152 | tf_op jit(solution)/shard_map/all_to_all | solution.py:213
  45.9 0.0 copy-start.2
  45.9 0.0 copy-start.3
  45.9 4.5 %all-to-all-start.2 = ((bf16[16,256,128]{2,1,0:T(8,128)(2,1)}), bf16[16,256,128]{2,1,0:T(8,128)(2,1)S(1)}, u32[]{:S(2)}, u32[]{:S(2)}) async-start(bf16[16,256,128]{2,1,0:T(8,128)(2,1)} %get-tuple-element.11), calls=%async_computation.2 | async-start | bytes 2097152 | tf_op jit(solution)/shard_map/all_to_all | solution.py:213
  50.4 0.0 copy-done.2
  50.4 0.0 copy-done.3
  50.5 0.1 slice_reduce_fusion
  50.6 0.1 fusion.32
  50.7 0.0 copy-start.1
  50.7 1.2 %copy-done.1 = bf16[16,256,128]{2,1,0:T(8,128)(2,1)S(1)} copy-done((bf16[16,256,128]{2,1,0:T(8,128)(2,1)S(1)}, bf16[16,256,128]{2,1,0:T(8,128)(2,1)}, u32[]{:S(2)}) %copy-start.1) | copy-done | bytes 1048600
  51.9 13.9 %shard_map.55 = (f32[4,1,512]{2,1,0:T(1,128)S(1)}, f32[4,1,512]{2,1,0:T(1,128)S(1)}, f32[4,512,128]{2,1,0:T(8,128)S(1)}) custom-call(s32[4,9]{1,0:T(4,128)S(1)} %get-tuple-element.23.owner_ref, s32[4]{0:T(128)S(1)} %get-tuple-element.22.count_ref, bf16[4,512,128]{2,1,0:T(8,128)(2,1)S(1)} %bitcast.38, bf16[16,256,128]{2,1,0:T(8,128)(2,1)S(1)} %copy-done.1), custom_call_target="tpu_custom_call" | custom-call | tf_op jit(solution)/shard_map/pallas_call | solution.py:140
  65.9 9.4 %all-to-all-done.2.refs_1_ = bf16[16,256,128]{2,1,0:T(8,128)(2,1)S(1)} async-done(((bf16[16,256,128]{2,1,0:T(8,128)(2,1)}), bf16[16,256,128]{2,1,0:T(8,128)(2,1)S(1)}, u32[]{:S(2)}, u32[]{:S(2)}) %all-to-all-start.2) | async-done | bytes 1048608 | tf_op jit(solution)/shard_map/all_to_all | solution.py:213
  75.2 6.4 %shard_map.56 = bf16[4,256,128]{2,1,0:T(8,128)(2,1)S(1)} custom-call(s32[4,9]{1,0:T(4,128)S(1)} %get-tuple-element.23.owner_ref, s32[4]{0:T(128)S(1)} %get-tuple-element.22.count_ref, s32[1]{0:T(128)} %bitcast.half_ref, bf16[4,512,128]{2,1,0:T(8,128)(2,1)S(1)} %bitcast.39, bf16[16,256,128]{2,1,0:T(8,128)(2,1)S(1)} %all-to-all-done.2.refs_1_, ...), custom_call_target="tpu_custom_call" | custom-call | tf_op jit(solution)/shard_map/pallas_call | solution.py:172
  81.6 0.7 copy.48
  82.3 3.4 %collective-permute-start = (bf16[2,512,128]{2,1,0:T(8,128)(2,1)}, bf16[2,512,128]{2,1,0:T(8,128)(2,1)}, u32[]{:S(2)}, u32[]{:S(2)}) collective-permute-start(bf16[2,512,128]{2,1,0:T(8,128)(2,1)} %bitcast.11), channel_id=1, source_target_pairs={{1,2},{3,4},{5,6},{7,8},{9,10},{11,12},{13,14},{2,1},{4,3},{6,5},{... | collective-permute-start | bytes 786440 | tf_op jit(solution)/shard_map/ppermute | solution.py:232
  85.7 6.4 %shard_map.57 = bf16[4,256,128]{2,1,0:T(8,128)(2,1)S(1)} custom-call(s32[4,9]{1,0:T(4,128)S(1)} %get-tuple-element.23.owner_ref, s32[4]{0:T(128)S(1)} %get-tuple-element.22.count_ref, s32[1]{0:T(128)S(6)} %sub.17.half_ref, bf16[4,512,128]{2,1,0:T(8,128)(2,1)S(1)} %bitcast.40, bf16[16,256,128]{2,1,0:T(8,128)(2,1)S(1)} %all-to-all-done.2.refs_1_, ...), custom_call_target="tpu_custom_call" | custom-call | tf_op jit(solution)/shard_map/pallas_call | solution.py:172
  92.2 0.1 collective-permute-start.1
  92.3 1.1 %maximum_select_fusion = bf16[4,512,128]{2,1,0:T(8,128)(2,1)S(1)} fusion(bf16[2,512,128]{2,1,0:T(8,128)(2,1)S(1)} %bitcast.48, bf16[2,512,128]{2,1,0:T(8,128)(2,1)} %bitcast.11, pred[]{:T(512)S(6)} %eq.13), kind=kLoop, calls=%fused_computation.33 | loop fusion | flops 786432 | bytes 1048577 | tf_op jit(solution)/shard_map/jit(_where)/select_n | solution.py:234
  93.4 0.0 collective-permute-done
  93.4 0.4 collective-permute-done.1
  93.8 1.0 broadcast_select_fusion.3
  94.8 0.1 maximum_bitcast_fusion
  94.9 0.7 copy.56
  95.6 0.1 pad.clone
  95.7 0.0 copy-start.5
  95.7 0.1 copy.52
  95.8 0.0 copy-done
  95.8 0.5 copy-done.5
  96.4 0.0 copy-start.4
  96.4 2.0 %fusion.5 = bf16[6,1,8,65,128]{4,2,3,0,1:T(8,128)(2,1)S(1)} fusion(bf16[3,3,128,128]{3,2,1,0:T(8,128)(2,1)S(1)} %copy-done, bf16[8,1,7,2,128]{4,2,3,0,1:T(8,128)(2,1)S(1)} %slice.22, bf16[8,1,8,65,128]{4,2,3,0,1:T(8,128)(2,1)S(1)} %copy.52, pred[6]{0:T(512)(128)(4,1)S(1)} %or_and_fusion, pred[8,65]{0,1:T(8,128)(4,1)S(1)} %copy-done.5), kind=kOutput, calls=%fused_computation.11 | convolution fusion | flops 925415424 | bytes 2187790 | tf_op jit(solution)/shard_map/conv_general_dilated | solution.py:40
  98.4 0.0 copy-done.4
  98.4 1.4 %fusion.16 = f32[4,8,65,128]{3,1,2,0:T(8,128)S(1)} fusion(bf16[3,3,128,128]{3,2,1,0:T(8,128)(2,1)S(1)} %copy-done.4, bf16[6,1,7,1,128]{4,2,3,0,1:T(8,128)(2,1)S(1)} %get-tuple-element.17, bf16[6,1,7,1,128]{4,2,3,0,1:T(8,128)(2,1)S(1)} %get-tuple-element.16, bf16[6,1,8,65,128]{4,2,3,0,1:T(8,128)(2,1)S(1)} %fusion.5), kind=kOutput, calls=%fused_computation.25 | convolution fusion | flops 617533440 | bytes 2180096 | tf_op jit(solution)/shard_map/conv_general_dilated | solution.py:40
  99.9 0.3 copy.53
  100.2 0.1 slice.25
  100.2 0.9 fusion.13
  (9 shorter events, 0.1 us)
Async XLA Ops:
  0.0 95.8 %copy-start = (bf16[3,3,128,128]{3,2,1,0:T(8,128)(2,1)S(1)}, bf16[3,3,128,128]{3,2,1,0:T(8,128)(2,1)}, u32[]{:S(2)}) copy-start(bf16[3,3,128,128]{3,2,1,0:T(8,128)(2,1)} %param.10) | copy-start | bytes 884740
  1.4 11.2 %all-to-all-start = ((s32[16,1,36]{2,1,0:T(1,128)}), s32[16,1,36]{2,1,0:T(1,128)S(1)}, u32[]{:S(2)}, u32[]{:S(2)}) async-start(s32[16,1,36]{2,1,0:T(1,128)} %broadcast_in_dim.48), calls=%async_computation | async-start | bytes 16384 | tf_op jit(solution)/shard_map/all_to_all | solution.py:203
  45.9 4.5 %copy-start.2 = (bf16[4,512,128]{2,1,0:T(8,128)(2,1)S(1)}, bf16[4,512,128]{2,1,0:T(8,128)(2,1)}, u32[]{:S(2)}) copy-start(bf16[4,512,128]{2,1,0:T(8,128)(2,1)} %param.7) | copy-start | bytes 1572868
  45.9 4.6 %copy-start.3 = (s32[4,9]{1,0:T(4,128)S(1)}, s32[4,9]{1,0:T(4,128)}, u32[]{:S(2)}) copy-start(s32[4,9]{1,0:T(4,128)} %param.9) | copy-start | bytes 436
  45.9 29.4 %all-to-all-start.2 = ((bf16[16,256,128]{2,1,0:T(8,128)(2,1)}), bf16[16,256,128]{2,1,0:T(8,128)(2,1)S(1)}, u32[]{:S(2)}, u32[]{:S(2)}) async-start(bf16[16,256,128]{2,1,0:T(8,128)(2,1)} %get-tuple-element.11), calls=%async_computation.2 | async-start | bytes 2097152 | tf_op jit(solution)/shard_map/all_to_all | solution.py:213
  50.7 1.2 %copy-start.1 = (bf16[16,256,128]{2,1,0:T(8,128)(2,1)S(1)}, bf16[16,256,128]{2,1,0:T(8,128)(2,1)}, u32[]{:S(2)}) copy-start(bf16[16,256,128]{2,1,0:T(8,128)(2,1)} %all_to_all.19.k_ref) | copy-start | bytes 3145732
  82.3 11.0 %collective-permute-start = (bf16[2,512,128]{2,1,0:T(8,128)(2,1)}, bf16[2,512,128]{2,1,0:T(8,128)(2,1)}, u32[]{:S(2)}, u32[]{:S(2)}) collective-permute-start(bf16[2,512,128]{2,1,0:T(8,128)(2,1)} %bitcast.11), channel_id=1, source_target_pairs={{1,2},{3,4},{5,6},{7,8},{9,10},{11,12},{13,14},{2,1},{4,3},{6,5},{... | collective-permute-start | bytes 786440 | tf_op jit(solution)/shard_map/ppermute | solution.py:232
  92.2 1.6 %collective-permute-start.1 = (bf16[2,512,128]{2,1,0:T(8,128)(2,1)S(1)}, bf16[2,512,128]{2,1,0:T(8,128)(2,1)S(1)}, u32[]{:S(2)}, u32[]{:S(2)}) collective-permute-start(bf16[2,512,128]{2,1,0:T(8,128)(2,1)S(1)} %bitcast.47), channel_id=1, source_target_pairs={{0,1},{1,0},{2,3},{3,2},{4,5},{5,4},{6,7},{7,6},{8,9},{9,8},{10,11... | collective-permute-start | bytes 786440 | tf_op jit(solution)/shard_map/ppermute | solution.py:233
  95.7 0.7 copy-start.5
  96.4 2.1 %copy-start.4 = (bf16[3,3,128,128]{3,2,1,0:T(8,128)(2,1)S(1)}, bf16[3,3,128,128]{3,2,1,0:T(8,128)(2,1)}, u32[]{:S(2)}) copy-start(bf16[3,3,128,128]{3,2,1,0:T(8,128)(2,1)} %param.11) | copy-start | bytes 884740

commit v13 on v12

--- a/solution.py
+++ b/solution.py
@@ -231,14 +231,17 @@
     links = [(i, i + 1) for i in range(1, count - 1, 2)] + [(i + 1, i) for i in range(1, count - 1, 2)]
     across = lax.ppermute(crossing_rows, "row", links)
     same_chip = lax.ppermute(staying_rows, "row", [(i, i ^ 1) for i in range(count)])
-    warped = jnp.where(
-        even,
-        jnp.concatenate([crossing_rows, staying_rows], axis=0),
-        jnp.concatenate([staying_rows, crossing_rows], axis=0),
-    )
-    from_above = jnp.where(even, across, same_chip)
-    from_below = jnp.where(even, same_chip, across)
-    extended = jnp.concatenate([from_above, warped, from_below], axis=0)
+    half_rows = crossing_rows.shape[0]
+    extended = jnp.zeros((band_rows + 2 * half_rows, band_width, channels), crossing_rows.dtype)
+    outer = jnp.where(even, 0, band_rows + half_rows)
+    inner = jnp.where(even, band_rows + half_rows, 0)
+    for rows, at in (
+        (crossing_rows, half_rows + crossing[0] * half_rows),
+        (staying_rows, half_rows + staying[0] * half_rows),
+        (across, outer),
+        (same_chip, inner),
+    ):
+        extended = lax.dynamic_update_slice(extended, rows, (at, 0, 0))
     hidden = jax.nn.relu(native_conv(extended, conv_one)).astype(jnp.bfloat16)
     row_ids = jnp.arange(band_rows + 2)
     inside = ((row_ids > 0) | (me > 0)) & ((row_ids < band_rows + 1) | (me < owners - 1))

time: 102 us -> 105 us (1.029)
  waiting for transfers between devices: 13.2 us -> 18.1 us
  other arithmetic: 4.62 us -> 2.39 us
  local copies, waits for them, and re-layouts: 7.93 us -> 9.07 us
    ppermute x1, waiting for transfers between devices: 0.01 us -> 5.88 us  [on_device(): across = lax.ppermute(crossing_rows, 'row', links)]
    select_n x2 -> x0, other arithmetic: 2.1 us -> none  [the longest x1 1.12 us: on_device(): jnp.where(even, jnp.concatenate([crossing_rows, staying_rows], axis=0), j...]
    dynamic_update_slice x0 -> x6, local copies, waits for them, and re-layouts: none -> 2.02 us  [on_device(): extended = lax.dynamic_update_slice(extended, rows, (at, 0, 0))]
    unnamed x13 -> x12, local copies, waits for them, and re-layouts: 2.44 us -> 2.33 us
  transfers between devices with their start and end apart: 4 -> 4, of which waited for: 3 -> 3; matrix products, arithmetic and copies ran while one was open for 2% -> 3% of each run, Pallas kernels for 20% -> 13%
where the time goes in v13:
time: 105 us
  blocking collectives  30.3 us (29%)
  Pallas kernels  26.7 us (25%)
  waiting for transfers between devices  18.1 us (17%)
  starting transfers between devices  14.6 us (14%)
  local copies, waits for them, and re-layouts  9.07 us (9%)
  matrix products  3.46 us (3%)
  other arithmetic  2.39 us (2%)
    all_to_all x1, blocking collectives, on_device(): lax.all_to_all(sending, 'row', split_axis=0, concat_axis=0, tiled=True)  30.3 us
    pallas_call x1, Pallas kernels, attend_chunk(): pl.pallas_call(functools.partial(attend_kernel, scale=scale, first=first,...  13.9 us
    pallas_call x2, Pallas kernels, attend_last_half(): pl.pallas_call(kernel, grid_spec=grid_spec, out_shape=jax.ShapeDtypeStruc...  12.7 us
    all_to_all x1, waiting for transfers between devices, on_device(): lax.all_to_all(sending, 'row', split_axis=0, concat_axis=0, tiled=True)  8.73 us
    all_to_all x1, starting transfers between devices, on_device(): lax.all_to_all(lists_everywhere, 'row', split_axis=0, concat_axis=0, tile...  6.61 us
    ppermute x1, waiting for transfers between devices, on_device(): across = lax.ppermute(crossing_rows, 'row', links)  5.88 us
    all_to_all x1, starting transfers between devices, on_device(): lax.all_to_all(sending, 'row', split_axis=0, concat_axis=0, tiled=True)  4.51 us
    all_to_all x1, waiting for transfers between devices, on_device(): lax.all_to_all(lists_everywhere, 'row', split_axis=0, concat_axis=0, tile...  3.49 us
  transfers between devices with their start and end apart: 4, of which 3 were waited for; matrix products, arithmetic and copies ran while one was open for 3% of the time, Pallas kernels for 13%

profile of v13, /device:TPU:9, one launch (start us, length us, event | category | flops | bytes accessed | tf_op | source)
XLA Modules:
  0.0 105.0 jit_solution(5481350319300858598)
XLA Ops:
  0.0 0.0 copy-start
  0.0 0.8 broadcast_in_dim.57
  0.8 0.6 broadcast_in_dim.58
  1.4 6.6 %all-to-all-start = ((s32[16,1,36]{2,1,0:T(1,128)}), s32[16,1,36]{2,1,0:T(1,128)S(1)}, u32[]{:S(2)}, u32[]{:S(2)}) async-start(s32[16,1,36]{2,1,0:T(1,128)} %broadcast_in_dim.58), calls=%async_computation | async-start | bytes 16384 | tf_op jit(solution)/shard_map/all_to_all | solution.py:203
  8.0 1.1 %copy.59 = bf16[4,4,128,128]{3,2,1,0:T(8,128)(2,1)S(1)} copy(bf16[4,4,128,128]{3,2,0,1:T(8,128)(2,1)} %bitcast.57) | data formatting | bytes 1048576 | tf_op jit(solution)/shard_map/transpose | solution.py:191
  9.2 3.5 %all-to-all-done = s32[16,1,36]{2,1,0:T(1,128)S(1)} async-done(((s32[16,1,36]{2,1,0:T(1,128)}), s32[16,1,36]{2,1,0:T(1,128)S(1)}, u32[]{:S(2)}, u32[]{:S(2)}) %all-to-all-start) | async-done | bytes 2336 | tf_op jit(solution)/shard_map/all_to_all | solution.py:203
  12.6 0.1 fusion.29
  12.8 0.7 gather_fusion
  13.6 0.7 gather_fusion.1
  14.3 1.2 %broadcast_select_fusion = (bf16[16,256,128]{2,1,0:T(8,128)(2,1)}, bf16[16,256,128]{2,1,0:T(8,128)(2,1)S(1)}) fusion(bf16[16,256,128]{2,1,0:T(8,128)(2,1)S(1)} %gather_fusion.1, pred[16]{0:T(512)(128)(4,1)S(1)} %compare_and_fusion, bf16[16,256,128]{2,1,0:T(8,128)(2,1)S(1)} %gather_fusion), kind=kLoop, calls=%fused_computation.20 | loop fusion | flops 1048576 | bytes 4194320 | tf_op jit(solution)/shard_map/jit(_take)/select_n | solution.py:210
  15.5 30.3 %all_to_all.19.k_ref = bf16[16,256,128]{2,1,0:T(8,128)(2,1)} all-to-all(bf16[16,256,128]{2,1,0:T(8,128)(2,1)S(1)} %get-tuple-element.23), channel_id=1, replica_groups=mesh['pairs'=2,'row'=16] {'row'}, dimensions={0} | all-to-all | bytes 2097152 | tf_op jit(solution)/shard_map/all_to_all | solution.py:213
  45.9 0.0 copy-start.2
  45.9 4.5 %all-to-all-start.2 = ((bf16[16,256,128]{2,1,0:T(8,128)(2,1)}), bf16[16,256,128]{2,1,0:T(8,128)(2,1)S(1)}, u32[]{:S(2)}, u32[]{:S(2)}) async-start(bf16[16,256,128]{2,1,0:T(8,128)(2,1)} %get-tuple-element.11), calls=%async_computation.2 | async-start | bytes 2097152 | tf_op jit(solution)/shard_map/all_to_all | solution.py:213
  50.4 0.0 copy-start.3
  50.4 0.0 copy-done.2
  50.5 0.6 copy-done.3
  51.1 0.1 slice_reduce_fusion
  51.2 0.1 fusion.32
  51.3 0.0 copy-start.1
  51.3 1.2 %copy-done.1 = bf16[16,256,128]{2,1,0:T(8,128)(2,1)S(1)} copy-done((bf16[16,256,128]{2,1,0:T(8,128)(2,1)S(1)}, bf16[16,256,128]{2,1,0:T(8,128)(2,1)}, u32[]{:S(2)}) %copy-start.1) | copy-done | bytes 1048600
  52.6 13.9 %shard_map.55 = (f32[4,1,512]{2,1,0:T(1,128)S(1)}, f32[4,1,512]{2,1,0:T(1,128)S(1)}, f32[4,512,128]{2,1,0:T(8,128)S(1)}) custom-call(s32[4,9]{1,0:T(4,128)S(1)} %get-tuple-element.21.owner_ref, s32[4]{0:T(128)S(1)} %get-tuple-element.20.count_ref, bf16[4,512,128]{2,1,0:T(8,128)(2,1)S(1)} %bitcast.44, bf16[16,256,128]{2,1,0:T(8,128)(2,1)S(1)} %copy-done.1), custom_call_target="tpu_custom_call" | custom-call | tf_op jit(solution)/shard_map/pallas_call | solution.py:140
  66.5 8.7 %all-to-all-done.2.refs_1_ = bf16[16,256,128]{2,1,0:T(8,128)(2,1)S(1)} async-done(((bf16[16,256,128]{2,1,0:T(8,128)(2,1)}), bf16[16,256,128]{2,1,0:T(8,128)(2,1)S(1)}, u32[]{:S(2)}, u32[]{:S(2)}) %all-to-all-start.2) | async-done | bytes 1048608 | tf_op jit(solution)/shard_map/all_to_all | solution.py:213
  75.2 6.4 %shard_map.57 = bf16[4,256,128]{2,1,0:T(8,128)(2,1)S(1)} custom-call(s32[4,9]{1,0:T(4,128)S(1)} %get-tuple-element.21.owner_ref, s32[4]{0:T(128)S(1)} %get-tuple-element.20.count_ref, s32[1]{0:T(128)S(6)} %sub.17.half_ref, bf16[4,512,128]{2,1,0:T(8,128)(2,1)S(1)} %bitcast.45, bf16[16,256,128]{2,1,0:T(8,128)(2,1)S(1)} %all-to-all-done.2.refs_1_, ...), custom_call_target="tpu_custom_call" | custom-call | tf_op jit(solution)/shard_map/pallas_call | solution.py:172
  81.7 6.4 %shard_map.56 = bf16[4,256,128]{2,1,0:T(8,128)(2,1)S(1)} custom-call(s32[4,9]{1,0:T(4,128)S(1)} %get-tuple-element.21.owner_ref, s32[4]{0:T(128)S(1)} %get-tuple-element.20.count_ref, s32[1]{0:T(128)} %bitcast.half_ref, bf16[4,512,128]{2,1,0:T(8,128)(2,1)S(1)} %bitcast.46, bf16[16,256,128]{2,1,0:T(8,128)(2,1)S(1)} %all-to-all-done.2.refs_1_, ...), custom_call_target="tpu_custom_call" | custom-call | tf_op jit(solution)/shard_map/pallas_call | solution.py:172
  88.1 3.4 %collective-permute-start = (bf16[2,512,128]{2,1,0:T(8,128)(2,1)S(1)}, bf16[2,512,128]{2,1,0:T(8,128)(2,1)S(1)}, u32[]{:S(2)}, u32[]{:S(2)}) collective-permute-start(bf16[2,512,128]{2,1,0:T(8,128)(2,1)S(1)} %bitcast.55), channel_id=1, source_target_pairs={{1,2},{3,4},{5,6},{7,8},{9,10},{11,12},{13,14},{2,1},{4,3},{6,5},{... | collective-permute-start | bytes 786440 | tf_op jit(solution)/shard_map/ppermute | solution.py:232
  91.5 0.1 collective-permute-start.1
  91.6 0.1 broadcast.82
  91.7 0.5 copy_dynamic-update-slice_fusion.3
  92.2 0.5 copy_dynamic-update-slice_fusion.2
  92.6 5.9 %collective-permute-done = bf16[2,512,128]{2,1,0:T(8,128)(2,1)S(1)} collective-permute-done((bf16[2,512,128]{2,1,0:T(8,128)(2,1)S(1)}, bf16[2,512,128]{2,1,0:T(8,128)(2,1)S(1)}, u32[]{:S(2)}, u32[]{:S(2)}) %collective-permute-start) | collective-permute-done | bytes 262176 | tf_op jit(solution)/shard_map/ppermute | solution.py:232
  98.5 0.4 copy_dynamic-update-slice_fusion.1
  99.0 0.0 collective-permute-done.1
  99.0 0.5 copy_dynamic-update-slice_fusion
  99.4 0.1 pad
  99.5 0.0 copy-start.5
  99.5 0.1 copy.67
  99.7 0.0 copy-done
  99.7 0.5 copy-done.5
  100.2 0.0 copy-start.4
  100.2 2.1 %fusion.5 = bf16[6,1,8,65,128]{4,2,3,0,1:T(8,128)(2,1)S(1)} fusion(bf16[3,3,128,128]{3,2,1,0:T(8,128)(2,1)S(1)} %copy-done, bf16[8,1,7,2,128]{4,2,3,0,1:T(8,128)(2,1)S(1)} %slice.22, bf16[8,1,8,65,128]{4,2,3,0,1:T(8,128)(2,1)S(1)} %copy.67, pred[6]{0:T(512)(128)(4,1)S(1)} %or_and_fusion, pred[8,65]{0,1:T(8,128)(4,1)S(1)} %copy-done.5), kind=kOutput, calls=%fused_computation.11 | convolution fusion | flops 925415424 | bytes 2187790 | tf_op jit(solution)/shard_map/conv_general_dilated | solution.py:40
  102.3 0.0 copy-done.4
  102.3 1.4 %fusion.16 = f32[4,8,65,128]{3,1,2,0:T(8,128)S(1)} fusion(bf16[3,3,128,128]{3,2,1,0:T(8,128)(2,1)S(1)} %copy-done.4, bf16[6,1,7,1,128]{4,2,3,0,1:T(8,128)(2,1)S(1)} %get-tuple-element.17, bf16[6,1,7,1,128]{4,2,3,0,1:T(8,128)(2,1)S(1)} %get-tuple-element.16, bf16[6,1,8,65,128]{4,2,3,0,1:T(8,128)(2,1)S(1)} %fusion.5), kind=kOutput, calls=%fused_computation.24 | convolution fusion | flops 617533440 | bytes 2180096 | tf_op jit(solution)/shard_map/conv_general_dilated | solution.py:40
  103.7 0.3 copy.68
  104.0 0.1 slice.25
  104.1 0.9 fusion.13
  (10 shorter events, 0.2 us)
Async XLA Ops:
  0.0 99.7 %copy-start = (bf16[3,3,128,128]{3,2,1,0:T(8,128)(2,1)S(1)}, bf16[3,3,128,128]{3,2,1,0:T(8,128)(2,1)}, u32[]{:S(2)}) copy-start(bf16[3,3,128,128]{3,2,1,0:T(8,128)(2,1)} %param.10) | copy-start | bytes 884740
  1.4 11.2 %all-to-all-start = ((s32[16,1,36]{2,1,0:T(1,128)}), s32[16,1,36]{2,1,0:T(1,128)S(1)}, u32[]{:S(2)}, u32[]{:S(2)}) async-start(s32[16,1,36]{2,1,0:T(1,128)} %broadcast_in_dim.58), calls=%async_computation | async-start | bytes 16384 | tf_op jit(solution)/shard_map/all_to_all | solution.py:203
  45.9 4.5 %copy-start.2 = (bf16[4,512,128]{2,1,0:T(8,128)(2,1)S(1)}, bf16[4,512,128]{2,1,0:T(8,128)(2,1)}, u32[]{:S(2)}) copy-start(bf16[4,512,128]{2,1,0:T(8,128)(2,1)} %param.7) | copy-start | bytes 1572868
  45.9 29.4 %all-to-all-start.2 = ((bf16[16,256,128]{2,1,0:T(8,128)(2,1)}), bf16[16,256,128]{2,1,0:T(8,128)(2,1)S(1)}, u32[]{:S(2)}, u32[]{:S(2)}) async-start(bf16[16,256,128]{2,1,0:T(8,128)(2,1)} %get-tuple-element.11), calls=%async_computation.2 | async-start | bytes 2097152 | tf_op jit(solution)/shard_map/all_to_all | solution.py:213
  50.4 0.7 copy-start.3
  51.3 1.2 %copy-start.1 = (bf16[16,256,128]{2,1,0:T(8,128)(2,1)S(1)}, bf16[16,256,128]{2,1,0:T(8,128)(2,1)}, u32[]{:S(2)}) copy-start(bf16[16,256,128]{2,1,0:T(8,128)(2,1)} %all_to_all.19.k_ref) | copy-start | bytes 3145732
  88.1 10.5 %collective-permute-start = (bf16[2,512,128]{2,1,0:T(8,128)(2,1)S(1)}, bf16[2,512,128]{2,1,0:T(8,128)(2,1)S(1)}, u32[]{:S(2)}, u32[]{:S(2)}) collective-permute-start(bf16[2,512,128]{2,1,0:T(8,128)(2,1)S(1)} %bitcast.55), channel_id=1, source_target_pairs={{1,2},{3,4},{5,6},{7,8},{9,10},{11,12},{13,14},{2,1},{4,3},{6,5},{... | collective-permute-start | bytes 786440 | tf_op jit(solution)/shard_map/ppermute | solution.py:232
  91.5 7.5 %collective-permute-start.1 = (bf16[2,512,128]{2,1,0:T(8,128)(2,1)S(1)}, bf16[2,512,128]{2,1,0:T(8,128)(2,1)S(1)}, u32[]{:S(2)}, u32[]{:S(2)}) collective-permute-start(bf16[2,512,128]{2,1,0:T(8,128)(2,1)S(1)} %bitcast.53), channel_id=1, source_target_pairs={{0,1},{1,0},{2,3},{3,2},{4,5},{5,4},{6,7},{7,6},{8,9},{9,8},{10,11... | collective-permute-start | bytes 786440 | tf_op jit(solution)/shard_map/ppermute | solution.py:233
  99.5 0.7 copy-start.5
  100.2 2.1 %copy-start.4 = (bf16[3,3,128,128]{3,2,1,0:T(8,128)(2,1)S(1)}, bf16[3,3,128,128]{3,2,1,0:T(8,128)(2,1)}, u32[]{:S(2)}) copy-start(bf16[3,3,128,128]{3,2,1,0:T(8,128)(2,1)} %param.11) | copy-start | bytes 884740

commit v14 on v12

--- a/solution.py
+++ b/solution.py
@@ -53,7 +53,9 @@
 
 
 def attend_kernel(owner_ref, count_ref, q_ref, k_ref, *refs, scale, first, last):
-    if first:
+    if first and last:
+        o_ref, kall_ref = refs
+    elif first:
         m_out, t_out, a_out, kall_ref = refs
     elif last:
         m_in, t_in, a_in, o_ref, kall_ref = refs
@@ -146,6 +148,7 @@
 
 
 def attend_last_half(state, queries, chunk, slot_owner, counts, half, scale):
+    first = len(state) == 0
     tiles, tile_size, channels = queries.shape
     owners, chunk_len, _ = chunk.shape
     slots = slot_owner.shape[1]
@@ -158,16 +161,14 @@
         in_specs=[
             acc_spec,
             pl.BlockSpec((owners, chunk_len, channels), lambda t, o, c, h: (0, 0, 0)),
-            row_spec,
-            row_spec,
-            acc_spec,
-        ],
+        ]
+        + ([] if first else [row_spec, row_spec, acc_spec]),
         out_specs=pl.BlockSpec((1, part, channels), lambda t, o, c, h: (t, 0, 0)),
         scratch_shapes=[pltpu.VMEM((slots * chunk_len, channels), jnp.bfloat16)],
     )
 
     def kernel(owner_ref, count_ref, half_ref, *refs):
-        attend_kernel(owner_ref, count_ref, *refs, scale=scale, first=False, last=True)
+        attend_kernel(owner_ref, count_ref, *refs, scale=scale, first=first, last=True)
 
     return pl.pallas_call(
         kernel,
@@ -203,7 +204,7 @@
     lists_of = lax.all_to_all(lists_everywhere, "row", split_axis=0, concat_axis=0, tiled=True)
     mine = (lists_of >= 0) & (lists_of // per_device == me)
     asked = jnp.max(jnp.where(mine, lists_of % per_device, 0), axis=1)
-    edges = [0, tile_size // 2, tile_size]
+    edges = [0, tile_size]
     state = ()
     previous = None
     for index, (start, stop) in enumerate(zip(edges[:-1], edges[1:])):
@@ -218,7 +219,8 @@
     crossing = jnp.where(even, 0, 1).astype(jnp.int32).reshape(1)
     staying = (1 - crossing).astype(jnp.int32)
     crossing_tiles = attend_last_half(state, query_tiles, previous, slot_owner, counts, crossing, scale)
-    staying_tiles = attend_last_half(state, query_tiles, previous, slot_owner, counts, staying, scale)
+    crossing_tiles, later_queries = lax.optimization_barrier((crossing_tiles, query_tiles))
+    staying_tiles = attend_last_half(state, later_queries, previous, slot_owner, counts, staying, scale)
 
     def to_rows(tiles):
         return tiles.reshape(per_device, -1, tile_cols, channels).transpose(1, 0, 2, 3).reshape(

time: 102 us -> 106 us (1.039)
  waiting for transfers between devices: 13.2 us -> 55.4 us
  blocking collectives: 30.3 us -> 0 us
  Pallas kernels: 26.7 us -> 19.5 us
  local copies, waits for them, and re-layouts: 7.93 us -> 5.34 us
  starting transfers between devices: 14.6 us -> 17.1 us
  other arithmetic: 4.62 us -> 3.02 us
    all_to_all x1, waiting for transfers between devices: 9.35 us -> 45.7 us  [on_device(): lax.all_to_all(sending, 'row', split_axis=0, concat_axis=0, tiled=True)]
    all_to_all x1 -> x0, blocking collectives: 30.3 us -> none  [on_device(): lax.all_to_all(sending, 'row', split_axis=0, concat_axis=0, tiled=True)]
    pallas_call x1 -> x0, Pallas kernels: 13.9 us -> none  [attend_chunk(): pl.pallas_call(functools.partial(attend_kernel, scale=scale, first=first,...]
    pallas_call x2, Pallas kernels: 12.8 us -> 19.5 us  [attend_last_half(): pl.pallas_call(kernel, grid_spec=grid_spec, out_shape=jax.ShapeDtypeStruc...]
    ppermute x1, waiting for transfers between devices: 0.01 us -> 6.16 us  [on_device(): across = lax.ppermute(crossing_rows, 'row', links)]
    unnamed x13 -> x11, local copies, waits for them, and re-layouts: 2.44 us -> 1.13 us
    ppermute x1, starting transfers between devices: 3.39 us -> 4.68 us  [on_device(): across = lax.ppermute(crossing_rows, 'row', links)]
  transfers between devices with their start and end apart: 4 -> 4, of which waited for: 3 -> 3; matrix products, arithmetic and copies ran while one was open for 2% -> 1% of each run, Pallas kernels for 20% -> 0%
where the time goes in v14:
time: 106 us; the launch traced here: 104 us
  waiting for transfers between devices  55.4 us (52%)
  Pallas kernels  19.5 us (18%)
  starting transfers between devices  17.1 us (16%)
  local copies, waits for them, and re-layouts  5.34 us (5%)
  matrix products  3.51 us (3%)
  other arithmetic  3.02 us (3%)
    all_to_all x1, waiting for transfers between devices, on_device(): lax.all_to_all(sending, 'row', split_axis=0, concat_axis=0, tiled=True)  45.7 us
    pallas_call x2, Pallas kernels, attend_last_half(): pl.pallas_call(kernel, grid_spec=grid_spec, out_shape=jax.ShapeDtypeStruc...  19.5 us
    all_to_all x1, starting transfers between devices, on_device(): lax.all_to_all(lists_everywhere, 'row', split_axis=0, concat_axis=0, tile...  6.61 us
    ppermute x1, waiting for transfers between devices, on_device(): across = lax.ppermute(crossing_rows, 'row', links)  6.16 us
    all_to_all x1, starting transfers between devices, on_device(): lax.all_to_all(sending, 'row', split_axis=0, concat_axis=0, tiled=True)  5.47 us
    ppermute x1, starting transfers between devices, on_device(): across = lax.ppermute(crossing_rows, 'row', links)  4.68 us
    all_to_all x1, waiting for transfers between devices, on_device(): lax.all_to_all(lists_everywhere, 'row', split_axis=0, concat_axis=0, tile...  3.54 us
    conv_general_dilated x2, matrix products, native_conv(): lax.conv_general_dilated(rows[None], weights, window_strides=(1, 1), padd...  3.51 us
  transfers between devices with their start and end apart: 4, of which 3 were waited for; matrix products, arithmetic and copies ran while one was open for 1% of the time, Pallas kernels for 0%

profile of v14, /device:TPU:9, one launch (start us, length us, event | category | flops | bytes accessed | tf_op | source)
XLA Modules:
  0.0 104.1 jit_solution(3673115601353836115)
XLA Ops:
  0.0 0.0 copy-start
  0.0 0.8 broadcast_in_dim.48
  0.8 0.6 broadcast_in_dim.49
  1.4 6.6 %all-to-all-start = ((s32[16,1,36]{2,1,0:T(1,128)}), s32[16,1,36]{2,1,0:T(1,128)S(1)}, u32[]{:S(2)}, u32[]{:S(2)}) async-start(s32[16,1,36]{2,1,0:T(1,128)} %broadcast_in_dim.49), calls=%async_computation | async-start | bytes 16384 | tf_op jit(solution)/shard_map/all_to_all | solution.py:204
  8.0 1.1 %copy.47 = bf16[4,4,128,128]{3,2,1,0:T(8,128)(2,1)S(1)} copy(bf16[4,4,128,128]{3,2,0,1:T(8,128)(2,1)} %bitcast.54) | data formatting | bytes 1048576 | tf_op jit(solution)/shard_map/transpose | solution.py:192
  9.1 3.5 %all-to-all-done = s32[16,1,36]{2,1,0:T(1,128)S(1)} async-done(((s32[16,1,36]{2,1,0:T(1,128)}), s32[16,1,36]{2,1,0:T(1,128)S(1)}, u32[]{:S(2)}, u32[]{:S(2)}) %all-to-all-start) | async-done | bytes 2336 | tf_op jit(solution)/shard_map/all_to_all | solution.py:204
  12.6 0.1 fusion.29
  12.8 1.0 gather_fusion
  13.8 1.6 %broadcast_select_fusion = bf16[16,512,128]{2,1,0:T(8,128)(2,1)} fusion(bf16[16,512,128]{2,1,0:T(8,128)(2,1)S(1)} %gather_fusion, pred[16]{0:T(512)(128)(4,1)S(1)} %compare_and_fusion), kind=kLoop, calls=%fused_computation.3 | loop fusion | flops 1048576 | bytes 4194320 | tf_op jit(solution)/shard_map/jit(_take)/select_n | solution.py:211
  15.4 0.0 copy-start.1
  15.4 0.0 copy-start.2
  15.4 5.5 %all-to-all-start.1 = ((bf16[16,512,128]{2,1,0:T(8,128)(2,1)}), bf16[16,512,128]{2,1,0:T(8,128)(2,1)S(1)}, u32[]{:S(2)}, u32[]{:S(2)}) async-start(bf16[16,512,128]{2,1,0:T(8,128)(2,1)} %broadcast_select_fusion), calls=%async_computation.1 | async-start | bytes 4194304 | tf_op jit(solution)/shard_map/all_to_all | solution.py:214
  20.8 0.0 copy-done.1
  20.9 0.0 copy-done.2
  20.9 0.1 slice_reduce_fusion
  21.0 0.1 fusion.32
  21.1 45.7 %all-to-all-done.1.refs_1_ = bf16[16,512,128]{2,1,0:T(8,128)(2,1)S(1)} async-done(((bf16[16,512,128]{2,1,0:T(8,128)(2,1)}), bf16[16,512,128]{2,1,0:T(8,128)(2,1)S(1)}, u32[]{:S(2)}, u32[]{:S(2)}) %all-to-all-start.1) | async-done | bytes 2097184 | tf_op jit(solution)/shard_map/all_to_all | solution.py:214
  66.9 9.8 %shard_map.55 = bf16[4,256,128]{2,1,0:T(8,128)(2,1)S(1)} custom-call(s32[4,9]{1,0:T(4,128)S(1)} %get-tuple-element.14.owner_ref, s32[4]{0:T(128)S(1)} %get-tuple-element.13.count_ref, s32[1]{0:T(128)} %bitcast.half_ref, bf16[4,512,128]{2,1,0:T(8,128)(2,1)S(1)} %bitcast.42, bf16[16,512,128]{2,1,0:T(8,128)(2,1)S(1)} %all-to-all-done.1.refs_1_), custom_call_target="tpu_custom_call" | custom-call | tf_op jit(solution)/shard_map/pallas_call | solution.py:173
  76.6 9.8 %shard_map.56 = bf16[4,256,128]{2,1,0:T(8,128)(2,1)S(1)} custom-call(s32[4,9]{1,0:T(4,128)S(1)} %get-tuple-element.14.owner_ref, s32[4]{0:T(128)S(1)} %get-tuple-element.13.count_ref, s32[1]{0:T(128)S(6)} %sub.17.half_ref, bf16[4,512,128]{2,1,0:T(8,128)(2,1)S(1)} %bitcast.43, bf16[16,512,128]{2,1,0:T(8,128)(2,1)S(1)} %all-to-all-done.1.refs_1_), custom_call_target="tpu_custom_call" | custom-call | tf_op jit(solution)/shard_map/pallas_call | solution.py:173
  86.5 0.3 collective-permute-start.1
  86.8 4.7 %collective-permute-start = (bf16[2,512,128]{2,1,0:T(8,128)(2,1)S(1)}, bf16[2,512,128]{2,1,0:T(8,128)(2,1)S(1)}, u32[]{:S(2)}, u32[]{:S(2)}) collective-permute-start(bf16[2,512,128]{2,1,0:T(8,128)(2,1)S(1)} %bitcast.50), channel_id=1, source_target_pairs={{1,2},{3,4},{5,6},{7,8},{9,10},{11,12},{13,14},{2,1},{4,3},{6,5},{... | collective-permute-start | bytes 786440 | tf_op jit(solution)/shard_map/ppermute | solution.py:234
  91.5 0.1 maximum_select_fusion
  91.6 0.0 collective-permute-done.1
  91.6 6.2 %collective-permute-done = bf16[2,512,128]{2,1,0:T(8,128)(2,1)S(1)} collective-permute-done((bf16[2,512,128]{2,1,0:T(8,128)(2,1)S(1)}, bf16[2,512,128]{2,1,0:T(8,128)(2,1)S(1)}, u32[]{:S(2)}, u32[]{:S(2)}) %collective-permute-start) | collective-permute-done | bytes 262176 | tf_op jit(solution)/shard_map/ppermute | solution.py:234
  97.8 0.1 maximum_bitcast_fusion
  97.9 0.7 copy.56
  98.6 0.0 copy-start.4
  98.6 0.1 pad.clone
  98.7 0.1 copy.52
  98.9 0.0 copy-done
  98.9 0.4 copy-done.4
  99.3 0.0 copy-start.3
  99.3 2.1 %fusion.5 = bf16[6,1,8,65,128]{4,2,3,0,1:T(8,128)(2,1)S(1)} fusion(bf16[3,3,128,128]{3,2,1,0:T(8,128)(2,1)S(1)} %copy-done, bf16[8,1,7,2,128]{4,2,3,0,1:T(8,128)(2,1)S(1)} %slice.10, bf16[8,1,8,65,128]{4,2,3,0,1:T(8,128)(2,1)S(1)} %copy.52, pred[6]{0:T(512)(128)(4,1)S(1)} %or_and_fusion, pred[8,65]{0,1:T(8,128)(4,1)S(1)} %copy-done.4), kind=kOutput, calls=%fused_computation.11 | convolution fusion | flops 925415424 | bytes 2187790 | tf_op jit(solution)/shard_map/conv_general_dilated | solution.py:40
  101.4 0.0 copy-done.3
  101.4 1.5 %fusion.16 = f32[4,8,65,128]{3,1,2,0:T(8,128)S(1)} fusion(bf16[3,3,128,128]{3,2,1,0:T(8,128)(2,1)S(1)} %copy-done.3, bf16[6,1,7,1,128]{4,2,3,0,1:T(8,128)(2,1)S(1)} %get-tuple-element.10, bf16[6,1,7,1,128]{4,2,3,0,1:T(8,128)(2,1)S(1)} %get-tuple-element.9, bf16[6,1,8,65,128]{4,2,3,0,1:T(8,128)(2,1)S(1)} %fusion.5), kind=kOutput, calls=%fused_computation.23 | convolution fusion | flops 617533440 | bytes 2180096 | tf_op jit(solution)/shard_map/conv_general_dilated | solution.py:40
  102.9 0.3 copy.53
  103.1 0.1 slice.13
  103.2 0.9 fusion.13
  (10 shorter events, 0.2 us)
Async XLA Ops:
  0.0 98.9 %copy-start = (bf16[3,3,128,128]{3,2,1,0:T(8,128)(2,1)S(1)}, bf16[3,3,128,128]{3,2,1,0:T(8,128)(2,1)}, u32[]{:S(2)}) copy-start(bf16[3,3,128,128]{3,2,1,0:T(8,128)(2,1)} %param.8) | copy-start | bytes 884740
  1.4 11.2 %all-to-all-start = ((s32[16,1,36]{2,1,0:T(1,128)}), s32[16,1,36]{2,1,0:T(1,128)S(1)}, u32[]{:S(2)}, u32[]{:S(2)}) async-start(s32[16,1,36]{2,1,0:T(1,128)} %broadcast_in_dim.49), calls=%async_computation | async-start | bytes 16384 | tf_op jit(solution)/shard_map/all_to_all | solution.py:204
  15.4 5.5 %copy-start.1 = (bf16[4,512,128]{2,1,0:T(8,128)(2,1)S(1)}, bf16[4,512,128]{2,1,0:T(8,128)(2,1)}, u32[]{:S(2)}) copy-start(bf16[4,512,128]{2,1,0:T(8,128)(2,1)} %param.5) | copy-start | bytes 1572868
  15.4 5.5 %copy-start.2 = (s32[4,9]{1,0:T(4,128)S(1)}, s32[4,9]{1,0:T(4,128)}, u32[]{:S(2)}) copy-start(s32[4,9]{1,0:T(4,128)} %param.7) | copy-start | bytes 436
  15.4 51.5 %all-to-all-start.1 = ((bf16[16,512,128]{2,1,0:T(8,128)(2,1)}), bf16[16,512,128]{2,1,0:T(8,128)(2,1)S(1)}, u32[]{:S(2)}, u32[]{:S(2)}) async-start(bf16[16,512,128]{2,1,0:T(8,128)(2,1)} %broadcast_select_fusion), calls=%async_computation.1 | async-start | bytes 4194304 | tf_op jit(solution)/shard_map/all_to_all | solution.py:214
  86.5 5.1 %collective-permute-start.1 = (bf16[2,512,128]{2,1,0:T(8,128)(2,1)S(1)}, bf16[2,512,128]{2,1,0:T(8,128)(2,1)S(1)}, u32[]{:S(2)}, u32[]{:S(2)}) collective-permute-start(bf16[2,512,128]{2,1,0:T(8,128)(2,1)S(1)} %bitcast.52), channel_id=1, source_target_pairs={{0,1},{1,0},{2,3},{3,2},{4,5},{5,4},{6,7},{7,6},{8,9},{9,8},{10,11... | collective-permute-start | bytes 786440 | tf_op jit(solution)/shard_map/ppermute | solution.py:235
  86.8 11.0 %collective-permute-start = (bf16[2,512,128]{2,1,0:T(8,128)(2,1)S(1)}, bf16[2,512,128]{2,1,0:T(8,128)(2,1)S(1)}, u32[]{:S(2)}, u32[]{:S(2)}) collective-permute-start(bf16[2,512,128]{2,1,0:T(8,128)(2,1)S(1)} %bitcast.50), channel_id=1, source_target_pairs={{1,2},{3,4},{5,6},{7,8},{9,10},{11,12},{13,14},{2,1},{4,3},{6,5},{... | collective-permute-start | bytes 786440 | tf_op jit(solution)/shard_map/ppermute | solution.py:234
  98.6 0.7 copy-start.4
  99.3 2.1 %copy-start.3 = (bf16[3,3,128,128]{3,2,1,0:T(8,128)(2,1)S(1)}, bf16[3,3,128,128]{3,2,1,0:T(8,128)(2,1)}, u32[]{:S(2)}) copy-start(bf16[3,3,128,128]{3,2,1,0:T(8,128)(2,1)} %param.9) | copy-start | bytes 884740

commit v15 on v12

--- a/solution.py
+++ b/solution.py
@@ -157,7 +157,7 @@
         grid=(tiles,),
         in_specs=[
             acc_spec,
-            pl.BlockSpec((owners, chunk_len, channels), lambda t, o, c, h: (0, 0, 0)),
+            pl.BlockSpec(memory_space=pltpu.MemorySpace.VMEM),
             row_spec,
             row_spec,
             acc_spec,

time: 102 us -> 102 us (level)
  no operation moved by 1% of the time
where the time goes in v15:
time: 102 us; the launch traced here: 101 us
  blocking collectives  30.3 us (30%)
  Pallas kernels  26.7 us (26%)
  starting transfers between devices  14.6 us (14%)
  waiting for transfers between devices  13.2 us (13%)
  local copies, waits for them, and re-layouts  7.93 us (8%)
  other arithmetic  4.62 us (5%)
  matrix products  3.47 us (3%)
    all_to_all x1, blocking collectives, on_device(): lax.all_to_all(sending, 'row', split_axis=0, concat_axis=0, tiled=True)  30.3 us
    pallas_call x1, Pallas kernels, attend_chunk(): pl.pallas_call(functools.partial(attend_kernel, scale=scale, first=first,...  13.9 us
    pallas_call x2, Pallas kernels, attend_last_half(): pl.pallas_call(kernel, grid_spec=grid_spec, out_shape=jax.ShapeDtypeStruc...  12.8 us
    all_to_all x1, waiting for transfers between devices, on_device(): lax.all_to_all(sending, 'row', split_axis=0, concat_axis=0, tiled=True)  9.35 us
    all_to_all x1, starting transfers between devices, on_device(): lax.all_to_all(lists_everywhere, 'row', split_axis=0, concat_axis=0, tile...  6.61 us
    all_to_all x1, starting transfers between devices, on_device(): lax.all_to_all(sending, 'row', split_axis=0, concat_axis=0, tiled=True)  4.51 us
    all_to_all x1, waiting for transfers between devices, on_device(): lax.all_to_all(lists_everywhere, 'row', split_axis=0, concat_axis=0, tile...  3.49 us
    conv_general_dilated x2, matrix products, native_conv(): lax.conv_general_dilated(rows[None], weights, window_strides=(1, 1), padd...  3.47 us
  transfers between devices with their start and end apart: 4, of which 3 were waited for; matrix products, arithmetic and copies ran while one was open for 2% of the time, Pallas kernels for 20%

profile of v15, /device:TPU:9, one launch (start us, length us, event | category | flops | bytes accessed | tf_op | source)
XLA Modules:
  0.0 101.1 jit_solution(2148444722267207472)
XLA Ops:
  0.0 0.0 copy-start
  0.0 0.8 broadcast_in_dim.47
  0.8 0.6 broadcast_in_dim.48
  1.4 6.6 %all-to-all-start = ((s32[16,1,36]{2,1,0:T(1,128)}), s32[16,1,36]{2,1,0:T(1,128)S(1)}, u32[]{:S(2)}, u32[]{:S(2)}) async-start(s32[16,1,36]{2,1,0:T(1,128)} %broadcast_in_dim.48), calls=%async_computation | async-start | bytes 16384 | tf_op jit(solution)/shard_map/all_to_all | solution.py:203
  8.0 1.1 %copy.47 = bf16[4,4,128,128]{3,2,1,0:T(8,128)(2,1)S(1)} copy(bf16[4,4,128,128]{3,2,0,1:T(8,128)(2,1)} %bitcast.49) | data formatting | bytes 1048576 | tf_op jit(solution)/shard_map/transpose | solution.py:191
  9.2 3.5 %all-to-all-done = s32[16,1,36]{2,1,0:T(1,128)S(1)} async-done(((s32[16,1,36]{2,1,0:T(1,128)}), s32[16,1,36]{2,1,0:T(1,128)S(1)}, u32[]{:S(2)}, u32[]{:S(2)}) %all-to-all-start) | async-done | bytes 2336 | tf_op jit(solution)/shard_map/all_to_all | solution.py:203
  12.6 0.1 fusion.29
  12.8 0.7 gather_fusion.1
  13.6 0.7 gather_fusion
  14.3 1.2 %broadcast_select_fusion = (bf16[16,256,128]{2,1,0:T(8,128)(2,1)}, bf16[16,256,128]{2,1,0:T(8,128)(2,1)S(1)}) fusion(bf16[16,256,128]{2,1,0:T(8,128)(2,1)S(1)} %gather_fusion.1, pred[16]{0:T(512)(128)(4,1)S(1)} %compare_and_fusion, bf16[16,256,128]{2,1,0:T(8,128)(2,1)S(1)} %gather_fusion), kind=kLoop, calls=%fused_computation.21 | loop fusion | flops 1048576 | bytes 4194320 | tf_op jit(solution)/shard_map/jit(_take)/select_n | solution.py:210
  15.5 30.3 %all_to_all.19.k_ref = bf16[16,256,128]{2,1,0:T(8,128)(2,1)} all-to-all(bf16[16,256,128]{2,1,0:T(8,128)(2,1)S(1)} %get-tuple-element.25), channel_id=1, replica_groups=mesh['pairs'=2,'row'=16] {'row'}, dimensions={0} | all-to-all | bytes 2097152 | tf_op jit(solution)/shard_map/all_to_all | solution.py:213
  45.9 0.0 copy-start.2
  45.9 0.0 copy-start.3
  45.9 4.5 %all-to-all-start.2 = ((bf16[16,256,128]{2,1,0:T(8,128)(2,1)}), bf16[16,256,128]{2,1,0:T(8,128)(2,1)S(1)}, u32[]{:S(2)}, u32[]{:S(2)}) async-start(bf16[16,256,128]{2,1,0:T(8,128)(2,1)} %get-tuple-element.11), calls=%async_computation.2 | async-start | bytes 2097152 | tf_op jit(solution)/shard_map/all_to_all | solution.py:213
  50.4 0.0 copy-done.2
  50.4 0.0 copy-done.3
  50.5 0.1 slice_reduce_fusion
  50.6 0.1 fusion.32
  50.7 0.0 copy-start.1
  50.7 1.2 %copy-done.1 = bf16[16,256,128]{2,1,0:T(8,128)(2,1)S(1)} copy-done((bf16[16,256,128]{2,1,0:T(8,128)(2,1)S(1)}, bf16[16,256,128]{2,1,0:T(8,128)(2,1)}, u32[]{:S(2)}) %copy-start.1) | copy-done | bytes 1048600
  51.9 13.9 %shard_map.55 = (f32[4,1,512]{2,1,0:T(1,128)S(1)}, f32[4,1,512]{2,1,0:T(1,128)S(1)}, f32[4,512,128]{2,1,0:T(8,128)S(1)}) custom-call(s32[4,9]{1,0:T(4,128)S(1)} %get-tuple-element.23.owner_ref, s32[4]{0:T(128)S(1)} %get-tuple-element.22.count_ref, bf16[4,512,128]{2,1,0:T(8,128)(2,1)S(1)} %bitcast.38, bf16[16,256,128]{2,1,0:T(8,128)(2,1)S(1)} %copy-done.1), custom_call_target="tpu_custom_call" | custom-call | tf_op jit(solution)/shard_map/pallas_call | solution.py:140
  65.9 9.4 %all-to-all-done.2.refs_1_ = bf16[16,256,128]{2,1,0:T(8,128)(2,1)S(1)} async-done(((bf16[16,256,128]{2,1,0:T(8,128)(2,1)}), bf16[16,256,128]{2,1,0:T(8,128)(2,1)S(1)}, u32[]{:S(2)}, u32[]{:S(2)}) %all-to-all-start.2) | async-done | bytes 1048608 | tf_op jit(solution)/shard_map/all_to_all | solution.py:213
  75.2 6.4 %shard_map.56 = bf16[4,256,128]{2,1,0:T(8,128)(2,1)S(1)} custom-call(s32[4,9]{1,0:T(4,128)S(1)} %get-tuple-element.23.owner_ref, s32[4]{0:T(128)S(1)} %get-tuple-element.22.count_ref, s32[1]{0:T(128)} %bitcast.half_ref, bf16[4,512,128]{2,1,0:T(8,128)(2,1)S(1)} %bitcast.39, bf16[16,256,128]{2,1,0:T(8,128)(2,1)S(1)} %all-to-all-done.2.refs_1_, ...), custom_call_target="tpu_custom_call" | custom-call | tf_op jit(solution)/shard_map/pallas_call | solution.py:172
  81.6 0.7 copy.48
  82.3 3.4 %collective-permute-start = (bf16[2,512,128]{2,1,0:T(8,128)(2,1)}, bf16[2,512,128]{2,1,0:T(8,128)(2,1)}, u32[]{:S(2)}, u32[]{:S(2)}) collective-permute-start(bf16[2,512,128]{2,1,0:T(8,128)(2,1)} %bitcast.11), channel_id=1, source_target_pairs={{1,2},{3,4},{5,6},{7,8},{9,10},{11,12},{13,14},{2,1},{4,3},{6,5},{... | collective-permute-start | bytes 786440 | tf_op jit(solution)/shard_map/ppermute | solution.py:232
  85.7 6.4 %shard_map.57 = bf16[4,256,128]{2,1,0:T(8,128)(2,1)S(1)} custom-call(s32[4,9]{1,0:T(4,128)S(1)} %get-tuple-element.23.owner_ref, s32[4]{0:T(128)S(1)} %get-tuple-element.22.count_ref, s32[1]{0:T(128)S(6)} %sub.17.half_ref, bf16[4,512,128]{2,1,0:T(8,128)(2,1)S(1)} %bitcast.40, bf16[16,256,128]{2,1,0:T(8,128)(2,1)S(1)} %all-to-all-done.2.refs_1_, ...), custom_call_target="tpu_custom_call" | custom-call | tf_op jit(solution)/shard_map/pallas_call | solution.py:172
  92.2 0.1 collective-permute-start.1
  92.3 1.1 %maximum_select_fusion = bf16[4,512,128]{2,1,0:T(8,128)(2,1)S(1)} fusion(bf16[2,512,128]{2,1,0:T(8,128)(2,1)S(1)} %bitcast.48, bf16[2,512,128]{2,1,0:T(8,128)(2,1)} %bitcast.11, pred[]{:T(512)S(6)} %eq.13), kind=kLoop, calls=%fused_computation.33 | loop fusion | flops 786432 | bytes 1048577 | tf_op jit(solution)/shard_map/jit(_where)/select_n | solution.py:234
  93.4 0.0 collective-permute-done
  93.4 0.4 collective-permute-done.1
  93.8 1.0 broadcast_select_fusion.3
  94.8 0.1 maximum_bitcast_fusion
  94.9 0.7 copy.56
  95.6 0.1 pad.clone
  95.7 0.0 copy-start.5
  95.7 0.1 copy.52
  95.8 0.0 copy-done
  95.8 0.5 copy-done.5
  96.4 0.0 copy-start.4
  96.4 2.0 %fusion.5 = bf16[6,1,8,65,128]{4,2,3,0,1:T(8,128)(2,1)S(1)} fusion(bf16[3,3,128,128]{3,2,1,0:T(8,128)(2,1)S(1)} %copy-done, bf16[8,1,7,2,128]{4,2,3,0,1:T(8,128)(2,1)S(1)} %slice.22, bf16[8,1,8,65,128]{4,2,3,0,1:T(8,128)(2,1)S(1)} %copy.52, pred[6]{0:T(512)(128)(4,1)S(1)} %or_and_fusion, pred[8,65]{0,1:T(8,128)(4,1)S(1)} %copy-done.5), kind=kOutput, calls=%fused_computation.11 | convolution fusion | flops 925415424 | bytes 2187790 | tf_op jit(solution)/shard_map/conv_general_dilated | solution.py:40
  98.4 0.0 copy-done.4
  98.4 1.4 %fusion.16 = f32[4,8,65,128]{3,1,2,0:T(8,128)S(1)} fusion(bf16[3,3,128,128]{3,2,1,0:T(8,128)(2,1)S(1)} %copy-done.4, bf16[6,1,7,1,128]{4,2,3,0,1:T(8,128)(2,1)S(1)} %get-tuple-element.17, bf16[6,1,7,1,128]{4,2,3,0,1:T(8,128)(2,1)S(1)} %get-tuple-element.16, bf16[6,1,8,65,128]{4,2,3,0,1:T(8,128)(2,1)S(1)} %fusion.5), kind=kOutput, calls=%fused_computation.25 | convolution fusion | flops 617533440 | bytes 2180096 | tf_op jit(solution)/shard_map/conv_general_dilated | solution.py:40
  99.9 0.3 copy.53
  100.2 0.1 slice.25
  100.2 0.9 fusion.13
  (9 shorter events, 0.1 us)
Async XLA Ops:
  0.0 95.8 %copy-start = (bf16[3,3,128,128]{3,2,1,0:T(8,128)(2,1)S(1)}, bf16[3,3,128,128]{3,2,1,0:T(8,128)(2,1)}, u32[]{:S(2)}) copy-start(bf16[3,3,128,128]{3,2,1,0:T(8,128)(2,1)} %param.10) | copy-start | bytes 884740
  1.4 11.2 %all-to-all-start = ((s32[16,1,36]{2,1,0:T(1,128)}), s32[16,1,36]{2,1,0:T(1,128)S(1)}, u32[]{:S(2)}, u32[]{:S(2)}) async-start(s32[16,1,36]{2,1,0:T(1,128)} %broadcast_in_dim.48), calls=%async_computation | async-start | bytes 16384 | tf_op jit(solution)/shard_map/all_to_all | solution.py:203
  45.9 4.5 %copy-start.2 = (bf16[4,512,128]{2,1,0:T(8,128)(2,1)S(1)}, bf16[4,512,128]{2,1,0:T(8,128)(2,1)}, u32[]{:S(2)}) copy-start(bf16[4,512,128]{2,1,0:T(8,128)(2,1)} %param.7) | copy-start | bytes 1572868
  45.9 4.6 %copy-start.3 = (s32[4,9]{1,0:T(4,128)S(1)}, s32[4,9]{1,0:T(4,128)}, u32[]{:S(2)}) copy-start(s32[4,9]{1,0:T(4,128)} %param.9) | copy-start | bytes 436
  45.9 29.4 %all-to-all-start.2 = ((bf16[16,256,128]{2,1,0:T(8,128)(2,1)}), bf16[16,256,128]{2,1,0:T(8,128)(2,1)S(1)}, u32[]{:S(2)}, u32[]{:S(2)}) async-start(bf16[16,256,128]{2,1,0:T(8,128)(2,1)} %get-tuple-element.11), calls=%async_computation.2 | async-start | bytes 2097152 | tf_op jit(solution)/shard_map/all_to_all | solution.py:213
  50.7 1.2 %copy-start.1 = (bf16[16,256,128]{2,1,0:T(8,128)(2,1)S(1)}, bf16[16,256,128]{2,1,0:T(8,128)(2,1)}, u32[]{:S(2)}) copy-start(bf16[16,256,128]{2,1,0:T(8,128)(2,1)} %all_to_all.19.k_ref) | copy-start | bytes 3145732
  82.3 11.0 %collective-permute-start = (bf16[2,512,128]{2,1,0:T(8,128)(2,1)}, bf16[2,512,128]{2,1,0:T(8,128)(2,1)}, u32[]{:S(2)}, u32[]{:S(2)}) collective-permute-start(bf16[2,512,128]{2,1,0:T(8,128)(2,1)} %bitcast.11), channel_id=1, source_target_pairs={{1,2},{3,4},{5,6},{7,8},{9,10},{11,12},{13,14},{2,1},{4,3},{6,5},{... | collective-permute-start | bytes 786440 | tf_op jit(solution)/shard_map/ppermute | solution.py:232
  92.2 1.6 %collective-permute-start.1 = (bf16[2,512,128]{2,1,0:T(8,128)(2,1)S(1)}, bf16[2,512,128]{2,1,0:T(8,128)(2,1)S(1)}, u32[]{:S(2)}, u32[]{:S(2)}) collective-permute-start(bf16[2,512,128]{2,1,0:T(8,128)(2,1)S(1)} %bitcast.47), channel_id=1, source_target_pairs={{0,1},{1,0},{2,3},{3,2},{4,5},{5,4},{6,7},{7,6},{8,9},{9,8},{10,11... | collective-permute-start | bytes 786440 | tf_op jit(solution)/shard_map/ppermute | solution.py:233
  95.7 0.7 copy-start.5
  96.4 2.1 %copy-start.4 = (bf16[3,3,128,128]{3,2,1,0:T(8,128)(2,1)S(1)}, bf16[3,3,128,128]{3,2,1,0:T(8,128)(2,1)}, u32[]{:S(2)}) copy-start(bf16[3,3,128,128]{3,2,1,0:T(8,128)(2,1)} %param.11) | copy-start | bytes 884740

commit v16 on v15

--- a/solution.py
+++ b/solution.py
@@ -102,7 +102,7 @@
         mixed = a_in[0] * column(alpha, width) + mixed
         total = t_in[0] * alpha + total
     if last:
-        o_ref[0] = (mixed / column(total, width)).astype(o_ref.dtype)
+        o_ref[...] = (mixed / column(total, width)).astype(o_ref.dtype).reshape(o_ref.shape)
     else:
         m_out[0] = m_new
         t_out[0] = total
@@ -145,7 +145,7 @@
     )(slot_owner, counts, queries, chunk, *([] if first else state))
 
 
-def attend_last_half(state, queries, chunk, slot_owner, counts, half, scale):
+def attend_last_half(state, queries, chunk, slot_owner, counts, half, scale, tile_cols):
     tiles, tile_size, channels = queries.shape
     owners, chunk_len, _ = chunk.shape
     slots = slot_owner.shape[1]
@@ -162,7 +162,7 @@
             row_spec,
             acc_spec,
         ],
-        out_specs=pl.BlockSpec((1, part, channels), lambda t, o, c, h: (t, 0, 0)),
+        out_specs=pl.BlockSpec((part // tile_cols, tile_cols, channels), lambda t, o, c, h: (0, t, 0)),
         scratch_shapes=[pltpu.VMEM((slots * chunk_len, channels), jnp.bfloat16)],
     )
 
@@ -172,7 +172,7 @@
     return pl.pallas_call(
         kernel,
         grid_spec=grid_spec,
-        out_shape=jax.ShapeDtypeStruct((tiles, part, channels), jnp.bfloat16),
+        out_shape=jax.ShapeDtypeStruct((part // tile_cols, tiles * tile_cols, channels), jnp.bfloat16),
         compiler_params=pltpu.CompilerParams(vmem_limit_bytes=48 * 1024 * 1024),
     )(slot_owner, counts, half, queries, chunk, *state)
 
@@ -217,16 +217,13 @@
     even = me % 2 == 0
     crossing = jnp.where(even, 0, 1).astype(jnp.int32).reshape(1)
     staying = (1 - crossing).astype(jnp.int32)
-    crossing_tiles = attend_last_half(state, query_tiles, previous, slot_owner, counts, crossing, scale)
-    staying_tiles = attend_last_half(state, query_tiles, previous, slot_owner, counts, staying, scale)
-
-    def to_rows(tiles):
-        return tiles.reshape(per_device, -1, tile_cols, channels).transpose(1, 0, 2, 3).reshape(
-            -1, band_width, channels
-        )
-
-    crossing_rows = to_rows(crossing_tiles)
-    staying_rows = to_rows(staying_tiles)
+    crossing_rows = attend_last_half(
+        state, query_tiles, previous, slot_owner, counts, crossing, scale, tile_cols
+    )
+    staying_rows = attend_last_half(
+        state, query_tiles, previous, slot_owner, counts, staying, scale, tile_cols
+    )
+
     count = lax.axis_size("row")
     links = [(i, i + 1) for i in range(1, count - 1, 2)] + [(i + 1, i) for i in range(1, count - 1, 2)]
     across = lax.ppermute(crossing_rows, "row", links)

time: 102 us -> 102 us (level)
  other arithmetic: 4.62 us -> 3.6 us
    select_n x1, other arithmetic: 1.12 us -> 0.08 us  [on_device(): jnp.where(even, jnp.concatenate([crossing_rows, staying_rows], axis=0), j...]
    unnamed x13 -> x15, local copies, waits for them, and re-layouts: 2.44 us -> 3.4 us
  transfers between devices with their start and end apart: 4 -> 4, of which waited for: 3 -> 4; matrix products, arithmetic and copies ran while one was open for 2% -> 1% of each run, Pallas kernels for 20% -> 20%
where the time goes in v16:
time: 102 us
  blocking collectives  30.4 us (30%)
  Pallas kernels  26.8 us (26%)
  starting transfers between devices  14.6 us (14%)
  waiting for transfers between devices  14.2 us (14%)
  local copies, waits for them, and re-layouts  8.16 us (8%)
  other arithmetic  3.6 us (4%)
  matrix products  3.5 us (3%)
    all_to_all x1, blocking collectives, on_device(): lax.all_to_all(sending, 'row', split_axis=0, concat_axis=0, tiled=True)  30.4 us
    pallas_call x1, Pallas kernels, attend_chunk(): pl.pallas_call(functools.partial(attend_kernel, scale=scale, first=first,...  13.9 us
    pallas_call x2, Pallas kernels, attend_last_half(): pl.pallas_call(kernel, grid_spec=grid_spec, out_shape=jax.ShapeDtypeStruc...  12.9 us
    all_to_all x1, waiting for transfers between devices, on_device(): lax.all_to_all(sending, 'row', split_axis=0, concat_axis=0, tiled=True)  9.35 us
    all_to_all x1, starting transfers between devices, on_device(): lax.all_to_all(lists_everywhere, 'row', split_axis=0, concat_axis=0, tile...  6.61 us
    all_to_all x1, starting transfers between devices, on_device(): lax.all_to_all(sending, 'row', split_axis=0, concat_axis=0, tiled=True)  4.51 us
    conv_general_dilated x2, matrix products, native_conv(): lax.conv_general_dilated(rows[None], weights, window_strides=(1, 1), padd...  3.5 us
    all_to_all x1, waiting for transfers between devices, on_device(): lax.all_to_all(lists_everywhere, 'row', split_axis=0, concat_axis=0, tile...  3.49 us
  transfers between devices with their start and end apart: 4, of which 4 were waited for; matrix products, arithmetic and copies ran while one was open for 1% of the time, Pallas kernels for 20%

profile of v16, /device:TPU:9, one launch (start us, length us, event | category | flops | bytes accessed | tf_op | source)
XLA Modules:
  0.0 101.5 jit_solution(6110638095097044595)
XLA Ops:
  0.0 0.0 copy-start
  0.0 0.8 broadcast_in_dim.47
  0.8 0.6 broadcast_in_dim.48
  1.4 6.6 %all-to-all-start = ((s32[16,1,36]{2,1,0:T(1,128)}), s32[16,1,36]{2,1,0:T(1,128)S(1)}, u32[]{:S(2)}, u32[]{:S(2)}) async-start(s32[16,1,36]{2,1,0:T(1,128)} %broadcast_in_dim.48), calls=%async_computation | async-start | bytes 16384 | tf_op jit(solution)/shard_map/all_to_all | solution.py:203
  8.0 1.1 %copy.41 = bf16[4,4,128,128]{3,2,1,0:T(8,128)(2,1)S(1)} copy(bf16[4,4,128,128]{3,2,0,1:T(8,128)(2,1)} %bitcast.37) | data formatting | bytes 1048576 | tf_op jit(solution)/shard_map/transpose | solution.py:191
  9.2 3.5 %all-to-all-done = s32[16,1,36]{2,1,0:T(1,128)S(1)} async-done(((s32[16,1,36]{2,1,0:T(1,128)}), s32[16,1,36]{2,1,0:T(1,128)S(1)}, u32[]{:S(2)}, u32[]{:S(2)}) %all-to-all-start) | async-done | bytes 2336 | tf_op jit(solution)/shard_map/all_to_all | solution.py:203
  12.6 0.1 fusion.29
  12.8 0.7 gather_fusion.1
  13.6 0.7 gather_fusion
  14.3 1.2 %broadcast_select_fusion = (bf16[16,256,128]{2,1,0:T(8,128)(2,1)}, bf16[16,256,128]{2,1,0:T(8,128)(2,1)S(1)}) fusion(bf16[16,256,128]{2,1,0:T(8,128)(2,1)S(1)} %gather_fusion.1, pred[16]{0:T(512)(128)(4,1)S(1)} %compare_and_fusion, bf16[16,256,128]{2,1,0:T(8,128)(2,1)S(1)} %gather_fusion), kind=kLoop, calls=%fused_computation.21 | loop fusion | flops 1048576 | bytes 4194320 | tf_op jit(solution)/shard_map/jit(_take)/select_n | solution.py:210
  15.6 30.4 %all_to_all.19.k_ref = bf16[16,256,128]{2,1,0:T(8,128)(2,1)} all-to-all(bf16[16,256,128]{2,1,0:T(8,128)(2,1)S(1)} %get-tuple-element.25), channel_id=1, replica_groups=mesh['pairs'=2,'row'=16] {'row'}, dimensions={0} | all-to-all | bytes 2097152 | tf_op jit(solution)/shard_map/all_to_all | solution.py:213
  45.9 0.0 copy-start.2
  45.9 0.0 copy-start.4
  45.9 4.5 %all-to-all-start.2 = ((bf16[16,256,128]{2,1,0:T(8,128)(2,1)}), bf16[16,256,128]{2,1,0:T(8,128)(2,1)S(1)}, u32[]{:S(2)}, u32[]{:S(2)}) async-start(bf16[16,256,128]{2,1,0:T(8,128)(2,1)} %get-tuple-element.11), calls=%async_computation.2 | async-start | bytes 2097152 | tf_op jit(solution)/shard_map/all_to_all | solution.py:213
  50.4 0.0 copy-done.2
  50.5 0.0 copy-done.4
  50.5 0.1 slice_reduce_fusion
  50.6 0.1 fusion.32
  50.7 0.0 copy-start.1
  50.7 1.2 %copy-done.1 = bf16[16,256,128]{2,1,0:T(8,128)(2,1)S(1)} copy-done((bf16[16,256,128]{2,1,0:T(8,128)(2,1)S(1)}, bf16[16,256,128]{2,1,0:T(8,128)(2,1)}, u32[]{:S(2)}) %copy-start.1) | copy-done | bytes 1048600
  52.0 13.9 %shard_map.55 = (f32[4,1,512]{2,1,0:T(1,128)S(1)}, f32[4,1,512]{2,1,0:T(1,128)S(1)}, f32[4,512,128]{2,1,0:T(8,128)S(1)}) custom-call(s32[4,9]{1,0:T(4,128)S(1)} %get-tuple-element.23.owner_ref, s32[4]{0:T(128)S(1)} %get-tuple-element.22.count_ref, bf16[4,512,128]{2,1,0:T(8,128)(2,1)S(1)} %bitcast.30, bf16[16,256,128]{2,1,0:T(8,128)(2,1)S(1)} %copy-done.1), custom_call_target="tpu_custom_call" | custom-call | tf_op jit(solution)/shard_map/pallas_call | solution.py:140
  65.9 9.3 %all-to-all-done.2.refs_1_ = bf16[16,256,128]{2,1,0:T(8,128)(2,1)S(1)} async-done(((bf16[16,256,128]{2,1,0:T(8,128)(2,1)}), bf16[16,256,128]{2,1,0:T(8,128)(2,1)S(1)}, u32[]{:S(2)}, u32[]{:S(2)}) %all-to-all-start.2) | async-done | bytes 1048608 | tf_op jit(solution)/shard_map/all_to_all | solution.py:213
  75.3 6.4 %shard_map.56 = bf16[2,512,128]{2,1,0:T(8,128)(2,1)S(1)} custom-call(s32[4,9]{1,0:T(4,128)S(1)} %get-tuple-element.23.owner_ref, s32[4]{0:T(128)S(1)} %get-tuple-element.22.count_ref, s32[1]{0:T(128)} %bitcast.half_ref, bf16[4,512,128]{2,1,0:T(8,128)(2,1)S(1)} %bitcast.31, bf16[16,256,128]{2,1,0:T(8,128)(2,1)S(1)} %all-to-all-done.2.refs_1_, ...), custom_call_target="tpu_custom_call" | custom-call | tf_op jit(solution)/shard_map/pallas_call | solution.py:172
  81.7 3.4 %collective-permute-start = (bf16[2,512,128]{2,1,0:T(8,128)(2,1)S(1)}, bf16[2,512,128]{2,1,0:T(8,128)(2,1)}, u32[]{:S(2)}, u32[]{:S(2)}) collective-permute-start(bf16[2,512,128]{2,1,0:T(8,128)(2,1)S(1)} %shard_map.56), channel_id=1, source_target_pairs={{1,2},{3,4},{5,6},{7,8},{9,10},{11,12},{13,14},{2,1},{4,3},{6,5},{... | collective-permute-start | bytes 786440 | tf_op jit(solution)/shard_map/ppermute | solution.py:229
  85.1 6.4 %shard_map.57 = bf16[2,512,128]{2,1,0:T(8,128)(2,1)S(1)} custom-call(s32[4,9]{1,0:T(4,128)S(1)} %get-tuple-element.23.owner_ref, s32[4]{0:T(128)S(1)} %get-tuple-element.22.count_ref, s32[1]{0:T(128)S(6)} %sub.17.half_ref, bf16[4,512,128]{2,1,0:T(8,128)(2,1)S(1)} %bitcast.32, bf16[16,256,128]{2,1,0:T(8,128)(2,1)S(1)} %all-to-all-done.2.refs_1_, ...), custom_call_target="tpu_custom_call" | custom-call | tf_op jit(solution)/shard_map/pallas_call | solution.py:172
  91.6 0.1 collective-permute-start.1
  91.7 0.1 maximum_select_fusion
  91.8 0.5 collective-permute-done
  92.3 0.9 collective-permute-done.1
  93.2 1.0 broadcast_select_fusion.3
  94.2 0.1 maximum_bitcast_fusion
  94.3 0.7 copy.48
  95.0 0.1 pad.clone
  95.1 0.0 copy-start.6
  95.1 0.1 copy.44
  95.2 0.0 copy-done
  95.2 0.5 copy-done.6
  95.8 0.0 copy-start.5
  95.8 2.1 %fusion.5 = bf16[6,1,8,65,128]{4,2,3,0,1:T(8,128)(2,1)S(1)} fusion(bf16[3,3,128,128]{3,2,1,0:T(8,128)(2,1)S(1)} %copy-done, bf16[8,1,7,2,128]{4,2,3,0,1:T(8,128)(2,1)S(1)} %slice.22, bf16[8,1,8,65,128]{4,2,3,0,1:T(8,128)(2,1)S(1)} %copy.44, pred[6]{0:T(512)(128)(4,1)S(1)} %or_and_fusion, pred[8,65]{0,1:T(8,128)(4,1)S(1)} %copy-done.6), kind=kOutput, calls=%fused_computation.11 | convolution fusion | flops 925415424 | bytes 2187790 | tf_op jit(solution)/shard_map/conv_general_dilated | solution.py:40
  97.8 0.0 copy-done.5
  97.8 1.4 %fusion.16 = f32[4,8,65,128]{3,1,2,0:T(8,128)S(1)} fusion(bf16[3,3,128,128]{3,2,1,0:T(8,128)(2,1)S(1)} %copy-done.5, bf16[6,1,7,1,128]{4,2,3,0,1:T(8,128)(2,1)S(1)} %get-tuple-element.17, bf16[6,1,7,1,128]{4,2,3,0,1:T(8,128)(2,1)S(1)} %get-tuple-element.16, bf16[6,1,8,65,128]{4,2,3,0,1:T(8,128)(2,1)S(1)} %fusion.5), kind=kOutput, calls=%fused_computation.25 | convolution fusion | flops 617533440 | bytes 2180096 | tf_op jit(solution)/shard_map/conv_general_dilated | solution.py:40
  99.3 0.3 copy.45
  99.6 0.0 copy-start.3
  99.6 0.1 slice.25
  99.7 1.0 copy-done.3
  100.6 0.9 fusion.13
  (8 shorter events, 0.1 us)
Async XLA Ops:
  0.0 95.2 %copy-start = (bf16[3,3,128,128]{3,2,1,0:T(8,128)(2,1)S(1)}, bf16[3,3,128,128]{3,2,1,0:T(8,128)(2,1)}, u32[]{:S(2)}) copy-start(bf16[3,3,128,128]{3,2,1,0:T(8,128)(2,1)} %param.10) | copy-start | bytes 884740
  1.4 11.2 %all-to-all-start = ((s32[16,1,36]{2,1,0:T(1,128)}), s32[16,1,36]{2,1,0:T(1,128)S(1)}, u32[]{:S(2)}, u32[]{:S(2)}) async-start(s32[16,1,36]{2,1,0:T(1,128)} %broadcast_in_dim.48), calls=%async_computation | async-start | bytes 16384 | tf_op jit(solution)/shard_map/all_to_all | solution.py:203
  45.9 4.5 %copy-start.2 = (bf16[4,512,128]{2,1,0:T(8,128)(2,1)S(1)}, bf16[4,512,128]{2,1,0:T(8,128)(2,1)}, u32[]{:S(2)}) copy-start(bf16[4,512,128]{2,1,0:T(8,128)(2,1)} %param.7) | copy-start | bytes 1572868
  45.9 4.6 %copy-start.4 = (s32[4,9]{1,0:T(4,128)S(1)}, s32[4,9]{1,0:T(4,128)}, u32[]{:S(2)}) copy-start(s32[4,9]{1,0:T(4,128)} %param.9) | copy-start | bytes 436
  45.9 29.4 %all-to-all-start.2 = ((bf16[16,256,128]{2,1,0:T(8,128)(2,1)}), bf16[16,256,128]{2,1,0:T(8,128)(2,1)S(1)}, u32[]{:S(2)}, u32[]{:S(2)}) async-start(bf16[16,256,128]{2,1,0:T(8,128)(2,1)} %get-tuple-element.11), calls=%async_computation.2 | async-start | bytes 2097152 | tf_op jit(solution)/shard_map/all_to_all | solution.py:213
  50.7 1.2 %copy-start.1 = (bf16[16,256,128]{2,1,0:T(8,128)(2,1)S(1)}, bf16[16,256,128]{2,1,0:T(8,128)(2,1)}, u32[]{:S(2)}) copy-start(bf16[16,256,128]{2,1,0:T(8,128)(2,1)} %all_to_all.19.k_ref) | copy-start | bytes 3145732
  81.7 10.6 %collective-permute-start = (bf16[2,512,128]{2,1,0:T(8,128)(2,1)S(1)}, bf16[2,512,128]{2,1,0:T(8,128)(2,1)}, u32[]{:S(2)}, u32[]{:S(2)}) collective-permute-start(bf16[2,512,128]{2,1,0:T(8,128)(2,1)S(1)} %shard_map.56), channel_id=1, source_target_pairs={{1,2},{3,4},{5,6},{7,8},{9,10},{11,12},{13,14},{2,1},{4,3},{6,5},{... | collective-permute-start | bytes 786440 | tf_op jit(solution)/shard_map/ppermute | solution.py:229
  91.6 1.6 %collective-permute-start.1 = (bf16[2,512,128]{2,1,0:T(8,128)(2,1)S(1)}, bf16[2,512,128]{2,1,0:T(8,128)(2,1)S(1)}, u32[]{:S(2)}, u32[]{:S(2)}) collective-permute-start(bf16[2,512,128]{2,1,0:T(8,128)(2,1)S(1)} %shard_map.57), channel_id=1, source_target_pairs={{0,1},{1,0},{2,3},{3,2},{4,5},{5,4},{6,7},{7,6},{8,9},{9,8},{10,11... | collective-permute-start | bytes 786440 | tf_op jit(solution)/shard_map/ppermute | solution.py:230
  95.1 0.7 copy-start.6
  95.8 2.1 %copy-start.5 = (bf16[3,3,128,128]{3,2,1,0:T(8,128)(2,1)S(1)}, bf16[3,3,128,128]{3,2,1,0:T(8,128)(2,1)}, u32[]{:S(2)}) copy-start(bf16[3,3,128,128]{3,2,1,0:T(8,128)(2,1)} %param.11) | copy-start | bytes 884740
  99.6 1.0 %copy-start.3 = (bf16[4,512,128]{2,1,0:T(8,128)(2,1)S(1)}, bf16[4,512,128]{2,1,0:T(8,128)(2,1)}, u32[]{:S(2)}) copy-start(bf16[4,512,128]{2,1,0:T(8,128)(2,1)} %param.7) | copy-start | bytes 1572868

commit v17 on v15

--- a/solution.py
+++ b/solution.py
@@ -243,8 +243,13 @@
     row_ids = jnp.arange(band_rows + 2)
     inside = ((row_ids > 0) | (me > 0)) & ((row_ids < band_rows + 1) | (me < owners - 1))
     hidden = jnp.where(inside[:, None, None], hidden, jnp.zeros_like(hidden))
-    branch = native_conv(hidden, conv_two)
-    return (frame_one.astype(jnp.float32) + branch).astype(jnp.bfloat16)
+    taps = conv_two.shape[0]
+    centre = (jnp.arange(taps)[:, None] == taps // 2) & (jnp.arange(taps)[None, :] == taps // 2)
+    identity = (centre[:, :, None, None] & jnp.eye(channels, dtype=bool)[None, None]).astype(conv_two.dtype)
+    weights = jnp.concatenate([conv_two, identity], axis=2)
+    residual = jnp.pad(frame_one, ((1, 1), (0, 0), (0, 0)))
+    stacked = jnp.concatenate([hidden, residual], axis=2)
+    return native_conv(stacked, weights).astype(jnp.bfloat16)
 
 
 def solution(mesh):

time: 102 us -> 109 us (1.069)
  local copies, waits for them, and re-layouts: 7.93 us -> 14.2 us
  matrix products: 3.47 us -> 4.72 us
    conv_general_dilated x4 -> x5, local copies, waits for them, and re-layouts: 0.5 us -> 2.94 us  [native_conv(): lax.conv_general_dilated(rows[None], weights, window_strides=(1, 1), padd...]
    convert_element_type x0 -> x5, local copies, waits for them, and re-layouts: none -> 1.63 us  [the longest x3 1.25 us: on_device(): return native_conv(stacked, weights).astype(jnp.bfloat16)]
    broadcast_in_dim x1 -> x2, local copies, waits for them, and re-layouts: 0.07 us -> 1.63 us  [native_conv(): rows[None]]
    conv_general_dilated x2, matrix products: 3.47 us -> 4.72 us  [native_conv(): lax.conv_general_dilated(rows[None], weights, window_strides=(1, 1), padd...]
  transfers between devices with their start and end apart: 4 -> 4, of which waited for: 3 -> 3; matrix products, arithmetic and copies ran while one was open for 2% -> 3% of each run, Pallas kernels for 20% -> 19%
where the time goes in v17:
time: 109 us; the launch traced here: 108 us
  blocking collectives  30.5 us (28%)
  Pallas kernels  26.7 us (24%)
  starting transfers between devices  14.6 us (13%)
  local copies, waits for them, and re-layouts  14.2 us (13%)
  waiting for transfers between devices  13 us (12%)
  matrix products  4.72 us (4%)
  other arithmetic  4.21 us (4%)
    all_to_all x1, blocking collectives, on_device(): lax.all_to_all(sending, 'row', split_axis=0, concat_axis=0, tiled=True)  30.5 us
    pallas_call x1, Pallas kernels, attend_chunk(): pl.pallas_call(functools.partial(attend_kernel, scale=scale, first=first,...  13.9 us
    pallas_call x2, Pallas kernels, attend_last_half(): pl.pallas_call(kernel, grid_spec=grid_spec, out_shape=jax.ShapeDtypeStruc...  12.8 us
    all_to_all x1, waiting for transfers between devices, on_device(): lax.all_to_all(sending, 'row', split_axis=0, concat_axis=0, tiled=True)  9.27 us
    all_to_all x1, starting transfers between devices, on_device(): lax.all_to_all(lists_everywhere, 'row', split_axis=0, concat_axis=0, tile...  6.61 us
    conv_general_dilated x2, matrix products, native_conv(): lax.conv_general_dilated(rows[None], weights, window_strides=(1, 1), padd...  4.72 us
    all_to_all x1, starting transfers between devices, on_device(): lax.all_to_all(sending, 'row', split_axis=0, concat_axis=0, tiled=True)  4.51 us
    all_to_all x1, waiting for transfers between devices, on_device(): lax.all_to_all(lists_everywhere, 'row', split_axis=0, concat_axis=0, tile...  3.49 us
  transfers between devices with their start and end apart: 4, of which 3 were waited for; matrix products, arithmetic and copies ran while one was open for 3% of the time, Pallas kernels for 19%

profile of v17, /device:TPU:9, one launch (start us, length us, event | category | flops | bytes accessed | tf_op | source)
XLA Modules:
  0.0 108.1 jit_solution(9367825338034851172)
XLA Ops:
  0.0 0.8 broadcast_in_dim.53
  0.8 0.6 broadcast_in_dim.54
  1.4 6.6 %all-to-all-start = ((s32[16,1,36]{2,1,0:T(1,128)}), s32[16,1,36]{2,1,0:T(1,128)S(1)}, u32[]{:S(2)}, u32[]{:S(2)}) async-start(s32[16,1,36]{2,1,0:T(1,128)} %broadcast_in_dim.54), calls=%async_computation | async-start | bytes 16384 | tf_op jit(solution)/shard_map/all_to_all | solution.py:203
  8.0 1.1 copy.43
  9.2 3.5 %all-to-all-done = s32[16,1,36]{2,1,0:T(1,128)S(1)} async-done(((s32[16,1,36]{2,1,0:T(1,128)}), s32[16,1,36]{2,1,0:T(1,128)S(1)}, u32[]{:S(2)}, u32[]{:S(2)}) %all-to-all-start) | async-done | bytes 2336 | tf_op jit(solution)/shard_map/all_to_all | solution.py:203
  12.6 0.1 fusion.32
  12.8 0.7 gather_fusion.1
  13.6 0.7 gather_fusion
  14.3 1.2 %broadcast_select_fusion = (bf16[16,256,128]{2,1,0:T(8,128)(2,1)}, bf16[16,256,128]{2,1,0:T(8,128)(2,1)S(1)}) fusion(bf16[16,256,128]{2,1,0:T(8,128)(2,1)S(1)} %gather_fusion.1, pred[16]{0:T(512)(128)(4,1)S(1)} %compare_and_fusion, bf16[16,256,128]{2,1,0:T(8,128)(2,1)S(1)} %gather_fusion), kind=kLoop, calls=%fused_computation.25 | loop fusion | flops 1048576 | bytes 4194320 | tf_op jit(solution)/shard_map/jit(_take)/select_n | solution.py:210
  15.5 30.5 %all_to_all.19.k_ref = bf16[16,256,128]{2,1,0:T(8,128)(2,1)} all-to-all(bf16[16,256,128]{2,1,0:T(8,128)(2,1)S(1)} %get-tuple-element.23), channel_id=1, replica_groups=mesh['pairs'=2,'row'=16] {'row'}, dimensions={0} | all-to-all | bytes 2097152 | tf_op jit(solution)/shard_map/all_to_all | solution.py:213
  46.0 4.5 %all-to-all-start.2 = ((bf16[16,256,128]{2,1,0:T(8,128)(2,1)}), bf16[16,256,128]{2,1,0:T(8,128)(2,1)S(1)}, u32[]{:S(2)}, u32[]{:S(2)}) async-start(bf16[16,256,128]{2,1,0:T(8,128)(2,1)} %get-tuple-element.11), calls=%async_computation.2 | async-start | bytes 2097152 | tf_op jit(solution)/shard_map/all_to_all | solution.py:213
  50.5 0.0 copy-done.2
  50.6 0.1 slice_reduce_fusion
  50.7 0.1 broadcast_and_fusion
  50.8 0.1 fusion.35
  50.9 1.2 %copy-done.1 = bf16[16,256,128]{2,1,0:T(8,128)(2,1)S(1)} copy-done((bf16[16,256,128]{2,1,0:T(8,128)(2,1)S(1)}, bf16[16,256,128]{2,1,0:T(8,128)(2,1)}, u32[]{:S(2)}) %copy-start.1) | copy-done | bytes 1048600
  52.2 13.9 %shard_map.55 = (f32[4,1,512]{2,1,0:T(1,128)S(1)}, f32[4,1,512]{2,1,0:T(1,128)S(1)}, f32[4,512,128]{2,1,0:T(8,128)S(1)}) custom-call(s32[4,9]{1,0:T(4,128)S(1)} %get-tuple-element.21.owner_ref, s32[4]{0:T(128)S(1)} %get-tuple-element.20.count_ref, bf16[4,512,128]{2,1,0:T(8,128)(2,1)S(1)} %bitcast.45, bf16[16,256,128]{2,1,0:T(8,128)(2,1)S(1)} %copy-done.1), custom_call_target="tpu_custom_call" | custom-call | tf_op jit(solution)/shard_map/pallas_call | solution.py:140
  66.1 9.3 %all-to-all-done.2.refs_1_ = bf16[16,256,128]{2,1,0:T(8,128)(2,1)S(1)} async-done(((bf16[16,256,128]{2,1,0:T(8,128)(2,1)}), bf16[16,256,128]{2,1,0:T(8,128)(2,1)S(1)}, u32[]{:S(2)}, u32[]{:S(2)}) %all-to-all-start.2) | async-done | bytes 1048608 | tf_op jit(solution)/shard_map/all_to_all | solution.py:213
  75.4 6.4 %shard_map.56 = bf16[4,256,128]{2,1,0:T(8,128)(2,1)S(1)} custom-call(s32[4,9]{1,0:T(4,128)S(1)} %get-tuple-element.21.owner_ref, s32[4]{0:T(128)S(1)} %get-tuple-element.20.count_ref, s32[1]{0:T(128)} %bitcast.half_ref, bf16[4,512,128]{2,1,0:T(8,128)(2,1)S(1)} %bitcast.46, bf16[16,256,128]{2,1,0:T(8,128)(2,1)S(1)} %all-to-all-done.2.refs_1_, ...), custom_call_target="tpu_custom_call" | custom-call | tf_op jit(solution)/shard_map/pallas_call | solution.py:172
  81.8 0.7 copy.44
  82.5 3.4 %collective-permute-start = (bf16[2,512,128]{2,1,0:T(8,128)(2,1)}, bf16[2,512,128]{2,1,0:T(8,128)(2,1)}, u32[]{:S(2)}, u32[]{:S(2)}) collective-permute-start(bf16[2,512,128]{2,1,0:T(8,128)(2,1)} %bitcast.11), channel_id=1, source_target_pairs={{1,2},{3,4},{5,6},{7,8},{9,10},{11,12},{13,14},{2,1},{4,3},{6,5},{... | collective-permute-start | bytes 786440 | tf_op jit(solution)/shard_map/ppermute | solution.py:232
  85.9 6.4 %shard_map.57 = bf16[4,256,128]{2,1,0:T(8,128)(2,1)S(1)} custom-call(s32[4,9]{1,0:T(4,128)S(1)} %get-tuple-element.21.owner_ref, s32[4]{0:T(128)S(1)} %get-tuple-element.20.count_ref, s32[1]{0:T(128)S(6)} %sub.17.half_ref, bf16[4,512,128]{2,1,0:T(8,128)(2,1)S(1)} %bitcast.47, bf16[16,256,128]{2,1,0:T(8,128)(2,1)S(1)} %all-to-all-done.2.refs_1_, ...), custom_call_target="tpu_custom_call" | custom-call | tf_op jit(solution)/shard_map/pallas_call | solution.py:172
  92.3 0.1 collective-permute-start.1
  92.4 0.1 and_convert_fusion
  92.5 1.1 %maximum_select_fusion = bf16[4,512,128]{2,1,0:T(8,128)(2,1)S(1)} fusion(bf16[2,512,128]{2,1,0:T(8,128)(2,1)S(1)} %bitcast.55, bf16[2,512,128]{2,1,0:T(8,128)(2,1)} %bitcast.11, pred[]{:T(512)S(6)} %eq.34), kind=kLoop, calls=%fused_computation.36 | loop fusion | flops 786432 | bytes 1048577 | tf_op jit(solution)/shard_map/jit(_where)/select_n | solution.py:234
  93.6 0.0 collective-permute-done
  93.7 0.2 collective-permute-done.1
  93.9 1.0 broadcast_select_fusion.3
  94.9 0.1 maximum_bitcast_fusion
  95.0 0.7 copy.54
  95.7 0.1 pad.5.clone
  95.8 0.0 copy-start.5
  95.8 0.1 copy.48
  96.0 0.5 copy-done.5
  96.5 2.0 %maximum_convert_fusion = bf16[6,8,65,128]{3,1,2,0:T(8,128)(2,1)S(1)} fusion(bf16[3,3,128,128]{3,2,1,0:T(8,128)(2,1)S(1)} %copy-done, bf16[8,1,7,2,128]{4,2,3,0,1:T(8,128)(2,1)S(1)} %slice.22, bf16[8,1,8,65,128]{4,2,3,0,1:T(8,128)(2,1)S(1)} %copy.48, pred[8,65]{0,1:T(8,128)(4,1)S(1)} %copy-done.5), kind=kOutput, calls=%fused_computation.14 | convolution fusion | flops 924616704 | bytes 2187784 | tf_op jit(solution)/shard_map/conv_general_dilated | solution.py:40
  98.5 0.1 copy.49
  98.7 0.3 reshape.113
  98.9 0.1 fusion.25
  99.1 0.1 fusion.11
  99.2 1.6 %pad.7 = bf16[6,1,520,256]{3,2,0,1:T(8,128)(2,1)} pad(bf16[6,1,512,256]{3,2,0,1:T(8,128)(2,1)S(1)} %fusion.11, bf16[]{:T(256)} %constant.83.clone.1), padding=0_0x0_0x1_7x0_0 | pad | bytes 3170306 | tf_op jit(solution)/shard_map/broadcast_in_dim | solution.py:41
  100.8 2.4 %reshape.116 = bf16[6,1,8,65,256]{4,3,2,0,1:T(8,128)(2,1)S(1)} reshape(bf16[6,1,520,256]{3,2,0,1:T(8,128)(2,1)} %pad.7) | data formatting | bytes 3194880 | tf_op jit(solution)/shard_map/conv_general_dilated | solution.py:40
  103.2 0.0 copy-start.4
  103.2 0.3 copy.51
  103.6 0.6 copy-done.4
  104.2 2.7 %fusion.15 = bf16[4,8,65,128]{3,1,2,0:T(8,128)(2,1)S(1)} fusion(bf16[6,1,7,2,256]{4,2,3,0,1:T(8,128)(2,1)S(1)} %slice.24, bf16[6,1,8,65,256]{4,2,3,0,1:T(8,128)(2,1)S(1)} %copy.51, bf16[3,3,128,128]{3,2,1,0:T(8,128)(2,1)S(1)} %and_convert_fusion, bf16[3,3,128,128]{3,2,1,0:T(8,128)(2,1)S(1)} %copy-done.4, pred[8,65]{0,1:T(8,128)(4,1)S(1)} %copy-done.5), kind=kOutput, calls=%fused_computation.18 | convolution fusion | flops 1233485824 | bytes 2763272 | tf_op jit(solution)/shard_map/conv_general_dilated | solution.py:40
  106.9 0.2 copy.52
  107.1 0.2 slice_bitcast_fusion.1
  107.3 0.9 copy.53
  (17 shorter events, 0.2 us)
Async XLA Ops:
  0.0 96.0 %copy-start = (bf16[3,3,128,128]{3,2,1,0:T(8,128)(2,1)S(1)}, bf16[3,3,128,128]{3,2,1,0:T(8,128)(2,1)}, u32[]{:S(2)}) copy-start(bf16[3,3,128,128]{3,2,1,0:T(8,128)(2,1)} %param.10) | copy-start | bytes 884740
  1.4 11.2 %all-to-all-start = ((s32[16,1,36]{2,1,0:T(1,128)}), s32[16,1,36]{2,1,0:T(1,128)S(1)}, u32[]{:S(2)}, u32[]{:S(2)}) async-start(s32[16,1,36]{2,1,0:T(1,128)} %broadcast_in_dim.54), calls=%async_computation | async-start | bytes 16384 | tf_op jit(solution)/shard_map/all_to_all | solution.py:203
  15.5 35.0 %copy-start.2 = (bf16[4,512,128]{2,1,0:T(8,128)(2,1)S(1)}, bf16[4,512,128]{2,1,0:T(8,128)(2,1)}, u32[]{:S(2)}) copy-start(bf16[4,512,128]{2,1,0:T(8,128)(2,1)} %param.7) | copy-start | bytes 1572868
  46.0 4.6 %copy-start.3 = (s32[4,9]{1,0:T(4,128)S(1)}, s32[4,9]{1,0:T(4,128)}, u32[]{:S(2)}) copy-start(s32[4,9]{1,0:T(4,128)} %param.9) | copy-start | bytes 436
  46.0 29.4 %all-to-all-start.2 = ((bf16[16,256,128]{2,1,0:T(8,128)(2,1)}), bf16[16,256,128]{2,1,0:T(8,128)(2,1)S(1)}, u32[]{:S(2)}, u32[]{:S(2)}) async-start(bf16[16,256,128]{2,1,0:T(8,128)(2,1)} %get-tuple-element.11), calls=%async_computation.2 | async-start | bytes 2097152 | tf_op jit(solution)/shard_map/all_to_all | solution.py:213
  50.9 1.2 %copy-start.1 = (bf16[16,256,128]{2,1,0:T(8,128)(2,1)S(1)}, bf16[16,256,128]{2,1,0:T(8,128)(2,1)}, u32[]{:S(2)}) copy-start(bf16[16,256,128]{2,1,0:T(8,128)(2,1)} %all_to_all.19.k_ref) | copy-start | bytes 3145732
  82.5 11.2 %collective-permute-start = (bf16[2,512,128]{2,1,0:T(8,128)(2,1)}, bf16[2,512,128]{2,1,0:T(8,128)(2,1)}, u32[]{:S(2)}, u32[]{:S(2)}) collective-permute-start(bf16[2,512,128]{2,1,0:T(8,128)(2,1)} %bitcast.11), channel_id=1, source_target_pairs={{1,2},{3,4},{5,6},{7,8},{9,10},{11,12},{13,14},{2,1},{4,3},{6,5},{... | collective-permute-start | bytes 786440 | tf_op jit(solution)/shard_map/ppermute | solution.py:232
  92.3 1.6 %collective-permute-start.1 = (bf16[2,512,128]{2,1,0:T(8,128)(2,1)S(1)}, bf16[2,512,128]{2,1,0:T(8,128)(2,1)S(1)}, u32[]{:S(2)}, u32[]{:S(2)}) collective-permute-start(bf16[2,512,128]{2,1,0:T(8,128)(2,1)S(1)} %bitcast.54), channel_id=1, source_target_pairs={{0,1},{1,0},{2,3},{3,2},{4,5},{5,4},{6,7},{7,6},{8,9},{9,8},{10,11... | collective-permute-start | bytes 786440 | tf_op jit(solution)/shard_map/ppermute | solution.py:233
  95.8 0.7 copy-start.5
  103.2 1.0 copy-start.4

commit v18 on v15

--- a/solution.py
+++ b/solution.py
@@ -207,7 +207,7 @@
     state = ()
     previous = None
     for index, (start, stop) in enumerate(zip(edges[:-1], edges[1:])):
-        sending = jnp.take(own_keys[:, start:stop], asked, axis=0)
+        sending = jnp.take(own_keys[:, start:stop], asked, axis=0, mode="clip")
         if previous is not None:
             previous, sending, state = lax.optimization_barrier((previous, sending, state))
         current = lax.all_to_all(sending, "row", split_axis=0, concat_axis=0, tiled=True)

time: 102 us -> 102 us (level)
  blocking collectives: 30.3 us -> 0 us
  waiting for transfers between devices: 13.2 us -> 36.7 us
  starting transfers between devices: 14.6 us -> 20.3 us
  local copies, waits for them, and re-layouts: 7.93 us -> 10.5 us
  other arithmetic: 4.62 us -> 3.39 us
    all_to_all x1 -> x0, blocking collectives: 30.3 us -> none  [on_device(): lax.all_to_all(sending, 'row', split_axis=0, concat_axis=0, tiled=True)]
    all_to_all x1 -> x2, waiting for transfers between devices: 9.35 us -> 32.9 us  [on_device(): lax.all_to_all(sending, 'row', split_axis=0, concat_axis=0, tiled=True)]
    all_to_all x1 -> x2, starting transfers between devices: 4.51 us -> 10.2 us  [on_device(): lax.all_to_all(sending, 'row', split_axis=0, concat_axis=0, tiled=True)]
    gather x2, local copies, waits for them, and re-layouts: 1.5 us -> 3.33 us  [on_device(): sending = jnp.take(own_keys[:, start:stop], asked, axis=0, mode='clip')]
    select_n x2 -> x0, other arithmetic: 1.22 us -> none  [on_device(): sending = jnp.take(own_keys[:, start:stop], asked, axis=0)]
    unnamed x13 -> x15, local copies, waits for them, and re-layouts: 2.44 us -> 3.13 us
  transfers between devices with their start and end apart: 4 -> 5, of which waited for: 3 -> 4; matrix products, arithmetic and copies ran while one was open for 2% -> 4% of each run, Pallas kernels for 20% -> 20%
where the time goes in v18:
time: 102 us; the launch traced here: 101 us
  waiting for transfers between devices  36.7 us (36%)
  Pallas kernels  26.7 us (26%)
  starting transfers between devices  20.3 us (20%)
  local copies, waits for them, and re-layouts  10.5 us (10%)
  matrix products  3.47 us (3%)
  other arithmetic  3.39 us (3%)
    all_to_all x2, waiting for transfers between devices, on_device(): lax.all_to_all(sending, 'row', split_axis=0, concat_axis=0, tiled=True)  32.9 us
    pallas_call x1, Pallas kernels, attend_chunk(): pl.pallas_call(functools.partial(attend_kernel, scale=scale, first=first,...  13.9 us
    pallas_call x2, Pallas kernels, attend_last_half(): pl.pallas_call(kernel, grid_spec=grid_spec, out_shape=jax.ShapeDtypeStruc...  12.8 us
    all_to_all x2, starting transfers between devices, on_device(): lax.all_to_all(sending, 'row', split_axis=0, concat_axis=0, tiled=True)  10.2 us
    all_to_all x1, starting transfers between devices, on_device(): lax.all_to_all(lists_everywhere, 'row', split_axis=0, concat_axis=0, tile...  6.61 us
    all_to_all x1, waiting for transfers between devices, on_device(): lax.all_to_all(lists_everywhere, 'row', split_axis=0, concat_axis=0, tile...  3.49 us
    conv_general_dilated x2, matrix products, native_conv(): lax.conv_general_dilated(rows[None], weights, window_strides=(1, 1), padd...  3.47 us
    ppermute x1, starting transfers between devices, on_device(): across = lax.ppermute(crossing_rows, 'row', links)  3.39 us
  transfers between devices with their start and end apart: 5, of which 4 were waited for; matrix products, arithmetic and copies ran while one was open for 4% of the time, Pallas kernels for 20%

profile of v18, /device:TPU:9, one launch (start us, length us, event | category | flops | bytes accessed | tf_op | source)
XLA Modules:
  0.0 101.3 jit_solution(1648031948371136647)
XLA Ops:
  0.0 0.0 copy-start
  0.0 0.8 broadcast_in_dim.43
  0.8 0.6 broadcast_in_dim.44
  1.4 6.6 %all-to-all-start = ((s32[16,1,36]{2,1,0:T(1,128)}), s32[16,1,36]{2,1,0:T(1,128)S(1)}, u32[]{:S(2)}, u32[]{:S(2)}) async-start(s32[16,1,36]{2,1,0:T(1,128)} %broadcast_in_dim.44), calls=%async_computation | async-start | bytes 16384 | tf_op jit(solution)/shard_map/all_to_all | solution.py:203
  8.0 1.1 %copy.47 = bf16[4,4,128,128]{3,2,1,0:T(8,128)(2,1)S(1)} copy(bf16[4,4,128,128]{3,2,0,1:T(8,128)(2,1)} %bitcast.49) | data formatting | bytes 1048576 | tf_op jit(solution)/shard_map/transpose | solution.py:191
  9.2 3.5 %all-to-all-done = s32[16,1,36]{2,1,0:T(1,128)S(1)} async-done(((s32[16,1,36]{2,1,0:T(1,128)}), s32[16,1,36]{2,1,0:T(1,128)S(1)}, u32[]{:S(2)}, u32[]{:S(2)}) %all-to-all-start) | async-done | bytes 2336 | tf_op jit(solution)/shard_map/all_to_all | solution.py:203
  12.6 0.1 fusion.29
  12.8 1.7 %gather_fusion = bf16[16,256,128]{2,1,0:T(8,128)(2,1)} fusion(bf16[4,256,128]{2,1,0:T(8,128)(2,1)S(1)} %get-tuple-element.20, s32[1024]{0:T(1024)S(1)} %pad_clamp_fusion), kind=kCustom, calls=%fused_computation | custom fusion | bytes 2097216 | tf_op jit(solution)/shard_map/jit(_take)/gather | solution.py:210
  14.5 5.3 %all-to-all-start.1 = ((bf16[16,256,128]{2,1,0:T(8,128)(2,1)}), bf16[16,256,128]{2,1,0:T(8,128)(2,1)S(1)}, u32[]{:S(2)}, u32[]{:S(2)}) async-start(bf16[16,256,128]{2,1,0:T(8,128)(2,1)} %gather_fusion), calls=%async_computation.1 | async-start | bytes 2097152 | tf_op jit(solution)/shard_map/all_to_all | solution.py:213
  19.7 1.6 %gather_fusion.1 = bf16[16,256,128]{2,1,0:T(8,128)(2,1)} fusion(bf16[4,256,128]{2,1,0:T(8,128)(2,1)S(1)} %get-tuple-element.19, s32[1024]{0:T(1024)S(1)} %pad_clamp_fusion), kind=kCustom, calls=%fused_computation.1 | custom fusion | bytes 2097216 | tf_op jit(solution)/shard_map/jit(_take)/gather | solution.py:210
  21.4 0.0 copy-start.3
  21.4 0.0 copy-start.4
  21.4 23.2 %all-to-all-done.1.k_ref = bf16[16,256,128]{2,1,0:T(8,128)(2,1)S(1)} async-done(((bf16[16,256,128]{2,1,0:T(8,128)(2,1)}), bf16[16,256,128]{2,1,0:T(8,128)(2,1)S(1)}, u32[]{:S(2)}, u32[]{:S(2)}) %all-to-all-start.1) | async-done | bytes 1048608 | tf_op jit(solution)/shard_map/all_to_all | solution.py:213
  44.6 0.0 copy-start.1
  44.6 1.0 copy-done.1
  45.6 4.9 %all-to-all-start.2 = ((bf16[16,256,128]{2,1,0:T(8,128)(2,1)}), bf16[16,256,128]{2,1,0:T(8,128)(2,1)S(1)}, u32[]{:S(2)}, u32[]{:S(2)}) async-start(bf16[16,256,128]{2,1,0:T(8,128)(2,1)} %gather_fusion.1), calls=%async_computation.2 | async-start | bytes 2097152 | tf_op jit(solution)/shard_map/all_to_all | solution.py:213
  50.6 0.0 copy-start.2
  50.6 0.0 copy-done.3
  50.6 0.0 copy-done.4
  50.6 0.1 slice_reduce_fusion
  50.7 0.1 fusion.32
  50.9 0.9 copy-done.2
  51.8 13.9 %shard_map.55 = (f32[4,1,512]{2,1,0:T(1,128)S(1)}, f32[4,1,512]{2,1,0:T(1,128)S(1)}, f32[4,512,128]{2,1,0:T(8,128)S(1)}) custom-call(s32[4,9]{1,0:T(4,128)S(1)} %get-tuple-element.22.owner_ref, s32[4]{0:T(128)S(1)} %get-tuple-element.21.count_ref, bf16[4,512,128]{2,1,0:T(8,128)(2,1)S(1)} %bitcast.38, bf16[16,256,128]{2,1,0:T(8,128)(2,1)S(1)} %copy-done.2), custom_call_target="tpu_custom_call" | custom-call | tf_op jit(solution)/shard_map/pallas_call | solution.py:140
  65.7 9.7 %all-to-all-done.2.refs_1_ = bf16[16,256,128]{2,1,0:T(8,128)(2,1)S(1)} async-done(((bf16[16,256,128]{2,1,0:T(8,128)(2,1)}), bf16[16,256,128]{2,1,0:T(8,128)(2,1)S(1)}, u32[]{:S(2)}, u32[]{:S(2)}) %all-to-all-start.2) | async-done | bytes 1048608 | tf_op jit(solution)/shard_map/all_to_all | solution.py:213
  75.4 6.4 %shard_map.56 = bf16[4,256,128]{2,1,0:T(8,128)(2,1)S(1)} custom-call(s32[4,9]{1,0:T(4,128)S(1)} %get-tuple-element.22.owner_ref, s32[4]{0:T(128)S(1)} %get-tuple-element.21.count_ref, s32[1]{0:T(128)} %bitcast.half_ref, bf16[4,512,128]{2,1,0:T(8,128)(2,1)S(1)} %bitcast.39, bf16[16,256,128]{2,1,0:T(8,128)(2,1)S(1)} %all-to-all-done.2.refs_1_, ...), custom_call_target="tpu_custom_call" | custom-call | tf_op jit(solution)/shard_map/pallas_call | solution.py:172
  81.8 0.7 copy.48
  82.5 3.4 %collective-permute-start = (bf16[2,512,128]{2,1,0:T(8,128)(2,1)}, bf16[2,512,128]{2,1,0:T(8,128)(2,1)}, u32[]{:S(2)}, u32[]{:S(2)}) collective-permute-start(bf16[2,512,128]{2,1,0:T(8,128)(2,1)} %bitcast.11), channel_id=1, source_target_pairs={{1,2},{3,4},{5,6},{7,8},{9,10},{11,12},{13,14},{2,1},{4,3},{6,5},{... | collective-permute-start | bytes 786440 | tf_op jit(solution)/shard_map/ppermute | solution.py:232
  85.9 6.4 %shard_map.57 = bf16[4,256,128]{2,1,0:T(8,128)(2,1)S(1)} custom-call(s32[4,9]{1,0:T(4,128)S(1)} %get-tuple-element.22.owner_ref, s32[4]{0:T(128)S(1)} %get-tuple-element.21.count_ref, s32[1]{0:T(128)S(6)} %sub.17.half_ref, bf16[4,512,128]{2,1,0:T(8,128)(2,1)S(1)} %bitcast.40, bf16[16,256,128]{2,1,0:T(8,128)(2,1)S(1)} %all-to-all-done.2.refs_1_, ...), custom_call_target="tpu_custom_call" | custom-call | tf_op jit(solution)/shard_map/pallas_call | solution.py:172
  92.3 0.1 collective-permute-start.1
  92.4 1.1 %maximum_select_fusion = bf16[4,512,128]{2,1,0:T(8,128)(2,1)S(1)} fusion(bf16[2,512,128]{2,1,0:T(8,128)(2,1)S(1)} %bitcast.48, bf16[2,512,128]{2,1,0:T(8,128)(2,1)} %bitcast.11, pred[]{:T(512)S(6)} %eq.13), kind=kLoop, calls=%fused_computation.31 | loop fusion | flops 786432 | bytes 1048577 | tf_op jit(solution)/shard_map/jit(_where)/select_n | solution.py:234
  93.5 0.0 collective-permute-done
  93.5 0.4 collective-permute-done.1
  93.9 1.0 broadcast_select_fusion.1
  94.9 0.1 maximum_bitcast_fusion
  95.0 0.7 copy.56
  95.7 0.1 pad.clone
  95.8 0.0 copy-start.6
  95.8 0.1 copy.52
  96.0 0.0 copy-done
  96.0 0.5 copy-done.6
  96.5 0.0 copy-start.5
  96.5 2.0 %fusion.5 = bf16[6,1,8,65,128]{4,2,3,0,1:T(8,128)(2,1)S(1)} fusion(bf16[3,3,128,128]{3,2,1,0:T(8,128)(2,1)S(1)} %copy-done, bf16[8,1,7,2,128]{4,2,3,0,1:T(8,128)(2,1)S(1)} %slice.22, bf16[8,1,8,65,128]{4,2,3,0,1:T(8,128)(2,1)S(1)} %copy.52, pred[6]{0:T(512)(128)(4,1)S(1)} %or_and_fusion, pred[8,65]{0,1:T(8,128)(4,1)S(1)} %copy-done.6), kind=kOutput, calls=%fused_computation.11 | convolution fusion | flops 925415424 | bytes 2187790 | tf_op jit(solution)/shard_map/conv_general_dilated | solution.py:40
  98.6 0.0 copy-done.5
  98.6 1.4 %fusion.16 = f32[4,8,65,128]{3,1,2,0:T(8,128)S(1)} fusion(bf16[3,3,128,128]{3,2,1,0:T(8,128)(2,1)S(1)} %copy-done.5, bf16[6,1,7,1,128]{4,2,3,0,1:T(8,128)(2,1)S(1)} %get-tuple-element.16, bf16[6,1,7,1,128]{4,2,3,0,1:T(8,128)(2,1)S(1)} %get-tuple-element.15, bf16[6,1,8,65,128]{4,2,3,0,1:T(8,128)(2,1)S(1)} %fusion.5), kind=kOutput, calls=%fused_computation.23 | convolution fusion | flops 617533440 | bytes 2180096 | tf_op jit(solution)/shard_map/conv_general_dilated | solution.py:40
  100.0 0.3 copy.53
  100.3 0.1 slice.25
  100.4 0.9 fusion.13
  (7 shorter events, 0.1 us)
Async XLA Ops:
  0.0 96.0 %copy-start = (bf16[3,3,128,128]{3,2,1,0:T(8,128)(2,1)S(1)}, bf16[3,3,128,128]{3,2,1,0:T(8,128)(2,1)}, u32[]{:S(2)}) copy-start(bf16[3,3,128,128]{3,2,1,0:T(8,128)(2,1)} %param.8) | copy-start | bytes 884740
  1.4 11.2 %all-to-all-start = ((s32[16,1,36]{2,1,0:T(1,128)}), s32[16,1,36]{2,1,0:T(1,128)S(1)}, u32[]{:S(2)}, u32[]{:S(2)}) async-start(s32[16,1,36]{2,1,0:T(1,128)} %broadcast_in_dim.44), calls=%async_computation | async-start | bytes 16384 | tf_op jit(solution)/shard_map/all_to_all | solution.py:203
  14.5 30.1 %all-to-all-start.1 = ((bf16[16,256,128]{2,1,0:T(8,128)(2,1)}), bf16[16,256,128]{2,1,0:T(8,128)(2,1)S(1)}, u32[]{:S(2)}, u32[]{:S(2)}) async-start(bf16[16,256,128]{2,1,0:T(8,128)(2,1)} %gather_fusion), calls=%async_computation.1 | async-start | bytes 2097152 | tf_op jit(solution)/shard_map/all_to_all | solution.py:213
  21.4 29.2 %copy-start.3 = (bf16[4,512,128]{2,1,0:T(8,128)(2,1)S(1)}, bf16[4,512,128]{2,1,0:T(8,128)(2,1)}, u32[]{:S(2)}) copy-start(bf16[4,512,128]{2,1,0:T(8,128)(2,1)} %param.5) | copy-start | bytes 1572868
  21.4 29.2 %copy-start.4 = (s32[4,9]{1,0:T(4,128)S(1)}, s32[4,9]{1,0:T(4,128)}, u32[]{:S(2)}) copy-start(s32[4,9]{1,0:T(4,128)} %param.7) | copy-start | bytes 436
  44.6 1.0 copy-start.1
  45.6 29.8 %all-to-all-start.2 = ((bf16[16,256,128]{2,1,0:T(8,128)(2,1)}), bf16[16,256,128]{2,1,0:T(8,128)(2,1)S(1)}, u32[]{:S(2)}, u32[]{:S(2)}) async-start(bf16[16,256,128]{2,1,0:T(8,128)(2,1)} %gather_fusion.1), calls=%async_computation.2 | async-start | bytes 2097152 | tf_op jit(solution)/shard_map/all_to_all | solution.py:213
  50.6 1.2 %copy-start.2 = (bf16[16,256,128]{2,1,0:T(8,128)(2,1)S(1)}, bf16[16,256,128]{2,1,0:T(8,128)(2,1)}, u32[]{:S(2)}) copy-start(bf16[16,256,128]{2,1,0:T(8,128)(2,1)} %copy-done.1) | copy-start | bytes 3145732
  82.5 11.0 %collective-permute-start = (bf16[2,512,128]{2,1,0:T(8,128)(2,1)}, bf16[2,512,128]{2,1,0:T(8,128)(2,1)}, u32[]{:S(2)}, u32[]{:S(2)}) collective-permute-start(bf16[2,512,128]{2,1,0:T(8,128)(2,1)} %bitcast.11), channel_id=1, source_target_pairs={{1,2},{3,4},{5,6},{7,8},{9,10},{11,12},{13,14},{2,1},{4,3},{6,5},{... | collective-permute-start | bytes 786440 | tf_op jit(solution)/shard_map/ppermute | solution.py:232
  92.3 1.6 %collective-permute-start.1 = (bf16[2,512,128]{2,1,0:T(8,128)(2,1)S(1)}, bf16[2,512,128]{2,1,0:T(8,128)(2,1)S(1)}, u32[]{:S(2)}, u32[]{:S(2)}) collective-permute-start(bf16[2,512,128]{2,1,0:T(8,128)(2,1)S(1)} %bitcast.47), channel_id=1, source_target_pairs={{0,1},{1,0},{2,3},{3,2},{4,5},{5,4},{6,7},{7,6},{8,9},{9,8},{10,11... | collective-permute-start | bytes 786440 | tf_op jit(solution)/shard_map/ppermute | solution.py:233
  95.8 0.7 copy-start.6
  96.5 2.1 %copy-start.5 = (bf16[3,3,128,128]{3,2,1,0:T(8,128)(2,1)S(1)}, bf16[3,3,128,128]{3,2,1,0:T(8,128)(2,1)}, u32[]{:S(2)}) copy-start(bf16[3,3,128,128]{3,2,1,0:T(8,128)(2,1)} %param.9) | copy-start | bytes 884740

commit v19 on v18

--- a/solution.py
+++ b/solution.py
@@ -207,7 +207,10 @@
     state = ()
     previous = None
     for index, (start, stop) in enumerate(zip(edges[:-1], edges[1:])):
-        sending = jnp.take(own_keys[:, start:stop], asked, axis=0, mode="clip")
+        part = own_keys[:, start:stop]
+        sending = jnp.broadcast_to(part[0][None], (owners,) + part.shape[1:])
+        for local in range(1, per_device):
+            sending = jnp.where((asked == local)[:, None, None], part[local][None], sending)
         if previous is not None:
             previous, sending, state = lax.optimization_barrier((previous, sending, state))
         current = lax.all_to_all(sending, "row", split_axis=0, concat_axis=0, tiled=True)

time: 102 us -> 101 us (level)
  blocking collectives: 0 us -> 30.4 us
  waiting for transfers between devices: 36.7 us -> 13.2 us
  starting transfers between devices: 20.3 us -> 14.6 us
  local copies, waits for them, and re-layouts: 10.5 us -> 6.44 us
  other arithmetic: 3.39 us -> 4.85 us
    all_to_all x0 -> x1, blocking collectives: none -> 30.4 us  [on_device(): lax.all_to_all(sending, 'row', split_axis=0, concat_axis=0, tiled=True)]
    all_to_all x2 -> x1, waiting for transfers between devices: 32.9 us -> 9.35 us  [on_device(): lax.all_to_all(sending, 'row', split_axis=0, concat_axis=0, tiled=True)]
    all_to_all x2 -> x1, starting transfers between devices: 10.2 us -> 4.51 us  [on_device(): lax.all_to_all(sending, 'row', split_axis=0, concat_axis=0, tiled=True)]
    gather x2 -> x0, local copies, waits for them, and re-layouts: 3.33 us -> none  [on_device(): sending = jnp.take(own_keys[:, start:stop], asked, axis=0, mode='clip')]
    select_n x0 -> x1, other arithmetic: none -> 1.46 us  [on_device(): jnp.where((asked == local)[:, None, None], part[local][None], sending)]
    unnamed x15 -> x13, local copies, waits for them, and re-layouts: 3.13 us -> 2.44 us
  transfers between devices with their start and end apart: 5 -> 4, of which waited for: 4 -> 3; matrix products, arithmetic and copies ran while one was open for 4% -> 3% of each run, Pallas kernels for 20% -> 20%
where the time goes in v19:
time: 101 us; the launch traced here: 99.8 us
  blocking collectives  30.4 us (30%)
  Pallas kernels  26.7 us (26%)
  starting transfers between devices  14.6 us (14%)
  waiting for transfers between devices  13.2 us (13%)
  local copies, waits for them, and re-layouts  6.44 us (6%)
  other arithmetic  4.85 us (5%)
  matrix products  3.47 us (3%)
    all_to_all x1, blocking collectives, on_device(): lax.all_to_all(sending, 'row', split_axis=0, concat_axis=0, tiled=True)  30.4 us
    pallas_call x1, Pallas kernels, attend_chunk(): pl.pallas_call(functools.partial(attend_kernel, scale=scale, first=first,...  13.9 us
    pallas_call x2, Pallas kernels, attend_last_half(): pl.pallas_call(kernel, grid_spec=grid_spec, out_shape=jax.ShapeDtypeStruc...  12.7 us
    all_to_all x1, waiting for transfers between devices, on_device(): lax.all_to_all(sending, 'row', split_axis=0, concat_axis=0, tiled=True)  9.35 us
    all_to_all x1, starting transfers between devices, on_device(): lax.all_to_all(lists_everywhere, 'row', split_axis=0, concat_axis=0, tile...  6.61 us
    all_to_all x1, starting transfers between devices, on_device(): lax.all_to_all(sending, 'row', split_axis=0, concat_axis=0, tiled=True)  4.51 us
    all_to_all x1, waiting for transfers between devices, on_device(): lax.all_to_all(lists_everywhere, 'row', split_axis=0, concat_axis=0, tile...  3.49 us
    conv_general_dilated x2, matrix products, native_conv(): lax.conv_general_dilated(rows[None], weights, window_strides=(1, 1), padd...  3.47 us
  transfers between devices with their start and end apart: 4, of which 3 were waited for; matrix products, arithmetic and copies ran while one was open for 3% of the time, Pallas kernels for 20%

profile of v19, /device:TPU:9, one launch (start us, length us, event | category | flops | bytes accessed | tf_op | source)
XLA Modules:
  0.0 99.8 jit_solution(8985163226870257006)
XLA Ops:
  0.0 0.0 copy-start
  0.0 0.8 broadcast_in_dim.130
  0.8 0.6 broadcast_in_dim.131
  1.4 6.6 %all-to-all-start = ((s32[16,1,36]{2,1,0:T(1,128)}), s32[16,1,36]{2,1,0:T(1,128)S(1)}, u32[]{:S(2)}, u32[]{:S(2)}) async-start(s32[16,1,36]{2,1,0:T(1,128)} %broadcast_in_dim.131), calls=%async_computation | async-start | bytes 16384 | tf_op jit(solution)/shard_map/all_to_all | solution.py:203
  8.0 1.1 %copy.39 = bf16[4,4,128,128]{3,2,1,0:T(8,128)(2,1)S(1)} copy(bf16[4,4,128,128]{3,2,0,1:T(8,128)(2,1)} %bitcast.65) | data formatting | bytes 1048576 | tf_op jit(solution)/shard_map/transpose | solution.py:191
  9.2 3.5 %all-to-all-done = s32[16,1,36]{2,1,0:T(1,128)S(1)} async-done(((s32[16,1,36]{2,1,0:T(1,128)}), s32[16,1,36]{2,1,0:T(1,128)S(1)}, u32[]{:S(2)}, u32[]{:S(2)}) %all-to-all-start) | async-done | bytes 2336 | tf_op jit(solution)/shard_map/all_to_all | solution.py:203
  12.6 0.1 fusion.29
  12.8 1.5 %select_select_fusion = (bf16[16,256,128]{2,1,0:T(8,128)(2,1)}, bf16[16,256,128]{2,1,0:T(8,128)(2,1)S(1)}) fusion(pred[16]{0:T(512)(128)(4,1)S(1)} %get-tuple-element.32, pred[16]{0:T(512)(128)(4,1)S(1)} %get-tuple-element.33, pred[16]{0:T(512)(128)(4,1)S(1)} %get-tuple-element.31, bf16[256,128]{1,0:T(8,128)(2,1)S(1)} %get-tuple-element.20, ...), kind=kLoop, calls=%fused_computation.19 | loop fusion | flops 3145728 | bytes 2621488 | tf_op jit(solution)/shard_map/jit(_where)/select_n | solution.py:213
  14.2 30.4 %all_to_all.19.k_ref = bf16[16,256,128]{2,1,0:T(8,128)(2,1)} all-to-all(bf16[16,256,128]{2,1,0:T(8,128)(2,1)S(1)} %get-tuple-element.30), channel_id=1, replica_groups=mesh['pairs'=2,'row'=16] {'row'}, dimensions={0} | all-to-all | bytes 2097152 | tf_op jit(solution)/shard_map/all_to_all | solution.py:216
  44.6 0.0 copy-start.2
  44.6 0.0 copy-start.3
  44.6 4.5 %all-to-all-start.2 = ((bf16[16,256,128]{2,1,0:T(8,128)(2,1)}), bf16[16,256,128]{2,1,0:T(8,128)(2,1)S(1)}, u32[]{:S(2)}, u32[]{:S(2)}) async-start(bf16[16,256,128]{2,1,0:T(8,128)(2,1)} %get-tuple-element.10), calls=%async_computation.2 | async-start | bytes 2097152 | tf_op jit(solution)/shard_map/all_to_all | solution.py:216
  49.1 0.0 copy-done.2
  49.2 0.0 copy-done.3
  49.2 0.1 slice_reduce_fusion
  49.3 0.1 fusion.32
  49.4 0.0 copy-start.1
  49.4 1.2 %copy-done.1 = bf16[16,256,128]{2,1,0:T(8,128)(2,1)S(1)} copy-done((bf16[16,256,128]{2,1,0:T(8,128)(2,1)S(1)}, bf16[16,256,128]{2,1,0:T(8,128)(2,1)}, u32[]{:S(2)}) %copy-start.1) | copy-done | bytes 1048600
  50.7 13.9 %shard_map.55 = (f32[4,1,512]{2,1,0:T(1,128)S(1)}, f32[4,1,512]{2,1,0:T(1,128)S(1)}, f32[4,512,128]{2,1,0:T(8,128)S(1)}) custom-call(s32[4,9]{1,0:T(4,128)S(1)} %get-tuple-element.28.owner_ref, s32[4]{0:T(128)S(1)} %get-tuple-element.27.count_ref, bf16[4,512,128]{2,1,0:T(8,128)(2,1)S(1)} %bitcast.54, bf16[16,256,128]{2,1,0:T(8,128)(2,1)S(1)} %copy-done.1), custom_call_target="tpu_custom_call" | custom-call | tf_op jit(solution)/shard_map/pallas_call | solution.py:140
  64.6 9.4 %all-to-all-done.2.refs_1_ = bf16[16,256,128]{2,1,0:T(8,128)(2,1)S(1)} async-done(((bf16[16,256,128]{2,1,0:T(8,128)(2,1)}), bf16[16,256,128]{2,1,0:T(8,128)(2,1)S(1)}, u32[]{:S(2)}, u32[]{:S(2)}) %all-to-all-start.2) | async-done | bytes 1048608 | tf_op jit(solution)/shard_map/all_to_all | solution.py:216
  74.0 6.4 %shard_map.56 = bf16[4,256,128]{2,1,0:T(8,128)(2,1)S(1)} custom-call(s32[4,9]{1,0:T(4,128)S(1)} %get-tuple-element.28.owner_ref, s32[4]{0:T(128)S(1)} %get-tuple-element.27.count_ref, s32[1]{0:T(128)} %bitcast.half_ref, bf16[4,512,128]{2,1,0:T(8,128)(2,1)S(1)} %bitcast.55, bf16[16,256,128]{2,1,0:T(8,128)(2,1)S(1)} %all-to-all-done.2.refs_1_, ...), custom_call_target="tpu_custom_call" | custom-call | tf_op jit(solution)/shard_map/pallas_call | solution.py:172
  80.3 0.7 copy.40
  81.1 3.4 %collective-permute-start = (bf16[2,512,128]{2,1,0:T(8,128)(2,1)}, bf16[2,512,128]{2,1,0:T(8,128)(2,1)}, u32[]{:S(2)}, u32[]{:S(2)}) collective-permute-start(bf16[2,512,128]{2,1,0:T(8,128)(2,1)} %bitcast.19), channel_id=1, source_target_pairs={{1,2},{3,4},{5,6},{7,8},{9,10},{11,12},{13,14},{2,1},{4,3},{6,5},{... | collective-permute-start | bytes 786440 | tf_op jit(solution)/shard_map/ppermute | solution.py:235
  84.5 6.4 %shard_map.57 = bf16[4,256,128]{2,1,0:T(8,128)(2,1)S(1)} custom-call(s32[4,9]{1,0:T(4,128)S(1)} %get-tuple-element.28.owner_ref, s32[4]{0:T(128)S(1)} %get-tuple-element.27.count_ref, s32[1]{0:T(128)S(6)} %sub.17.half_ref, bf16[4,512,128]{2,1,0:T(8,128)(2,1)S(1)} %bitcast.56, bf16[16,256,128]{2,1,0:T(8,128)(2,1)S(1)} %all-to-all-done.2.refs_1_, ...), custom_call_target="tpu_custom_call" | custom-call | tf_op jit(solution)/shard_map/pallas_call | solution.py:172
  90.9 0.1 collective-permute-start.1
  91.0 1.1 %maximum_select_fusion = bf16[4,512,128]{2,1,0:T(8,128)(2,1)S(1)} fusion(bf16[2,512,128]{2,1,0:T(8,128)(2,1)S(1)} %bitcast.64, bf16[2,512,128]{2,1,0:T(8,128)(2,1)} %bitcast.19, pred[]{:T(512)S(6)} %eq.37), kind=kLoop, calls=%fused_computation.31 | loop fusion | flops 786432 | bytes 1048577 | tf_op jit(solution)/shard_map/jit(_where)/select_n | solution.py:237
  92.1 0.0 collective-permute-done
  92.1 0.4 collective-permute-done.1
  92.5 1.0 broadcast_select_fusion.1
  93.5 0.1 maximum_bitcast_fusion
  93.6 0.7 copy.48
  94.3 0.1 pad.clone
  94.4 0.0 copy-start.5
  94.4 0.1 copy.44
  94.5 0.0 copy-done
  94.6 0.5 copy-done.5
  95.1 0.0 copy-start.4
  95.1 2.0 %fusion.5 = bf16[6,1,8,65,128]{4,2,3,0,1:T(8,128)(2,1)S(1)} fusion(bf16[3,3,128,128]{3,2,1,0:T(8,128)(2,1)S(1)} %copy-done, bf16[8,1,7,2,128]{4,2,3,0,1:T(8,128)(2,1)S(1)} %slice.58, bf16[8,1,8,65,128]{4,2,3,0,1:T(8,128)(2,1)S(1)} %copy.44, pred[6]{0:T(512)(128)(4,1)S(1)} %or_and_fusion, pred[8,65]{0,1:T(8,128)(4,1)S(1)} %copy-done.5), kind=kOutput, calls=%fused_computation.9 | convolution fusion | flops 925415424 | bytes 2187790 | tf_op jit(solution)/shard_map/conv_general_dilated | solution.py:40
  97.1 0.0 copy-done.4
  97.2 1.4 %fusion.16 = f32[4,8,65,128]{3,1,2,0:T(8,128)S(1)} fusion(bf16[3,3,128,128]{3,2,1,0:T(8,128)(2,1)S(1)} %copy-done.4, bf16[6,1,7,1,128]{4,2,3,0,1:T(8,128)(2,1)S(1)} %get-tuple-element.16, bf16[6,1,7,1,128]{4,2,3,0,1:T(8,128)(2,1)S(1)} %get-tuple-element.15, bf16[6,1,8,65,128]{4,2,3,0,1:T(8,128)(2,1)S(1)} %fusion.5), kind=kOutput, calls=%fused_computation.23 | convolution fusion | flops 617533440 | bytes 2180096 | tf_op jit(solution)/shard_map/conv_general_dilated | solution.py:40
  98.6 0.3 copy.45
  98.9 0.1 slice.61
  98.9 0.9 fusion.13
  (7 shorter events, 0.1 us)
Async XLA Ops:
  0.0 94.5 %copy-start = (bf16[3,3,128,128]{3,2,1,0:T(8,128)(2,1)S(1)}, bf16[3,3,128,128]{3,2,1,0:T(8,128)(2,1)}, u32[]{:S(2)}) copy-start(bf16[3,3,128,128]{3,2,1,0:T(8,128)(2,1)} %param.8) | copy-start | bytes 884740
  1.4 11.2 %all-to-all-start = ((s32[16,1,36]{2,1,0:T(1,128)}), s32[16,1,36]{2,1,0:T(1,128)S(1)}, u32[]{:S(2)}, u32[]{:S(2)}) async-start(s32[16,1,36]{2,1,0:T(1,128)} %broadcast_in_dim.131), calls=%async_computation | async-start | bytes 16384 | tf_op jit(solution)/shard_map/all_to_all | solution.py:203
  44.6 4.5 %copy-start.2 = (bf16[4,512,128]{2,1,0:T(8,128)(2,1)S(1)}, bf16[4,512,128]{2,1,0:T(8,128)(2,1)}, u32[]{:S(2)}) copy-start(bf16[4,512,128]{2,1,0:T(8,128)(2,1)} %param.5) | copy-start | bytes 1572868
  44.6 4.6 %copy-start.3 = (s32[4,9]{1,0:T(4,128)S(1)}, s32[4,9]{1,0:T(4,128)}, u32[]{:S(2)}) copy-start(s32[4,9]{1,0:T(4,128)} %param.7) | copy-start | bytes 436
  44.6 29.4 %all-to-all-start.2 = ((bf16[16,256,128]{2,1,0:T(8,128)(2,1)}), bf16[16,256,128]{2,1,0:T(8,128)(2,1)S(1)}, u32[]{:S(2)}, u32[]{:S(2)}) async-start(bf16[16,256,128]{2,1,0:T(8,128)(2,1)} %get-tuple-element.10), calls=%async_computation.2 | async-start | bytes 2097152 | tf_op jit(solution)/shard_map/all_to_all | solution.py:216
  49.4 1.2 %copy-start.1 = (bf16[16,256,128]{2,1,0:T(8,128)(2,1)S(1)}, bf16[16,256,128]{2,1,0:T(8,128)(2,1)}, u32[]{:S(2)}) copy-start(bf16[16,256,128]{2,1,0:T(8,128)(2,1)} %all_to_all.19.k_ref) | copy-start | bytes 3145732
  81.1 11.0 %collective-permute-start = (bf16[2,512,128]{2,1,0:T(8,128)(2,1)}, bf16[2,512,128]{2,1,0:T(8,128)(2,1)}, u32[]{:S(2)}, u32[]{:S(2)}) collective-permute-start(bf16[2,512,128]{2,1,0:T(8,128)(2,1)} %bitcast.19), channel_id=1, source_target_pairs={{1,2},{3,4},{5,6},{7,8},{9,10},{11,12},{13,14},{2,1},{4,3},{6,5},{... | collective-permute-start | bytes 786440 | tf_op jit(solution)/shard_map/ppermute | solution.py:235
  90.9 1.6 %collective-permute-start.1 = (bf16[2,512,128]{2,1,0:T(8,128)(2,1)S(1)}, bf16[2,512,128]{2,1,0:T(8,128)(2,1)S(1)}, u32[]{:S(2)}, u32[]{:S(2)}) collective-permute-start(bf16[2,512,128]{2,1,0:T(8,128)(2,1)S(1)} %bitcast.63), channel_id=1, source_target_pairs={{0,1},{1,0},{2,3},{3,2},{4,5},{5,4},{6,7},{7,6},{8,9},{9,8},{10,11... | collective-permute-start | bytes 786440 | tf_op jit(solution)/shard_map/ppermute | solution.py:236
  94.4 0.7 copy-start.5
  95.1 2.1 %copy-start.4 = (bf16[3,3,128,128]{3,2,1,0:T(8,128)(2,1)S(1)}, bf16[3,3,128,128]{3,2,1,0:T(8,128)(2,1)}, u32[]{:S(2)}) copy-start(bf16[3,3,128,128]{3,2,1,0:T(8,128)(2,1)} %param.9) | copy-start | bytes 884740

commit v20 on v19

--- a/solution.py
+++ b/solution.py
@@ -208,9 +208,12 @@
     previous = None
     for index, (start, stop) in enumerate(zip(edges[:-1], edges[1:])):
         part = own_keys[:, start:stop]
+        picks = asked
+        if previous is not None:
+            part, picks = lax.optimization_barrier((part, picks))
         sending = jnp.broadcast_to(part[0][None], (owners,) + part.shape[1:])
         for local in range(1, per_device):
-            sending = jnp.where((asked == local)[:, None, None], part[local][None], sending)
+            sending = jnp.where((picks == local)[:, None, None], part[local][None], sending)
         if previous is not None:
             previous, sending, state = lax.optimization_barrier((previous, sending, state))
         current = lax.all_to_all(sending, "row", split_axis=0, concat_axis=0, tiled=True)

time: 101 us -> 102 us (level)
  blocking collectives: 30.4 us -> 0 us
  waiting for transfers between devices: 13.2 us -> 37.1 us
  starting transfers between devices: 14.6 us -> 20.3 us
  other arithmetic: 4.85 us -> 5.95 us
    all_to_all x1 -> x0, blocking collectives: 30.4 us -> none  [on_device(): lax.all_to_all(sending, 'row', split_axis=0, concat_axis=0, tiled=True)]
    all_to_all x1 -> x2, waiting for transfers between devices: 9.35 us -> 33.2 us  [on_device(): lax.all_to_all(sending, 'row', split_axis=0, concat_axis=0, tiled=True)]
    all_to_all x1 -> x2, starting transfers between devices: 4.51 us -> 10.2 us  [on_device(): lax.all_to_all(sending, 'row', split_axis=0, concat_axis=0, tiled=True)]
    select_n x1 -> x2, other arithmetic: 1.46 us -> 2.56 us  [on_device(): jnp.where((picks == local)[:, None, None], part[local][None], sending)]
    unnamed x13 -> x15, local copies, waits for them, and re-layouts: 2.44 us -> 3.13 us
  transfers between devices with their start and end apart: 4 -> 5, of which waited for: 3 -> 4; matrix products, arithmetic and copies ran while one was open for 3% -> 4% of each run, Pallas kernels for 20% -> 20%
where the time goes in v20:
time: 102 us; the launch traced here: 101 us
  waiting for transfers between devices  37.1 us (36%)
  Pallas kernels  26.7 us (26%)
  starting transfers between devices  20.3 us (20%)
  local copies, waits for them, and re-layouts  7.14 us (7%)
  other arithmetic  5.95 us (6%)
  matrix products  3.47 us (3%)
    all_to_all x2, waiting for transfers between devices, on_device(): lax.all_to_all(sending, 'row', split_axis=0, concat_axis=0, tiled=True)  33.2 us
    pallas_call x1, Pallas kernels, attend_chunk(): pl.pallas_call(functools.partial(attend_kernel, scale=scale, first=first,...  13.9 us
    pallas_call x2, Pallas kernels, attend_last_half(): pl.pallas_call(kernel, grid_spec=grid_spec, out_shape=jax.ShapeDtypeStruc...  12.8 us
    all_to_all x2, starting transfers between devices, on_device(): lax.all_to_all(sending, 'row', split_axis=0, concat_axis=0, tiled=True)  10.2 us
    all_to_all x1, starting transfers between devices, on_device(): lax.all_to_all(lists_everywhere, 'row', split_axis=0, concat_axis=0, tile...  6.61 us
    all_to_all x1, waiting for transfers between devices, on_device(): lax.all_to_all(lists_everywhere, 'row', split_axis=0, concat_axis=0, tile...  3.5 us
    conv_general_dilated x2, matrix products, native_conv(): lax.conv_general_dilated(rows[None], weights, window_strides=(1, 1), padd...  3.47 us
    ppermute x1, starting transfers between devices, on_device(): across = lax.ppermute(crossing_rows, 'row', links)  3.39 us
  transfers between devices with their start and end apart: 5, of which 4 were waited for; matrix products, arithmetic and copies ran while one was open for 4% of the time, Pallas kernels for 20%

profile of v20, /device:TPU:9, one launch (start us, length us, event | category | flops | bytes accessed | tf_op | source)
XLA Modules:
  0.0 100.9 jit_solution(14501355083586774052)
XLA Ops:
  0.0 0.0 copy-start
  0.0 0.8 broadcast_in_dim.136
  0.8 0.6 broadcast_in_dim.137
  1.4 6.6 %all-to-all-start = ((s32[16,1,36]{2,1,0:T(1,128)}), s32[16,1,36]{2,1,0:T(1,128)S(1)}, u32[]{:S(2)}, u32[]{:S(2)}) async-start(s32[16,1,36]{2,1,0:T(1,128)} %broadcast_in_dim.137), calls=%async_computation | async-start | bytes 16384 | tf_op jit(solution)/shard_map/all_to_all | solution.py:203
  8.0 1.1 %copy.39 = bf16[4,4,128,128]{3,2,1,0:T(8,128)(2,1)S(1)} copy(bf16[4,4,128,128]{3,2,0,1:T(8,128)(2,1)} %bitcast.66) | data formatting | bytes 1048576 | tf_op jit(solution)/shard_map/transpose | solution.py:191
  9.1 3.5 %all-to-all-done = s32[16,1,36]{2,1,0:T(1,128)S(1)} async-done(((s32[16,1,36]{2,1,0:T(1,128)}), s32[16,1,36]{2,1,0:T(1,128)S(1)}, u32[]{:S(2)}, u32[]{:S(2)}) %all-to-all-start) | async-done | bytes 2336 | tf_op jit(solution)/shard_map/all_to_all | solution.py:203
  12.6 0.1 fusion.29
  12.8 1.3 %select_select_fusion.1 = bf16[16,256,128]{2,1,0:T(8,128)(2,1)} fusion(pred[16]{0:T(512)(128)(4,1)S(1)} %get-tuple-element.37, pred[16]{0:T(512)(128)(4,1)S(1)} %get-tuple-element.38, pred[16]{0:T(512)(128)(4,1)S(1)} %get-tuple-element.36, bf16[256,128]{1,0:T(8,128)(2,1)S(1)} %get-tuple-element.24, bf16[256,128]{1,0:T(8,128)(2,1)S(1)} %get-tuple-element.25, ...), kind=kLoop, calls=%fused_computation.20 | loop fusion | flops 1572864 | bytes 1310768 | tf_op jit(solution)/shard_map/jit(_where)/select_n | solution.py:216
  14.1 5.3 %all-to-all-start.1 = ((bf16[16,256,128]{2,1,0:T(8,128)(2,1)}), bf16[16,256,128]{2,1,0:T(8,128)(2,1)S(1)}, u32[]{:S(2)}, u32[]{:S(2)}) async-start(bf16[16,256,128]{2,1,0:T(8,128)(2,1)} %select_select_fusion.1), calls=%async_computation.1 | async-start | bytes 2097152 | tf_op jit(solution)/shard_map/all_to_all | solution.py:219
  19.4 1.3 %select_select_fusion = bf16[16,256,128]{2,1,0:T(8,128)(2,1)} fusion(pred[16]{0:T(512)(128)(4,1)S(1)} %get-tuple-element.34, pred[16]{0:T(512)(128)(4,1)S(1)} %get-tuple-element.35, pred[16]{0:T(512)(128)(4,1)S(1)} %get-tuple-element.33, bf16[256,128]{1,0:T(8,128)(2,1)S(1)} %get-tuple-element.28, bf16[256,128]{1,0:T(8,128)(2,1)S(1)} %get-tuple-element.29, ...), kind=kLoop, calls=%fused_computation.19 | loop fusion | flops 1572864 | bytes 1310768 | tf_op jit(solution)/shard_map/jit(_where)/select_n | solution.py:216
  20.7 0.0 copy-start.3
  20.7 0.0 copy-start.4
  20.7 23.5 %all-to-all-done.1.k_ref = bf16[16,256,128]{2,1,0:T(8,128)(2,1)S(1)} async-done(((bf16[16,256,128]{2,1,0:T(8,128)(2,1)}), bf16[16,256,128]{2,1,0:T(8,128)(2,1)S(1)}, u32[]{:S(2)}, u32[]{:S(2)}) %all-to-all-start.1) | async-done | bytes 1048608 | tf_op jit(solution)/shard_map/all_to_all | solution.py:219
  44.2 0.0 copy-start.1
  44.2 1.0 copy-done.1
  45.2 4.9 %all-to-all-start.2 = ((bf16[16,256,128]{2,1,0:T(8,128)(2,1)}), bf16[16,256,128]{2,1,0:T(8,128)(2,1)S(1)}, u32[]{:S(2)}, u32[]{:S(2)}) async-start(bf16[16,256,128]{2,1,0:T(8,128)(2,1)} %select_select_fusion), calls=%async_computation.2 | async-start | bytes 2097152 | tf_op jit(solution)/shard_map/all_to_all | solution.py:219
  50.2 0.0 copy-start.2
  50.2 0.0 copy-done.3
  50.2 0.0 copy-done.4
  50.2 0.1 slice_reduce_fusion
  50.3 0.1 fusion.32
  50.5 0.9 copy-done.2
  51.4 13.9 %shard_map.55 = (f32[4,1,512]{2,1,0:T(1,128)S(1)}, f32[4,1,512]{2,1,0:T(1,128)S(1)}, f32[4,512,128]{2,1,0:T(8,128)S(1)}) custom-call(s32[4,9]{1,0:T(4,128)S(1)} %get-tuple-element.32.owner_ref, s32[4]{0:T(128)S(1)} %get-tuple-element.31.count_ref, bf16[4,512,128]{2,1,0:T(8,128)(2,1)S(1)} %bitcast.54, bf16[16,256,128]{2,1,0:T(8,128)(2,1)S(1)} %copy-done.2), custom_call_target="tpu_custom_call" | custom-call | tf_op jit(solution)/shard_map/pallas_call | solution.py:140
  65.3 9.7 %all-to-all-done.2.refs_1_ = bf16[16,256,128]{2,1,0:T(8,128)(2,1)S(1)} async-done(((bf16[16,256,128]{2,1,0:T(8,128)(2,1)}), bf16[16,256,128]{2,1,0:T(8,128)(2,1)S(1)}, u32[]{:S(2)}, u32[]{:S(2)}) %all-to-all-start.2) | async-done | bytes 1048608 | tf_op jit(solution)/shard_map/all_to_all | solution.py:219
  75.0 6.4 %shard_map.56 = bf16[4,256,128]{2,1,0:T(8,128)(2,1)S(1)} custom-call(s32[4,9]{1,0:T(4,128)S(1)} %get-tuple-element.32.owner_ref, s32[4]{0:T(128)S(1)} %get-tuple-element.31.count_ref, s32[1]{0:T(128)} %bitcast.half_ref, bf16[4,512,128]{2,1,0:T(8,128)(2,1)S(1)} %bitcast.55, bf16[16,256,128]{2,1,0:T(8,128)(2,1)S(1)} %all-to-all-done.2.refs_1_, ...), custom_call_target="tpu_custom_call" | custom-call | tf_op jit(solution)/shard_map/pallas_call | solution.py:172
  81.4 0.7 copy.40
  82.1 3.4 %collective-permute-start = (bf16[2,512,128]{2,1,0:T(8,128)(2,1)}, bf16[2,512,128]{2,1,0:T(8,128)(2,1)}, u32[]{:S(2)}, u32[]{:S(2)}) collective-permute-start(bf16[2,512,128]{2,1,0:T(8,128)(2,1)} %bitcast.19), channel_id=1, source_target_pairs={{1,2},{3,4},{5,6},{7,8},{9,10},{11,12},{13,14},{2,1},{4,3},{6,5},{... | collective-permute-start | bytes 786440 | tf_op jit(solution)/shard_map/ppermute | solution.py:238
  85.5 6.4 %shard_map.57 = bf16[4,256,128]{2,1,0:T(8,128)(2,1)S(1)} custom-call(s32[4,9]{1,0:T(4,128)S(1)} %get-tuple-element.32.owner_ref, s32[4]{0:T(128)S(1)} %get-tuple-element.31.count_ref, s32[1]{0:T(128)S(6)} %sub.17.half_ref, bf16[4,512,128]{2,1,0:T(8,128)(2,1)S(1)} %bitcast.56, bf16[16,256,128]{2,1,0:T(8,128)(2,1)S(1)} %all-to-all-done.2.refs_1_, ...), custom_call_target="tpu_custom_call" | custom-call | tf_op jit(solution)/shard_map/pallas_call | solution.py:172
  91.9 0.1 collective-permute-start.1
  92.0 1.1 %maximum_select_fusion = bf16[4,512,128]{2,1,0:T(8,128)(2,1)S(1)} fusion(bf16[2,512,128]{2,1,0:T(8,128)(2,1)S(1)} %bitcast.65, bf16[2,512,128]{2,1,0:T(8,128)(2,1)} %bitcast.19, pred[]{:T(512)S(6)} %eq.43), kind=kLoop, calls=%fused_computation.31 | loop fusion | flops 786432 | bytes 1048577 | tf_op jit(solution)/shard_map/jit(_where)/select_n | solution.py:240
  93.1 0.0 collective-permute-done
  93.2 0.4 collective-permute-done.1
  93.5 1.0 broadcast_select_fusion.1
  94.5 0.1 maximum_bitcast_fusion
  94.7 0.7 copy.48
  95.3 0.1 pad.clone
  95.4 0.0 copy-start.6
  95.4 0.1 copy.44
  95.6 0.0 copy-done
  95.6 0.5 copy-done.6
  96.1 0.0 copy-start.5
  96.1 2.0 %fusion.5 = bf16[6,1,8,65,128]{4,2,3,0,1:T(8,128)(2,1)S(1)} fusion(bf16[3,3,128,128]{3,2,1,0:T(8,128)(2,1)S(1)} %copy-done, bf16[8,1,7,2,128]{4,2,3,0,1:T(8,128)(2,1)S(1)} %slice.54, bf16[8,1,8,65,128]{4,2,3,0,1:T(8,128)(2,1)S(1)} %copy.44, pred[6]{0:T(512)(128)(4,1)S(1)} %or_and_fusion, pred[8,65]{0,1:T(8,128)(4,1)S(1)} %copy-done.6), kind=kOutput, calls=%fused_computation.9 | convolution fusion | flops 925415424 | bytes 2187790 | tf_op jit(solution)/shard_map/conv_general_dilated | solution.py:40
  98.2 0.0 copy-done.5
  98.2 1.4 %fusion.16 = f32[4,8,65,128]{3,1,2,0:T(8,128)S(1)} fusion(bf16[3,3,128,128]{3,2,1,0:T(8,128)(2,1)S(1)} %copy-done.5, bf16[6,1,7,1,128]{4,2,3,0,1:T(8,128)(2,1)S(1)} %get-tuple-element.20, bf16[6,1,7,1,128]{4,2,3,0,1:T(8,128)(2,1)S(1)} %get-tuple-element.19, bf16[6,1,8,65,128]{4,2,3,0,1:T(8,128)(2,1)S(1)} %fusion.5), kind=kOutput, calls=%fused_computation.23 | convolution fusion | flops 617533440 | bytes 2180096 | tf_op jit(solution)/shard_map/conv_general_dilated | solution.py:40
  99.6 0.3 copy.45
  99.9 0.1 slice.57
  100.0 0.9 fusion.13
  (10 shorter events, 0.2 us)
Async XLA Ops:
  0.0 95.6 %copy-start = (bf16[3,3,128,128]{3,2,1,0:T(8,128)(2,1)S(1)}, bf16[3,3,128,128]{3,2,1,0:T(8,128)(2,1)}, u32[]{:S(2)}) copy-start(bf16[3,3,128,128]{3,2,1,0:T(8,128)(2,1)} %param.8) | copy-start | bytes 884740
  1.4 11.2 %all-to-all-start = ((s32[16,1,36]{2,1,0:T(1,128)}), s32[16,1,36]{2,1,0:T(1,128)S(1)}, u32[]{:S(2)}, u32[]{:S(2)}) async-start(s32[16,1,36]{2,1,0:T(1,128)} %broadcast_in_dim.137), calls=%async_computation | async-start | bytes 16384 | tf_op jit(solution)/shard_map/all_to_all | solution.py:203
  14.1 30.1 %all-to-all-start.1 = ((bf16[16,256,128]{2,1,0:T(8,128)(2,1)}), bf16[16,256,128]{2,1,0:T(8,128)(2,1)S(1)}, u32[]{:S(2)}, u32[]{:S(2)}) async-start(bf16[16,256,128]{2,1,0:T(8,128)(2,1)} %select_select_fusion.1), calls=%async_computation.1 | async-start | bytes 2097152 | tf_op jit(solution)/shard_map/all_to_all | solution.py:219
  20.7 29.5 %copy-start.3 = (bf16[4,512,128]{2,1,0:T(8,128)(2,1)S(1)}, bf16[4,512,128]{2,1,0:T(8,128)(2,1)}, u32[]{:S(2)}) copy-start(bf16[4,512,128]{2,1,0:T(8,128)(2,1)} %param.5) | copy-start | bytes 1572868
  20.7 29.5 %copy-start.4 = (s32[4,9]{1,0:T(4,128)S(1)}, s32[4,9]{1,0:T(4,128)}, u32[]{:S(2)}) copy-start(s32[4,9]{1,0:T(4,128)} %param.7) | copy-start | bytes 436
  44.2 1.0 copy-start.1
  45.2 29.8 %all-to-all-start.2 = ((bf16[16,256,128]{2,1,0:T(8,128)(2,1)}), bf16[16,256,128]{2,1,0:T(8,128)(2,1)S(1)}, u32[]{:S(2)}, u32[]{:S(2)}) async-start(bf16[16,256,128]{2,1,0:T(8,128)(2,1)} %select_select_fusion), calls=%async_computation.2 | async-start | bytes 2097152 | tf_op jit(solution)/shard_map/all_to_all | solution.py:219
  50.2 1.2 %copy-start.2 = (bf16[16,256,128]{2,1,0:T(8,128)(2,1)S(1)}, bf16[16,256,128]{2,1,0:T(8,128)(2,1)}, u32[]{:S(2)}) copy-start(bf16[16,256,128]{2,1,0:T(8,128)(2,1)} %copy-done.1) | copy-start | bytes 3145732
  82.1 11.0 %collective-permute-start = (bf16[2,512,128]{2,1,0:T(8,128)(2,1)}, bf16[2,512,128]{2,1,0:T(8,128)(2,1)}, u32[]{:S(2)}, u32[]{:S(2)}) collective-permute-start(bf16[2,512,128]{2,1,0:T(8,128)(2,1)} %bitcast.19), channel_id=1, source_target_pairs={{1,2},{3,4},{5,6},{7,8},{9,10},{11,12},{13,14},{2,1},{4,3},{6,5},{... | collective-permute-start | bytes 786440 | tf_op jit(solution)/shard_map/ppermute | solution.py:238
  91.9 1.6 %collective-permute-start.1 = (bf16[2,512,128]{2,1,0:T(8,128)(2,1)S(1)}, bf16[2,512,128]{2,1,0:T(8,128)(2,1)S(1)}, u32[]{:S(2)}, u32[]{:S(2)}) collective-permute-start(bf16[2,512,128]{2,1,0:T(8,128)(2,1)S(1)} %bitcast.64), channel_id=1, source_target_pairs={{0,1},{1,0},{2,3},{3,2},{4,5},{5,4},{6,7},{7,6},{8,9},{9,8},{10,11... | collective-permute-start | bytes 786440 | tf_op jit(solution)/shard_map/ppermute | solution.py:239
  95.4 0.7 copy-start.6
  96.1 2.1 %copy-start.5 = (bf16[3,3,128,128]{3,2,1,0:T(8,128)(2,1)S(1)}, bf16[3,3,128,128]{3,2,1,0:T(8,128)(2,1)}, u32[]{:S(2)}) copy-start(bf16[3,3,128,128]{3,2,1,0:T(8,128)(2,1)} %param.9) | copy-start | bytes 884740

commit v21 on v19

--- a/solution.py
+++ b/solution.py
@@ -201,6 +201,8 @@
     flat_lists = tile_lists.reshape(1, -1)
     lists_everywhere = jnp.broadcast_to(flat_lists, (owners, flat_lists.shape[1]))
     lists_of = lax.all_to_all(lists_everywhere, "row", split_axis=0, concat_axis=0, tiled=True)
+    lists_of, frame_one_late = lax.optimization_barrier((lists_of, frame_one))
+    query_tiles = band_to_tiles(frame_one_late)
     mine = (lists_of >= 0) & (lists_of // per_device == me)
     asked = jnp.max(jnp.where(mine, lists_of % per_device, 0), axis=1)
     edges = [0, tile_size // 2, tile_size]

time: 101 us -> 101 us (level)
  no operation moved by 1% of the time
where the time goes in v21:
time: 101 us; the launch traced here: 99.8 us
  blocking collectives  30.4 us (30%)
  Pallas kernels  26.7 us (26%)
  starting transfers between devices  14.6 us (14%)
  waiting for transfers between devices  13.2 us (13%)
  local copies, waits for them, and re-layouts  6.43 us (6%)
  other arithmetic  4.85 us (5%)
  matrix products  3.47 us (3%)
    all_to_all x1, blocking collectives, on_device(): lax.all_to_all(sending, 'row', split_axis=0, concat_axis=0, tiled=True)  30.4 us
    pallas_call x1, Pallas kernels, attend_chunk(): pl.pallas_call(functools.partial(attend_kernel, scale=scale, first=first,...  13.9 us
    pallas_call x2, Pallas kernels, attend_last_half(): pl.pallas_call(kernel, grid_spec=grid_spec, out_shape=jax.ShapeDtypeStruc...  12.7 us
    all_to_all x1, waiting for transfers between devices, on_device(): lax.all_to_all(sending, 'row', split_axis=0, concat_axis=0, tiled=True)  9.36 us
    all_to_all x1, starting transfers between devices, on_device(): lax.all_to_all(lists_everywhere, 'row', split_axis=0, concat_axis=0, tile...  6.61 us
    all_to_all x1, starting transfers between devices, on_device(): lax.all_to_all(sending, 'row', split_axis=0, concat_axis=0, tiled=True)  4.51 us
    all_to_all x1, waiting for transfers between devices, on_device(): lax.all_to_all(lists_everywhere, 'row', split_axis=0, concat_axis=0, tile...  3.49 us
    conv_general_dilated x2, matrix products, native_conv(): lax.conv_general_dilated(rows[None], weights, window_strides=(1, 1), padd...  3.47 us
  transfers between devices with their start and end apart: 4, of which 3 were waited for; matrix products, arithmetic and copies ran while one was open for 3% of the time, Pallas kernels for 20%

profile of v21, /device:TPU:9, one launch (start us, length us, event | category | flops | bytes accessed | tf_op | source)
XLA Modules:
  0.0 99.8 jit_solution(16766742629640823576)
XLA Ops:
  0.0 0.0 copy-start
  0.0 0.8 broadcast_in_dim.130
  0.8 0.6 broadcast_in_dim.131
  1.4 6.6 %all-to-all-start = ((s32[16,1,36]{2,1,0:T(1,128)}), s32[16,1,36]{2,1,0:T(1,128)S(1)}, u32[]{:S(2)}, u32[]{:S(2)}) async-start(s32[16,1,36]{2,1,0:T(1,128)} %broadcast_in_dim.131), calls=%async_computation | async-start | bytes 16384 | tf_op jit(solution)/shard_map/all_to_all | solution.py:203
  8.0 1.1 %copy.39 = bf16[4,4,128,128]{3,2,1,0:T(8,128)(2,1)S(1)} copy(bf16[4,4,128,128]{3,2,0,1:T(8,128)(2,1)} %bitcast.65) | data formatting | bytes 1048576 | tf_op jit(solution)/shard_map/transpose | solution.py:191
  9.2 3.5 %all-to-all-done = s32[16,1,36]{2,1,0:T(1,128)S(1)} async-done(((s32[16,1,36]{2,1,0:T(1,128)}), s32[16,1,36]{2,1,0:T(1,128)S(1)}, u32[]{:S(2)}, u32[]{:S(2)}) %all-to-all-start) | async-done | bytes 2336 | tf_op jit(solution)/shard_map/all_to_all | solution.py:203
  12.6 0.1 fusion.29
  12.8 1.5 %select_select_fusion = (bf16[16,256,128]{2,1,0:T(8,128)(2,1)}, bf16[16,256,128]{2,1,0:T(8,128)(2,1)S(1)}) fusion(pred[16]{0:T(512)(128)(4,1)S(1)} %get-tuple-element.36, pred[16]{0:T(512)(128)(4,1)S(1)} %get-tuple-element.37, pred[16]{0:T(512)(128)(4,1)S(1)} %get-tuple-element.35, bf16[256,128]{1,0:T(8,128)(2,1)S(1)} %get-tuple-element.24, ...), kind=kLoop, calls=%fused_computation.19 | loop fusion | flops 3145728 | bytes 2621488 | tf_op jit(solution)/shard_map/jit(_where)/select_n | solution.py:215
  14.2 30.4 %all_to_all.19.k_ref = bf16[16,256,128]{2,1,0:T(8,128)(2,1)} all-to-all(bf16[16,256,128]{2,1,0:T(8,128)(2,1)S(1)} %get-tuple-element.34), channel_id=1, replica_groups=mesh['pairs'=2,'row'=16] {'row'}, dimensions={0} | all-to-all | bytes 2097152 | tf_op jit(solution)/shard_map/all_to_all | solution.py:218
  44.6 0.0 copy-start.3
  44.6 0.0 copy-start.2
  44.6 4.5 %all-to-all-start.2 = ((bf16[16,256,128]{2,1,0:T(8,128)(2,1)}), bf16[16,256,128]{2,1,0:T(8,128)(2,1)S(1)}, u32[]{:S(2)}, u32[]{:S(2)}) async-start(bf16[16,256,128]{2,1,0:T(8,128)(2,1)} %get-tuple-element.14), calls=%async_computation.2 | async-start | bytes 2097152 | tf_op jit(solution)/shard_map/all_to_all | solution.py:218
  49.1 0.0 copy-done.3
  49.1 0.1 slice_reduce_fusion
  49.2 0.1 fusion.32
  49.4 0.0 copy-done.2
  49.4 0.0 copy-start.1
  49.4 1.2 %copy-done.1 = bf16[16,256,128]{2,1,0:T(8,128)(2,1)S(1)} copy-done((bf16[16,256,128]{2,1,0:T(8,128)(2,1)S(1)}, bf16[16,256,128]{2,1,0:T(8,128)(2,1)}, u32[]{:S(2)}) %copy-start.1) | copy-done | bytes 1048600
  50.6 13.9 %shard_map.55 = (f32[4,1,512]{2,1,0:T(1,128)S(1)}, f32[4,1,512]{2,1,0:T(1,128)S(1)}, f32[4,512,128]{2,1,0:T(8,128)S(1)}) custom-call(s32[4,9]{1,0:T(4,128)S(1)} %get-tuple-element.32.owner_ref, s32[4]{0:T(128)S(1)} %get-tuple-element.31.count_ref, bf16[4,512,128]{2,1,0:T(8,128)(2,1)S(1)} %bitcast.54, bf16[16,256,128]{2,1,0:T(8,128)(2,1)S(1)} %copy-done.1), custom_call_target="tpu_custom_call" | custom-call | tf_op jit(solution)/shard_map/pallas_call | solution.py:140
  64.6 9.4 %all-to-all-done.2.refs_1_ = bf16[16,256,128]{2,1,0:T(8,128)(2,1)S(1)} async-done(((bf16[16,256,128]{2,1,0:T(8,128)(2,1)}), bf16[16,256,128]{2,1,0:T(8,128)(2,1)S(1)}, u32[]{:S(2)}, u32[]{:S(2)}) %all-to-all-start.2) | async-done | bytes 1048608 | tf_op jit(solution)/shard_map/all_to_all | solution.py:218
  74.0 6.4 %shard_map.56 = bf16[4,256,128]{2,1,0:T(8,128)(2,1)S(1)} custom-call(s32[4,9]{1,0:T(4,128)S(1)} %get-tuple-element.32.owner_ref, s32[4]{0:T(128)S(1)} %get-tuple-element.31.count_ref, s32[1]{0:T(128)} %bitcast.half_ref, bf16[4,512,128]{2,1,0:T(8,128)(2,1)S(1)} %bitcast.55, bf16[16,256,128]{2,1,0:T(8,128)(2,1)S(1)} %all-to-all-done.2.refs_1_, ...), custom_call_target="tpu_custom_call" | custom-call | tf_op jit(solution)/shard_map/pallas_call | solution.py:172
  80.3 0.7 copy.40
  81.1 3.4 %collective-permute-start = (bf16[2,512,128]{2,1,0:T(8,128)(2,1)}, bf16[2,512,128]{2,1,0:T(8,128)(2,1)}, u32[]{:S(2)}, u32[]{:S(2)}) collective-permute-start(bf16[2,512,128]{2,1,0:T(8,128)(2,1)} %bitcast.19), channel_id=1, source_target_pairs={{1,2},{3,4},{5,6},{7,8},{9,10},{11,12},{13,14},{2,1},{4,3},{6,5},{... | collective-permute-start | bytes 786440 | tf_op jit(solution)/shard_map/ppermute | solution.py:237
  84.5 6.4 %shard_map.57 = bf16[4,256,128]{2,1,0:T(8,128)(2,1)S(1)} custom-call(s32[4,9]{1,0:T(4,128)S(1)} %get-tuple-element.32.owner_ref, s32[4]{0:T(128)S(1)} %get-tuple-element.31.count_ref, s32[1]{0:T(128)S(6)} %sub.17.half_ref, bf16[4,512,128]{2,1,0:T(8,128)(2,1)S(1)} %bitcast.56, bf16[16,256,128]{2,1,0:T(8,128)(2,1)S(1)} %all-to-all-done.2.refs_1_, ...), custom_call_target="tpu_custom_call" | custom-call | tf_op jit(solution)/shard_map/pallas_call | solution.py:172
  90.9 0.1 collective-permute-start.1
  91.0 1.1 %maximum_select_fusion = bf16[4,512,128]{2,1,0:T(8,128)(2,1)S(1)} fusion(bf16[2,512,128]{2,1,0:T(8,128)(2,1)S(1)} %bitcast.64, bf16[2,512,128]{2,1,0:T(8,128)(2,1)} %bitcast.19, pred[]{:T(512)S(6)} %eq.37), kind=kLoop, calls=%fused_computation.31 | loop fusion | flops 786432 | bytes 1048577 | tf_op jit(solution)/shard_map/jit(_where)/select_n | solution.py:239
  92.1 0.0 collective-permute-done
  92.1 0.4 collective-permute-done.1
  92.5 1.0 broadcast_select_fusion.1
  93.5 0.1 maximum_bitcast_fusion
  93.6 0.7 copy.48
  94.3 0.1 pad.clone
  94.4 0.0 copy-start.5
  94.4 0.1 copy.44
  94.5 0.0 copy-done
  94.6 0.5 copy-done.5
  95.1 0.0 copy-start.4
  95.1 2.0 %fusion.5 = bf16[6,1,8,65,128]{4,2,3,0,1:T(8,128)(2,1)S(1)} fusion(bf16[3,3,128,128]{3,2,1,0:T(8,128)(2,1)S(1)} %copy-done, bf16[8,1,7,2,128]{4,2,3,0,1:T(8,128)(2,1)S(1)} %slice.58, bf16[8,1,8,65,128]{4,2,3,0,1:T(8,128)(2,1)S(1)} %copy.44, pred[6]{0:T(512)(128)(4,1)S(1)} %or_and_fusion, pred[8,65]{0,1:T(8,128)(4,1)S(1)} %copy-done.5), kind=kOutput, calls=%fused_computation.9 | convolution fusion | flops 925415424 | bytes 2187790 | tf_op jit(solution)/shard_map/conv_general_dilated | solution.py:40
  97.1 0.0 copy-done.4
  97.2 1.4 %fusion.16 = f32[4,8,65,128]{3,1,2,0:T(8,128)S(1)} fusion(bf16[3,3,128,128]{3,2,1,0:T(8,128)(2,1)S(1)} %copy-done.4, bf16[6,1,7,1,128]{4,2,3,0,1:T(8,128)(2,1)S(1)} %get-tuple-element.20, bf16[6,1,7,1,128]{4,2,3,0,1:T(8,128)(2,1)S(1)} %get-tuple-element.19, bf16[6,1,8,65,128]{4,2,3,0,1:T(8,128)(2,1)S(1)} %fusion.5), kind=kOutput, calls=%fused_computation.23 | convolution fusion | flops 617533440 | bytes 2180096 | tf_op jit(solution)/shard_map/conv_general_dilated | solution.py:40
  98.6 0.3 copy.45
  98.9 0.1 slice.61
  98.9 0.9 fusion.13
  (7 shorter events, 0.1 us)
Async XLA Ops:
  0.0 94.5 %copy-start = (bf16[3,3,128,128]{3,2,1,0:T(8,128)(2,1)S(1)}, bf16[3,3,128,128]{3,2,1,0:T(8,128)(2,1)}, u32[]{:S(2)}) copy-start(bf16[3,3,128,128]{3,2,1,0:T(8,128)(2,1)} %param.8) | copy-start | bytes 884740
  1.4 11.2 %all-to-all-start = ((s32[16,1,36]{2,1,0:T(1,128)}), s32[16,1,36]{2,1,0:T(1,128)S(1)}, u32[]{:S(2)}, u32[]{:S(2)}) async-start(s32[16,1,36]{2,1,0:T(1,128)} %broadcast_in_dim.131), calls=%async_computation | async-start | bytes 16384 | tf_op jit(solution)/shard_map/all_to_all | solution.py:203
  44.6 4.5 %copy-start.3 = (s32[4,9]{1,0:T(4,128)S(1)}, s32[4,9]{1,0:T(4,128)}, u32[]{:S(2)}) copy-start(s32[4,9]{1,0:T(4,128)} %param.7) | copy-start | bytes 436
  44.6 4.8 %copy-start.2 = (bf16[4,512,128]{2,1,0:T(8,128)(2,1)S(1)}, bf16[4,512,128]{2,1,0:T(8,128)(2,1)}, u32[]{:S(2)}) copy-start(bf16[4,512,128]{2,1,0:T(8,128)(2,1)} %param.5) | copy-start | bytes 1572868
  44.6 29.4 %all-to-all-start.2 = ((bf16[16,256,128]{2,1,0:T(8,128)(2,1)}), bf16[16,256,128]{2,1,0:T(8,128)(2,1)S(1)}, u32[]{:S(2)}, u32[]{:S(2)}) async-start(bf16[16,256,128]{2,1,0:T(8,128)(2,1)} %get-tuple-element.14), calls=%async_computation.2 | async-start | bytes 2097152 | tf_op jit(solution)/shard_map/all_to_all | solution.py:218
  49.4 1.2 %copy-start.1 = (bf16[16,256,128]{2,1,0:T(8,128)(2,1)S(1)}, bf16[16,256,128]{2,1,0:T(8,128)(2,1)}, u32[]{:S(2)}) copy-start(bf16[16,256,128]{2,1,0:T(8,128)(2,1)} %all_to_all.19.k_ref) | copy-start | bytes 3145732
  81.1 11.0 %collective-permute-start = (bf16[2,512,128]{2,1,0:T(8,128)(2,1)}, bf16[2,512,128]{2,1,0:T(8,128)(2,1)}, u32[]{:S(2)}, u32[]{:S(2)}) collective-permute-start(bf16[2,512,128]{2,1,0:T(8,128)(2,1)} %bitcast.19), channel_id=1, source_target_pairs={{1,2},{3,4},{5,6},{7,8},{9,10},{11,12},{13,14},{2,1},{4,3},{6,5},{... | collective-permute-start | bytes 786440 | tf_op jit(solution)/shard_map/ppermute | solution.py:237
  90.9 1.6 %collective-permute-start.1 = (bf16[2,512,128]{2,1,0:T(8,128)(2,1)S(1)}, bf16[2,512,128]{2,1,0:T(8,128)(2,1)S(1)}, u32[]{:S(2)}, u32[]{:S(2)}) collective-permute-start(bf16[2,512,128]{2,1,0:T(8,128)(2,1)S(1)} %bitcast.63), channel_id=1, source_target_pairs={{0,1},{1,0},{2,3},{3,2},{4,5},{5,4},{6,7},{7,6},{8,9},{9,8},{10,11... | collective-permute-start | bytes 786440 | tf_op jit(solution)/shard_map/ppermute | solution.py:238
  94.4 0.7 copy-start.5
  95.1 2.1 %copy-start.4 = (bf16[3,3,128,128]{3,2,1,0:T(8,128)(2,1)S(1)}, bf16[3,3,128,128]{3,2,1,0:T(8,128)(2,1)}, u32[]{:S(2)}) copy-start(bf16[3,3,128,128]{3,2,1,0:T(8,128)(2,1)} %param.9) | copy-start | bytes 884740

commit v22 on v19

--- a/solution.py
+++ b/solution.py
@@ -141,7 +141,7 @@
         functools.partial(attend_kernel, scale=scale, first=first, last=last),
         grid_spec=grid_spec,
         out_shape=out_shape,
-        compiler_params=pltpu.CompilerParams(vmem_limit_bytes=48 * 1024 * 1024),
+        compiler_params=pltpu.CompilerParams(vmem_limit_bytes=24 * 1024 * 1024),
     )(slot_owner, counts, queries, chunk, *([] if first else state))
 
 
@@ -173,7 +173,7 @@
         kernel,
         grid_spec=grid_spec,
         out_shape=jax.ShapeDtypeStruct((tiles, part, channels), jnp.bfloat16),
-        compiler_params=pltpu.CompilerParams(vmem_limit_bytes=48 * 1024 * 1024),
+        compiler_params=pltpu.CompilerParams(vmem_limit_bytes=24 * 1024 * 1024),
     )(slot_owner, counts, half, queries, chunk, *state)
 
 

time: 101 us -> 101 us (level)
  no operation moved by 1% of the time
where the time goes in v22:
time: 101 us; the launch traced here: 99.8 us
  blocking collectives  30.4 us (30%)
  Pallas kernels  26.7 us (26%)
  starting transfers between devices  14.6 us (14%)
  waiting for transfers between devices  13.2 us (13%)
  local copies, waits for them, and re-layouts  6.44 us (6%)
  other arithmetic  4.85 us (5%)
  matrix products  3.47 us (3%)
    all_to_all x1, blocking collectives, on_device(): lax.all_to_all(sending, 'row', split_axis=0, concat_axis=0, tiled=True)  30.4 us
    pallas_call x1, Pallas kernels, attend_chunk(): pl.pallas_call(functools.partial(attend_kernel, scale=scale, first=first,...  13.9 us
    pallas_call x2, Pallas kernels, attend_last_half(): pl.pallas_call(kernel, grid_spec=grid_spec, out_shape=jax.ShapeDtypeStruc...  12.7 us
    all_to_all x1, waiting for transfers between devices, on_device(): lax.all_to_all(sending, 'row', split_axis=0, concat_axis=0, tiled=True)  9.35 us
    all_to_all x1, starting transfers between devices, on_device(): lax.all_to_all(lists_everywhere, 'row', split_axis=0, concat_axis=0, tile...  6.61 us
    all_to_all x1, starting transfers between devices, on_device(): lax.all_to_all(sending, 'row', split_axis=0, concat_axis=0, tiled=True)  4.51 us
    all_to_all x1, waiting for transfers between devices, on_device(): lax.all_to_all(lists_everywhere, 'row', split_axis=0, concat_axis=0, tile...  3.49 us
    conv_general_dilated x2, matrix products, native_conv(): lax.conv_general_dilated(rows[None], weights, window_strides=(1, 1), padd...  3.47 us
  transfers between devices with their start and end apart: 4, of which 3 were waited for; matrix products, arithmetic and copies ran while one was open for 3% of the time, Pallas kernels for 20%

profile of v22, /device:TPU:9, one launch (start us, length us, event | category | flops | bytes accessed | tf_op | source)
XLA Modules:
  0.0 99.8 jit_solution(15994092046707467441)
XLA Ops:
  0.0 0.0 copy-start
  0.0 0.8 broadcast_in_dim.130
  0.8 0.6 broadcast_in_dim.131
  1.4 6.6 %all-to-all-start = ((s32[16,1,36]{2,1,0:T(1,128)}), s32[16,1,36]{2,1,0:T(1,128)S(1)}, u32[]{:S(2)}, u32[]{:S(2)}) async-start(s32[16,1,36]{2,1,0:T(1,128)} %broadcast_in_dim.131), calls=%async_computation | async-start | bytes 16384 | tf_op jit(solution)/shard_map/all_to_all | solution.py:203
  8.0 1.1 %copy.39 = bf16[4,4,128,128]{3,2,1,0:T(8,128)(2,1)S(1)} copy(bf16[4,4,128,128]{3,2,0,1:T(8,128)(2,1)} %bitcast.65) | data formatting | bytes 1048576 | tf_op jit(solution)/shard_map/transpose | solution.py:191
  9.2 3.5 %all-to-all-done = s32[16,1,36]{2,1,0:T(1,128)S(1)} async-done(((s32[16,1,36]{2,1,0:T(1,128)}), s32[16,1,36]{2,1,0:T(1,128)S(1)}, u32[]{:S(2)}, u32[]{:S(2)}) %all-to-all-start) | async-done | bytes 2336 | tf_op jit(solution)/shard_map/all_to_all | solution.py:203
  12.6 0.1 fusion.29
  12.8 1.5 %select_select_fusion = (bf16[16,256,128]{2,1,0:T(8,128)(2,1)}, bf16[16,256,128]{2,1,0:T(8,128)(2,1)S(1)}) fusion(pred[16]{0:T(512)(128)(4,1)S(1)} %get-tuple-element.32, pred[16]{0:T(512)(128)(4,1)S(1)} %get-tuple-element.33, pred[16]{0:T(512)(128)(4,1)S(1)} %get-tuple-element.31, bf16[256,128]{1,0:T(8,128)(2,1)S(1)} %get-tuple-element.20, ...), kind=kLoop, calls=%fused_computation.19 | loop fusion | flops 3145728 | bytes 2621488 | tf_op jit(solution)/shard_map/jit(_where)/select_n | solution.py:213
  14.2 30.4 %all_to_all.19.k_ref = bf16[16,256,128]{2,1,0:T(8,128)(2,1)} all-to-all(bf16[16,256,128]{2,1,0:T(8,128)(2,1)S(1)} %get-tuple-element.30), channel_id=1, replica_groups=mesh['pairs'=2,'row'=16] {'row'}, dimensions={0} | all-to-all | bytes 2097152 | tf_op jit(solution)/shard_map/all_to_all | solution.py:216
  44.6 0.0 copy-start.2
  44.6 0.0 copy-start.3
  44.6 4.5 %all-to-all-start.2 = ((bf16[16,256,128]{2,1,0:T(8,128)(2,1)}), bf16[16,256,128]{2,1,0:T(8,128)(2,1)S(1)}, u32[]{:S(2)}, u32[]{:S(2)}) async-start(bf16[16,256,128]{2,1,0:T(8,128)(2,1)} %get-tuple-element.10), calls=%async_computation.2 | async-start | bytes 2097152 | tf_op jit(solution)/shard_map/all_to_all | solution.py:216
  49.1 0.0 copy-done.2
  49.2 0.0 copy-done.3
  49.2 0.1 slice_reduce_fusion
  49.3 0.1 fusion.32
  49.4 0.0 copy-start.1
  49.4 1.2 %copy-done.1 = bf16[16,256,128]{2,1,0:T(8,128)(2,1)S(1)} copy-done((bf16[16,256,128]{2,1,0:T(8,128)(2,1)S(1)}, bf16[16,256,128]{2,1,0:T(8,128)(2,1)}, u32[]{:S(2)}) %copy-start.1) | copy-done | bytes 1048600
  50.7 13.9 %shard_map.55 = (f32[4,1,512]{2,1,0:T(1,128)S(1)}, f32[4,1,512]{2,1,0:T(1,128)S(1)}, f32[4,512,128]{2,1,0:T(8,128)S(1)}) custom-call(s32[4,9]{1,0:T(4,128)S(1)} %get-tuple-element.28.owner_ref, s32[4]{0:T(128)S(1)} %get-tuple-element.27.count_ref, bf16[4,512,128]{2,1,0:T(8,128)(2,1)S(1)} %bitcast.54, bf16[16,256,128]{2,1,0:T(8,128)(2,1)S(1)} %copy-done.1), custom_call_target="tpu_custom_call" | custom-call | tf_op jit(solution)/shard_map/pallas_call | solution.py:140
  64.6 9.4 %all-to-all-done.2.refs_1_ = bf16[16,256,128]{2,1,0:T(8,128)(2,1)S(1)} async-done(((bf16[16,256,128]{2,1,0:T(8,128)(2,1)}), bf16[16,256,128]{2,1,0:T(8,128)(2,1)S(1)}, u32[]{:S(2)}, u32[]{:S(2)}) %all-to-all-start.2) | async-done | bytes 1048608 | tf_op jit(solution)/shard_map/all_to_all | solution.py:216
  74.0 6.4 %shard_map.56 = bf16[4,256,128]{2,1,0:T(8,128)(2,1)S(1)} custom-call(s32[4,9]{1,0:T(4,128)S(1)} %get-tuple-element.28.owner_ref, s32[4]{0:T(128)S(1)} %get-tuple-element.27.count_ref, s32[1]{0:T(128)} %bitcast.half_ref, bf16[4,512,128]{2,1,0:T(8,128)(2,1)S(1)} %bitcast.55, bf16[16,256,128]{2,1,0:T(8,128)(2,1)S(1)} %all-to-all-done.2.refs_1_, ...), custom_call_target="tpu_custom_call" | custom-call | tf_op jit(solution)/shard_map/pallas_call | solution.py:172
  80.3 0.7 copy.40
  81.1 3.4 %collective-permute-start = (bf16[2,512,128]{2,1,0:T(8,128)(2,1)}, bf16[2,512,128]{2,1,0:T(8,128)(2,1)}, u32[]{:S(2)}, u32[]{:S(2)}) collective-permute-start(bf16[2,512,128]{2,1,0:T(8,128)(2,1)} %bitcast.19), channel_id=1, source_target_pairs={{1,2},{3,4},{5,6},{7,8},{9,10},{11,12},{13,14},{2,1},{4,3},{6,5},{... | collective-permute-start | bytes 786440 | tf_op jit(solution)/shard_map/ppermute | solution.py:235
  84.5 6.4 %shard_map.57 = bf16[4,256,128]{2,1,0:T(8,128)(2,1)S(1)} custom-call(s32[4,9]{1,0:T(4,128)S(1)} %get-tuple-element.28.owner_ref, s32[4]{0:T(128)S(1)} %get-tuple-element.27.count_ref, s32[1]{0:T(128)S(6)} %sub.17.half_ref, bf16[4,512,128]{2,1,0:T(8,128)(2,1)S(1)} %bitcast.56, bf16[16,256,128]{2,1,0:T(8,128)(2,1)S(1)} %all-to-all-done.2.refs_1_, ...), custom_call_target="tpu_custom_call" | custom-call | tf_op jit(solution)/shard_map/pallas_call | solution.py:172
  90.9 0.1 collective-permute-start.1
  91.0 1.1 %maximum_select_fusion = bf16[4,512,128]{2,1,0:T(8,128)(2,1)S(1)} fusion(bf16[2,512,128]{2,1,0:T(8,128)(2,1)S(1)} %bitcast.64, bf16[2,512,128]{2,1,0:T(8,128)(2,1)} %bitcast.19, pred[]{:T(512)S(6)} %eq.37), kind=kLoop, calls=%fused_computation.31 | loop fusion | flops 786432 | bytes 1048577 | tf_op jit(solution)/shard_map/jit(_where)/select_n | solution.py:237
  92.1 0.0 collective-permute-done
  92.1 0.4 collective-permute-done.1
  92.5 1.0 broadcast_select_fusion.1
  93.5 0.1 maximum_bitcast_fusion
  93.6 0.7 copy.48
  94.3 0.1 pad.clone
  94.4 0.0 copy-start.5
  94.4 0.1 copy.44
  94.5 0.0 copy-done
  94.6 0.5 copy-done.5
  95.1 0.0 copy-start.4
  95.1 2.0 %fusion.5 = bf16[6,1,8,65,128]{4,2,3,0,1:T(8,128)(2,1)S(1)} fusion(bf16[3,3,128,128]{3,2,1,0:T(8,128)(2,1)S(1)} %copy-done, bf16[8,1,7,2,128]{4,2,3,0,1:T(8,128)(2,1)S(1)} %slice.58, bf16[8,1,8,65,128]{4,2,3,0,1:T(8,128)(2,1)S(1)} %copy.44, pred[6]{0:T(512)(128)(4,1)S(1)} %or_and_fusion, pred[8,65]{0,1:T(8,128)(4,1)S(1)} %copy-done.5), kind=kOutput, calls=%fused_computation.9 | convolution fusion | flops 925415424 | bytes 2187790 | tf_op jit(solution)/shard_map/conv_general_dilated | solution.py:40
  97.1 0.0 copy-done.4
  97.2 1.4 %fusion.16 = f32[4,8,65,128]{3,1,2,0:T(8,128)S(1)} fusion(bf16[3,3,128,128]{3,2,1,0:T(8,128)(2,1)S(1)} %copy-done.4, bf16[6,1,7,1,128]{4,2,3,0,1:T(8,128)(2,1)S(1)} %get-tuple-element.16, bf16[6,1,7,1,128]{4,2,3,0,1:T(8,128)(2,1)S(1)} %get-tuple-element.15, bf16[6,1,8,65,128]{4,2,3,0,1:T(8,128)(2,1)S(1)} %fusion.5), kind=kOutput, calls=%fused_computation.23 | convolution fusion | flops 617533440 | bytes 2180096 | tf_op jit(solution)/shard_map/conv_general_dilated | solution.py:40
  98.6 0.3 copy.45
  98.9 0.1 slice.61
  98.9 0.9 fusion.13
  (7 shorter events, 0.1 us)
Async XLA Ops:
  0.0 94.5 %copy-start = (bf16[3,3,128,128]{3,2,1,0:T(8,128)(2,1)S(1)}, bf16[3,3,128,128]{3,2,1,0:T(8,128)(2,1)}, u32[]{:S(2)}) copy-start(bf16[3,3,128,128]{3,2,1,0:T(8,128)(2,1)} %param.8) | copy-start | bytes 884740
  1.4 11.2 %all-to-all-start = ((s32[16,1,36]{2,1,0:T(1,128)}), s32[16,1,36]{2,1,0:T(1,128)S(1)}, u32[]{:S(2)}, u32[]{:S(2)}) async-start(s32[16,1,36]{2,1,0:T(1,128)} %broadcast_in_dim.131), calls=%async_computation | async-start | bytes 16384 | tf_op jit(solution)/shard_map/all_to_all | solution.py:203
  44.6 4.5 %copy-start.2 = (bf16[4,512,128]{2,1,0:T(8,128)(2,1)S(1)}, bf16[4,512,128]{2,1,0:T(8,128)(2,1)}, u32[]{:S(2)}) copy-start(bf16[4,512,128]{2,1,0:T(8,128)(2,1)} %param.5) | copy-start | bytes 1572868
  44.6 4.6 %copy-start.3 = (s32[4,9]{1,0:T(4,128)S(1)}, s32[4,9]{1,0:T(4,128)}, u32[]{:S(2)}) copy-start(s32[4,9]{1,0:T(4,128)} %param.7) | copy-start | bytes 436
  44.6 29.4 %all-to-all-start.2 = ((bf16[16,256,128]{2,1,0:T(8,128)(2,1)}), bf16[16,256,128]{2,1,0:T(8,128)(2,1)S(1)}, u32[]{:S(2)}, u32[]{:S(2)}) async-start(bf16[16,256,128]{2,1,0:T(8,128)(2,1)} %get-tuple-element.10), calls=%async_computation.2 | async-start | bytes 2097152 | tf_op jit(solution)/shard_map/all_to_all | solution.py:216
  49.4 1.2 %copy-start.1 = (bf16[16,256,128]{2,1,0:T(8,128)(2,1)S(1)}, bf16[16,256,128]{2,1,0:T(8,128)(2,1)}, u32[]{:S(2)}) copy-start(bf16[16,256,128]{2,1,0:T(8,128)(2,1)} %all_to_all.19.k_ref) | copy-start | bytes 3145732
  81.1 11.0 %collective-permute-start = (bf16[2,512,128]{2,1,0:T(8,128)(2,1)}, bf16[2,512,128]{2,1,0:T(8,128)(2,1)}, u32[]{:S(2)}, u32[]{:S(2)}) collective-permute-start(bf16[2,512,128]{2,1,0:T(8,128)(2,1)} %bitcast.19), channel_id=1, source_target_pairs={{1,2},{3,4},{5,6},{7,8},{9,10},{11,12},{13,14},{2,1},{4,3},{6,5},{... | collective-permute-start | bytes 786440 | tf_op jit(solution)/shard_map/ppermute | solution.py:235
  90.9 1.6 %collective-permute-start.1 = (bf16[2,512,128]{2,1,0:T(8,128)(2,1)S(1)}, bf16[2,512,128]{2,1,0:T(8,128)(2,1)S(1)}, u32[]{:S(2)}, u32[]{:S(2)}) collective-permute-start(bf16[2,512,128]{2,1,0:T(8,128)(2,1)S(1)} %bitcast.63), channel_id=1, source_target_pairs={{0,1},{1,0},{2,3},{3,2},{4,5},{5,4},{6,7},{7,6},{8,9},{9,8},{10,11... | collective-permute-start | bytes 786440 | tf_op jit(solution)/shard_map/ppermute | solution.py:236
  94.4 0.7 copy-start.5
  95.1 2.1 %copy-start.4 = (bf16[3,3,128,128]{3,2,1,0:T(8,128)(2,1)S(1)}, bf16[3,3,128,128]{3,2,1,0:T(8,128)(2,1)}, u32[]{:S(2)}) copy-start(bf16[3,3,128,128]{3,2,1,0:T(8,128)(2,1)} %param.9) | copy-start | bytes 884740

commit v23 on v16

--- a/solution.py
+++ b/solution.py
@@ -207,7 +207,10 @@
     state = ()
     previous = None
     for index, (start, stop) in enumerate(zip(edges[:-1], edges[1:])):
-        sending = jnp.take(own_keys[:, start:stop], asked, axis=0)
+        part = own_keys[:, start:stop]
+        sending = jnp.broadcast_to(part[0][None], (owners,) + part.shape[1:])
+        for local in range(1, per_device):
+            sending = jnp.where((asked == local)[:, None, None], part[local][None], sending)
         if previous is not None:
             previous, sending, state = lax.optimization_barrier((previous, sending, state))
         current = lax.all_to_all(sending, "row", split_axis=0, concat_axis=0, tiled=True)

time: 102 us -> 101 us (level)
  local copies, waits for them, and re-layouts: 8.16 us -> 6.66 us
    gather x2 -> x0, local copies, waits for them, and re-layouts: 1.5 us -> none  [on_device(): sending = jnp.take(own_keys[:, start:stop], asked, axis=0)]
where the time goes in v23:
time: 101 us; the launch traced here: 100 us
  blocking collectives  30.3 us (30%)
  Pallas kernels  26.8 us (27%)
  starting transfers between devices  14.6 us (14%)
  waiting for transfers between devices  14.2 us (14%)
  local copies, waits for them, and re-layouts  6.66 us (7%)
  other arithmetic  3.81 us (4%)
  matrix products  3.5 us (3%)
    all_to_all x1, blocking collectives, on_device(): lax.all_to_all(sending, 'row', split_axis=0, concat_axis=0, tiled=True)  30.3 us
    pallas_call x1, Pallas kernels, attend_chunk(): pl.pallas_call(functools.partial(attend_kernel, scale=scale, first=first,...  13.9 us
    pallas_call x2, Pallas kernels, attend_last_half(): pl.pallas_call(kernel, grid_spec=grid_spec, out_shape=jax.ShapeDtypeStruc...  12.8 us
    all_to_all x1, waiting for transfers between devices, on_device(): lax.all_to_all(sending, 'row', split_axis=0, concat_axis=0, tiled=True)  9.35 us
    all_to_all x1, starting transfers between devices, on_device(): lax.all_to_all(lists_everywhere, 'row', split_axis=0, concat_axis=0, tile...  6.61 us
    all_to_all x1, starting transfers between devices, on_device(): lax.all_to_all(sending, 'row', split_axis=0, concat_axis=0, tiled=True)  4.51 us
    conv_general_dilated x2, matrix products, native_conv(): lax.conv_general_dilated(rows[None], weights, window_strides=(1, 1), padd...  3.5 us
    all_to_all x1, waiting for transfers between devices, on_device(): lax.all_to_all(lists_everywhere, 'row', split_axis=0, concat_axis=0, tile...  3.49 us
  transfers between devices with their start and end apart: 4, of which 4 were waited for; matrix products, arithmetic and copies ran while one was open for 1% of the time, Pallas kernels for 20%

profile of v23, /device:TPU:9, one launch (start us, length us, event | category | flops | bytes accessed | tf_op | source)
XLA Modules:
  0.0 100.2 jit_solution(7581538982200687014)
XLA Ops:
  0.0 0.0 copy-start
  0.0 0.8 broadcast_in_dim.130
  0.8 0.6 broadcast_in_dim.131
  1.4 6.6 %all-to-all-start = ((s32[16,1,36]{2,1,0:T(1,128)}), s32[16,1,36]{2,1,0:T(1,128)S(1)}, u32[]{:S(2)}, u32[]{:S(2)}) async-start(s32[16,1,36]{2,1,0:T(1,128)} %broadcast_in_dim.131), calls=%async_computation | async-start | bytes 16384 | tf_op jit(solution)/shard_map/all_to_all | solution.py:203
  8.0 1.1 %copy.35 = bf16[4,4,128,128]{3,2,1,0:T(8,128)(2,1)S(1)} copy(bf16[4,4,128,128]{3,2,0,1:T(8,128)(2,1)} %bitcast.53) | data formatting | bytes 1048576 | tf_op jit(solution)/shard_map/transpose | solution.py:191
  9.2 3.5 %all-to-all-done = s32[16,1,36]{2,1,0:T(1,128)S(1)} async-done(((s32[16,1,36]{2,1,0:T(1,128)}), s32[16,1,36]{2,1,0:T(1,128)S(1)}, u32[]{:S(2)}, u32[]{:S(2)}) %all-to-all-start) | async-done | bytes 2336 | tf_op jit(solution)/shard_map/all_to_all | solution.py:203
  12.6 0.1 fusion.29
  12.8 1.5 %select_select_fusion = (bf16[16,256,128]{2,1,0:T(8,128)(2,1)}, bf16[16,256,128]{2,1,0:T(8,128)(2,1)S(1)}) fusion(pred[16]{0:T(512)(128)(4,1)S(1)} %get-tuple-element.32, pred[16]{0:T(512)(128)(4,1)S(1)} %get-tuple-element.33, pred[16]{0:T(512)(128)(4,1)S(1)} %get-tuple-element.31, bf16[256,128]{1,0:T(8,128)(2,1)S(1)} %get-tuple-element.20, ...), kind=kLoop, calls=%fused_computation.19 | loop fusion | flops 3145728 | bytes 2621488 | tf_op jit(solution)/shard_map/jit(_where)/select_n | solution.py:213
  14.2 30.3 %all_to_all.19.k_ref = bf16[16,256,128]{2,1,0:T(8,128)(2,1)} all-to-all(bf16[16,256,128]{2,1,0:T(8,128)(2,1)S(1)} %get-tuple-element.30), channel_id=1, replica_groups=mesh['pairs'=2,'row'=16] {'row'}, dimensions={0} | all-to-all | bytes 2097152 | tf_op jit(solution)/shard_map/all_to_all | solution.py:216
  44.6 0.0 copy-start.2
  44.6 0.0 copy-start.4
  44.6 4.5 %all-to-all-start.2 = ((bf16[16,256,128]{2,1,0:T(8,128)(2,1)}), bf16[16,256,128]{2,1,0:T(8,128)(2,1)S(1)}, u32[]{:S(2)}, u32[]{:S(2)}) async-start(bf16[16,256,128]{2,1,0:T(8,128)(2,1)} %get-tuple-element.10), calls=%async_computation.2 | async-start | bytes 2097152 | tf_op jit(solution)/shard_map/all_to_all | solution.py:216
  49.1 0.0 copy-done.2
  49.1 0.0 copy-done.4
  49.2 0.1 slice_reduce_fusion
  49.3 0.1 fusion.32
  49.4 0.0 copy-start.1
  49.4 1.2 %copy-done.1 = bf16[16,256,128]{2,1,0:T(8,128)(2,1)S(1)} copy-done((bf16[16,256,128]{2,1,0:T(8,128)(2,1)S(1)}, bf16[16,256,128]{2,1,0:T(8,128)(2,1)}, u32[]{:S(2)}) %copy-start.1) | copy-done | bytes 1048600
  50.6 13.9 %shard_map.55 = (f32[4,1,512]{2,1,0:T(1,128)S(1)}, f32[4,1,512]{2,1,0:T(1,128)S(1)}, f32[4,512,128]{2,1,0:T(8,128)S(1)}) custom-call(s32[4,9]{1,0:T(4,128)S(1)} %get-tuple-element.28.owner_ref, s32[4]{0:T(128)S(1)} %get-tuple-element.27.count_ref, bf16[4,512,128]{2,1,0:T(8,128)(2,1)S(1)} %bitcast.46, bf16[16,256,128]{2,1,0:T(8,128)(2,1)S(1)} %copy-done.1), custom_call_target="tpu_custom_call" | custom-call | tf_op jit(solution)/shard_map/pallas_call | solution.py:140
  64.6 9.3 %all-to-all-done.2.refs_1_ = bf16[16,256,128]{2,1,0:T(8,128)(2,1)S(1)} async-done(((bf16[16,256,128]{2,1,0:T(8,128)(2,1)}), bf16[16,256,128]{2,1,0:T(8,128)(2,1)S(1)}, u32[]{:S(2)}, u32[]{:S(2)}) %all-to-all-start.2) | async-done | bytes 1048608 | tf_op jit(solution)/shard_map/all_to_all | solution.py:216
  73.9 6.4 %shard_map.56 = bf16[2,512,128]{2,1,0:T(8,128)(2,1)S(1)} custom-call(s32[4,9]{1,0:T(4,128)S(1)} %get-tuple-element.28.owner_ref, s32[4]{0:T(128)S(1)} %get-tuple-element.27.count_ref, s32[1]{0:T(128)} %bitcast.half_ref, bf16[4,512,128]{2,1,0:T(8,128)(2,1)S(1)} %bitcast.47, bf16[16,256,128]{2,1,0:T(8,128)(2,1)S(1)} %all-to-all-done.2.refs_1_, ...), custom_call_target="tpu_custom_call" | custom-call | tf_op jit(solution)/shard_map/pallas_call | solution.py:172
  80.4 3.4 %collective-permute-start = (bf16[2,512,128]{2,1,0:T(8,128)(2,1)S(1)}, bf16[2,512,128]{2,1,0:T(8,128)(2,1)}, u32[]{:S(2)}, u32[]{:S(2)}) collective-permute-start(bf16[2,512,128]{2,1,0:T(8,128)(2,1)S(1)} %shard_map.56), channel_id=1, source_target_pairs={{1,2},{3,4},{5,6},{7,8},{9,10},{11,12},{13,14},{2,1},{4,3},{6,5},{... | collective-permute-start | bytes 786440 | tf_op jit(solution)/shard_map/ppermute | solution.py:232
  83.8 6.4 %shard_map.57 = bf16[2,512,128]{2,1,0:T(8,128)(2,1)S(1)} custom-call(s32[4,9]{1,0:T(4,128)S(1)} %get-tuple-element.28.owner_ref, s32[4]{0:T(128)S(1)} %get-tuple-element.27.count_ref, s32[1]{0:T(128)S(6)} %sub.17.half_ref, bf16[4,512,128]{2,1,0:T(8,128)(2,1)S(1)} %bitcast.48, bf16[16,256,128]{2,1,0:T(8,128)(2,1)S(1)} %all-to-all-done.2.refs_1_, ...), custom_call_target="tpu_custom_call" | custom-call | tf_op jit(solution)/shard_map/pallas_call | solution.py:172
  90.2 0.1 collective-permute-start.1
  90.3 0.1 maximum_select_fusion
  90.4 0.5 collective-permute-done
  90.9 0.9 collective-permute-done.1
  91.8 1.0 broadcast_select_fusion.1
  92.8 0.1 maximum_bitcast_fusion
  92.9 0.7 copy.42
  93.6 0.1 pad.clone
  93.7 0.0 copy-start.6
  93.7 0.1 copy.38
  93.9 0.0 copy-done
  93.9 0.5 copy-done.6
  94.4 0.0 copy-start.5
  94.4 2.1 %fusion.5 = bf16[6,1,8,65,128]{4,2,3,0,1:T(8,128)(2,1)S(1)} fusion(bf16[3,3,128,128]{3,2,1,0:T(8,128)(2,1)S(1)} %copy-done, bf16[8,1,7,2,128]{4,2,3,0,1:T(8,128)(2,1)S(1)} %slice.58, bf16[8,1,8,65,128]{4,2,3,0,1:T(8,128)(2,1)S(1)} %copy.38, pred[6]{0:T(512)(128)(4,1)S(1)} %or_and_fusion, pred[8,65]{0,1:T(8,128)(4,1)S(1)} %copy-done.6), kind=kOutput, calls=%fused_computation.9 | convolution fusion | flops 925415424 | bytes 2187790 | tf_op jit(solution)/shard_map/conv_general_dilated | solution.py:40
  96.5 0.0 copy-done.5
  96.5 1.4 %fusion.16 = f32[4,8,65,128]{3,1,2,0:T(8,128)S(1)} fusion(bf16[3,3,128,128]{3,2,1,0:T(8,128)(2,1)S(1)} %copy-done.5, bf16[6,1,7,1,128]{4,2,3,0,1:T(8,128)(2,1)S(1)} %get-tuple-element.16, bf16[6,1,7,1,128]{4,2,3,0,1:T(8,128)(2,1)S(1)} %get-tuple-element.15, bf16[6,1,8,65,128]{4,2,3,0,1:T(8,128)(2,1)S(1)} %fusion.5), kind=kOutput, calls=%fused_computation.23 | convolution fusion | flops 617533440 | bytes 2180096 | tf_op jit(solution)/shard_map/conv_general_dilated | solution.py:40
  98.0 0.3 copy.39
  98.2 0.0 copy-start.3
  98.3 0.1 slice.61
  98.3 1.0 copy-done.3
  99.3 0.9 fusion.13
  (6 shorter events, 0.1 us)
Async XLA Ops:
  0.0 93.9 %copy-start = (bf16[3,3,128,128]{3,2,1,0:T(8,128)(2,1)S(1)}, bf16[3,3,128,128]{3,2,1,0:T(8,128)(2,1)}, u32[]{:S(2)}) copy-start(bf16[3,3,128,128]{3,2,1,0:T(8,128)(2,1)} %param.8) | copy-start | bytes 884740
  1.4 11.2 %all-to-all-start = ((s32[16,1,36]{2,1,0:T(1,128)}), s32[16,1,36]{2,1,0:T(1,128)S(1)}, u32[]{:S(2)}, u32[]{:S(2)}) async-start(s32[16,1,36]{2,1,0:T(1,128)} %broadcast_in_dim.131), calls=%async_computation | async-start | bytes 16384 | tf_op jit(solution)/shard_map/all_to_all | solution.py:203
  44.6 4.5 %copy-start.2 = (bf16[4,512,128]{2,1,0:T(8,128)(2,1)S(1)}, bf16[4,512,128]{2,1,0:T(8,128)(2,1)}, u32[]{:S(2)}) copy-start(bf16[4,512,128]{2,1,0:T(8,128)(2,1)} %param.5) | copy-start | bytes 1572868
  44.6 4.6 %copy-start.4 = (s32[4,9]{1,0:T(4,128)S(1)}, s32[4,9]{1,0:T(4,128)}, u32[]{:S(2)}) copy-start(s32[4,9]{1,0:T(4,128)} %param.7) | copy-start | bytes 436
  44.6 29.4 %all-to-all-start.2 = ((bf16[16,256,128]{2,1,0:T(8,128)(2,1)}), bf16[16,256,128]{2,1,0:T(8,128)(2,1)S(1)}, u32[]{:S(2)}, u32[]{:S(2)}) async-start(bf16[16,256,128]{2,1,0:T(8,128)(2,1)} %get-tuple-element.10), calls=%async_computation.2 | async-start | bytes 2097152 | tf_op jit(solution)/shard_map/all_to_all | solution.py:216
  49.4 1.2 %copy-start.1 = (bf16[16,256,128]{2,1,0:T(8,128)(2,1)S(1)}, bf16[16,256,128]{2,1,0:T(8,128)(2,1)}, u32[]{:S(2)}) copy-start(bf16[16,256,128]{2,1,0:T(8,128)(2,1)} %all_to_all.19.k_ref) | copy-start | bytes 3145732
  80.4 10.6 %collective-permute-start = (bf16[2,512,128]{2,1,0:T(8,128)(2,1)S(1)}, bf16[2,512,128]{2,1,0:T(8,128)(2,1)}, u32[]{:S(2)}, u32[]{:S(2)}) collective-permute-start(bf16[2,512,128]{2,1,0:T(8,128)(2,1)S(1)} %shard_map.56), channel_id=1, source_target_pairs={{1,2},{3,4},{5,6},{7,8},{9,10},{11,12},{13,14},{2,1},{4,3},{6,5},{... | collective-permute-start | bytes 786440 | tf_op jit(solution)/shard_map/ppermute | solution.py:232
  90.2 1.6 %collective-permute-start.1 = (bf16[2,512,128]{2,1,0:T(8,128)(2,1)S(1)}, bf16[2,512,128]{2,1,0:T(8,128)(2,1)S(1)}, u32[]{:S(2)}, u32[]{:S(2)}) collective-permute-start(bf16[2,512,128]{2,1,0:T(8,128)(2,1)S(1)} %shard_map.57), channel_id=1, source_target_pairs={{0,1},{1,0},{2,3},{3,2},{4,5},{5,4},{6,7},{7,6},{8,9},{9,8},{10,11... | collective-permute-start | bytes 786440 | tf_op jit(solution)/shard_map/ppermute | solution.py:233
  93.7 0.7 copy-start.6
  94.4 2.1 %copy-start.5 = (bf16[3,3,128,128]{3,2,1,0:T(8,128)(2,1)S(1)}, bf16[3,3,128,128]{3,2,1,0:T(8,128)(2,1)}, u32[]{:S(2)}) copy-start(bf16[3,3,128,128]{3,2,1,0:T(8,128)(2,1)} %param.9) | copy-start | bytes 884740
  98.2 1.0 %copy-start.3 = (bf16[4,512,128]{2,1,0:T(8,128)(2,1)S(1)}, bf16[4,512,128]{2,1,0:T(8,128)(2,1)}, u32[]{:S(2)}) copy-start(bf16[4,512,128]{2,1,0:T(8,128)(2,1)} %param.5) | copy-start | bytes 1572868

commit v24 on v19

--- a/solution.py
+++ b/solution.py
@@ -198,9 +198,9 @@
     slot_owner = jnp.maximum(jnp.where(valid, tile_lists, tile_lists[:, :1]), 0) // per_device
     counts = jnp.sum(valid.astype(jnp.int32), axis=1)
     me = lax.axis_index("row")
-    flat_lists = tile_lists.reshape(1, -1)
-    lists_everywhere = jnp.broadcast_to(flat_lists, (owners, flat_lists.shape[1]))
+    lists_everywhere = jnp.tile(tile_lists, (owners, 1))
     lists_of = lax.all_to_all(lists_everywhere, "row", split_axis=0, concat_axis=0, tiled=True)
+    lists_of = lists_of.reshape(owners, -1)
     mine = (lists_of >= 0) & (lists_of // per_device == me)
     asked = jnp.max(jnp.where(mine, lists_of % per_device, 0), axis=1)
     edges = [0, tile_size // 2, tile_size]

time: 101 us -> 101 us (level)
    broadcast_in_dim x2 -> x0, local copies, waits for them, and re-layouts: 1.41 us -> none  [on_device(): jnp.broadcast_to(flat_lists, (owners, flat_lists.shape[1]))]
    another operation x0 -> x1, local copies, waits for them, and re-layouts: none -> 1.34 us  [on_device(): lists_everywhere = jnp.tile(tile_lists, (owners, 1))]
where the time goes in v24:
time: 101 us; the launch traced here: 100 us
  blocking collectives  30.3 us (30%)
  Pallas kernels  26.7 us (26%)
  starting transfers between devices  14.6 us (14%)
  waiting for transfers between devices  13.6 us (13%)
  local copies, waits for them, and re-layouts  6.37 us (6%)
  other arithmetic  5.12 us (5%)
  matrix products  3.47 us (3%)
    all_to_all x1, blocking collectives, on_device(): lax.all_to_all(sending, 'row', split_axis=0, concat_axis=0, tiled=True)  30.3 us
    pallas_call x1, Pallas kernels, attend_chunk(): pl.pallas_call(functools.partial(attend_kernel, scale=scale, first=first,...  13.9 us
    pallas_call x2, Pallas kernels, attend_last_half(): pl.pallas_call(kernel, grid_spec=grid_spec, out_shape=jax.ShapeDtypeStruc...  12.8 us
    all_to_all x1, waiting for transfers between devices, on_device(): lax.all_to_all(sending, 'row', split_axis=0, concat_axis=0, tiled=True)  9.35 us
    all_to_all x1, starting transfers between devices, on_device(): lax.all_to_all(lists_everywhere, 'row', split_axis=0, concat_axis=0, tile...  6.61 us
    all_to_all x1, starting transfers between devices, on_device(): lax.all_to_all(sending, 'row', split_axis=0, concat_axis=0, tiled=True)  4.51 us
    all_to_all x1, waiting for transfers between devices, on_device(): lax.all_to_all(lists_everywhere, 'row', split_axis=0, concat_axis=0, tile...  3.89 us
    conv_general_dilated x2, matrix products, native_conv(): lax.conv_general_dilated(rows[None], weights, window_strides=(1, 1), padd...  3.47 us
  transfers between devices with their start and end apart: 4, of which 3 were waited for; matrix products, arithmetic and copies ran while one was open for 3% of the time, Pallas kernels for 20%

profile of v24, /device:TPU:9, one launch (start us, length us, event | category | flops | bytes accessed | tf_op | source)
XLA Modules:
  0.0 100.4 jit_solution(1340325954952282880)
XLA Ops:
  0.0 0.0 copy-start
  0.0 1.3 %tile.2 = s32[16,4,9]{2,1,0:T(4,128)} broadcast(s32[4,9]{1,0:T(4,128)} %param.7), dimensions={1,2} | broadcast | bytes 2448 | tf_op jit(solution)/shard_map/tile | solution.py:201
  1.3 6.6 %all-to-all-start = ((s32[16,4,9]{2,1,0:T(4,128)}), s32[16,4,9]{2,1,0:T(4,128)S(1)}, u32[]{:S(2)}, u32[]{:S(2)}) async-start(s32[16,4,9]{2,1,0:T(4,128)} %tile.2), calls=%async_computation | async-start | bytes 65536 | tf_op jit(solution)/shard_map/all_to_all | solution.py:202
  8.0 1.1 %copy.54 = bf16[4,4,128,128]{3,2,1,0:T(8,128)(2,1)S(1)} copy(bf16[4,4,128,128]{3,2,0,1:T(8,128)(2,1)} %bitcast.64) | data formatting | bytes 1048576 | tf_op jit(solution)/shard_map/transpose | solution.py:191
  9.1 3.9 %all-to-all-done = s32[16,4,9]{2,1,0:T(4,128)S(1)} async-done(((s32[16,4,9]{2,1,0:T(4,128)}), s32[16,4,9]{2,1,0:T(4,128)S(1)}, u32[]{:S(2)}, u32[]{:S(2)}) %all-to-all-start) | async-done | bytes 2336 | tf_op jit(solution)/shard_map/all_to_all | solution.py:202
  13.0 0.4 fusion.29
  13.4 1.5 %select_select_fusion = (bf16[16,256,128]{2,1,0:T(8,128)(2,1)}, bf16[16,256,128]{2,1,0:T(8,128)(2,1)S(1)}) fusion(pred[16]{0:T(512)(128)(4,1)S(1)} %get-tuple-element.33, pred[16]{0:T(512)(128)(4,1)S(1)} %get-tuple-element.32, pred[16]{0:T(512)(128)(4,1)S(1)} %get-tuple-element.31, bf16[256,128]{1,0:T(8,128)(2,1)S(1)} %get-tuple-element.20, ...), kind=kLoop, calls=%fused_computation.19 | loop fusion | flops 3145728 | bytes 2621488 | tf_op jit(solution)/shard_map/jit(_where)/select_n | solution.py:213
  14.8 30.3 %all_to_all.16.k_ref = bf16[16,256,128]{2,1,0:T(8,128)(2,1)} all-to-all(bf16[16,256,128]{2,1,0:T(8,128)(2,1)S(1)} %get-tuple-element.30), channel_id=1, replica_groups=mesh['pairs'=2,'row'=16] {'row'}, dimensions={0} | all-to-all | bytes 2097152 | tf_op jit(solution)/shard_map/all_to_all | solution.py:216
  45.1 0.0 copy-start.2
  45.1 0.0 copy-start.3
  45.1 4.5 %all-to-all-start.2 = ((bf16[16,256,128]{2,1,0:T(8,128)(2,1)}), bf16[16,256,128]{2,1,0:T(8,128)(2,1)S(1)}, u32[]{:S(2)}, u32[]{:S(2)}) async-start(bf16[16,256,128]{2,1,0:T(8,128)(2,1)} %get-tuple-element.10), calls=%async_computation.2 | async-start | bytes 2097152 | tf_op jit(solution)/shard_map/all_to_all | solution.py:216
  49.6 0.0 copy-done.2
  49.7 0.0 copy-done.3
  49.7 0.1 slice_reduce_fusion
  49.8 0.1 fusion.32
  49.9 0.0 copy-start.1
  49.9 1.2 %copy-done.1 = bf16[16,256,128]{2,1,0:T(8,128)(2,1)S(1)} copy-done((bf16[16,256,128]{2,1,0:T(8,128)(2,1)S(1)}, bf16[16,256,128]{2,1,0:T(8,128)(2,1)}, u32[]{:S(2)}) %copy-start.1) | copy-done | bytes 1048600
  51.2 13.9 %shard_map.55 = (f32[4,1,512]{2,1,0:T(1,128)S(1)}, f32[4,1,512]{2,1,0:T(1,128)S(1)}, f32[4,512,128]{2,1,0:T(8,128)S(1)}) custom-call(s32[4,9]{1,0:T(4,128)S(1)} %get-tuple-element.28.owner_ref, s32[4]{0:T(128)S(1)} %get-tuple-element.27.count_ref, bf16[4,512,128]{2,1,0:T(8,128)(2,1)S(1)} %bitcast.53, bf16[16,256,128]{2,1,0:T(8,128)(2,1)S(1)} %copy-done.1), custom_call_target="tpu_custom_call" | custom-call | tf_op jit(solution)/shard_map/pallas_call | solution.py:140
  65.1 9.4 %all-to-all-done.2.refs_1_ = bf16[16,256,128]{2,1,0:T(8,128)(2,1)S(1)} async-done(((bf16[16,256,128]{2,1,0:T(8,128)(2,1)}), bf16[16,256,128]{2,1,0:T(8,128)(2,1)S(1)}, u32[]{:S(2)}, u32[]{:S(2)}) %all-to-all-start.2) | async-done | bytes 1048608 | tf_op jit(solution)/shard_map/all_to_all | solution.py:216
  74.5 6.4 %shard_map.56 = bf16[4,256,128]{2,1,0:T(8,128)(2,1)S(1)} custom-call(s32[4,9]{1,0:T(4,128)S(1)} %get-tuple-element.28.owner_ref, s32[4]{0:T(128)S(1)} %get-tuple-element.27.count_ref, s32[1]{0:T(128)} %bitcast.half_ref, bf16[4,512,128]{2,1,0:T(8,128)(2,1)S(1)} %bitcast.54, bf16[16,256,128]{2,1,0:T(8,128)(2,1)S(1)} %all-to-all-done.2.refs_1_, ...), custom_call_target="tpu_custom_call" | custom-call | tf_op jit(solution)/shard_map/pallas_call | solution.py:172
  80.8 0.7 copy.55
  81.6 3.4 %collective-permute-start = (bf16[2,512,128]{2,1,0:T(8,128)(2,1)}, bf16[2,512,128]{2,1,0:T(8,128)(2,1)}, u32[]{:S(2)}, u32[]{:S(2)}) collective-permute-start(bf16[2,512,128]{2,1,0:T(8,128)(2,1)} %bitcast.18), channel_id=1, source_target_pairs={{1,2},{3,4},{5,6},{7,8},{9,10},{11,12},{13,14},{2,1},{4,3},{6,5},{... | collective-permute-start | bytes 786440 | tf_op jit(solution)/shard_map/ppermute | solution.py:235
  85.0 6.4 %shard_map.57 = bf16[4,256,128]{2,1,0:T(8,128)(2,1)S(1)} custom-call(s32[4,9]{1,0:T(4,128)S(1)} %get-tuple-element.28.owner_ref, s32[4]{0:T(128)S(1)} %get-tuple-element.27.count_ref, s32[1]{0:T(128)S(6)} %sub.17.half_ref, bf16[4,512,128]{2,1,0:T(8,128)(2,1)S(1)} %bitcast.55, bf16[16,256,128]{2,1,0:T(8,128)(2,1)S(1)} %all-to-all-done.2.refs_1_, ...), custom_call_target="tpu_custom_call" | custom-call | tf_op jit(solution)/shard_map/pallas_call | solution.py:172
  91.4 0.1 collective-permute-start.1
  91.5 1.1 %maximum_select_fusion = bf16[4,512,128]{2,1,0:T(8,128)(2,1)S(1)} fusion(bf16[2,512,128]{2,1,0:T(8,128)(2,1)S(1)} %bitcast.63, bf16[2,512,128]{2,1,0:T(8,128)(2,1)} %bitcast.18, pred[]{:T(512)S(6)} %eq.39), kind=kLoop, calls=%fused_computation.31 | loop fusion | flops 786432 | bytes 1048577 | tf_op jit(solution)/shard_map/jit(_where)/select_n | solution.py:237
  92.6 0.0 collective-permute-done
  92.6 0.4 collective-permute-done.1
  93.0 1.0 broadcast_select_fusion.1
  94.0 0.1 maximum_bitcast_fusion
  94.1 0.7 copy.64
  94.8 0.1 pad.clone
  94.9 0.0 copy-start.5
  94.9 0.1 copy.59
  95.1 0.0 copy-done
  95.1 0.5 copy-done.5
  95.6 0.0 copy-start.4
  95.6 2.0 %fusion.5 = bf16[6,1,8,65,128]{4,2,3,0,1:T(8,128)(2,1)S(1)} fusion(bf16[3,3,128,128]{3,2,1,0:T(8,128)(2,1)S(1)} %copy-done, bf16[8,1,7,2,128]{4,2,3,0,1:T(8,128)(2,1)S(1)} %slice.58, bf16[8,1,8,65,128]{4,2,3,0,1:T(8,128)(2,1)S(1)} %copy.59, pred[6]{0:T(512)(128)(4,1)S(1)} %or_and_fusion, pred[8,65]{0,1:T(8,128)(4,1)S(1)} %copy-done.5), kind=kOutput, calls=%fused_computation.9 | convolution fusion | flops 925415424 | bytes 2187790 | tf_op jit(solution)/shard_map/conv_general_dilated | solution.py:40
  97.7 0.0 copy-done.4
  97.7 1.4 %fusion.16 = f32[4,8,65,128]{3,1,2,0:T(8,128)S(1)} fusion(bf16[3,3,128,128]{3,2,1,0:T(8,128)(2,1)S(1)} %copy-done.4, bf16[6,1,7,1,128]{4,2,3,0,1:T(8,128)(2,1)S(1)} %get-tuple-element.16, bf16[6,1,7,1,128]{4,2,3,0,1:T(8,128)(2,1)S(1)} %get-tuple-element.15, bf16[6,1,8,65,128]{4,2,3,0,1:T(8,128)(2,1)S(1)} %fusion.5), kind=kOutput, calls=%fused_computation.23 | convolution fusion | flops 617533440 | bytes 2180096 | tf_op jit(solution)/shard_map/conv_general_dilated | solution.py:40
  99.1 0.3 copy.60
  99.4 0.1 slice.61
  99.5 0.9 fusion.13
  (7 shorter events, 0.1 us)
Async XLA Ops:
  0.0 95.1 %copy-start = (bf16[3,3,128,128]{3,2,1,0:T(8,128)(2,1)S(1)}, bf16[3,3,128,128]{3,2,1,0:T(8,128)(2,1)}, u32[]{:S(2)}) copy-start(bf16[3,3,128,128]{3,2,1,0:T(8,128)(2,1)} %param.8) | copy-start | bytes 884740
  1.3 11.6 %all-to-all-start = ((s32[16,4,9]{2,1,0:T(4,128)}), s32[16,4,9]{2,1,0:T(4,128)S(1)}, u32[]{:S(2)}, u32[]{:S(2)}) async-start(s32[16,4,9]{2,1,0:T(4,128)} %tile.2), calls=%async_computation | async-start | bytes 65536 | tf_op jit(solution)/shard_map/all_to_all | solution.py:202
  45.1 4.5 %copy-start.2 = (bf16[4,512,128]{2,1,0:T(8,128)(2,1)S(1)}, bf16[4,512,128]{2,1,0:T(8,128)(2,1)}, u32[]{:S(2)}) copy-start(bf16[4,512,128]{2,1,0:T(8,128)(2,1)} %param.5) | copy-start | bytes 1572868
  45.1 4.6 %copy-start.3 = (s32[4,9]{1,0:T(4,128)S(1)}, s32[4,9]{1,0:T(4,128)}, u32[]{:S(2)}) copy-start(s32[4,9]{1,0:T(4,128)} %param.7) | copy-start | bytes 436
  45.1 29.4 %all-to-all-start.2 = ((bf16[16,256,128]{2,1,0:T(8,128)(2,1)}), bf16[16,256,128]{2,1,0:T(8,128)(2,1)S(1)}, u32[]{:S(2)}, u32[]{:S(2)}) async-start(bf16[16,256,128]{2,1,0:T(8,128)(2,1)} %get-tuple-element.10), calls=%async_computation.2 | async-start | bytes 2097152 | tf_op jit(solution)/shard_map/all_to_all | solution.py:216
  49.9 1.2 %copy-start.1 = (bf16[16,256,128]{2,1,0:T(8,128)(2,1)S(1)}, bf16[16,256,128]{2,1,0:T(8,128)(2,1)}, u32[]{:S(2)}) copy-start(bf16[16,256,128]{2,1,0:T(8,128)(2,1)} %all_to_all.16.k_ref) | copy-start | bytes 3145732
  81.6 11.0 %collective-permute-start = (bf16[2,512,128]{2,1,0:T(8,128)(2,1)}, bf16[2,512,128]{2,1,0:T(8,128)(2,1)}, u32[]{:S(2)}, u32[]{:S(2)}) collective-permute-start(bf16[2,512,128]{2,1,0:T(8,128)(2,1)} %bitcast.18), channel_id=1, source_target_pairs={{1,2},{3,4},{5,6},{7,8},{9,10},{11,12},{13,14},{2,1},{4,3},{6,5},{... | collective-permute-start | bytes 786440 | tf_op jit(solution)/shard_map/ppermute | solution.py:235
  91.4 1.6 %collective-permute-start.1 = (bf16[2,512,128]{2,1,0:T(8,128)(2,1)S(1)}, bf16[2,512,128]{2,1,0:T(8,128)(2,1)S(1)}, u32[]{:S(2)}, u32[]{:S(2)}) collective-permute-start(bf16[2,512,128]{2,1,0:T(8,128)(2,1)S(1)} %bitcast.62), channel_id=1, source_target_pairs={{0,1},{1,0},{2,3},{3,2},{4,5},{5,4},{6,7},{7,6},{8,9},{9,8},{10,11... | collective-permute-start | bytes 786440 | tf_op jit(solution)/shard_map/ppermute | solution.py:236
  94.9 0.7 copy-start.5
  95.6 2.1 %copy-start.4 = (bf16[3,3,128,128]{3,2,1,0:T(8,128)(2,1)S(1)}, bf16[3,3,128,128]{3,2,1,0:T(8,128)(2,1)}, u32[]{:S(2)}) copy-start(bf16[3,3,128,128]{3,2,1,0:T(8,128)(2,1)} %param.9) | copy-start | bytes 884740
